TPU v7x, 128 devices: a whole 4x4x4 slice. The times are simulated.
128 devices in a mesh: seq: 16 (over y, x), tp: 8 (over z, core).
Axes of the slice: x: 4, y: 4, z: 4, core: 2. Of those that a mesh axis runs over, the one named last changes fastest.
Arguments:
- tokens: bfloat16 [24576, 2048], P('seq'), may hold values from -6 to 6
- w_query: bfloat16 [2048, 2048], P(None, 'tp'), may hold values from -0.125 to 0.125
- w_key: bfloat16 [2048, 2048], P(None, 'tp'), may hold values from -0.125 to 0.125
- w_value: bfloat16 [2048, 2048], P(None, 'tp'), may hold values from -0.125 to 0.125
- w_out: bfloat16 [2048, 2048], P('tp'), may hold values from -0.125 to 0.125
- readers: int32 [192, 192], replicated, may hold values from 0 to 1, as said below
- lengths: int32 [192], replicated, may hold values from 1 to 128, as said below
Outputs:
- attended: bfloat16 [24576, 2048], P('seq', 'tp')
Inputs may be any that keep to these rules, and one draw needn't show every extreme that they name: The groups form sessions of consecutive groups, the first starting at group 0; readers[c, e] is 1 exactly where e < c and e lies in the same session as c. lengths[c] is 128 on every group but the last of its session; at least one group has 128 live tokens and one has a single one.
All inputs are finite; a program needn't handle non-finite values.
Results may differ from a plain program's by a relative error of at most 0.009.
Values may be sent and summed in bfloat16 or wider, within the bound.
No kernel may reach another device: no remote copies, remote signals or barrier semaphores. Data moves between devices by JAX's collectives and lax.ppermute only.
A program may use at most 128 MiB of HBM per device.

v0:
```python
import jax
import jax.numpy as jnp
from jax import lax
from jax.sharding import PartitionSpec as P

HS = 128
CH = 128


def group_states(key_blocks, value_blocks):
    return jnp.einsum(
        "cshd,cshe->chde", key_blocks, value_blocks, preferred_element_type=jnp.float32
    ).astype(jnp.bfloat16)


def local(tokens, w_query, w_key, w_value, w_out, readers, lengths):
    group_local = tokens.shape[0] // CH
    local_width = w_query.shape[1]
    head_dev = local_width // HS
    first_group = lax.axis_index("seq") * group_local
    local_lengths = lax.dynamic_slice_in_dim(lengths, first_group, group_local, 0)
    reader_rows = lax.dynamic_slice_in_dim(readers, first_group, group_local, 0)
    reader_bf = reader_rows.astype(jnp.bfloat16)
    offsets = jnp.arange(CH, dtype=jnp.int32)
    live_mask = (offsets[None, :] < local_lengths[:, None]).reshape(-1)[:, None]
    query_rows = jnp.dot(tokens, w_query, preferred_element_type=jnp.float32).astype(jnp.bfloat16)
    key_rows = jnp.where(
        live_mask, jnp.dot(tokens, w_key, preferred_element_type=jnp.float32), 0.0
    ).astype(jnp.bfloat16)
    value_rows = jnp.where(
        live_mask, jnp.dot(tokens, w_value, preferred_element_type=jnp.float32), 0.0
    ).astype(jnp.bfloat16)
    query_blocks = query_rows.reshape(group_local, CH, head_dev, HS)
    key_blocks = key_rows.reshape(group_local, CH, head_dev, HS)
    value_blocks = value_rows.reshape(group_local, CH, head_dev, HS)
    key_groups = key_rows.reshape(group_local, CH, local_width)
    value_groups = value_rows.reshape(group_local, CH, local_width)
    pieces = (
        lax.all_gather(key_groups, "seq", axis=0, tiled=True),
        lax.all_gather(value_groups, "seq", axis=0, tiled=True),
    )
    count_here = pieces[0].shape[0]
    key_piece = pieces[0].reshape(count_here, CH, head_dev, HS)
    value_piece = pieces[1].reshape(count_here, CH, head_dev, HS)
    prefix = jnp.einsum(
        "xc,chde->xhde",
        reader_bf,
        group_states(key_piece, value_piece),
        preferred_element_type=jnp.float32,
    )
    prefix = prefix.astype(jnp.bfloat16)
    carried = jnp.einsum(
        "cthd,chde->cthe", query_blocks, prefix, preferred_element_type=jnp.float32
    )
    scores = jnp.einsum(
        "cthd,cshd->chts", query_blocks, key_blocks, preferred_element_type=jnp.float32
    )
    causal = offsets[:, None] >= offsets[None, :]
    weights = jnp.where(causal[None, None], scores, 0.0).astype(jnp.bfloat16)
    within = jnp.einsum(
        "chts,cshe->cthe", weights, value_blocks, preferred_element_type=jnp.float32
    )
    length_float = lengths.astype(jnp.float32)
    keys_read = local_lengths.astype(jnp.float32) + jnp.dot(
        reader_rows.astype(jnp.float32), length_float, precision=lax.Precision.HIGHEST
    )
    row_scale = lax.rsqrt(HS * keys_read)
    mixed = (carried + within) * row_scale[:, None, None, None]
    mixed = jnp.where(live_mask.reshape(group_local, CH, 1, 1), mixed, 0.0).astype(jnp.bfloat16)
    mixed = mixed.reshape(group_local * CH, local_width)
    partial_out = jnp.dot(mixed, w_out, preferred_element_type=jnp.float32)
    return lax.psum_scatter(partial_out, "tp", scatter_dimension=1, tiled=True).astype(jnp.bfloat16)


def solution(mesh):
    return jax.shard_map(
        local,
        mesh=mesh,
        in_specs=(
            P("seq", None),
            P(None, "tp"),
            P(None, "tp"),
            P(None, "tp"),
            P("tp", None),
            P(),
            P(),
        ),
        out_specs=P("seq", "tp"),
        check_vma=False,
    )
```

profile of v0, /device:TPU:1, one launch (start us, length us, event | category | flops | bytes accessed | tf_op | source)
XLA Modules:
  0.0 336.6 jit_solution(12828138155233370783)
XLA Ops:
  6.5 0.0 copy-start
  6.5 0.0 all-gather.3.cloned.1.call-start
  6.5 0.8 dynamic_slice.6
  7.4 0.1 iota_compare_fusion.1
  7.5 5.7 %fusion.2 = bf16[1536,256]{1,0:T(8,128)(2,1)} fusion(bf16[1536,2048]{1,0:T(8,128)(2,1)} %param.7, bf16[2048,256]{1,0:T(8,128)(2,1)} %param.9, pred[1536]{0:T(1024)(128)(4,1)S(1)} %get-tuple-element.6), kind=kOutput, calls=%fused_computation.5 | convolution fusion | flops 1611399168 | bytes 8128000 | tf_op jit(solution)/shard_map/dot_general | solution.py:28
  13.2 0.0 all-gather.3.cloned.1.call-update
  13.2 0.0 copy-start.1
  13.2 0.0 copy-start.2
  13.2 0.0 all-gather.5.cloned.1.call-start
  13.3 5.8 %fusion.3 = bf16[1536,256]{1,0:T(8,128)(2,1)} fusion(bf16[1536,2048]{1,0:T(8,128)(2,1)} %param.7, bf16[2048,256]{1,0:T(8,128)(2,1)} %param.10, pred[1536]{0:T(1024)(128)(4,1)S(1)} %get-tuple-element.6), kind=kOutput, calls=%fused_computation.6 | convolution fusion | flops 1611399168 | bytes 8128000 | tf_op jit(solution)/shard_map/dot_general | solution.py:31
  19.1 0.0 all-gather.5.cloned.1.call-update
  19.1 0.0 reduce-scatter.2.cloned.1.call-start
  19.1 2.7 reshape.77
  21.9 0.0 copy-done.1
  21.9 1.1 reshape.78
  22.9 0.0 copy-done.2
  23.0 4.9 %convolution_convert_fusion.1 = bf16[1536,256]{1,0:T(8,128)(2,1)S(1)} fusion(bf16[1536,2048]{1,0:T(8,128)(2,1)} %param.7, bf16[2048,256]{1,0:T(8,128)(2,1)} %param.8), kind=kOutput, calls=%fused_computation.7 | convolution fusion | flops 1611005952 | bytes 8126464 | tf_op jit(solution)/shard_map/dot_general | solution.py:26
  27.8 0.2 reshape.76
  28.0 0.9 fusion.10
  28.9 77.1 %all-gather.3.cloned.1.call-done = bf16[192,128,256]{2,1,0:T(8,128)(2,1)} async-done(((bf16[12,128,256]{2,1,0:T(8,128)(2,1)}), bf16[192,128,256]{2,1,0:T(8,128)(2,1)}) %all-gather.3.cloned.1.call-update) | async-done | bytes 12582928 | tf_op jit(solution)/shard_map/all_gather | solution.py:39
  106.0 16.6 %copy.21 = bf16[192,128,256]{1,2,0:T(8,128)(2,1)} copy(bf16[192,128,256]{2,1,0:T(8,128)(2,1)} %all-gather.3.cloned.1.call-done) | data formatting | bytes 25165824 | tf_op jit(solution)/shard_map/all_gather | solution.py:39
  122.7 74.9 %all-gather.5.cloned.1.call-done = bf16[192,128,256]{2,1,0:T(8,128)(2,1)} async-done(((bf16[12,128,256]{2,1,0:T(8,128)(2,1)}), bf16[192,128,256]{2,1,0:T(8,128)(2,1)}) %all-gather.5.cloned.1.call-update) | async-done | bytes 12582928 | tf_op jit(solution)/shard_map/all_gather | solution.py:40
  197.6 16.1 %copy.22 = bf16[192,128,256]{1,2,0:T(8,128)(2,1)} copy(bf16[192,128,256]{2,1,0:T(8,128)(2,1)} %all-gather.5.cloned.1.call-done) | data formatting | bytes 25165824 | tf_op jit(solution)/shard_map/all_gather | solution.py:40
  213.7 18.0 %convolution_convert_fusion = bf16[192,2,128,128]{3,2,1,0:T(8,128)(2,1)} fusion(bf16[192,128,2,128]{1,3,2,0:T(8,128)(2,1)} %bitcast.37, bf16[192,128,2,128]{1,3,2,0:T(8,128)(2,1)} %bitcast.38), kind=kOutput, calls=%fused_computation.2 | convolution fusion | flops 1616904192 | bytes 37748736 | tf_op jit(solution)/shard_map/cshd,cshe->chde/dot_general | solution.py:11
  231.7 11.3 %fusion.4 = bf16[12,2,128,128]{3,0,2,1:T(8,128)(2,1)S(1)} fusion(bf16[192,2,128,128]{3,2,1,0:T(8,128)(2,1)} %convolution_convert_fusion, s32[192,192]{1,0:T(8,128)} %param.12, s32[]{:T(128)S(6)} %select_n.20), kind=kOutput, calls=%fused_computation.10 | convolution fusion | flops 151390464 | bytes 13385732 | tf_op jit(solution)/shard_map/xc,chde->xhde/dot_general | solution.py:45
  243.0 0.7 fusion.17
  243.7 3.5 %fusion.7 = bf16[12,128,2,128]{1,3,2,0:T(8,128)(2,1)} fusion(f32[12,2,128,128]{3,2,1,0:T(8,128)S(1)} %fusion.17, bf16[12,128,2,128]{3,2,1,0:T(2,128)(2,1)} %reshape.77, bf16[12,128,2,128]{3,2,1,0:T(2,128)(2,1)} %reshape.78, f32[12]{0:T(128)S(1)} %fusion.10, pred[128,128]{1,0:T(8,128)(4,1)S(1)} %iota_compare_fusion, ...), kind=kOutput, calls=%fused_computation.11 | convolution fusion | flops 203685888 | bytes 4736560 | tf_op jit(solution)/shard_map/chts,cshe->cthe/dot_general | solution.py:60
  247.2 2.3 copy.30
  249.4 0.0 copy-done
  249.4 6.3 %fusion.11 = f32[1536,2048]{1,0:T(8,128)} fusion(bf16[256,2048]{1,0:T(8,128)(2,1)S(1)} %copy-done, bf16[192,8,2,128]{3,2,1,0:T(2,128)(2,1)S(1)} %bitcast.39), kind=kOutput, calls=%fused_computation.16 | convolution fusion | flops 1610612736 | bytes 14417920 | tf_op jit(solution)/shard_map/dot_general | solution.py:71
  255.8 0.0 reduce-scatter.2.cloned.1.call-update
  255.8 71.9 %reduce-scatter.2.cloned.1.call-done = f32[1536,256]{1,0:T(8,128)} async-done(((f32[1536,2048]{1,0:T(8,128)}), f32[1536,256]{1,0:T(8,128)}) %reduce-scatter.2.cloned.1.call-update) | async-done | bytes 1572880 | tf_op jit(solution)/shard_map/reduce_scatter | solution.py:72
  327.7 2.4 convert_element_type.51
  (2 shorter events, 0.0 us)
Async XLA Ops:
  6.5 242.9 %copy-start = (bf16[256,2048]{1,0:T(8,128)(2,1)S(1)}, bf16[256,2048]{1,0:T(8,128)(2,1)}, u32[]{:S(2)}) copy-start(bf16[256,2048]{1,0:T(8,128)(2,1)} %param.11) | copy-start | bytes 3145732
  6.5 99.5 %all-gather.3.cloned.1.call-start = ((), (), s32[]{:S(2)}) async-start(), calls=%async_computation.1 | async-start | bytes 13369344 | tf_op jit(solution)/shard_map/all_gather | solution.py:39
  13.2 8.7 %copy-start.1 = (bf16[1536,256]{1,0:T(8,128)(2,1)S(1)}, bf16[1536,256]{1,0:T(8,128)(2,1)}, u32[]{:S(2)}) copy-start(bf16[1536,256]{1,0:T(8,128)(2,1)} %fusion.2) | copy-start | bytes 2359300
  13.2 9.7 %copy-start.2 = (s32[192]{0:T(256)S(1)}, s32[192]{0:T(256)}, u32[]{:S(2)}) copy-start(s32[192]{0:T(256)} %param.13) | copy-start | bytes 2308
  13.2 184.3 %all-gather.5.cloned.1.call-start = ((), (), s32[]{:S(2)}) async-start(), calls=%async_computation.2 | async-start | bytes 13369344 | tf_op jit(solution)/shard_map/all_gather | solution.py:40
  19.1 308.6 %reduce-scatter.2.cloned.1.call-start = ((), (), s32[]{:S(2)}) async-start(), calls=%async_computation.3 | async-start | bytes 14155776 | tf_op jit(solution)/shard_map/reduce_scatter | solution.py:72
Sparse Core Ops, SparseCore 0:
  13.3 92.6 all-gather.2
  108.2 89.3 all-gather.4
  255.9 71.7 reduce-scatter.1
where the time goes:
time: 338 us; the launch traced here: 337 us
  waiting for transfers between devices  224 us (66%)
  matrix products  57.1 us (17%)
  local copies, waits for them, and re-layouts  39.9 us (12%)
  between operations  13.2 us (4%)
    all_gather x1, waiting for transfers between devices, local(): lax.all_gather(key_groups, 'seq', axis=0, tiled=True)  77.1 us
    all_gather x1, waiting for transfers between devices, local(): lax.all_gather(value_groups, 'seq', axis=0, tiled=True)  74.9 us
    reduce_scatter x1, waiting for transfers between devices, local(): lax.psum_scatter(partial_out, 'tp', scatter_dimension=1, tiled=True)  71.9 us
    dot_general x1, matrix products, group_states(): jnp.einsum('cshd,cshe->chde', key_blocks, value_blocks, preferred_element...  18 us
    all_gather x1, local copies, waits for them, and re-layouts, local(): lax.all_gather(key_groups, 'seq', axis=0, tiled=True)  16.6 us
    all_gather x1, local copies, waits for them, and re-layouts, local(): lax.all_gather(value_groups, 'seq', axis=0, tiled=True)  16.1 us
    dot_general x1, matrix products, local(): jnp.einsum('xc,chde->xhde', reader_bf, group_states(key_piece, value_piec...  11.3 us
  transfers between devices with their start and end apart: 3, of which 3 were waited for; matrix products, arithmetic and copies ran while one was open for 10% of the time, Pallas kernels for 0%

commit v1 on v0

v1 whole, which is shorter than its diff:
```python
import jax
import jax.numpy as jnp
from jax import lax
from jax.sharding import PartitionSpec as P

HS = 128
CH = 128


def local(tokens, w_query, w_key, w_value, w_out, readers, lengths):
    group_local = tokens.shape[0] // CH
    local_width = w_query.shape[1]
    head_dev = local_width // HS
    seq_count = readers.shape[0] // group_local
    first_group = lax.axis_index("seq") * group_local

    tp_count = w_out.shape[1] // local_width
    w_out_cols = lax.all_to_all(
        w_out.reshape(local_width, tp_count, local_width), "tp", 1, 0, tiled=True
    ).reshape(tp_count * local_width, local_width)

    local_lengths = lax.dynamic_slice_in_dim(lengths, first_group, group_local, 0)
    reader_rows = lax.dynamic_slice_in_dim(readers, first_group, group_local, 0)
    offsets = jnp.arange(CH, dtype=jnp.int32)
    live_mask = (offsets[None, :] < local_lengths[:, None]).reshape(-1)[:, None]
    key_rows = jnp.where(
        live_mask, jnp.dot(tokens, w_key, preferred_element_type=jnp.float32), 0.0
    ).astype(jnp.bfloat16)
    value_rows = jnp.where(
        live_mask, jnp.dot(tokens, w_value, preferred_element_type=jnp.float32), 0.0
    ).astype(jnp.bfloat16)
    query_rows = jnp.dot(tokens, w_query, preferred_element_type=jnp.float32).astype(jnp.bfloat16)
    query_blocks = query_rows.reshape(group_local, CH, head_dev, HS)
    key_blocks = key_rows.reshape(group_local, CH, head_dev, HS)
    value_blocks = value_rows.reshape(group_local, CH, head_dev, HS)

    states = jnp.einsum(
        "cshd,cshe->chde", key_blocks, value_blocks, preferred_element_type=jnp.float32
    ).astype(jnp.bfloat16)

    local_readers = lax.dynamic_slice_in_dim(reader_rows, first_group, group_local, 1)
    last_row = local_readers[group_local - 1].at[group_local - 1].set(1)
    states_f32 = states.astype(jnp.float32)
    tail = jnp.einsum(
        "c,chde->hde",
        last_row.astype(jnp.float32),
        states_f32,
        precision=lax.Precision.HIGHEST,
        preferred_element_type=jnp.float32,
    )
    tails = lax.all_gather(tail, "seq", axis=0, tiled=False)
    tail_weights = reader_rows.reshape(group_local, seq_count, group_local)[:, :, group_local - 1]
    carried_in = jnp.einsum(
        "cd,dhij->chij",
        tail_weights.astype(jnp.float32),
        tails,
        precision=lax.Precision.HIGHEST,
        preferred_element_type=jnp.float32,
    )
    own = jnp.einsum(
        "ce,ehij->chij",
        local_readers.astype(jnp.float32),
        states_f32,
        precision=lax.Precision.HIGHEST,
        preferred_element_type=jnp.float32,
    )
    prefix = (carried_in + own).astype(jnp.bfloat16)

    carried = jnp.einsum(
        "cthd,chde->cthe", query_blocks, prefix, preferred_element_type=jnp.float32
    )
    scores = jnp.einsum(
        "cthd,cshd->chts", query_blocks, key_blocks, preferred_element_type=jnp.float32
    )
    causal = offsets[:, None] >= offsets[None, :]
    weights = jnp.where(causal[None, None], scores, 0.0).astype(jnp.bfloat16)
    within = jnp.einsum(
        "chts,cshe->cthe", weights, value_blocks, preferred_element_type=jnp.float32
    )
    length_float = lengths.astype(jnp.float32)
    keys_read = local_lengths.astype(jnp.float32) + jnp.dot(
        reader_rows.astype(jnp.float32), length_float, precision=lax.Precision.HIGHEST
    )
    row_scale = lax.rsqrt(HS * keys_read)
    mixed = (carried + within) * row_scale[:, None, None, None]
    mixed = jnp.where(live_mask.reshape(group_local, CH, 1, 1), mixed, 0.0).astype(jnp.bfloat16)
    mixed = mixed.reshape(group_local * CH, local_width)
    mixed_all = lax.all_gather(mixed, "tp", axis=1, tiled=True)
    return jnp.dot(mixed_all, w_out_cols, preferred_element_type=jnp.float32).astype(jnp.bfloat16)


def solution(mesh):
    return jax.shard_map(
        local,
        mesh=mesh,
        in_specs=(
            P("seq", None),
            P(None, "tp"),
            P(None, "tp"),
            P(None, "tp"),
            P("tp", None),
            P(),
            P(),
        ),
        out_specs=P("seq", "tp"),
        check_vma=False,
    )
```

time: 338 us -> 149 us (0.44)
  waiting for transfers between devices: 224 us -> 56.8 us
  blocking collectives: 0 us -> 29.1 us
  local copies, waits for them, and re-layouts: 39.9 us -> 11.5 us
  matrix products: 57.1 us -> 36.6 us
    all_gather x2, waiting for transfers between devices: 152 us -> 56.8 us  [the longest x1 33.5 us: local(): tails = lax.all_gather(tail, 'seq', axis=0, tiled=False)]
    reduce_scatter x1 -> x0, waiting for transfers between devices: 71.9 us -> none  [local(): lax.psum_scatter(partial_out, 'tp', scatter_dimension=1, tiled=True)]
    all_gather x2 -> x0, local copies, waits for them, and re-layouts: 32.8 us -> none  [the longest x1 16.6 us: local(): lax.all_gather(key_groups, 'seq', axis=0, tiled=True)]
    all_to_all x0 -> x1, blocking collectives: none -> 29.1 us  [local(): lax.all_to_all(w_out.reshape(local_width, tp_count, local_width), 'tp', 1...]
    dot_general x3 -> x5, matrix products: 35.7 us -> 16 us  [the longest x1 5.47 us: local(): jnp.dot(mixed_all, w_out_cols, preferred_element_type=jnp.float32)]
  transfers between devices with their start and end apart: 3 -> 2, of which waited for: 3 -> 2; matrix products, arithmetic and copies ran while one was open for 10% -> 10% of each run, Pallas kernels for 0% -> 0%
where the time goes in v1:
time: 149 us
  waiting for transfers between devices  56.8 us (38%)
  matrix products  36.6 us (25%)
  blocking collectives  29.1 us (20%)
  between operations  13.5 us (9%)
  local copies, waits for them, and re-layouts  11.5 us (8%)
    all_gather x1, waiting for transfers between devices, local(): tails = lax.all_gather(tail, 'seq', axis=0, tiled=False)  33.5 us
    all_to_all x1, blocking collectives, local(): lax.all_to_all(w_out.reshape(local_width, tp_count, local_width), 'tp', 1...  29.1 us
    all_gather x1, waiting for transfers between devices, local(): mixed_all = lax.all_gather(mixed, 'tp', axis=1, tiled=True)  23.3 us
    dot_general x1, matrix products, local(): jnp.dot(tokens, w_query, preferred_element_type=jnp.float32)  5.74 us
    dot_general x1, matrix products, local(): jnp.dot(mixed_all, w_out_cols, preferred_element_type=jnp.float32)  5.47 us
    dot_general x1, matrix products, local(): jnp.einsum('cd,dhij->chij', tail_weights.astype(jnp.float32), tails, prec...  5.12 us
    dot_general x1, matrix products, local(): jnp.dot(tokens, w_key, preferred_element_type=jnp.float32)  4.84 us
    dot_general x1, matrix products, local(): jnp.dot(tokens, w_value, preferred_element_type=jnp.float32)  4.58 us
  transfers between devices with their start and end apart: 2, of which 2 were waited for; matrix products, arithmetic and copies ran while one was open for 10% of the time, Pallas kernels for 0%

profile of v1, /device:TPU:1, one launch (start us, length us, event | category | flops | bytes accessed | tf_op | source)
XLA Modules:
  0.0 148.7 jit_solution(12261651278064252915)
XLA Ops:
  6.5 0.0 copy-start
  6.5 0.0 all-gather.6.cloned.1.call-start
  6.5 0.8 dynamic_slice.9
  7.4 0.7 iota_compare_fusion.1
  8.0 0.0 copy-done
  8.0 4.6 %fusion.1 = bf16[1536,256]{1,0:T(8,128)(2,1)S(1)} fusion(bf16[1536,2048]{1,0:T(8,128)(2,1)} %param.9, bf16[2048,256]{1,0:T(8,128)(2,1)S(1)} %copy-done, pred[1536]{0:T(1024)(128)(4,1)S(1)} %get-tuple-element.18), kind=kOutput, calls=%fused_computation.3 | convolution fusion | flops 1611399168 | bytes 8128000 | tf_op jit(solution)/shard_map/dot_general | solution.py:30
  12.6 0.2 reshape.97
  12.8 0.6 copy.48
  13.5 4.8 %fusion = bf16[1536,256]{1,0:T(8,128)(2,1)S(1)} fusion(bf16[1536,2048]{1,0:T(8,128)(2,1)} %param.9, bf16[2048,256]{1,0:T(8,128)(2,1)} %param.11, pred[1536]{0:T(1024)(128)(4,1)S(1)} %get-tuple-element.18), kind=kOutput, calls=%fused_computation.2 | convolution fusion | flops 1611399168 | bytes 8128000 | tf_op jit(solution)/shard_map/dot_general | solution.py:27
  18.3 0.2 reshape.96
  18.5 0.0 copy-start.3
  18.5 0.7 convolution_convert_fusion.2
  19.2 0.8 dynamic-slice_bitcast_fusion
  20.0 1.5 %fusion.10 = f32[1,2,128,128]{3,0,2,1:T(1,128)} fusion(bf16[12,2,128,128]{3,2,1,0:T(8,128)(2,1)S(1)} %convolution_convert_fusion.2, s32[12]{0:T(128)S(1)} %constant_dynamic-update-slice_fusion), kind=kOutput, calls=%fused_computation.17 | convolution fusion | flops 4718604 | bytes 917552 | tf_op jit(solution)/shard_map/c,chde->hde/dot_general | solution.py:44
  21.5 0.0 all-gather.6.cloned.1.call-update
  21.5 0.2 all-gather.4.cloned.1.call-start
  21.8 0.0 copy-done.3
  21.8 0.8 constant_dynamic-slice_fusion
  22.5 0.1 reshape.95
  22.6 5.7 %convolution_convert_fusion.1 = bf16[1536,256]{1,0:T(8,128)(2,1)} fusion(bf16[1536,2048]{1,0:T(8,128)(2,1)} %param.9, bf16[2048,256]{1,0:T(8,128)(2,1)} %param.10), kind=kOutput, calls=%fused_computation.5 | convolution fusion | flops 1611005952 | bytes 8126464 | tf_op jit(solution)/shard_map/dot_general | solution.py:32
  28.4 2.7 %reshape.98 = bf16[12,128,2,128]{3,2,1,0:T(2,128)(2,1)} reshape(bf16[1536,256]{1,0:T(8,128)(2,1)} %convolution_convert_fusion.1) | data formatting | bytes 1572864 | tf_op jit(solution)/shard_map/reshape | solution.py:33
  31.1 0.2 fusion.24
  31.3 0.1 fusion.9
  31.4 3.2 %fusion.12 = f32[12,2,128,128]{3,0,2,1:T(8,128)} fusion(bf16[12,2,128,128]{3,2,1,0:T(8,128)(2,1)S(1)} %convolution_convert_fusion.2, s32[192,192]{1,0:T(8,128)} %param.14, s32[]{:T(128)S(6)} %select_n.24), kind=kOutput, calls=%fused_computation.19 | convolution fusion | flops 56623248 | bytes 2367492 | tf_op jit(solution)/shard_map/ce,ehij->chij/dot_general | solution.py:60
  34.7 33.5 %all-gather.6.cloned.1.call-done = f32[32,128,128]{2,1,0:T(8,128)} async-done(((f32[2,128,128]{2,1,0:T(8,128)}), f32[32,128,128]{2,1,0:T(8,128)}) %all-gather.6.cloned.1.call-update) | async-done | bytes 2097168 | tf_op jit(solution)/shard_map/all_gather | solution.py:51
  68.2 0.0 copy-start.1
  68.2 5.1 %add_convert_fusion = bf16[12,2,128,128]{3,0,2,1:T(8,128)(2,1)S(1)} fusion(f32[12,2,128,128]{3,0,2,1:T(8,128)} %fusion.12, f32[16,2,128,128]{3,2,1,0:T(8,128)} %bitcast.58, f32[12,16]{1,0:T(8,128)S(1)} %fusion.24), kind=kOutput, calls=%fused_computation.8 | convolution fusion | flops 76283904 | bytes 4457216 | tf_op jit(solution)/shard_map/cd,dhij->chij/dot_general | solution.py:53
  73.3 0.0 copy-done.1
  73.3 0.0 copy-start.2
  73.3 1.9 %fusion.14 = f32[12,2,128,128]{3,2,1,0:T(8,128)} fusion(bf16[12,2,128,128]{3,0,2,1:T(8,128)(2,1)S(1)} %add_convert_fusion, bf16[12,128,2,128]{3,2,1,0:T(2,128)(2,1)S(1)} %copy-done.1), kind=kOutput, calls=%fused_computation.22 | convolution fusion | flops 100663296 | bytes 3145728 | tf_op jit(solution)/shard_map/cthd,chde->cthe/dot_general | solution.py:69
  75.2 0.0 copy-done.2
  75.2 3.5 %fusion.6 = bf16[12,128,2,128]{1,3,2,0:T(8,128)(2,1)} fusion(f32[12,2,128,128]{3,2,1,0:T(8,128)} %fusion.14, bf16[12,128,2,128]{1,3,2,0:T(8,128)(2,1)S(1)} %copy.48, f32[12]{0:T(128)S(1)} %fusion.9, pred[128,128]{1,0:T(8,128)(4,1)S(1)} %iota_compare_fusion, pred[12,128]{1,0:T(8,128)(4,1)S(1)} %copy-done.2, bf16[12,128,2,128]{3,2,1,0:T(2,128)(2,1)S(1)} %reshape.96, ...), kind=kOutput, calls=%fused_computation.12 | convolution fusion | flops 203685888 | bytes 4736560 | tf_op jit(solution)/shard_map/chts,cshe->cthe/dot_general | solution.py:77
  78.7 2.3 %copy.49 = bf16[12,128,2,128]{3,2,1,0:T(2,128)(2,1)S(1)} copy(bf16[12,128,2,128]{1,3,2,0:T(8,128)(2,1)} %fusion.6) | data formatting | bytes 1572864 | tf_op jit(solution)/shard_map/convert_element_type | solution.py:86
  80.9 1.0 copy.78
  81.9 0.0 all-gather.4.cloned.1.call-update
  82.0 1.5 copy.50
  83.4 29.1 %all_to_all.15 = bf16[256,8,256]{0,2,1:T(8,128)(2,1)S(1)} all-to-all(bf16[256,8,256]{0,2,1:T(8,128)(2,1)S(1)} %bitcast.55), channel_id=1, replica_groups=mesh['seq'=16,'tp'=8] {'tp'}, dimensions={1} | all-to-all | bytes 2097152 | tf_op jit(solution)/shard_map/all_to_all | solution.py:18
  112.6 0.5 copy.51
  113.1 23.3 %all-gather.4.cloned.1.call-done = bf16[1536,2048]{1,0:T(8,128)(2,1)} async-done(((bf16[1536,256]{1,0:T(8,128)(2,1)}), bf16[1536,2048]{1,0:T(8,128)(2,1)}) %all-gather.4.cloned.1.call-update) | async-done | bytes 6291472 | tf_op jit(solution)/shard_map/all_gather | solution.py:88
  136.3 5.5 %convolution_convert_fusion = bf16[1536,256]{1,0:T(8,128)(2,1)} fusion(bf16[1536,2048]{1,0:T(8,128)(2,1)} %all-gather.4.cloned.1.call-done, bf16[2048,256]{1,0:T(8,128)(2,1)S(1)} %bitcast.59), kind=kOutput, calls=%fused_computation.4 | convolution fusion | flops 1611005952 | bytes 8126464 | tf_op jit(solution)/shard_map/dot_general | solution.py:89
  (3 shorter events, 0.0 us)
Async XLA Ops:
  6.5 1.5 %copy-start = (bf16[2048,256]{1,0:T(8,128)(2,1)S(1)}, bf16[2048,256]{1,0:T(8,128)(2,1)}, u32[]{:S(2)}) copy-start(bf16[2048,256]{1,0:T(8,128)(2,1)} %param.12) | copy-start | bytes 3145732
  6.5 61.6 %all-gather.6.cloned.1.call-start = ((), (), s32[]{:S(2)}) async-start(), calls=%async_computation.2 | async-start | bytes 2228224 | tf_op jit(solution)/shard_map/all_gather | solution.py:51
  18.5 3.3 %copy-start.3 = (s32[192]{0:T(256)S(1)}, s32[192]{0:T(256)}, u32[]{:S(2)}) copy-start(s32[192]{0:T(256)} %param.15) | copy-start | bytes 2308
  21.5 114.8 %all-gather.4.cloned.1.call-start = ((), (), s32[]{:S(2)}) async-start(), calls=%async_computation.1 | async-start | bytes 7077888 | tf_op jit(solution)/shard_map/all_gather | solution.py:88
  68.2 5.1 %copy-start.1 = (bf16[12,128,2,128]{3,2,1,0:T(2,128)(2,1)S(1)}, bf16[12,128,2,128]{3,2,1,0:T(2,128)(2,1)}, u32[]{:S(2)}) copy-start(bf16[12,128,2,128]{3,2,1,0:T(2,128)(2,1)} %reshape.98) | copy-start | bytes 2359300
  73.3 1.9 %copy-start.2 = (pred[12,128]{1,0:T(8,128)(4,1)S(1)}, pred[12,128]{1,0:T(8,128)(4,1)}, u32[]{:S(2)}) copy-start(pred[12,128]{1,0:T(8,128)(4,1)} %get-tuple-element.17) | copy-start | bytes 4612
Sparse Core Ops, SparseCore 0:
  21.7 46.4 all-gather.5
  82.1 54.2 all-gather.3

commit v2 on v1

--- a/solution.py
+++ b/solution.py
@@ -15,9 +15,19 @@
     first_group = lax.axis_index("seq") * group_local
 
     tp_count = w_out.shape[1] // local_width
-    w_out_cols = lax.all_to_all(
-        w_out.reshape(local_width, tp_count, local_width), "tp", 1, 0, tiled=True
-    ).reshape(tp_count * local_width, local_width)
+    tp_index = lax.axis_index("tp")
+    seq_index = lax.axis_index("seq")
+    out_blocks = w_out.reshape(local_width, tp_count, local_width)
+    w_out_cols = jnp.zeros((tp_count, local_width, local_width), w_out.dtype)
+    for shift in range(tp_count):
+        piece = lax.dynamic_index_in_dim(out_blocks, (tp_index + shift) % tp_count, 1, False)
+        if shift:
+            pairs = [(i, (i + shift) % tp_count) for i in range(tp_count)]
+            piece = lax.ppermute(piece, "tp", pairs)
+        w_out_cols = lax.dynamic_update_index_in_dim(
+            w_out_cols, piece, (tp_index - shift) % tp_count, 0
+        )
+    w_out_cols = w_out_cols.reshape(tp_count * local_width, local_width)
 
     local_lengths = lax.dynamic_slice_in_dim(lengths, first_group, group_local, 0)
     reader_rows = lax.dynamic_slice_in_dim(readers, first_group, group_local, 0)
@@ -40,28 +50,27 @@
 
     local_readers = lax.dynamic_slice_in_dim(reader_rows, first_group, group_local, 1)
     last_row = local_readers[group_local - 1].at[group_local - 1].set(1)
-    states_f32 = states.astype(jnp.float32)
     tail = jnp.einsum(
-        "c,chde->hde",
-        last_row.astype(jnp.float32),
-        states_f32,
-        precision=lax.Precision.HIGHEST,
-        preferred_element_type=jnp.float32,
+        "c,chde->hde", last_row.astype(jnp.bfloat16), states, preferred_element_type=jnp.float32
     )
-    tails = lax.all_gather(tail, "seq", axis=0, tiled=False)
-    tail_weights = reader_rows.reshape(group_local, seq_count, group_local)[:, :, group_local - 1]
-    carried_in = jnp.einsum(
-        "cd,dhij->chij",
-        tail_weights.astype(jnp.float32),
-        tails,
-        precision=lax.Precision.HIGHEST,
-        preferred_element_type=jnp.float32,
-    )
+    last_group = first_group + group_local - 1
+    scan = tail
+    shift = 1
+    while shift < seq_count:
+        source = jnp.maximum(seq_index - shift, 0) * group_local + group_local - 1
+        joined = jnp.where(seq_index >= shift, readers[last_group, source], 0).astype(jnp.float32)
+        pairs = [(i, i + shift) for i in range(seq_count - shift)]
+        scan = scan + joined * lax.ppermute(scan, "seq", pairs)
+        shift *= 2
+    before = lax.ppermute(scan, "seq", [(i, i + 1) for i in range(seq_count - 1)])
+    enters = jnp.where(
+        seq_index > 0, lax.dynamic_index_in_dim(reader_rows, first_group - 1, 1, False), 0
+    ).astype(jnp.float32)
+    carried_in = enters[:, None, None, None] * before[None]
     own = jnp.einsum(
         "ce,ehij->chij",
-        local_readers.astype(jnp.float32),
-        states_f32,
-        precision=lax.Precision.HIGHEST,
+        local_readers.astype(jnp.bfloat16),
+        states,
         preferred_element_type=jnp.float32,
     )
     prefix = (carried_in + own).astype(jnp.bfloat16)

time: 149 us -> 145 us (0.973)
  the two profiles are of different devices: /device:TPU:1 before, /device:TPU:49 now
where the time goes in v2:
time: 145 us; the launch traced here: 144 us
  waiting for transfers between devices  53 us (37%)
  matrix products  28.5 us (20%)
  starting transfers between devices  26.1 us (18%)
  between operations  16.6 us (11%)
  local copies, waits for them, and re-layouts  12.7 us (9%)
  other arithmetic  6.85 us (5%)
    all_gather x1, waiting for transfers between devices, local(): mixed_all = lax.all_gather(mixed, 'tp', axis=1, tiled=True)  25.8 us
    ppermute x7, starting transfers between devices, local(): piece = lax.ppermute(piece, 'tp', pairs)  14.4 us
    ppermute x7, waiting for transfers between devices, local(): piece = lax.ppermute(piece, 'tp', pairs)  12.5 us
    ppermute x4, starting transfers between devices, local(): scan = scan + joined * lax.ppermute(scan, 'seq', pairs)  9.82 us
    ppermute x4, waiting for transfers between devices, local(): scan = scan + joined * lax.ppermute(scan, 'seq', pairs)  9.66 us
    dot_general x1, matrix products, local(): jnp.dot(tokens, w_query, preferred_element_type=jnp.float32)  5.74 us
    dot_general x1, matrix products, local(): jnp.dot(mixed_all, w_out_cols, preferred_element_type=jnp.float32)  5.47 us
    ppermute x1, waiting for transfers between devices, local(): lax.ppermute(scan, 'seq', [(i, i + 1) for i in range(seq_count - 1)])  5.01 us
  transfers between devices with their start and end apart: 13, of which 8 were waited for; matrix products, arithmetic and copies ran while one was open for 12% of the time, Pallas kernels for 0%

profile of v2, /device:TPU:49, one launch (start us, length us, event | category | flops | bytes accessed | tf_op | source)
XLA Modules:
  0.0 143.9 jit_solution(13905820681584145)
XLA Ops:
  6.5 0.8 dynamic_slice.50
  7.4 0.7 iota_compare_fusion.1
  8.1 4.6 %fusion.1 = bf16[1536,256]{1,0:T(8,128)(2,1)S(1)} fusion(bf16[1536,2048]{1,0:T(8,128)(2,1)} %param.9, bf16[2048,256]{1,0:T(8,128)(2,1)S(1)} %copy-done, pred[1536]{0:T(1024)(128)(4,1)S(1)} %get-tuple-element.30), kind=kOutput, calls=%fused_computation.3 | convolution fusion | flops 1611399168 | bytes 8128000 | tf_op jit(solution)/shard_map/dot_general | solution.py:40
  12.8 0.6 copy.24
  13.5 4.8 %fusion = bf16[1536,256]{1,0:T(8,128)(2,1)S(1)} fusion(bf16[1536,2048]{1,0:T(8,128)(2,1)} %param.9, bf16[2048,256]{1,0:T(8,128)(2,1)} %param.11, pred[1536]{0:T(1024)(128)(4,1)S(1)} %get-tuple-element.30), kind=kOutput, calls=%fused_computation.2 | convolution fusion | flops 1611399168 | bytes 8128000 | tf_op jit(solution)/shard_map/dot_general | solution.py:37
  18.5 0.7 convolution_convert_fusion.2
  19.2 0.8 dynamic-slice_bitcast_fusion
  20.1 0.5 fusion.7
  20.6 3.1 %collective-permute-start = (f32[2,128,128]{2,1,0:T(8,128)S(1)}, f32[2,128,128]{2,1,0:T(8,128)}, u32[]{:S(2)}, u32[]{:S(2)}) collective-permute-start(f32[2,128,128]{2,1,0:T(8,128)S(1)} %bitcast.78), channel_id=1, source_target_pairs={{0,8},{8,16},{16,24},{24,32},{32,40},{40,48},{48,56},{56,64},{64,7... | collective-permute-start | bytes 393224 | tf_op jit(solution)/shard_map/ppermute | solution.py:63
  23.7 1.5 %fusion.33 = (s32[1,1]{1,0:T(1,128)}, s32[1,1]{1,0:T(1,128)}, s32[1,1]{1,0:T(1,128)}, s32[1,1]{1,0:T(1,128)}) fusion(s32[192,192]{1,0:T(8,128)} %param.14, s32[]{:T(128)S(6)} %select_n.194, s32[]{:T(128)S(6)} %select_n.201, s32[]{:T(128)S(6)} %select_n.199, s32[]{:T(128)S(6)} %select_n.197, s32[]{:T(128)S(6)} %select_n.195), kind=kLoop, calls=%fused_computation.62 | loop fusion | bytes 52 | tf_op jit(solution)/shard_map/dynamic_slice | solution.py:61
  25.9 3.2 %collective-permute-done = f32[2,128,128]{2,1,0:T(8,128)} collective-permute-done((f32[2,128,128]{2,1,0:T(8,128)S(1)}, f32[2,128,128]{2,1,0:T(8,128)}, u32[]{:S(2)}, u32[]{:S(2)}) %collective-permute-start) | collective-permute-done | bytes 131104 | tf_op jit(solution)/shard_map/ppermute | solution.py:63
  29.1 1.6 %multiply_add_fusion.3 = f32[2,128,128]{2,1,0:T(8,128)} fusion(f32[2,128,128]{2,1,0:T(8,128)S(1)} %bitcast.79, f32[2,128,128]{2,1,0:T(8,128)} %collective-permute-done, f32[]{:T(128)S(6)} %convert_element_type.70), kind=kLoop, calls=%fused_computation.39 | loop fusion | flops 65536 | bytes 393220 | tf_op jit(solution)/shard_map/add | solution.py:63
  30.7 2.5 %collective-permute-start.1 = (f32[2,128,128]{2,1,0:T(8,128)}, f32[2,128,128]{2,1,0:T(8,128)}, u32[]{:S(2)}, u32[]{:S(2)}) collective-permute-start(f32[2,128,128]{2,1,0:T(8,128)} %multiply_add_fusion.3), channel_id=1, source_target_pairs={{0,16},{8,24},{16,32},{24,40},{32,48},{40,56},{48,64},{56,72},{64,... | collective-permute-start | bytes 393224 | tf_op jit(solution)/shard_map/ppermute | solution.py:63
  33.9 5.2 %collective-permute-done.1 = f32[2,128,128]{2,1,0:T(8,128)} collective-permute-done((f32[2,128,128]{2,1,0:T(8,128)}, f32[2,128,128]{2,1,0:T(8,128)}, u32[]{:S(2)}, u32[]{:S(2)}) %collective-permute-start.1) | collective-permute-done | bytes 131104 | tf_op jit(solution)/shard_map/ppermute | solution.py:63
  39.1 1.0 multiply_add_fusion.2
  40.1 2.9 %collective-permute-start.2 = (f32[2,128,128]{2,1,0:T(8,128)S(1)}, f32[2,128,128]{2,1,0:T(8,128)}, u32[]{:S(2)}, u32[]{:S(2)}) collective-permute-start(f32[2,128,128]{2,1,0:T(8,128)S(1)} %multiply_add_fusion.2), channel_id=1, source_target_pairs={{0,32},{8,40},{16,48},{24,56},{32,64},{40,72},{48,80},{56,88},{64,... | collective-permute-start | bytes 393224 | tf_op jit(solution)/shard_map/ppermute | solution.py:63
  43.0 5.7 %convolution_convert_fusion.1 = bf16[1536,256]{1,0:T(8,128)(2,1)} fusion(bf16[1536,2048]{1,0:T(8,128)(2,1)} %param.9, bf16[2048,256]{1,0:T(8,128)(2,1)} %param.10), kind=kOutput, calls=%fused_computation.5 | convolution fusion | flops 1611005952 | bytes 8126464 | tf_op jit(solution)/shard_map/dot_general | solution.py:42
  49.4 2.0 %reshape.104 = bf16[12,128,2,128]{3,2,1,0:T(2,128)(2,1)S(1)} reshape(bf16[1536,256]{1,0:T(8,128)(2,1)} %convolution_convert_fusion.1) | data formatting | bytes 1572864 | tf_op jit(solution)/shard_map/reshape | solution.py:43
  51.5 1.0 multiply_add_fusion.1
  52.5 1.3 collective-permute-start.3
  53.8 2.4 %fusion.2 = f32[12,2,128,128]{3,2,1,0:T(8,128)} fusion(bf16[12,128,2,128]{1,3,2,0:T(8,128)(2,1)S(1)} %copy.24, pred[128,128]{1,0:T(8,128)(4,1)S(1)} %iota_compare_fusion, bf16[12,128,2,128]{3,2,1,0:T(2,128)(2,1)S(1)} %reshape.102, bf16[12,128,2,128]{3,2,1,0:T(2,128)(2,1)S(1)} %reshape.104), kind=kOutput, calls=%fused_computation.10 | convolution fusion | flops 202113024 | bytes 3948544 | tf_op jit(solution)/shard_map/chts,cshe->cthe/dot_general | solution.py:86
  56.2 0.8 convert_element_type.80
  57.6 0.9 convert_reduce_fusion
  58.5 1.3 collective-permute-done.3
  59.8 0.9 multiply_add_fusion
  60.7 1.9 %collective-permute-start.4 = (f32[2,128,128]{2,1,0:T(8,128)S(1)}, f32[2,128,128]{2,1,0:T(8,128)S(1)}, u32[]{:S(2)}, u32[]{:S(2)}) collective-permute-start(f32[2,128,128]{2,1,0:T(8,128)S(1)} %multiply_add_fusion), channel_id=1, source_target_pairs={{0,8},{8,16},{16,24},{24,32},{32,40},{40,48},{48,56},{56,64},{64,7... | collective-permute-start | bytes 393224 | tf_op jit(solution)/shard_map/ppermute | solution.py:65
  62.6 0.9 fusion.6
  63.5 5.0 %collective-permute-done.4 = f32[2,128,128]{2,1,0:T(8,128)S(1)} collective-permute-done((f32[2,128,128]{2,1,0:T(8,128)S(1)}, f32[2,128,128]{2,1,0:T(8,128)S(1)}, u32[]{:S(2)}, u32[]{:S(2)}) %collective-permute-start.4) | collective-permute-done | bytes 131104 | tf_op jit(solution)/shard_map/ppermute | solution.py:65
  68.5 1.8 %add_convert_fusion = bf16[12,2,128,128]{3,0,2,1:T(8,128)(2,1)S(1)} fusion(f32[2,128,128]{2,1,0:T(8,128)S(1)} %collective-permute-done.4, f32[12]{0:T(128)S(1)} %convert_reduce_fusion, bf16[12,2,128,128]{3,2,1,0:T(8,128)(2,1)} %copy-done.2, s32[192,192]{1,0:T(8,128)} %param.14, s32[]{:T(128)S(6)} %select_n.188), kind=kOutput, calls=%fused_computation.6 | convolution fusion | flops 10616976 | bytes 1712180 | tf_op jit(solution)/shard_map/ce,ehij->chij/dot_general | solution.py:70
  70.4 1.6 %fusion.3 = bf16[12,128,2,128]{1,3,2,0:T(8,128)(2,1)} fusion(f32[12,2,128,128]{3,2,1,0:T(8,128)S(1)} %copy-done.1, bf16[12,2,128,128]{3,0,2,1:T(8,128)(2,1)S(1)} %add_convert_fusion, f32[12]{0:T(128)S(1)} %fusion.6, pred[12,128]{1,0:T(8,128)(4,1)S(1)} %copy-done.6, bf16[12,128,2,128]{3,2,1,0:T(2,128)(2,1)S(1)} %reshape.104), kind=kOutput, calls=%fused_computation.11 | convolution fusion | flops 102236160 | bytes 3933744 | tf_op jit(solution)/shard_map/cthd,chde->cthe/dot_general | solution.py:78
  72.0 2.3 %copy.25 = bf16[12,128,2,128]{3,2,1,0:T(2,128)(2,1)S(1)} copy(bf16[12,128,2,128]{1,3,2,0:T(8,128)(2,1)} %fusion.3) | data formatting | bytes 1572864 | tf_op jit(solution)/shard_map/convert_element_type | solution.py:95
  74.3 1.0 copy.58
  75.4 0.4 copy-done.3
  75.8 0.5 copy.26
  76.5 6.8 %collective-permute-start.5 = (bf16[256,256]{1,0:T(8,128)(2,1)S(1)}, bf16[256,256]{1,0:T(8,128)(2,1)S(1)}, u32[]{:S(2)}, u32[]{:S(2)}) collective-permute-start(bf16[256,256]{1,0:T(8,128)(2,1)S(1)} %bitcast.84), channel_id=1, source_target_pairs={{0,1},{1,2},{2,3},{3,4},{4,5},{5,6},{6,7},{7,0},{8,9},{9,10},{10,1... | collective-permute-start | bytes 393224 | tf_op jit(solution)/shard_map/ppermute | solution.py:26
  83.4 1.4 collective-permute-start.6
  84.9 0.3 collective-permute-start.7
  85.3 2.0 %collective-permute-start.8 = (bf16[256,256]{1,0:T(8,128)(2,1)S(1)}, bf16[256,256]{1,0:T(8,128)(2,1)S(1)}, u32[]{:S(2)}, u32[]{:S(2)}) collective-permute-start(bf16[256,256]{1,0:T(8,128)(2,1)S(1)} %bitcast.81), channel_id=1, source_target_pairs={{0,4},{1,5},{2,6},{3,7},{4,0},{5,1},{6,2},{7,3},{8,12},{9,13},{10,... | collective-permute-start | bytes 393224 | tf_op jit(solution)/shard_map/ppermute | solution.py:26
  87.4 1.1 collective-permute-start.9
  88.6 0.8 copy.33
  89.3 0.8 copy.34
  90.2 1.6 %collective-permute-start.10 = (bf16[256,256]{1,0:T(8,128)(2,1)}, bf16[256,256]{1,0:T(8,128)(2,1)S(1)}, u32[]{:S(2)}, u32[]{:S(2)}) collective-permute-start(bf16[256,256]{1,0:T(8,128)(2,1)} %bitcast.86), channel_id=1, source_target_pairs={{0,6},{1,7},{2,0},{3,1},{4,2},{5,3},{6,4},{7,5},{8,14},{9,15},{10,... | collective-permute-start | bytes 393224 | tf_op jit(solution)/shard_map/ppermute | solution.py:26
  91.8 1.3 collective-permute-start.11
  93.2 5.1 %collective-permute-done.9 = bf16[256,256]{1,0:T(8,128)(2,1)S(1)} collective-permute-done((bf16[256,256]{1,0:T(8,128)(2,1)S(1)}, bf16[256,256]{1,0:T(8,128)(2,1)S(1)}, u32[]{:S(2)}, u32[]{:S(2)}) %collective-permute-start.9) | collective-permute-done | bytes 131104 | tf_op jit(solution)/shard_map/ppermute | solution.py:26
  98.4 5.3 %collective-permute-done.10 = bf16[256,256]{1,0:T(8,128)(2,1)S(1)} collective-permute-done((bf16[256,256]{1,0:T(8,128)(2,1)}, bf16[256,256]{1,0:T(8,128)(2,1)S(1)}, u32[]{:S(2)}, u32[]{:S(2)}) %collective-permute-start.10) | collective-permute-done | bytes 131104 | tf_op jit(solution)/shard_map/ppermute | solution.py:26
  103.7 2.1 %collective-permute-done.11 = bf16[256,256]{1,0:T(8,128)(2,1)S(1)} collective-permute-done((bf16[256,256]{1,0:T(8,128)(2,1)S(1)}, bf16[256,256]{1,0:T(8,128)(2,1)S(1)}, u32[]{:S(2)}, u32[]{:S(2)}) %collective-permute-start.11) | collective-permute-done | bytes 131104 | tf_op jit(solution)/shard_map/ppermute | solution.py:26
  105.8 25.8 %all-gather.2.cloned.1.call-done = bf16[1536,2048]{1,0:T(8,128)(2,1)} async-done(((bf16[1536,256]{1,0:T(8,128)(2,1)}), bf16[1536,2048]{1,0:T(8,128)(2,1)}) %all-gather.2.cloned.1.call-update) | async-done | bytes 6291472 | tf_op jit(solution)/shard_map/all_gather | solution.py:97
  131.6 5.5 %convolution_convert_fusion = bf16[1536,256]{1,0:T(8,128)(2,1)} fusion(bf16[1536,2048]{1,0:T(8,128)(2,1)} %all-gather.2.cloned.1.call-done, bf16[2048,256]{1,0:T(8,128)(2,1)S(1)} %bitcast.77), kind=kOutput, calls=%fused_computation.4 | convolution fusion | flops 1611005952 | bytes 8126464 | tf_op jit(solution)/shard_map/dot_general | solution.py:98
  (40 shorter events, 1.3 us)
Async XLA Ops:
  6.5 1.5 %copy-start = (bf16[2048,256]{1,0:T(8,128)(2,1)S(1)}, bf16[2048,256]{1,0:T(8,128)(2,1)}, u32[]{:S(2)}) copy-start(bf16[2048,256]{1,0:T(8,128)(2,1)} %param.12) | copy-start | bytes 3145732
  6.5 125.0 %all-gather.2.cloned.1.call-start = ((), (), s32[]{:S(2)}) async-start(), calls=%async_computation | async-start | bytes 7077888 | tf_op jit(solution)/shard_map/all_gather | solution.py:97
  19.2 29.5 %copy-start.2 = (bf16[12,2,128,128]{3,2,1,0:T(8,128)(2,1)}, bf16[12,2,128,128]{3,2,1,0:T(8,128)(2,1)S(1)}, u32[]{:S(2)}) copy-start(bf16[12,2,128,128]{3,2,1,0:T(8,128)(2,1)S(1)} %convolution_convert_fusion.2) | copy-start | bytes 2359300
  20.6 8.5 %collective-permute-start = (f32[2,128,128]{2,1,0:T(8,128)S(1)}, f32[2,128,128]{2,1,0:T(8,128)}, u32[]{:S(2)}, u32[]{:S(2)}) collective-permute-start(f32[2,128,128]{2,1,0:T(8,128)S(1)} %bitcast.78), channel_id=1, source_target_pairs={{0,8},{8,16},{16,24},{24,32},{32,40},{40,48},{48,56},{56,64},{64,7... | collective-permute-start | bytes 393224 | tf_op jit(solution)/shard_map/ppermute | solution.py:63
  30.7 8.4 %collective-permute-start.1 = (f32[2,128,128]{2,1,0:T(8,128)}, f32[2,128,128]{2,1,0:T(8,128)}, u32[]{:S(2)}, u32[]{:S(2)}) collective-permute-start(f32[2,128,128]{2,1,0:T(8,128)} %multiply_add_fusion.3), channel_id=1, source_target_pairs={{0,16},{8,24},{16,32},{24,40},{32,48},{40,56},{48,64},{56,72},{64,... | collective-permute-start | bytes 393224 | tf_op jit(solution)/shard_map/ppermute | solution.py:63
  40.1 8.7 %copy-start.4 = (f32[2,128,128]{2,1,0:T(8,128)}, f32[2,128,128]{2,1,0:T(8,128)S(1)}, u32[]{:S(2)}) copy-start(f32[2,128,128]{2,1,0:T(8,128)S(1)} %multiply_add_fusion.2) | copy-start | bytes 393220
  40.1 11.4 %collective-permute-start.2 = (f32[2,128,128]{2,1,0:T(8,128)S(1)}, f32[2,128,128]{2,1,0:T(8,128)}, u32[]{:S(2)}, u32[]{:S(2)}) collective-permute-start(f32[2,128,128]{2,1,0:T(8,128)S(1)} %multiply_add_fusion.2), channel_id=1, source_target_pairs={{0,32},{8,40},{16,48},{24,56},{32,64},{40,72},{48,80},{56,88},{64,... | collective-permute-start | bytes 393224 | tf_op jit(solution)/shard_map/ppermute | solution.py:63
  52.5 7.3 %collective-permute-start.3 = (f32[2,128,128]{2,1,0:T(8,128)S(1)}, f32[2,128,128]{2,1,0:T(8,128)}, u32[]{:S(2)}, u32[]{:S(2)}) collective-permute-start(f32[2,128,128]{2,1,0:T(8,128)S(1)} %multiply_add_fusion.1), channel_id=1, source_target_pairs={{0,64},{8,72},{16,80},{24,88},{32,96},{40,104},{48,112},{56,120},{... | collective-permute-start | bytes 393224 | tf_op jit(solution)/shard_map/ppermute | solution.py:63
  56.1 14.2 %copy-start.1 = (f32[12,2,128,128]{3,2,1,0:T(8,128)S(1)}, f32[12,2,128,128]{3,2,1,0:T(8,128)}, u32[]{:S(2)}) copy-start(f32[12,2,128,128]{3,2,1,0:T(8,128)} %fusion.2) | copy-start | bytes 4718596
  56.1 14.3 %copy-start.6 = (pred[12,128]{1,0:T(8,128)(4,1)S(1)}, pred[12,128]{1,0:T(8,128)(4,1)}, u32[]{:S(2)}) copy-start(pred[12,128]{1,0:T(8,128)(4,1)} %get-tuple-element.29) | copy-start | bytes 4612
  60.7 7.8 %collective-permute-start.4 = (f32[2,128,128]{2,1,0:T(8,128)S(1)}, f32[2,128,128]{2,1,0:T(8,128)S(1)}, u32[]{:S(2)}, u32[]{:S(2)}) collective-permute-start(f32[2,128,128]{2,1,0:T(8,128)S(1)} %multiply_add_fusion), channel_id=1, source_target_pairs={{0,8},{8,16},{16,24},{24,32},{32,40},{40,48},{48,56},{56,64},{64,7... | collective-permute-start | bytes 393224 | tf_op jit(solution)/shard_map/ppermute | solution.py:65
  74.3 1.5 %copy-start.3 = (bf16[256,2048]{1,0:T(8,128)(2,1)S(1)}, bf16[256,2048]{1,0:T(8,128)(2,1)}, u32[]{:S(2)}) copy-start(bf16[256,2048]{1,0:T(8,128)(2,1)} %param.13) | copy-start | bytes 3145732
  76.5 13.7 %collective-permute-start.5 = (bf16[256,256]{1,0:T(8,128)(2,1)S(1)}, bf16[256,256]{1,0:T(8,128)(2,1)S(1)}, u32[]{:S(2)}, u32[]{:S(2)}) collective-permute-start(bf16[256,256]{1,0:T(8,128)(2,1)S(1)} %bitcast.84), channel_id=1, source_target_pairs={{0,1},{1,2},{2,3},{3,4},{4,5},{5,6},{6,7},{7,0},{8,9},{9,10},{10,1... | collective-permute-start | bytes 393224 | tf_op jit(solution)/shard_map/ppermute | solution.py:26
  83.4 8.4 %collective-permute-start.6 = (bf16[256,256]{1,0:T(8,128)(2,1)S(1)}, bf16[256,256]{1,0:T(8,128)(2,1)S(1)}, u32[]{:S(2)}, u32[]{:S(2)}) collective-permute-start(bf16[256,256]{1,0:T(8,128)(2,1)S(1)} %bitcast.83), channel_id=1, source_target_pairs={{0,2},{1,3},{2,4},{3,5},{4,6},{5,7},{6,0},{7,1},{8,10},{9,11},{10,... | collective-permute-start | bytes 393224 | tf_op jit(solution)/shard_map/ppermute | solution.py:26
  84.9 8.2 %collective-permute-start.7 = (bf16[256,256]{1,0:T(8,128)(2,1)S(1)}, bf16[256,256]{1,0:T(8,128)(2,1)S(1)}, u32[]{:S(2)}, u32[]{:S(2)}) collective-permute-start(bf16[256,256]{1,0:T(8,128)(2,1)S(1)} %bitcast.82), channel_id=1, source_target_pairs={{0,3},{1,4},{2,5},{3,6},{4,7},{5,0},{6,1},{7,2},{8,11},{9,12},{10,... | collective-permute-start | bytes 393224 | tf_op jit(solution)/shard_map/ppermute | solution.py:26
  85.3 7.9 %collective-permute-start.8 = (bf16[256,256]{1,0:T(8,128)(2,1)S(1)}, bf16[256,256]{1,0:T(8,128)(2,1)S(1)}, u32[]{:S(2)}, u32[]{:S(2)}) collective-permute-start(bf16[256,256]{1,0:T(8,128)(2,1)S(1)} %bitcast.81), channel_id=1, source_target_pairs={{0,4},{1,5},{2,6},{3,7},{4,0},{5,1},{6,2},{7,3},{8,12},{9,13},{10,... | collective-permute-start | bytes 393224 | tf_op jit(solution)/shard_map/ppermute | solution.py:26
  87.4 10.9 %collective-permute-start.9 = (bf16[256,256]{1,0:T(8,128)(2,1)S(1)}, bf16[256,256]{1,0:T(8,128)(2,1)S(1)}, u32[]{:S(2)}, u32[]{:S(2)}) collective-permute-start(bf16[256,256]{1,0:T(8,128)(2,1)S(1)} %bitcast.80), channel_id=1, source_target_pairs={{0,5},{1,6},{2,7},{3,0},{4,1},{5,2},{6,3},{7,4},{8,13},{9,14},{10,... | collective-permute-start | bytes 393224 | tf_op jit(solution)/shard_map/ppermute | solution.py:26
  90.1 1.7 %copy-start.5 = (bf16[256,1,256]{2,0,1:T(8,128)(2,1)S(1)}, bf16[256,1,256]{2,0,1:T(8,128)(2,1)}, u32[]{:S(2)}) copy-start(bf16[256,1,256]{2,0,1:T(8,128)(2,1)} %copy.34) | copy-start | bytes 393220
  90.2 13.5 %collective-permute-start.10 = (bf16[256,256]{1,0:T(8,128)(2,1)}, bf16[256,256]{1,0:T(8,128)(2,1)S(1)}, u32[]{:S(2)}, u32[]{:S(2)}) collective-permute-start(bf16[256,256]{1,0:T(8,128)(2,1)} %bitcast.86), channel_id=1, source_target_pairs={{0,6},{1,7},{2,0},{3,1},{4,2},{5,3},{6,4},{7,5},{8,14},{9,15},{10,... | collective-permute-start | bytes 393224 | tf_op jit(solution)/shard_map/ppermute | solution.py:26
  91.8 14.0 %collective-permute-start.11 = (bf16[256,256]{1,0:T(8,128)(2,1)S(1)}, bf16[256,256]{1,0:T(8,128)(2,1)S(1)}, u32[]{:S(2)}, u32[]{:S(2)}) collective-permute-start(bf16[256,256]{1,0:T(8,128)(2,1)S(1)} %bitcast.85), channel_id=1, source_target_pairs={{0,7},{1,0},{2,1},{3,2},{4,3},{5,4},{6,5},{7,6},{8,15},{9,8},{10,9... | collective-permute-start | bytes 393224 | tf_op jit(solution)/shard_map/ppermute | solution.py:26
Sparse Core Ops, SparseCore 0:
  75.4 56.1 all-gather.1

commit v3 on v2

--- a/solution.py
+++ b/solution.py
@@ -39,6 +39,7 @@
     value_rows = jnp.where(
         live_mask, jnp.dot(tokens, w_value, preferred_element_type=jnp.float32), 0.0
     ).astype(jnp.bfloat16)
+    w_query, w_out_cols = lax.optimization_barrier((w_query, w_out_cols))
     query_rows = jnp.dot(tokens, w_query, preferred_element_type=jnp.float32).astype(jnp.bfloat16)
     query_blocks = query_rows.reshape(group_local, CH, head_dev, HS)
     key_blocks = key_rows.reshape(group_local, CH, head_dev, HS)
@@ -53,20 +54,29 @@
     tail = jnp.einsum(
         "c,chde->hde", last_row.astype(jnp.bfloat16), states, preferred_element_type=jnp.float32
     )
-    last_group = first_group + group_local - 1
-    scan = tail
-    shift = 1
-    while shift < seq_count:
-        source = jnp.maximum(seq_index - shift, 0) * group_local + group_local - 1
-        joined = jnp.where(seq_index >= shift, readers[last_group, source], 0).astype(jnp.float32)
-        pairs = [(i, i + shift) for i in range(seq_count - shift)]
-        scan = scan + joined * lax.ppermute(scan, "seq", pairs)
-        shift *= 2
-    before = lax.ppermute(scan, "seq", [(i, i + 1) for i in range(seq_count - 1)])
-    enters = jnp.where(
-        seq_index > 0, lax.dynamic_index_in_dim(reader_rows, first_group - 1, 1, False), 0
-    ).astype(jnp.float32)
-    carried_in = enters[:, None, None, None] * before[None]
+    first_reader = first_group
+    last_reader = first_group + group_local - 1
+    inclusive = tail
+    entering = jnp.zeros_like(tail)
+    span = 1
+    while span < seq_count:
+        step_inclusive = inclusive
+        for j in range(1, 4):
+            shift = j * span
+            if shift >= seq_count:
+                break
+            pairs = [(i, i + shift) for i in range(seq_count - shift)]
+            moved = lax.ppermute(inclusive, "seq", pairs)
+            source = jnp.maximum(seq_index - shift, 0) * group_local + group_local - 1
+            has = seq_index >= shift
+            to_last = jnp.where(has, readers[last_reader, source], 0).astype(jnp.float32)
+            to_first = jnp.where(has, readers[first_reader, source], 0).astype(jnp.float32)
+            step_inclusive = step_inclusive + to_last * moved
+            entering = entering + to_first * moved
+        inclusive = step_inclusive
+        span *= 4
+    enters = local_readers[:, 0].at[0].set(1).astype(jnp.float32)
+    carried_in = enters[:, None, None, None] * entering[None]
     own = jnp.einsum(
         "ce,ehij->chij",
         local_readers.astype(jnp.bfloat16),

time: 145 us -> 151 us (1.041)
  the two profiles are of different devices: /device:TPU:49 before, /device:TPU:1 now
where the time goes in v3:
time: 151 us; the launch traced here: 150 us
  waiting for transfers between devices  41.5 us (27%)
  matrix products  30.9 us (20%)
  starting transfers between devices  29 us (19%)
  local copies, waits for them, and re-layouts  24.6 us (16%)
  between operations  19.6 us (13%)
  other arithmetic  4.15 us (3%)
    all_gather x1, waiting for transfers between devices, local(): mixed_all = lax.all_gather(mixed, 'tp', axis=1, tiled=True)  41.4 us
    ppermute x6, starting transfers between devices, local(): moved = lax.ppermute(inclusive, 'seq', pairs)  18 us
    ppermute x7, starting transfers between devices, local(): piece = lax.ppermute(piece, 'tp', pairs)  11.1 us
    dynamic_slice x9, local copies, waits for them, and re-layouts, local(): lax.dynamic_index_in_dim(out_blocks, (tp_index + shift) % tp_count, 1, Fa...  7.61 us
    dot_general x1, matrix products, local(): jnp.dot(tokens, w_query, preferred_element_type=jnp.float32)  5.6 us
    dot_general x1, matrix products, local(): jnp.dot(mixed_all, w_out_cols, preferred_element_type=jnp.float32)  5.46 us
    dot_general x1, matrix products, local(): jnp.dot(tokens, w_key, preferred_element_type=jnp.float32)  5.12 us
    dot_general x1, matrix products, local(): jnp.dot(tokens, w_value, preferred_element_type=jnp.float32)  4.58 us
  transfers between devices with their start and end apart: 14, of which 1 were waited for; matrix products, arithmetic and copies ran while one was open for 18% of the time, Pallas kernels for 0%

profile of v3, /device:TPU:1, one launch (start us, length us, event | category | flops | bytes accessed | tf_op | source)
XLA Modules:
  0.0 149.7 jit_solution(13797548744185986766)
XLA Ops:
  6.5 0.8 dynamic_slice.61
  7.4 0.7 iota_compare_fusion.1
  8.0 4.6 %fusion.1 = bf16[1536,256]{1,0:T(8,128)(2,1)S(1)} fusion(bf16[1536,2048]{1,0:T(8,128)(2,1)} %param.11, bf16[2048,256]{1,0:T(8,128)(2,1)S(1)} %copy-done, pred[1536]{0:T(1024)(128)(4,1)S(1)} %get-tuple-element.51), kind=kOutput, calls=%fused_computation.3 | convolution fusion | flops 1611399168 | bytes 8128000 | tf_op jit(solution)/shard_map/dot_general | solution.py:40
  12.6 0.2 reshape.112
  12.8 0.6 copy.35
  13.5 5.1 %fusion = bf16[1536,256]{1,0:T(8,128)(2,1)S(1)} fusion(bf16[1536,2048]{1,0:T(8,128)(2,1)} %param.11, bf16[2048,256]{1,0:T(8,128)(2,1)} %param.13, pred[1536]{0:T(1024)(128)(4,1)S(1)} %get-tuple-element.51), kind=kOutput, calls=%fused_computation.2 | convolution fusion | flops 1611399168 | bytes 8128000 | tf_op jit(solution)/shard_map/dot_general | solution.py:37
  18.8 0.8 dynamic-slice_bitcast_fusion
  19.7 0.7 convolution_convert_fusion.2
  20.4 1.2 fusion.7
  21.6 5.8 %collective-permute-start.2 = (f32[2,128,128]{2,1,0:T(8,128)}, f32[2,128,128]{2,1,0:T(8,128)}, u32[]{:S(2)}, u32[]{:S(2)}) collective-permute-start(f32[2,128,128]{2,1,0:T(8,128)} %bitcast.6), channel_id=1, source_target_pairs={{0,24},{8,32},{16,40},{24,48},{32,56},{40,64},{48,72},{56,80},{64,... | collective-permute-start | bytes 393224 | tf_op jit(solution)/shard_map/ppermute | solution.py:69
  27.4 4.1 %collective-permute-start.1 = (f32[2,128,128]{2,1,0:T(8,128)}, f32[2,128,128]{2,1,0:T(8,128)}, u32[]{:S(2)}, u32[]{:S(2)}) collective-permute-start(f32[2,128,128]{2,1,0:T(8,128)} %bitcast.6), channel_id=1, source_target_pairs={{0,16},{8,24},{16,32},{24,40},{32,48},{40,56},{48,64},{56,72},{64,... | collective-permute-start | bytes 393224 | tf_op jit(solution)/shard_map/ppermute | solution.py:69
  31.5 2.5 %collective-permute-start = (f32[2,128,128]{2,1,0:T(8,128)}, f32[2,128,128]{2,1,0:T(8,128)}, u32[]{:S(2)}, u32[]{:S(2)}) collective-permute-start(f32[2,128,128]{2,1,0:T(8,128)} %bitcast.6), channel_id=1, source_target_pairs={{0,8},{8,16},{16,24},{24,32},{32,40},{40,48},{48,56},{56,64},{64,7... | collective-permute-start | bytes 393224 | tf_op jit(solution)/shard_map/ppermute | solution.py:69
  34.0 1.5 copy.21
  35.6 0.8 constant_dynamic-slice_fusion
  36.4 1.7 %copy.23 = bf16[256,1,256]{2,0,1:T(8,128)(2,1)} copy(bf16[256,1,256]{0,2,1:T(8,128)(2,1)} %get-tuple-element.39) | data formatting | bytes 262144 | tf_op jit(solution)/shard_map/jit(dynamic_index_in_dim)/dynamic_slice | solution.py:23
  38.0 3.0 %collective-permute-start.6 = (bf16[256,256]{1,0:T(8,128)(2,1)}, bf16[256,256]{1,0:T(8,128)(2,1)}, u32[]{:S(2)}, u32[]{:S(2)}) collective-permute-start(bf16[256,256]{1,0:T(8,128)(2,1)} %bitcast.19), channel_id=1, source_target_pairs={{0,1},{1,2},{2,3},{3,4},{4,5},{5,6},{6,7},{7,0},{8,9},{9,10},{10,1... | collective-permute-start | bytes 393224 | tf_op jit(solution)/shard_map/ppermute | solution.py:26
  41.1 1.7 %copy.24 = bf16[256,1,256]{2,0,1:T(8,128)(2,1)} copy(bf16[256,1,256]{0,2,1:T(8,128)(2,1)} %get-tuple-element.38) | data formatting | bytes 262144 | tf_op jit(solution)/shard_map/jit(dynamic_index_in_dim)/dynamic_slice | solution.py:23
  42.7 1.6 %collective-permute-start.7 = (bf16[256,256]{1,0:T(8,128)(2,1)}, bf16[256,256]{1,0:T(8,128)(2,1)}, u32[]{:S(2)}, u32[]{:S(2)}) collective-permute-start(bf16[256,256]{1,0:T(8,128)(2,1)} %bitcast.21), channel_id=1, source_target_pairs={{0,2},{1,3},{2,4},{3,5},{4,6},{5,7},{6,0},{7,1},{8,10},{9,11},{10,... | collective-permute-start | bytes 393224 | tf_op jit(solution)/shard_map/ppermute | solution.py:26
  44.4 1.7 %copy.22 = bf16[256,1,256]{2,0,1:T(8,128)(2,1)} copy(bf16[256,1,256]{0,2,1:T(8,128)(2,1)} %get-tuple-element.40) | data formatting | bytes 262144 | tf_op jit(solution)/shard_map/jit(dynamic_index_in_dim)/dynamic_slice | solution.py:23
  46.1 0.9 bitcast_dynamic-update-slice_fusion.7
  47.0 1.4 fusion.6
  48.4 0.9 dynamic-slice_reduce_fusion
  49.3 0.5 convert_element_type.75
  49.9 1.6 %fusion.31 = (s32[1,1]{1,0:T(1,128)}, s32[1,1]{1,0:T(1,128)}, s32[1,1]{1,0:T(1,128)}, s32[1,1]{1,0:T(1,128)}, s32[1,1]{1,0:T(1,128)}, /*index=5*/s32[1,1]{1,0:T(...) fusion(s32[192,192]{1,0:T(8,128)} %param.16, s32[]{:T(128)S(6)} %select_n.196, s32[]{:T(128)S(6)} %select_n.198, ...), kind=kLoop, calls=%fused_computation.60 | loop fusion | bytes 104 | tf_op jit(solution)/shard_map/dynamic_slice | solution.py:73
  57.1 0.8 copy.29
  57.9 0.8 copy.28
  59.1 2.0 %collective-permute-start.8 = (bf16[256,256]{1,0:T(8,128)(2,1)S(1)}, bf16[256,256]{1,0:T(8,128)(2,1)S(1)}, u32[]{:S(2)}, u32[]{:S(2)}) collective-permute-start(bf16[256,256]{1,0:T(8,128)(2,1)S(1)} %bitcast.93), channel_id=1, source_target_pairs={{0,3},{1,4},{2,5},{3,6},{4,7},{5,0},{6,1},{7,2},{8,11},{9,12},{10,... | collective-permute-start | bytes 393224 | tf_op jit(solution)/shard_map/ppermute | solution.py:26
  61.1 2.3 %collective-permute-start.10 = (bf16[256,256]{1,0:T(8,128)(2,1)S(1)}, bf16[256,256]{1,0:T(8,128)(2,1)S(1)}, u32[]{:S(2)}, u32[]{:S(2)}) collective-permute-start(bf16[256,256]{1,0:T(8,128)(2,1)S(1)} %bitcast.91), channel_id=1, source_target_pairs={{0,5},{1,6},{2,7},{3,0},{4,1},{5,2},{6,3},{7,4},{8,13},{9,14},{10,... | collective-permute-start | bytes 393224 | tf_op jit(solution)/shard_map/ppermute | solution.py:26
  63.5 1.8 %multiply_add_fusion.1 = f32[2,128,128]{2,1,0:T(8,128)} fusion(f32[2,128,128]{2,1,0:T(8,128)} %collective-permute-done.2, f32[2,128,128]{2,1,0:T(8,128)} %collective-permute-done.1, f32[2,128,128]{2,1,0:T(8,128)} %bitcast.6, f32[2,128,128]{2,1,0:T(8,128)} %collective-permute-done, f32[]{:T(128)S(6)} %convert_element_type.86, f32[]{:T(128)S(6)} %convert_element_type.85, ...), kind=kLoop, calls=%fused_computation.36 | loop fusion | flops 196608 | bytes 655372 | tf_op jit(solution)/shard_map/add | solution.py:74
  65.2 0.9 collective-permute-start.11
  66.1 0.9 bitcast_dynamic-update-slice_fusion.6
  67.0 1.2 collective-permute-start.12
  68.2 0.9 bitcast_dynamic-update-slice_fusion.5
  69.1 1.3 collective-permute-start.5
  70.5 2.7 %collective-permute-start.4 = (f32[2,128,128]{2,1,0:T(8,128)}, f32[2,128,128]{2,1,0:T(8,128)S(1)}, u32[]{:S(2)}, u32[]{:S(2)}) collective-permute-start(f32[2,128,128]{2,1,0:T(8,128)} %multiply_add_fusion.1), channel_id=1, source_target_pairs={{0,64},{8,72},{16,80},{24,88},{32,96},{40,104},{48,112},{56,120},{... | collective-permute-start | bytes 393224 | tf_op jit(solution)/shard_map/ppermute | solution.py:69
  73.2 1.5 collective-permute-start.3
  74.8 0.9 copy-done.6
  75.8 5.6 %fusion.2 = bf16[1536,256]{0,1:T(8,128)(2,1)} fusion(bf16[2048,256]{1,0:T(8,128)(2,1)S(1)} %copy-done.12, bf16[1536,2048]{1,0:T(8,128)(2,1)} %param.11), kind=kOutput, calls=%fused_computation.6 | convolution fusion | flops 1611005952 | bytes 8126464 | tf_op jit(solution)/shard_map/dot_general | solution.py:43
  81.4 1.6 %reshape.122 = bf16[12,128,2,128]{1,0,3,2:T(8,128)(2,1)S(1)} reshape(bf16[1536,256]{0,1:T(8,128)(2,1)} %fusion.2) | data formatting | bytes 1572864 | tf_op jit(solution)/shard_map/reshape | solution.py:44
  83.0 1.5 %copy.32 = bf16[12,128,2,128]{3,1,2,0:T(8,128)(2,1)} copy(bf16[12,128,2,128]{1,0,3,2:T(8,128)(2,1)S(1)} %reshape.122) | data formatting | bytes 1572864 | tf_op jit(solution)/shard_map/reshape | solution.py:44
  84.6 1.2 multiply_add_fusion
  85.7 1.4 add_convert_fusion
  87.2 1.9 %fusion.11 = f32[12,2,128,128]{3,2,1,0:T(8,128)} fusion(bf16[12,128,2,128]{3,1,2,0:T(8,128)(2,1)S(1)} %copy-done.1, bf16[12,2,128,128]{3,0,2,1:T(8,128)(2,1)S(1)} %add_convert_fusion), kind=kOutput, calls=%fused_computation.21 | convolution fusion | flops 100663296 | bytes 3145728 | tf_op jit(solution)/shard_map/cthd,chde->cthe/dot_general | solution.py:88
  89.2 3.5 %fusion.3 = bf16[12,128,2,128]{1,3,2,0:T(8,128)(2,1)} fusion(f32[12,2,128,128]{3,2,1,0:T(8,128)} %fusion.11, bf16[12,128,2,128]{1,3,2,0:T(8,128)(2,1)S(1)} %copy-done.3, bf16[12,128,2,128]{3,1,2,0:T(8,128)(2,1)S(1)} %copy-done.1, f32[12]{0:T(128)S(1)} %copy-done.11, pred[128,128]{1,0:T(8,128)(4,1)S(1)} %iota_compare_fusion, ...), kind=kOutput, calls=%fused_computation.11 | convolution fusion | flops 203685888 | bytes 4736560 | tf_op jit(solution)/shard_map/chts,cshe->cthe/dot_general | solution.py:96
  92.7 2.3 %copy.36 = bf16[12,128,2,128]{3,2,1,0:T(2,128)(2,1)S(1)} copy(bf16[12,128,2,128]{1,3,2,0:T(8,128)(2,1)} %fusion.3) | data formatting | bytes 1572864 | tf_op jit(solution)/shard_map/convert_element_type | solution.py:105
  94.9 1.0 copy.57
  95.9 41.4 %all-gather.2.cloned.1.call-done = bf16[1536,2048]{1,0:T(8,128)(2,1)} async-done(((bf16[1536,256]{1,0:T(8,128)(2,1)}), bf16[1536,2048]{1,0:T(8,128)(2,1)}) %all-gather.2.cloned.1.call-update) | async-done | bytes 6291472 | tf_op jit(solution)/shard_map/all_gather | solution.py:107
  137.4 5.5 %convolution_convert_fusion = bf16[1536,256]{1,0:T(8,128)(2,1)} fusion(bf16[1536,2048]{1,0:T(8,128)(2,1)} %all-gather.2.cloned.1.call-done, bf16[2048,256]{1,0:T(8,128)(2,1)S(1)} %bitcast.88), kind=kOutput, calls=%fused_computation.4 | convolution fusion | flops 1611005952 | bytes 8126464 | tf_op jit(solution)/shard_map/dot_general | solution.py:108
  (57 shorter events, 0.8 us)
Async XLA Ops:
  6.5 1.5 %copy-start = (bf16[2048,256]{1,0:T(8,128)(2,1)S(1)}, bf16[2048,256]{1,0:T(8,128)(2,1)}, u32[]{:S(2)}) copy-start(bf16[2048,256]{1,0:T(8,128)(2,1)} %param.14) | copy-start | bytes 3145732
  6.5 130.8 %all-gather.2.cloned.1.call-start = ((), (), s32[]{:S(2)}) async-start(), calls=%async_computation | async-start | bytes 7077888 | tf_op jit(solution)/shard_map/all_gather | solution.py:107
  13.5 6.2 %copy-start.2 = (bf16[12,128,2,128]{1,3,2,0:T(8,128)(2,1)}, bf16[12,128,2,128]{1,3,2,0:T(8,128)(2,1)S(1)}, u32[]{:S(2)}) copy-start(bf16[12,128,2,128]{1,3,2,0:T(8,128)(2,1)S(1)} %copy.35) | copy-start | bytes 2359300
  18.8 2.8 %copy-start.4 = (bf16[12,128,2,128]{3,2,1,0:T(2,128)(2,1)}, bf16[12,128,2,128]{3,2,1,0:T(2,128)(2,1)S(1)}, u32[]{:S(2)}) copy-start(bf16[12,128,2,128]{3,2,1,0:T(2,128)(2,1)S(1)} %reshape.111) | copy-start | bytes 2359300
  21.6 37.5 %collective-permute-start.2 = (f32[2,128,128]{2,1,0:T(8,128)}, f32[2,128,128]{2,1,0:T(8,128)}, u32[]{:S(2)}, u32[]{:S(2)}) collective-permute-start(f32[2,128,128]{2,1,0:T(8,128)} %bitcast.6), channel_id=1, source_target_pairs={{0,24},{8,32},{16,40},{24,48},{32,56},{40,64},{48,72},{56,80},{64,... | collective-permute-start | bytes 393224 | tf_op jit(solution)/shard_map/ppermute | solution.py:69
  27.4 33.7 %collective-permute-start.1 = (f32[2,128,128]{2,1,0:T(8,128)}, f32[2,128,128]{2,1,0:T(8,128)}, u32[]{:S(2)}, u32[]{:S(2)}) collective-permute-start(f32[2,128,128]{2,1,0:T(8,128)} %bitcast.6), channel_id=1, source_target_pairs={{0,16},{8,24},{16,32},{24,40},{32,48},{40,56},{48,64},{56,72},{64,... | collective-permute-start | bytes 393224 | tf_op jit(solution)/shard_map/ppermute | solution.py:69
  31.5 29.6 %collective-permute-start = (f32[2,128,128]{2,1,0:T(8,128)}, f32[2,128,128]{2,1,0:T(8,128)}, u32[]{:S(2)}, u32[]{:S(2)}) collective-permute-start(f32[2,128,128]{2,1,0:T(8,128)} %bitcast.6), channel_id=1, source_target_pairs={{0,8},{8,16},{16,24},{24,32},{32,40},{40,48},{48,56},{56,64},{64,7... | collective-permute-start | bytes 393224 | tf_op jit(solution)/shard_map/ppermute | solution.py:69
  35.5 8.9 %copy-start.9 = (s32[192]{0:T(256)S(1)}, s32[192]{0:T(256)}, u32[]{:S(2)}) copy-start(s32[192]{0:T(256)} %param.17) | copy-start | bytes 2308
  38.0 27.2 %collective-permute-start.6 = (bf16[256,256]{1,0:T(8,128)(2,1)}, bf16[256,256]{1,0:T(8,128)(2,1)}, u32[]{:S(2)}, u32[]{:S(2)}) collective-permute-start(bf16[256,256]{1,0:T(8,128)(2,1)} %bitcast.19), channel_id=1, source_target_pairs={{0,1},{1,2},{2,3},{3,4},{4,5},{5,6},{6,7},{7,0},{8,9},{9,10},{10,1... | collective-permute-start | bytes 393224 | tf_op jit(solution)/shard_map/ppermute | solution.py:26
  42.7 24.3 %collective-permute-start.7 = (bf16[256,256]{1,0:T(8,128)(2,1)}, bf16[256,256]{1,0:T(8,128)(2,1)}, u32[]{:S(2)}, u32[]{:S(2)}) collective-permute-start(bf16[256,256]{1,0:T(8,128)(2,1)} %bitcast.21), channel_id=1, source_target_pairs={{0,2},{1,3},{2,4},{3,5},{4,6},{5,7},{6,0},{7,1},{8,10},{9,11},{10,... | collective-permute-start | bytes 393224 | tf_op jit(solution)/shard_map/ppermute | solution.py:26
  57.9 9.1 %copy-start.8 = (bf16[256,1,256]{2,0,1:T(8,128)(2,1)S(1)}, bf16[256,1,256]{2,0,1:T(8,128)(2,1)}, u32[]{:S(2)}) copy-start(bf16[256,1,256]{2,0,1:T(8,128)(2,1)} %copy.29) | copy-start | bytes 393220
  59.0 16.8 %copy-start.12 = (bf16[2048,256]{1,0:T(8,128)(2,1)S(1)}, bf16[2048,256]{1,0:T(8,128)(2,1)}, u32[]{:S(2)}) copy-start(bf16[2048,256]{1,0:T(8,128)(2,1)} %param.12) | copy-start | bytes 3145732
  59.1 10.1 %collective-permute-start.8 = (bf16[256,256]{1,0:T(8,128)(2,1)S(1)}, bf16[256,256]{1,0:T(8,128)(2,1)S(1)}, u32[]{:S(2)}, u32[]{:S(2)}) collective-permute-start(bf16[256,256]{1,0:T(8,128)(2,1)S(1)} %bitcast.93), channel_id=1, source_target_pairs={{0,3},{1,4},{2,5},{3,6},{4,7},{5,0},{6,1},{7,2},{8,11},{9,12},{10,... | collective-permute-start | bytes 393224 | tf_op jit(solution)/shard_map/ppermute | solution.py:26
  61.1 9.4 %collective-permute-start.9 = (bf16[256,256]{1,0:T(8,128)(2,1)S(1)}, bf16[256,256]{1,0:T(8,128)(2,1)S(1)}, u32[]{:S(2)}, u32[]{:S(2)}) collective-permute-start(bf16[256,256]{1,0:T(8,128)(2,1)S(1)} %bitcast.92), channel_id=1, source_target_pairs={{0,4},{1,5},{2,6},{3,7},{4,0},{5,1},{6,2},{7,3},{8,12},{9,13},{10,... | collective-permute-start | bytes 393224 | tf_op jit(solution)/shard_map/ppermute | solution.py:26
  61.1 12.1 %collective-permute-start.10 = (bf16[256,256]{1,0:T(8,128)(2,1)S(1)}, bf16[256,256]{1,0:T(8,128)(2,1)S(1)}, u32[]{:S(2)}, u32[]{:S(2)}) collective-permute-start(bf16[256,256]{1,0:T(8,128)(2,1)S(1)} %bitcast.91), channel_id=1, source_target_pairs={{0,5},{1,6},{2,7},{3,0},{4,1},{5,2},{6,3},{7,4},{8,13},{9,14},{10,... | collective-permute-start | bytes 393224 | tf_op jit(solution)/shard_map/ppermute | solution.py:26
  65.2 9.5 %collective-permute-start.11 = (bf16[256,256]{1,0:T(8,128)(2,1)}, bf16[256,256]{1,0:T(8,128)(2,1)S(1)}, u32[]{:S(2)}, u32[]{:S(2)}) collective-permute-start(bf16[256,256]{1,0:T(8,128)(2,1)} %bitcast.90), channel_id=1, source_target_pairs={{0,6},{1,7},{2,0},{3,1},{4,2},{5,3},{6,4},{7,5},{8,14},{9,15},{10,... | collective-permute-start | bytes 393224 | tf_op jit(solution)/shard_map/ppermute | solution.py:26
  67.0 7.8 %collective-permute-start.12 = (bf16[256,256]{1,0:T(8,128)(2,1)S(1)}, bf16[256,256]{1,0:T(8,128)(2,1)S(1)}, u32[]{:S(2)}, u32[]{:S(2)}) collective-permute-start(bf16[256,256]{1,0:T(8,128)(2,1)S(1)} %bitcast.89), channel_id=1, source_target_pairs={{0,7},{1,0},{2,1},{3,2},{4,3},{5,4},{6,5},{7,6},{8,15},{9,8},{10,9... | collective-permute-start | bytes 393224 | tf_op jit(solution)/shard_map/ppermute | solution.py:26
  69.1 15.4 %collective-permute-start.5 = (f32[2,128,128]{2,1,0:T(8,128)}, f32[2,128,128]{2,1,0:T(8,128)S(1)}, u32[]{:S(2)}, u32[]{:S(2)}) collective-permute-start(f32[2,128,128]{2,1,0:T(8,128)} %multiply_add_fusion.1), channel_id=1, source_target_pairs={{0,96},{8,104},{16,112},{24,120},{1,97},{9,105},{17,113},{25,121},... | collective-permute-start | bytes 393224 | tf_op jit(solution)/shard_map/ppermute | solution.py:69
  70.5 14.1 %collective-permute-start.4 = (f32[2,128,128]{2,1,0:T(8,128)}, f32[2,128,128]{2,1,0:T(8,128)S(1)}, u32[]{:S(2)}, u32[]{:S(2)}) collective-permute-start(f32[2,128,128]{2,1,0:T(8,128)} %multiply_add_fusion.1), channel_id=1, source_target_pairs={{0,64},{8,72},{16,80},{24,88},{32,96},{40,104},{48,112},{56,120},{... | collective-permute-start | bytes 393224 | tf_op jit(solution)/shard_map/ppermute | solution.py:69
  73.2 11.3 %collective-permute-start.3 = (f32[2,128,128]{2,1,0:T(8,128)}, f32[2,128,128]{2,1,0:T(8,128)S(1)}, u32[]{:S(2)}, u32[]{:S(2)}) collective-permute-start(f32[2,128,128]{2,1,0:T(8,128)} %multiply_add_fusion.1), channel_id=1, source_target_pairs={{0,32},{8,40},{16,48},{24,56},{32,64},{40,72},{48,80},{56,88},{64,... | collective-permute-start | bytes 393224 | tf_op jit(solution)/shard_map/ppermute | solution.py:69
  74.8 1.0 copy-start.6
  83.0 2.7 %copy-start.13 = (f32[12]{0:T(128)S(1)}, f32[12]{0:T(128)}, u32[]{:S(2)}) copy-start(f32[12]{0:T(128)} %convert_element_type.75) | copy-start | bytes 148
  84.6 2.6 %copy-start.1 = (bf16[12,128,2,128]{3,1,2,0:T(8,128)(2,1)S(1)}, bf16[12,128,2,128]{3,1,2,0:T(8,128)(2,1)}, u32[]{:S(2)}) copy-start(bf16[12,128,2,128]{3,1,2,0:T(8,128)(2,1)} %copy.32) | copy-start | bytes 2359300
  87.2 1.9 %copy-start.3 = (bf16[12,128,2,128]{1,3,2,0:T(8,128)(2,1)S(1)}, bf16[12,128,2,128]{1,3,2,0:T(8,128)(2,1)}, u32[]{:S(2)}) copy-start(bf16[12,128,2,128]{1,3,2,0:T(8,128)(2,1)} %copy-done.2) | copy-start | bytes 2359300
  87.2 1.9 %copy-start.5 = (bf16[12,128,2,128]{3,2,1,0:T(2,128)(2,1)S(1)}, bf16[12,128,2,128]{3,2,1,0:T(2,128)(2,1)}, u32[]{:S(2)}) copy-start(bf16[12,128,2,128]{3,2,1,0:T(2,128)(2,1)} %copy-done.4) | copy-start | bytes 2359300
  87.2 1.9 %copy-start.10 = (pred[12,128]{1,0:T(8,128)(4,1)S(1)}, pred[12,128]{1,0:T(8,128)(4,1)}, u32[]{:S(2)}) copy-start(pred[12,128]{1,0:T(8,128)(4,1)} %get-tuple-element.50) | copy-start | bytes 4612
  87.2 1.9 %copy-start.11 = (f32[12]{0:T(128)S(1)}, f32[12]{0:T(128)}, u32[]{:S(2)}) copy-start(f32[12]{0:T(128)} %fusion.6) | copy-start | bytes 148
  94.9 42.5 %copy-start.7 = (bf16[8,256,256]{2,1,0:T(8,128)(2,1)S(1)}, bf16[8,256,256]{2,1,0:T(8,128)(2,1)}, u32[]{:S(2)}) copy-start(bf16[8,256,256]{2,1,0:T(8,128)(2,1)} %copy-done.6) | copy-start | bytes 3145732
Sparse Core Ops, SparseCore 0:
  96.1 41.2 all-gather.1

commit v4 on v2

v4 whole, which is shorter than its diff:
```python
import jax
import jax.numpy as jnp
from jax import lax
from jax.sharding import PartitionSpec as P

HS = 128
CH = 128
ROW = 4
PAIR = 2


SEQ = ("sy", "sx")
TP = ("tz", "tc")


def local(tokens, w_query, w_key, w_value, w_out, readers, lengths):
    group_local = tokens.shape[0] // CH
    local_width = w_query.shape[1]
    head_dev = local_width // HS
    seq_count = readers.shape[0] // group_local
    row_count = seq_count // ROW
    tp_count = w_out.shape[1] // local_width
    chip_count = tp_count // PAIR
    chip_width = PAIR * local_width
    row_at = lax.axis_index("sy")
    seq_index = row_at * ROW + lax.axis_index("sx")
    core_at = lax.axis_index("tc")
    tp_index = lax.axis_index("tz") * PAIR + core_at
    first_group = seq_index * group_local

    out_blocks = w_out.reshape(local_width, chip_count, chip_width)
    w_out_chip = jnp.zeros((tp_count, local_width, chip_width), w_out.dtype)
    for shift in range(tp_count):
        target = (tp_index + shift) % tp_count
        piece = lax.dynamic_index_in_dim(out_blocks, target // PAIR, 1, False)
        if shift:
            pairs = [(i, (i + shift) % tp_count) for i in range(tp_count)]
            piece = lax.ppermute(piece, TP, pairs)
        w_out_chip = lax.dynamic_update_index_in_dim(
            w_out_chip, piece, (tp_index - shift) % tp_count, 0
        )
    w_out_chip = w_out_chip.reshape(tp_count * local_width, chip_width)

    local_lengths = lax.dynamic_slice_in_dim(lengths, first_group, group_local, 0)
    reader_rows = lax.dynamic_slice_in_dim(readers, first_group, group_local, 0)
    offsets = jnp.arange(CH, dtype=jnp.int32)
    live_mask = (offsets[None, :] < local_lengths[:, None]).reshape(-1)[:, None]
    key_rows = jnp.where(
        live_mask, jnp.dot(tokens, w_key, preferred_element_type=jnp.float32), 0.0
    ).astype(jnp.bfloat16)
    value_rows = jnp.where(
        live_mask, jnp.dot(tokens, w_value, preferred_element_type=jnp.float32), 0.0
    ).astype(jnp.bfloat16)
    w_query, w_out_chip = lax.optimization_barrier((w_query, w_out_chip))
    query_rows = jnp.dot(tokens, w_query, preferred_element_type=jnp.float32).astype(jnp.bfloat16)
    query_blocks = query_rows.reshape(group_local, CH, head_dev, HS)
    key_blocks = key_rows.reshape(group_local, CH, head_dev, HS)
    value_blocks = value_rows.reshape(group_local, CH, head_dev, HS)

    states = jnp.einsum(
        "cshd,cshe->chde", key_blocks, value_blocks, preferred_element_type=jnp.float32
    ).astype(jnp.bfloat16)

    local_readers = lax.dynamic_slice_in_dim(reader_rows, first_group, group_local, 1)
    last_row = local_readers[group_local - 1].at[group_local - 1].set(1)
    tail = jnp.einsum(
        "c,chde->hde", last_row.astype(jnp.bfloat16), states, preferred_element_type=jnp.float32
    )
    row_tails = lax.all_gather(tail, "sx", axis=0, tiled=False)
    row_lasts = (row_at * ROW + jnp.arange(ROW)) * group_local + group_local - 1
    in_row = readers[row_lasts[ROW - 1], row_lasts].at[ROW - 1].set(1).astype(jnp.float32)
    row_sum = (in_row[:, None, None, None] * row_tails).sum(0)
    row_sums = lax.all_gather(row_sum, "sy", axis=0, tiled=False)
    row_ends = (jnp.arange(row_count) * ROW + ROW - 1) * group_local + group_local - 1
    from_rows = readers[first_group, row_ends].astype(jnp.float32)
    from_row = readers[first_group, row_lasts].astype(jnp.float32)
    entering = (from_row[:, None, None, None] * row_tails).sum(0) + (
        from_rows[:, None, None, None] * row_sums
    ).sum(0)
    enters = local_readers[:, 0].at[0].set(1).astype(jnp.float32)
    carried_in = enters[:, None, None, None] * entering[None]
    own = jnp.einsum(
        "ce,ehij->chij",
        local_readers.astype(jnp.bfloat16),
        states,
        preferred_element_type=jnp.float32,
    )
    prefix = (carried_in + own).astype(jnp.bfloat16)

    carried = jnp.einsum(
        "cthd,chde->cthe", query_blocks, prefix, preferred_element_type=jnp.float32
    )
    scores = jnp.einsum(
        "cthd,cshd->chts", query_blocks, key_blocks, preferred_element_type=jnp.float32
    )
    causal = offsets[:, None] >= offsets[None, :]
    weights = jnp.where(causal[None, None], scores, 0.0).astype(jnp.bfloat16)
    within = jnp.einsum(
        "chts,cshe->cthe", weights, value_blocks, preferred_element_type=jnp.float32
    )
    length_float = lengths.astype(jnp.float32)
    keys_read = local_lengths.astype(jnp.float32) + jnp.dot(
        reader_rows.astype(jnp.float32), length_float, precision=lax.Precision.HIGHEST
    )
    row_scale = lax.rsqrt(HS * keys_read)
    mixed = (carried + within) * row_scale[:, None, None, None]
    mixed = jnp.where(live_mask.reshape(group_local, CH, 1, 1), mixed, 0.0).astype(jnp.bfloat16)
    mixed = mixed.reshape(group_local * CH, local_width)

    half = group_local * CH // PAIR
    pair_mixed = lax.all_gather(mixed, "tc", axis=1, tiled=True)
    mine = lax.dynamic_slice_in_dim(pair_mixed, core_at * half, half, 0)
    full = lax.all_gather(mine, "tz", axis=1, tiled=True)
    part = jnp.dot(full, w_out_chip, preferred_element_type=jnp.float32).astype(jnp.bfloat16)
    kept = lax.dynamic_slice_in_dim(part, core_at * local_width, local_width, 1)
    given = lax.dynamic_slice_in_dim(part, (1 - core_at) * local_width, local_width, 1)
    got = lax.ppermute(given, "tc", [(0, 1), (1, 0)])
    result = jnp.zeros((group_local * CH, local_width), part.dtype)
    result = lax.dynamic_update_slice_in_dim(result, kept, core_at * half, 0)
    return lax.dynamic_update_slice_in_dim(result, got, (1 - core_at) * half, 0)


def solution(mesh):
    seq_count, tp_count = mesh.devices.shape
    split = jax.sharding.Mesh(
        mesh.devices.reshape(seq_count // ROW, ROW, tp_count // PAIR, PAIR), ("sy", "sx", "tz", "tc")
    )
    seq = ("sy", "sx")
    tp = ("tz", "tc")
    return jax.shard_map(
        local,
        mesh=split,
        in_specs=(
            P(seq, None),
            P(None, tp),
            P(None, tp),
            P(None, tp),
            P(tp, None),
            P(),
            P(),
        ),
        out_specs=P(seq, tp),
        check_vma=False,
    )
```

time: 145 us -> 174 us (1.20)
  the two profiles are of different devices: /device:TPU:49 before, /device:TPU:1 now
where the time goes in v4:
time: 174 us
  waiting for transfers between devices  56.8 us (33%)
  local copies, waits for them, and re-layouts  31.4 us (18%)
  matrix products  29.9 us (17%)
  blocking collectives  22.2 us (13%)
  starting transfers between devices  17 us (10%)
  between operations  15.8 us (9%)
    all_gather x1, waiting for transfers between devices, local(): full = lax.all_gather(mine, 'tz', axis=1, tiled=True)  40.6 us
    ppermute x7, starting transfers between devices, local(): piece = lax.ppermute(piece, TP, pairs)  16 us
    all_gather x1, waiting for transfers between devices, local(): pair_mixed = lax.all_gather(mixed, 'tc', axis=1, tiled=True)  12.1 us
    all_gather x1, blocking collectives, local(): row_tails = lax.all_gather(tail, 'sx', axis=0, tiled=False)  11.6 us
    all_gather x1, blocking collectives, local(): row_sums = lax.all_gather(row_sum, 'sy', axis=0, tiled=False)  10.7 us
    dynamic_slice x9, local copies, waits for them, and re-layouts, local(): piece = lax.dynamic_index_in_dim(out_blocks, target // PAIR, 1, False)  9.81 us
    dot_general x1, matrix products, local(): jnp.dot(tokens, w_query, preferred_element_type=jnp.float32)  5.6 us
    dot_general x1, matrix products, local(): jnp.dot(tokens, w_key, preferred_element_type=jnp.float32)  5.15 us
  transfers between devices with their start and end apart: 10, of which 4 were waited for; matrix products, arithmetic and copies ran while one was open for 18% of the time, Pallas kernels for 0%

profile of v4, /device:TPU:1, one launch (start us, length us, event | category | flops | bytes accessed | tf_op | source)
XLA Modules:
  0.0 173.6 jit_solution(5985607037581063631)
XLA Ops:
  6.5 1.6 copy.40
  8.2 0.9 constant_dynamic-slice_fusion.2
  9.1 1.8 %copy.42 = bf16[256,1,512]{2,0,1:T(8,128)(2,1)} copy(bf16[256,1,512]{0,2,1:T(8,128)(2,1)} %get-tuple-element.53) | data formatting | bytes 524288 | tf_op jit(solution)/shard_map/jit(dynamic_index_in_dim)/dynamic_slice | solution.py:35
  10.9 3.0 %collective-permute-start = (bf16[256,512]{1,0:T(8,128)(2,1)}, bf16[256,512]{1,0:T(8,128)(2,1)}, u32[]{:S(2)}, u32[]{:S(2)}) collective-permute-start(bf16[256,512]{1,0:T(8,128)(2,1)} %bitcast.16), channel_id=1, source_target_pairs={{0,1},{1,2},{2,3},{3,4},{4,5},{5,6},{6,7},{7,0},{8,9},{9,10},{10,1... | collective-permute-start | bytes 786440 | tf_op jit(solution)/shard_map/ppermute | solution.py:38
  13.9 0.8 copy.43
  14.8 1.6 collective-permute-start.1
  16.4 0.8 copy.44
  17.2 1.9 %collective-permute-start.2 = (bf16[256,512]{1,0:T(8,128)(2,1)}, bf16[256,512]{1,0:T(8,128)(2,1)}, u32[]{:S(2)}, u32[]{:S(2)}) collective-permute-start(bf16[256,512]{1,0:T(8,128)(2,1)} %bitcast.20), channel_id=1, source_target_pairs={{0,3},{1,4},{2,5},{3,6},{4,7},{5,0},{6,1},{7,2},{8,11},{9,12},{10,... | collective-permute-start | bytes 786440 | tf_op jit(solution)/shard_map/ppermute | solution.py:38
  19.2 0.8 copy.45
  20.0 0.8 copy.46
  20.9 2.3 %collective-permute-start.4 = (bf16[256,512]{1,0:T(8,128)(2,1)}, bf16[256,512]{1,0:T(8,128)(2,1)}, u32[]{:S(2)}, u32[]{:S(2)}) collective-permute-start(bf16[256,512]{1,0:T(8,128)(2,1)} %bitcast.24), channel_id=1, source_target_pairs={{0,5},{1,6},{2,7},{3,0},{4,1},{5,2},{6,3},{7,4},{8,13},{9,14},{10,... | collective-permute-start | bytes 786440 | tf_op jit(solution)/shard_map/ppermute | solution.py:38
  23.2 0.6 slice.41
  25.1 0.8 copy.41
  26.1 4.6 %fusion.1 = bf16[1536,256]{1,0:T(8,128)(2,1)S(1)} fusion(bf16[1536,2048]{1,0:T(8,128)(2,1)} %param.13, bf16[2048,256]{1,0:T(8,128)(2,1)S(1)} %copy-done, pred[1536]{0:T(1024)(128)(4,1)S(1)} %get-tuple-element.58), kind=kOutput, calls=%fused_computation.6 | convolution fusion | flops 1611399168 | bytes 8128000 | tf_op jit(solution)/shard_map/dot_general | solution.py:52
  30.9 0.6 copy.54
  31.6 5.2 %fusion = bf16[1536,256]{1,0:T(8,128)(2,1)S(1)} fusion(bf16[1536,2048]{1,0:T(8,128)(2,1)} %param.13, bf16[2048,256]{1,0:T(8,128)(2,1)} %param.15, pred[1536]{0:T(1024)(128)(4,1)S(1)} %get-tuple-element.58), kind=kOutput, calls=%fused_computation.5 | convolution fusion | flops 1611399168 | bytes 8128000 | tf_op jit(solution)/shard_map/dot_general | solution.py:49
  36.7 1.1 reshape.186
  38.1 1.8 %convolution_convert_fusion.2 = bf16[12,2,128,128]{3,2,1,0:T(8,128)(2,1)S(1)} fusion(bf16[12,128,2,128]{1,3,2,0:T(8,128)(2,1)S(1)} %copy.54, bf16[12,128,2,128]{3,2,1,0:T(2,128)(2,1)} %reshape.186), kind=kOutput, calls=%fused_computation.13 | convolution fusion | flops 101056512 | bytes 2359296 | tf_op jit(solution)/shard_map/cshd,cshe->chde/dot_general | solution.py:60
  40.5 11.6 %all-gather = f32[8,128,128]{2,1,0:T(8,128)S(1)} all-gather(f32[2,128,128]{2,1,0:T(8,128)S(1)} %bitcast.89), channel_id=2, replica_groups=mesh['sy'=4,'sx'=4,'tz'=4,'tc'=2] {'sx'}, dimensions={0}, use_global_device_ids=true | all-gather | bytes 655360 | tf_op jit(solution)/shard_map/all_gather | solution.py:69
  52.7 0.6 gather_fusion.2
  53.4 0.6 gather_fusion
  54.2 10.7 %all-gather.1 = f32[8,128,128]{2,1,0:T(8,128)S(1)} all-gather(f32[2,128,128]{2,1,0:T(8,128)S(1)} %get-tuple-element.45), channel_id=3, replica_groups=mesh['sy'=4,'sx'=4,'tz'=4,'tc'=2] {'sy'}, dimensions={0}, use_global_device_ids=true | all-gather | bytes 655360 | tf_op jit(solution)/shard_map/all_gather | solution.py:73
  65.7 1.7 add_convert_fusion
  67.9 1.8 %copy.47 = bf16[256,1,512]{2,0,1:T(8,128)(2,1)} copy(bf16[256,1,512]{0,2,1:T(8,128)(2,1)} %get-tuple-element.48) | data formatting | bytes 524288 | tf_op jit(solution)/shard_map/jit(dynamic_index_in_dim)/dynamic_slice | solution.py:35
  69.7 1.1 copy.48
  70.8 1.2 collective-permute-start.5
  72.0 1.0 bitcast_dynamic-update-slice_fusion.6
  73.0 5.9 %collective-permute-start.6 = (bf16[256,512]{1,0:T(8,128)(2,1)S(1)}, bf16[256,512]{1,0:T(8,128)(2,1)S(1)}, u32[]{:S(2)}, u32[]{:S(2)}) collective-permute-start(bf16[256,512]{1,0:T(8,128)(2,1)S(1)} %bitcast.90), channel_id=1, source_target_pairs={{0,7},{1,0},{2,1},{3,2},{4,3},{5,4},{6,5},{7,6},{8,15},{9,8},{10,9... | collective-permute-start | bytes 786440 | tf_op jit(solution)/shard_map/ppermute | solution.py:38
  78.9 1.0 bitcast_dynamic-update-slice_fusion.5
  79.9 1.0 bitcast_dynamic-update-slice_fusion.4
  80.9 1.0 bitcast_dynamic-update-slice_fusion.3
  81.9 1.0 bitcast_dynamic-update-slice_fusion.2
  82.9 2.7 %collective-permute-done.6 = bf16[256,512]{1,0:T(8,128)(2,1)S(1)} collective-permute-done((bf16[256,512]{1,0:T(8,128)(2,1)S(1)}, bf16[256,512]{1,0:T(8,128)(2,1)S(1)}, u32[]{:S(2)}, u32[]{:S(2)}) %collective-permute-start.6) | collective-permute-done | bytes 262176 | tf_op jit(solution)/shard_map/ppermute | solution.py:38
  85.6 1.4 copy-done.5
  87.0 5.6 %fusion.2 = bf16[1536,256]{0,1:T(8,128)(2,1)} fusion(bf16[2048,256]{1,0:T(8,128)(2,1)S(1)} %copy-done.10, bf16[1536,2048]{1,0:T(8,128)(2,1)} %param.13), kind=kOutput, calls=%fused_computation.8 | convolution fusion | flops 1611005952 | bytes 8126464 | tf_op jit(solution)/shard_map/dot_general | solution.py:55
  92.6 1.6 reshape.217
  94.2 0.8 copy.51
  95.1 3.2 %fusion.10 = f32[12,2,128,128]{3,2,1,0:T(8,128)} fusion(bf16[12,128,2,128]{3,1,2,0:T(8,128)(2,1)S(1)} %copy.51, bf16[12,2,128,128]{3,0,2,1:T(8,128)(2,1)} %add_convert_fusion), kind=kOutput, calls=%fused_computation.23 | convolution fusion | flops 100663296 | bytes 3145728 | tf_op jit(solution)/shard_map/cthd,chde->cthe/dot_general | solution.py:90
  98.3 3.5 %fusion.3 = bf16[12,128,2,128]{1,3,2,0:T(8,128)(2,1)} fusion(f32[12,2,128,128]{3,2,1,0:T(8,128)} %fusion.10, bf16[12,128,2,128]{1,3,2,0:T(8,128)(2,1)S(1)} %copy-done.3, bf16[12,128,2,128]{3,1,2,0:T(8,128)(2,1)S(1)} %copy.51, f32[12]{0:T(128)S(1)} %fusion.6, pred[128,128]{1,0:T(8,128)(4,1)S(1)} %iota_compare_fusion, ...), kind=kOutput, calls=%fused_computation.14 | convolution fusion | flops 203685888 | bytes 4736560 | tf_op jit(solution)/shard_map/chts,cshe->cthe/dot_general | solution.py:98
  101.8 2.3 %copy.55 = bf16[12,128,2,128]{3,2,1,0:T(2,128)(2,1)S(1)} copy(bf16[12,128,2,128]{1,3,2,0:T(8,128)(2,1)} %fusion.3) | data formatting | bytes 1572864 | tf_op jit(solution)/shard_map/convert_element_type | solution.py:107
  104.1 1.0 copy.74
  105.1 12.1 %all-gather.5.cloned.1.call-done = bf16[1536,512]{1,0:T(8,128)(2,1)} async-done(((bf16[1536,256]{1,0:T(8,128)(2,1)}), bf16[1536,512]{1,0:T(8,128)(2,1)}) %all-gather.5.cloned.1.call-update) | async-done | bytes 1572880 | tf_op jit(solution)/shard_map/all_gather | solution.py:111
  117.2 2.1 %constant_dynamic-slice_fusion.1 = bf16[768,512]{1,0:T(8,128)(2,1)} fusion(bf16[1536,512]{1,0:T(8,128)(2,1)} %all-gather.5.cloned.1.call-done, s32[]{:T(128)S(6)} %select_n.250), kind=kLoop, calls=%fused_computation.49 | loop fusion | bytes 1572868 | tf_op jit(solution)/shard_map/dynamic_slice | solution.py:112
  119.3 40.6 %all-gather.7.cloned.1.call-done = bf16[768,2048]{1,0:T(8,128)(2,1)} async-done(((bf16[768,512]{1,0:T(8,128)(2,1)}), bf16[768,2048]{1,0:T(8,128)(2,1)}) %all-gather.7.cloned.1.call-update) | async-done | bytes 3145744 | tf_op jit(solution)/shard_map/all_gather | solution.py:113
  159.9 3.7 %convolution_convert_fusion.1 = bf16[768,512]{1,0:T(8,128)(2,1)S(1)} fusion(bf16[768,2048]{1,0:T(8,128)(2,1)} %all-gather.7.cloned.1.call-done, bf16[2048,512]{1,0:T(8,128)(2,1)S(1)} %bitcast.87), kind=kOutput, calls=%fused_computation.12 | convolution fusion | flops 1611005952 | bytes 6029312 | tf_op jit(solution)/shard_map/dot_general | solution.py:114
  163.7 0.9 collective-permute-start.7
  164.7 1.3 collective-permute-done.7
  166.0 0.8 constant_dynamic-update-slice_fusion
  (61 shorter events, 2.8 us)
Async XLA Ops:
  6.5 19.6 %copy-start = (bf16[2048,256]{1,0:T(8,128)(2,1)S(1)}, bf16[2048,256]{1,0:T(8,128)(2,1)}, u32[]{:S(2)}) copy-start(bf16[2048,256]{1,0:T(8,128)(2,1)} %param.16) | copy-start | bytes 3145732
  6.5 110.7 %all-gather.5.cloned.1.call-start = ((), (), s32[]{:S(2)}) async-start(), calls=%async_computation | async-start | bytes 2359296 | tf_op jit(solution)/shard_map/all_gather | solution.py:111
  9.1 16.8 %copy-start.9 = (s32[192]{0:T(256)S(1)}, s32[192]{0:T(256)}, u32[]{:S(2)}) copy-start(s32[192]{0:T(256)} %param.19) | copy-start | bytes 2308
  10.9 59.9 %collective-permute-start = (bf16[256,512]{1,0:T(8,128)(2,1)}, bf16[256,512]{1,0:T(8,128)(2,1)}, u32[]{:S(2)}, u32[]{:S(2)}) collective-permute-start(bf16[256,512]{1,0:T(8,128)(2,1)} %bitcast.16), channel_id=1, source_target_pairs={{0,1},{1,2},{2,3},{3,4},{4,5},{5,6},{6,7},{7,0},{8,9},{9,10},{10,1... | collective-permute-start | bytes 786440 | tf_op jit(solution)/shard_map/ppermute | solution.py:38
  14.8 58.2 %collective-permute-start.1 = (bf16[256,512]{1,0:T(8,128)(2,1)}, bf16[256,512]{1,0:T(8,128)(2,1)}, u32[]{:S(2)}, u32[]{:S(2)}) collective-permute-start(bf16[256,512]{1,0:T(8,128)(2,1)} %bitcast.18), channel_id=1, source_target_pairs={{0,2},{1,3},{2,4},{3,5},{4,6},{5,7},{6,0},{7,1},{8,10},{9,11},{10,... | collective-permute-start | bytes 786440 | tf_op jit(solution)/shard_map/ppermute | solution.py:38
  17.2 62.6 %collective-permute-start.2 = (bf16[256,512]{1,0:T(8,128)(2,1)}, bf16[256,512]{1,0:T(8,128)(2,1)}, u32[]{:S(2)}, u32[]{:S(2)}) collective-permute-start(bf16[256,512]{1,0:T(8,128)(2,1)} %bitcast.20), channel_id=1, source_target_pairs={{0,3},{1,4},{2,5},{3,6},{4,7},{5,0},{6,1},{7,2},{8,11},{9,12},{10,... | collective-permute-start | bytes 786440 | tf_op jit(solution)/shard_map/ppermute | solution.py:38
  20.0 60.8 %collective-permute-start.3 = (bf16[256,512]{1,0:T(8,128)(2,1)}, bf16[256,512]{1,0:T(8,128)(2,1)}, u32[]{:S(2)}, u32[]{:S(2)}) collective-permute-start(bf16[256,512]{1,0:T(8,128)(2,1)} %bitcast.22), channel_id=1, source_target_pairs={{0,4},{1,5},{2,6},{3,7},{4,0},{5,1},{6,2},{7,3},{8,12},{9,13},{10,... | collective-permute-start | bytes 786440 | tf_op jit(solution)/shard_map/ppermute | solution.py:38
  20.9 61.0 %collective-permute-start.4 = (bf16[256,512]{1,0:T(8,128)(2,1)}, bf16[256,512]{1,0:T(8,128)(2,1)}, u32[]{:S(2)}, u32[]{:S(2)}) collective-permute-start(bf16[256,512]{1,0:T(8,128)(2,1)} %bitcast.24), channel_id=1, source_target_pairs={{0,5},{1,6},{2,7},{3,0},{4,1},{5,2},{6,3},{7,4},{8,13},{9,14},{10,... | collective-permute-start | bytes 786440 | tf_op jit(solution)/shard_map/ppermute | solution.py:38
  31.5 6.6 %copy-start.2 = (bf16[12,128,2,128]{1,3,2,0:T(8,128)(2,1)}, bf16[12,128,2,128]{1,3,2,0:T(8,128)(2,1)S(1)}, u32[]{:S(2)}) copy-start(bf16[12,128,2,128]{1,3,2,0:T(8,128)(2,1)S(1)} %copy.54) | copy-start | bytes 2359300
  31.6 6.3 %copy-start.1 = (s32[192,192]{1,0:T(8,128)S(1)}, s32[192,192]{1,0:T(8,128)}, u32[]{:S(2)}) copy-start(s32[192,192]{1,0:T(8,128)} %param.18) | copy-start | bytes 442372
  65.7 1.9 %copy-start.7 = (bf16[256,1,512]{2,0,1:T(8,128)(2,1)S(1)}, bf16[256,1,512]{2,0,1:T(8,128)(2,1)}, u32[]{:S(2)}) copy-start(bf16[256,1,512]{2,0,1:T(8,128)(2,1)} %copy.41) | copy-start | bytes 786436
  70.8 16.2 %copy-start.10 = (bf16[2048,256]{1,0:T(8,128)(2,1)S(1)}, bf16[2048,256]{1,0:T(8,128)(2,1)}, u32[]{:S(2)}) copy-start(bf16[2048,256]{1,0:T(8,128)(2,1)} %param.14) | copy-start | bytes 3145732
  70.8 12.0 %collective-permute-start.5 = (bf16[256,512]{1,0:T(8,128)(2,1)}, bf16[256,512]{1,0:T(8,128)(2,1)S(1)}, u32[]{:S(2)}, u32[]{:S(2)}) collective-permute-start(bf16[256,512]{1,0:T(8,128)(2,1)} %bitcast.91), channel_id=1, source_target_pairs={{0,6},{1,7},{2,0},{3,1},{4,2},{5,3},{6,4},{7,5},{8,14},{9,15},{10,... | collective-permute-start | bytes 786440 | tf_op jit(solution)/shard_map/ppermute | solution.py:38
  73.0 12.6 %collective-permute-start.6 = (bf16[256,512]{1,0:T(8,128)(2,1)S(1)}, bf16[256,512]{1,0:T(8,128)(2,1)S(1)}, u32[]{:S(2)}, u32[]{:S(2)}) collective-permute-start(bf16[256,512]{1,0:T(8,128)(2,1)S(1)} %bitcast.90), channel_id=1, source_target_pairs={{0,7},{1,0},{2,1},{3,2},{4,3},{5,4},{6,5},{7,6},{8,15},{9,8},{10,9... | collective-permute-start | bytes 786440 | tf_op jit(solution)/shard_map/ppermute | solution.py:38
  85.6 1.4 copy-start.5
  95.1 3.2 %copy-start.3 = (bf16[12,128,2,128]{1,3,2,0:T(8,128)(2,1)S(1)}, bf16[12,128,2,128]{1,3,2,0:T(8,128)(2,1)}, u32[]{:S(2)}) copy-start(bf16[12,128,2,128]{1,3,2,0:T(8,128)(2,1)} %copy-done.2) | copy-start | bytes 2359300
  95.1 3.2 %copy-start.4 = (bf16[12,128,2,128]{3,2,1,0:T(2,128)(2,1)S(1)}, bf16[12,128,2,128]{3,2,1,0:T(2,128)(2,1)}, u32[]{:S(2)}) copy-start(bf16[12,128,2,128]{3,2,1,0:T(2,128)(2,1)} %reshape.186) | copy-start | bytes 2359300
  105.0 54.9 %copy-start.6 = (bf16[8,256,512]{2,1,0:T(8,128)(2,1)S(1)}, bf16[8,256,512]{2,1,0:T(8,128)(2,1)}, u32[]{:S(2)}) copy-start(bf16[8,256,512]{2,1,0:T(8,128)(2,1)} %copy-done.5) | copy-start | bytes 6291460
  105.1 54.9 %all-gather.7.cloned.1.call-start = ((), (), s32[]{:S(2)}) async-start(), calls=%async_computation.1 | async-start | bytes 3932160 | tf_op jit(solution)/shard_map/all_gather | solution.py:113
  163.7 2.3 %copy-start.8 = (bf16[1536,256]{1,0:T(8,128)(2,1)}, bf16[1536,256]{1,0:T(8,128)(2,1)S(1)}, u32[]{:S(2)}) copy-start(bf16[1536,256]{1,0:T(8,128)(2,1)S(1)} %get-tuple-element.56) | copy-start | bytes 2359300
  163.7 2.3 %collective-permute-start.7 = (bf16[768,256]{1,0:T(8,128)(2,1)S(1)}, bf16[768,256]{1,0:T(8,128)(2,1)S(1)}, u32[]{:S(2)}, u32[]{:S(2)}) collective-permute-start(bf16[768,256]{1,0:T(8,128)(2,1)S(1)} %get-tuple-element.55), channel_id=1, source_target_pairs={{0,1},{1,0},{2,3},{3,2},{4,5},{5,4},{6,7},{7,6},{8,9},{9,8},{10,11... | collective-permute-start | bytes 1179656 | tf_op jit(solution)/shard_map/ppermute | solution.py:117
Sparse Core Ops, SparseCore 0:
  105.2 11.9 all-gather.4
  119.4 40.4 all-gather.6

commit v5 on v4

--- a/solution.py
+++ b/solution.py
@@ -20,26 +20,23 @@
     seq_count = readers.shape[0] // group_local
     row_count = seq_count // ROW
     tp_count = w_out.shape[1] // local_width
-    chip_count = tp_count // PAIR
-    chip_width = PAIR * local_width
     row_at = lax.axis_index("sy")
     seq_index = row_at * ROW + lax.axis_index("sx")
     core_at = lax.axis_index("tc")
     tp_index = lax.axis_index("tz") * PAIR + core_at
     first_group = seq_index * group_local
 
-    out_blocks = w_out.reshape(local_width, chip_count, chip_width)
-    w_out_chip = jnp.zeros((tp_count, local_width, chip_width), w_out.dtype)
+    out_blocks = w_out.reshape(local_width, tp_count, local_width)
+    w_out_cols = jnp.zeros((tp_count, local_width, local_width), w_out.dtype)
     for shift in range(tp_count):
-        target = (tp_index + shift) % tp_count
-        piece = lax.dynamic_index_in_dim(out_blocks, target // PAIR, 1, False)
+        piece = lax.dynamic_index_in_dim(out_blocks, (tp_index + shift) % tp_count, 1, False)
         if shift:
             pairs = [(i, (i + shift) % tp_count) for i in range(tp_count)]
             piece = lax.ppermute(piece, TP, pairs)
-        w_out_chip = lax.dynamic_update_index_in_dim(
-            w_out_chip, piece, (tp_index - shift) % tp_count, 0
+        w_out_cols = lax.dynamic_update_index_in_dim(
+            w_out_cols, piece, (tp_index - shift) % tp_count, 0
         )
-    w_out_chip = w_out_chip.reshape(tp_count * local_width, chip_width)
+    w_out_cols = w_out_cols.reshape(tp_count * local_width, local_width)
 
     local_lengths = lax.dynamic_slice_in_dim(lengths, first_group, group_local, 0)
     reader_rows = lax.dynamic_slice_in_dim(readers, first_group, group_local, 0)
@@ -51,7 +48,7 @@
     value_rows = jnp.where(
         live_mask, jnp.dot(tokens, w_value, preferred_element_type=jnp.float32), 0.0
     ).astype(jnp.bfloat16)
-    w_query, w_out_chip = lax.optimization_barrier((w_query, w_out_chip))
+    w_query, w_out_cols = lax.optimization_barrier((w_query, w_out_cols))
     query_rows = jnp.dot(tokens, w_query, preferred_element_type=jnp.float32).astype(jnp.bfloat16)
     query_blocks = query_rows.reshape(group_local, CH, head_dev, HS)
     key_blocks = key_rows.reshape(group_local, CH, head_dev, HS)
@@ -107,17 +104,8 @@
     mixed = jnp.where(live_mask.reshape(group_local, CH, 1, 1), mixed, 0.0).astype(jnp.bfloat16)
     mixed = mixed.reshape(group_local * CH, local_width)
 
-    half = group_local * CH // PAIR
-    pair_mixed = lax.all_gather(mixed, "tc", axis=1, tiled=True)
-    mine = lax.dynamic_slice_in_dim(pair_mixed, core_at * half, half, 0)
-    full = lax.all_gather(mine, "tz", axis=1, tiled=True)
-    part = jnp.dot(full, w_out_chip, preferred_element_type=jnp.float32).astype(jnp.bfloat16)
-    kept = lax.dynamic_slice_in_dim(part, core_at * local_width, local_width, 1)
-    given = lax.dynamic_slice_in_dim(part, (1 - core_at) * local_width, local_width, 1)
-    got = lax.ppermute(given, "tc", [(0, 1), (1, 0)])
-    result = jnp.zeros((group_local * CH, local_width), part.dtype)
-    result = lax.dynamic_update_slice_in_dim(result, kept, core_at * half, 0)
-    return lax.dynamic_update_slice_in_dim(result, got, (1 - core_at) * half, 0)
+    mixed_all = lax.all_gather(mixed, TP, axis=1, tiled=True)
+    return jnp.dot(mixed_all, w_out_cols, preferred_element_type=jnp.float32).astype(jnp.bfloat16)
 
 
 def solution(mesh):

time: 174 us -> 153 us (0.88)
  waiting for transfers between devices: 56.8 us -> 44.6 us
  local copies, waits for them, and re-layouts: 31.4 us -> 21.9 us
  matrix products: 29.9 us -> 31.9 us
    all_gather x2 -> x1, waiting for transfers between devices: 52.7 us -> 44.6 us  [local(): mixed_all = lax.all_gather(mixed, TP, axis=1, tiled=True)]
    dynamic_slice x11 -> x9, local copies, waits for them, and re-layouts: 11.9 us -> 4.17 us  [local(): lax.dynamic_index_in_dim(out_blocks, (tp_index + shift) % tp_count, 1, Fa...]
    ppermute x7, waiting for transfers between devices: 2.73 us -> 0.02 us  [local(): piece = lax.ppermute(piece, TP, pairs)]
    dot_general x1, matrix products: 3.67 us -> 5.47 us  [local(): jnp.dot(mixed_all, w_out_cols, preferred_element_type=jnp.float32)]
    dynamic_update_slice x9 -> x8, local copies, waits for them, and re-layouts: 5.7 us -> 4.63 us  [local(): lax.dynamic_update_index_in_dim(w_out_cols, piece, (tp_index - shift) % t...]
    unnamed x24 -> x18, local copies, waits for them, and re-layouts: 3.95 us -> 3.57 us
  transfers between devices with their start and end apart: 10 -> 8, of which waited for: 4 -> 1; matrix products, arithmetic and copies ran while one was open for 18% -> 18% of each run, Pallas kernels for 0% -> 0%
where the time goes in v5:
time: 153 us
  waiting for transfers between devices  44.6 us (29%)
  matrix products  31.9 us (21%)
  blocking collectives  22.3 us (15%)
  local copies, waits for them, and re-layouts  21.9 us (14%)
  starting transfers between devices  16 us (10%)
  between operations  15.6 us (10%)
    all_gather x1, waiting for transfers between devices, local(): mixed_all = lax.all_gather(mixed, TP, axis=1, tiled=True)  44.6 us
    ppermute x7, starting transfers between devices, local(): piece = lax.ppermute(piece, TP, pairs)  16 us
    all_gather x1, blocking collectives, local(): row_tails = lax.all_gather(tail, 'sx', axis=0, tiled=False)  11.6 us
    all_gather x1, blocking collectives, local(): row_sums = lax.all_gather(row_sum, 'sy', axis=0, tiled=False)  10.7 us
    dot_general x1, matrix products, local(): jnp.dot(tokens, w_query, preferred_element_type=jnp.float32)  5.85 us
    dot_general x1, matrix products, local(): jnp.dot(mixed_all, w_out_cols, preferred_element_type=jnp.float32)  5.47 us
    dot_general x1, matrix products, local(): jnp.dot(tokens, w_key, preferred_element_type=jnp.float32)  5.12 us
    dynamic_update_slice x8, local copies, waits for them, and re-layouts, local(): lax.dynamic_update_index_in_dim(w_out_cols, piece, (tp_index - shift) % t...  4.63 us
  transfers between devices with their start and end apart: 8, of which 1 were waited for; matrix products, arithmetic and copies ran while one was open for 18% of the time, Pallas kernels for 0%

profile of v5, /device:TPU:1, one launch (start us, length us, event | category | flops | bytes accessed | tf_op | source)
XLA Modules:
  0.0 152.7 jit_solution(1968694047554005398)
XLA Ops:
  6.5 1.6 %copy.40 = bf16[256,2048]{0,1:T(8,128)(2,1)S(1)} copy(bf16[256,2048]{1,0:T(8,128)(2,1)} %param.17) | data formatting | bytes 2097152 | tf_op args[4]
  8.3 0.8 copy.42
  9.0 3.0 %collective-permute-start = (bf16[256,256]{1,0:T(8,128)(2,1)}, bf16[256,256]{1,0:T(8,128)(2,1)}, u32[]{:S(2)}, u32[]{:S(2)}) collective-permute-start(bf16[256,256]{1,0:T(8,128)(2,1)} %bitcast.16), channel_id=1, source_target_pairs={{0,1},{1,2},{2,3},{3,4},{4,5},{5,6},{6,7},{7,0},{8,9},{9,10},{10,1... | collective-permute-start | bytes 393224 | tf_op jit(solution)/shard_map/ppermute | solution.py:35
  12.0 0.8 copy.43
  12.8 1.6 %collective-permute-start.1 = (bf16[256,256]{1,0:T(8,128)(2,1)}, bf16[256,256]{1,0:T(8,128)(2,1)}, u32[]{:S(2)}, u32[]{:S(2)}) collective-permute-start(bf16[256,256]{1,0:T(8,128)(2,1)} %bitcast.18), channel_id=1, source_target_pairs={{0,2},{1,3},{2,4},{3,5},{4,6},{5,7},{6,0},{7,1},{8,10},{9,11},{10,... | collective-permute-start | bytes 393224 | tf_op jit(solution)/shard_map/ppermute | solution.py:35
  14.5 0.8 copy.44
  15.2 1.9 %collective-permute-start.2 = (bf16[256,256]{1,0:T(8,128)(2,1)}, bf16[256,256]{1,0:T(8,128)(2,1)}, u32[]{:S(2)}, u32[]{:S(2)}) collective-permute-start(bf16[256,256]{1,0:T(8,128)(2,1)} %bitcast.20), channel_id=1, source_target_pairs={{0,3},{1,4},{2,5},{3,6},{4,7},{5,0},{6,1},{7,2},{8,11},{9,12},{10,... | collective-permute-start | bytes 393224 | tf_op jit(solution)/shard_map/ppermute | solution.py:35
  17.2 0.7 copy.45
  17.9 0.8 copy.46
  18.7 2.3 %collective-permute-start.4 = (bf16[256,256]{1,0:T(8,128)(2,1)}, bf16[256,256]{1,0:T(8,128)(2,1)}, u32[]{:S(2)}, u32[]{:S(2)}) collective-permute-start(bf16[256,256]{1,0:T(8,128)(2,1)} %bitcast.24), channel_id=1, source_target_pairs={{0,5},{1,6},{2,7},{3,0},{4,1},{5,2},{6,3},{7,4},{8,13},{9,14},{10,... | collective-permute-start | bytes 393224 | tf_op jit(solution)/shard_map/ppermute | solution.py:35
  21.0 0.6 slice.41
  22.9 0.2 dynamic-slice_reduce_fusion
  23.2 0.6 gather_fusion
  24.4 0.6 gather_fusion.2
  25.1 0.6 gather_fusion.1
  25.8 4.6 %fusion.1 = bf16[1536,256]{1,0:T(8,128)(2,1)S(1)} fusion(bf16[1536,2048]{1,0:T(8,128)(2,1)} %param.13, bf16[2048,256]{1,0:T(8,128)(2,1)S(1)} %copy-done, pred[1536]{0:T(1024)(128)(4,1)S(1)} %get-tuple-element.56), kind=kOutput, calls=%fused_computation.6 | convolution fusion | flops 1611399168 | bytes 8128000 | tf_op jit(solution)/shard_map/dot_general | solution.py:49
  30.4 0.2 reshape.187
  30.6 0.6 copy.54
  31.3 5.1 %fusion = bf16[1536,256]{1,0:T(8,128)(2,1)S(1)} fusion(bf16[1536,2048]{1,0:T(8,128)(2,1)} %param.13, bf16[2048,256]{1,0:T(8,128)(2,1)} %param.15, pred[1536]{0:T(1024)(128)(4,1)S(1)} %get-tuple-element.56), kind=kOutput, calls=%fused_computation.5 | convolution fusion | flops 1611399168 | bytes 8128000 | tf_op jit(solution)/shard_map/dot_general | solution.py:46
  36.4 1.1 reshape.186
  37.5 1.8 %convolution_convert_fusion.2 = bf16[12,2,128,128]{3,2,1,0:T(8,128)(2,1)S(1)} fusion(bf16[12,128,2,128]{1,3,2,0:T(8,128)(2,1)S(1)} %copy.54, bf16[12,128,2,128]{3,2,1,0:T(2,128)(2,1)} %reshape.186), kind=kOutput, calls=%fused_computation.13 | convolution fusion | flops 101056512 | bytes 2359296 | tf_op jit(solution)/shard_map/cshd,cshe->chde/dot_general | solution.py:57
  39.3 0.5 fusion.7
  39.8 11.6 %all-gather = f32[8,128,128]{2,1,0:T(8,128)S(1)} all-gather(f32[2,128,128]{2,1,0:T(8,128)S(1)} %bitcast.89), channel_id=2, replica_groups=mesh['sy'=4,'sx'=4,'tz'=4,'tc'=2] {'sx'}, dimensions={0}, use_global_device_ids=true | all-gather | bytes 655360 | tf_op jit(solution)/shard_map/all_gather | solution.py:66
  51.4 0.2 multiply_reduce_fusion.1
  51.6 10.7 %all-gather.1 = f32[8,128,128]{2,1,0:T(8,128)S(1)} all-gather(f32[2,128,128]{2,1,0:T(8,128)S(1)} %get-tuple-element.45), channel_id=3, replica_groups=mesh['sy'=4,'sx'=4,'tz'=4,'tc'=2] {'sy'}, dimensions={0}, use_global_device_ids=true | all-gather | bytes 655360 | tf_op jit(solution)/shard_map/all_gather | solution.py:70
  62.3 0.1 copy.41
  62.4 0.1 multiply_reduce_fusion
  62.5 1.7 %add_convert_fusion = bf16[12,2,128,128]{3,0,2,1:T(8,128)(2,1)} fusion(bf16[12,2,128,128]{3,2,1,0:T(8,128)(2,1)S(1)} %convolution_convert_fusion.2, f32[2,128,128]{2,1,0:T(8,128)S(1)} %add.262, f32[12]{0:T(128)S(1)} %convert_element_type.65, s32[192,192]{1,0:T(8,128)S(1)} %copy-done.1, s32[]{:T(128)S(6)} %select_n.163), kind=kOutput, calls=%fused_computation.10 | convolution fusion | flops 10616976 | bytes 1712644 | tf_op jit(solution)/shard_map/ce,ehij->chij/dot_general | solution.py:79
  64.3 0.1 fusion.6
  64.5 0.1 copy.48
  64.6 0.1 copy.47
  64.8 1.2 collective-permute-start.5
  65.9 0.9 bitcast_dynamic-update-slice_fusion.6
  66.8 5.9 %collective-permute-start.6 = (bf16[256,256]{1,0:T(8,128)(2,1)S(1)}, bf16[256,256]{1,0:T(8,128)(2,1)S(1)}, u32[]{:S(2)}, u32[]{:S(2)}) collective-permute-start(bf16[256,256]{1,0:T(8,128)(2,1)S(1)} %bitcast.90), channel_id=1, source_target_pairs={{0,7},{1,0},{2,1},{3,2},{4,3},{5,4},{6,5},{7,6},{8,15},{9,8},{10,9... | collective-permute-start | bytes 393224 | tf_op jit(solution)/shard_map/ppermute | solution.py:35
  72.7 0.9 bitcast_dynamic-update-slice_fusion.5
  73.7 0.9 bitcast_dynamic-update-slice_fusion.4
  74.6 0.9 bitcast_dynamic-update-slice_fusion.3
  75.5 0.9 bitcast_dynamic-update-slice_fusion.2
  76.5 1.0 copy-done.5
  77.5 5.8 %fusion.2 = bf16[1536,256]{0,1:T(8,128)(2,1)} fusion(bf16[2048,256]{1,0:T(8,128)(2,1)} %param.14, bf16[1536,2048]{1,0:T(8,128)(2,1)} %param.13), kind=kOutput, calls=%fused_computation.9 | convolution fusion | flops 1611005952 | bytes 8126464 | tf_op jit(solution)/shard_map/dot_general | solution.py:52
  83.4 1.6 %reshape.217 = bf16[12,128,2,128]{1,0,3,2:T(8,128)(2,1)S(1)} reshape(bf16[1536,256]{0,1:T(8,128)(2,1)} %fusion.2) | data formatting | bytes 1572864 | tf_op jit(solution)/shard_map/reshape | solution.py:53
  85.0 0.8 copy.51
  85.9 3.2 %fusion.10 = f32[12,2,128,128]{3,2,1,0:T(8,128)} fusion(bf16[12,128,2,128]{3,1,2,0:T(8,128)(2,1)S(1)} %copy.51, bf16[12,2,128,128]{3,0,2,1:T(8,128)(2,1)} %add_convert_fusion), kind=kOutput, calls=%fused_computation.23 | convolution fusion | flops 100663296 | bytes 3145728 | tf_op jit(solution)/shard_map/cthd,chde->cthe/dot_general | solution.py:87
  89.1 3.5 %fusion.3 = bf16[12,128,2,128]{1,3,2,0:T(8,128)(2,1)} fusion(f32[12,2,128,128]{3,2,1,0:T(8,128)} %fusion.10, bf16[12,128,2,128]{1,3,2,0:T(8,128)(2,1)S(1)} %copy-done.3, bf16[12,128,2,128]{3,1,2,0:T(8,128)(2,1)S(1)} %copy.51, f32[12]{0:T(128)S(1)} %fusion.6, pred[128,128]{1,0:T(8,128)(4,1)S(1)} %iota_compare_fusion, ...), kind=kOutput, calls=%fused_computation.14 | convolution fusion | flops 203685888 | bytes 4736560 | tf_op jit(solution)/shard_map/chts,cshe->cthe/dot_general | solution.py:95
  92.6 2.3 %copy.55 = bf16[12,128,2,128]{3,2,1,0:T(2,128)(2,1)S(1)} copy(bf16[12,128,2,128]{1,3,2,0:T(8,128)(2,1)} %fusion.3) | data formatting | bytes 1572864 | tf_op jit(solution)/shard_map/convert_element_type | solution.py:104
  94.8 1.0 copy.74
  95.8 44.6 %all-gather.4.cloned.1.call-done = bf16[1536,2048]{1,0:T(8,128)(2,1)} async-done(((bf16[1536,256]{1,0:T(8,128)(2,1)}), bf16[1536,2048]{1,0:T(8,128)(2,1)}) %all-gather.4.cloned.1.call-update) | async-done | bytes 6291472 | tf_op jit(solution)/shard_map/all_gather | solution.py:107
  140.4 5.5 %convolution_convert_fusion = bf16[1536,256]{1,0:T(8,128)(2,1)} fusion(bf16[1536,2048]{1,0:T(8,128)(2,1)} %all-gather.4.cloned.1.call-done, bf16[2048,256]{1,0:T(8,128)(2,1)S(1)} %bitcast.88), kind=kOutput, calls=%fused_computation.7 | convolution fusion | flops 1611005952 | bytes 8126464 | tf_op jit(solution)/shard_map/dot_general | solution.py:108
  (46 shorter events, 0.7 us)
Async XLA Ops:
  6.5 19.3 %copy-start = (bf16[2048,256]{1,0:T(8,128)(2,1)S(1)}, bf16[2048,256]{1,0:T(8,128)(2,1)}, u32[]{:S(2)}) copy-start(bf16[2048,256]{1,0:T(8,128)(2,1)} %param.16) | copy-start | bytes 3145732
  6.5 133.9 %all-gather.4.cloned.1.call-start = ((), (), s32[]{:S(2)}) async-start(), calls=%async_computation | async-start | bytes 7077888 | tf_op jit(solution)/shard_map/all_gather | solution.py:107
  8.2 14.6 %copy-start.7 = (s32[192]{0:T(256)S(1)}, s32[192]{0:T(256)}, u32[]{:S(2)}) copy-start(s32[192]{0:T(256)} %param.19) | copy-start | bytes 2308
  8.2 14.7 %copy-start.1 = (s32[192,192]{1,0:T(8,128)S(1)}, s32[192,192]{1,0:T(8,128)}, u32[]{:S(2)}) copy-start(s32[192,192]{1,0:T(8,128)} %param.18) | copy-start | bytes 442372
  9.0 55.7 %collective-permute-start = (bf16[256,256]{1,0:T(8,128)(2,1)}, bf16[256,256]{1,0:T(8,128)(2,1)}, u32[]{:S(2)}, u32[]{:S(2)}) collective-permute-start(bf16[256,256]{1,0:T(8,128)(2,1)} %bitcast.16), channel_id=1, source_target_pairs={{0,1},{1,2},{2,3},{3,4},{4,5},{5,6},{6,7},{7,0},{8,9},{9,10},{10,1... | collective-permute-start | bytes 393224 | tf_op jit(solution)/shard_map/ppermute | solution.py:35
  12.8 54.0 %collective-permute-start.1 = (bf16[256,256]{1,0:T(8,128)(2,1)}, bf16[256,256]{1,0:T(8,128)(2,1)}, u32[]{:S(2)}, u32[]{:S(2)}) collective-permute-start(bf16[256,256]{1,0:T(8,128)(2,1)} %bitcast.18), channel_id=1, source_target_pairs={{0,2},{1,3},{2,4},{3,5},{4,6},{5,7},{6,0},{7,1},{8,10},{9,11},{10,... | collective-permute-start | bytes 393224 | tf_op jit(solution)/shard_map/ppermute | solution.py:35
  15.2 58.5 %collective-permute-start.2 = (bf16[256,256]{1,0:T(8,128)(2,1)}, bf16[256,256]{1,0:T(8,128)(2,1)}, u32[]{:S(2)}, u32[]{:S(2)}) collective-permute-start(bf16[256,256]{1,0:T(8,128)(2,1)} %bitcast.20), channel_id=1, source_target_pairs={{0,3},{1,4},{2,5},{3,6},{4,7},{5,0},{6,1},{7,2},{8,11},{9,12},{10,... | collective-permute-start | bytes 393224 | tf_op jit(solution)/shard_map/ppermute | solution.py:35
  17.9 56.7 %collective-permute-start.3 = (bf16[256,256]{1,0:T(8,128)(2,1)}, bf16[256,256]{1,0:T(8,128)(2,1)}, u32[]{:S(2)}, u32[]{:S(2)}) collective-permute-start(bf16[256,256]{1,0:T(8,128)(2,1)} %bitcast.22), channel_id=1, source_target_pairs={{0,4},{1,5},{2,6},{3,7},{4,0},{5,1},{6,2},{7,3},{8,12},{9,13},{10,... | collective-permute-start | bytes 393224 | tf_op jit(solution)/shard_map/ppermute | solution.py:35
  18.7 56.9 %collective-permute-start.4 = (bf16[256,256]{1,0:T(8,128)(2,1)}, bf16[256,256]{1,0:T(8,128)(2,1)}, u32[]{:S(2)}, u32[]{:S(2)}) collective-permute-start(bf16[256,256]{1,0:T(8,128)(2,1)} %bitcast.24), channel_id=1, source_target_pairs={{0,5},{1,6},{2,7},{3,0},{4,1},{5,2},{6,3},{7,4},{8,13},{9,14},{10,... | collective-permute-start | bytes 393224 | tf_op jit(solution)/shard_map/ppermute | solution.py:35
  31.3 6.2 %copy-start.2 = (bf16[12,128,2,128]{1,3,2,0:T(8,128)(2,1)}, bf16[12,128,2,128]{1,3,2,0:T(8,128)(2,1)S(1)}, u32[]{:S(2)}) copy-start(bf16[12,128,2,128]{1,3,2,0:T(8,128)(2,1)S(1)} %copy.54) | copy-start | bytes 2359300
  64.8 11.7 %collective-permute-start.5 = (bf16[256,256]{1,0:T(8,128)(2,1)S(1)}, bf16[256,256]{1,0:T(8,128)(2,1)S(1)}, u32[]{:S(2)}, u32[]{:S(2)}) collective-permute-start(bf16[256,256]{1,0:T(8,128)(2,1)S(1)} %bitcast.91), channel_id=1, source_target_pairs={{0,6},{1,7},{2,0},{3,1},{4,2},{5,3},{6,4},{7,5},{8,14},{9,15},{10,... | collective-permute-start | bytes 393224 | tf_op jit(solution)/shard_map/ppermute | solution.py:35
  66.8 9.7 %collective-permute-start.6 = (bf16[256,256]{1,0:T(8,128)(2,1)S(1)}, bf16[256,256]{1,0:T(8,128)(2,1)S(1)}, u32[]{:S(2)}, u32[]{:S(2)}) collective-permute-start(bf16[256,256]{1,0:T(8,128)(2,1)S(1)} %bitcast.90), channel_id=1, source_target_pairs={{0,7},{1,0},{2,1},{3,2},{4,3},{5,4},{6,5},{7,6},{8,15},{9,8},{10,9... | collective-permute-start | bytes 393224 | tf_op jit(solution)/shard_map/ppermute | solution.py:35
  76.5 1.0 copy-start.5
  85.8 3.2 %copy-start.3 = (bf16[12,128,2,128]{1,3,2,0:T(8,128)(2,1)S(1)}, bf16[12,128,2,128]{1,3,2,0:T(8,128)(2,1)}, u32[]{:S(2)}) copy-start(bf16[12,128,2,128]{1,3,2,0:T(8,128)(2,1)} %copy-done.2) | copy-start | bytes 2359300
  85.9 3.2 %copy-start.4 = (bf16[12,128,2,128]{3,2,1,0:T(2,128)(2,1)S(1)}, bf16[12,128,2,128]{3,2,1,0:T(2,128)(2,1)}, u32[]{:S(2)}) copy-start(bf16[12,128,2,128]{3,2,1,0:T(2,128)(2,1)} %reshape.186) | copy-start | bytes 2359300
  94.8 45.6 %copy-start.6 = (bf16[8,256,256]{2,1,0:T(8,128)(2,1)S(1)}, bf16[8,256,256]{2,1,0:T(8,128)(2,1)}, u32[]{:S(2)}) copy-start(bf16[8,256,256]{2,1,0:T(8,128)(2,1)} %copy-done.5) | copy-start | bytes 3145732
Sparse Core Ops, SparseCore 0:
  96.0 44.3 all-gather.3

commit v6 on v5

--- a/solution.py
+++ b/solution.py
@@ -26,17 +26,8 @@
     tp_index = lax.axis_index("tz") * PAIR + core_at
     first_group = seq_index * group_local
 
-    out_blocks = w_out.reshape(local_width, tp_count, local_width)
-    w_out_cols = jnp.zeros((tp_count, local_width, local_width), w_out.dtype)
-    for shift in range(tp_count):
-        piece = lax.dynamic_index_in_dim(out_blocks, (tp_index + shift) % tp_count, 1, False)
-        if shift:
-            pairs = [(i, (i + shift) % tp_count) for i in range(tp_count)]
-            piece = lax.ppermute(piece, TP, pairs)
-        w_out_cols = lax.dynamic_update_index_in_dim(
-            w_out_cols, piece, (tp_index - shift) % tp_count, 0
-        )
-    w_out_cols = w_out_cols.reshape(tp_count * local_width, local_width)
+    w_out_all = lax.all_gather(w_out, TP, axis=0, tiled=True)
+    w_out_cols = lax.dynamic_slice_in_dim(w_out_all, tp_index * local_width, local_width, 1)
 
     local_lengths = lax.dynamic_slice_in_dim(lengths, first_group, group_local, 0)
     reader_rows = lax.dynamic_slice_in_dim(readers, first_group, group_local, 0)
@@ -48,7 +39,6 @@
     value_rows = jnp.where(
         live_mask, jnp.dot(tokens, w_value, preferred_element_type=jnp.float32), 0.0
     ).astype(jnp.bfloat16)
-    w_query, w_out_cols = lax.optimization_barrier((w_query, w_out_cols))
     query_rows = jnp.dot(tokens, w_query, preferred_element_type=jnp.float32).astype(jnp.bfloat16)
     query_blocks = query_rows.reshape(group_local, CH, head_dev, HS)
     key_blocks = key_rows.reshape(group_local, CH, head_dev, HS)
@@ -104,6 +94,7 @@
     mixed = jnp.where(live_mask.reshape(group_local, CH, 1, 1), mixed, 0.0).astype(jnp.bfloat16)
     mixed = mixed.reshape(group_local * CH, local_width)
 
+    mixed, w_out_cols = lax.optimization_barrier((mixed, w_out_cols))
     mixed_all = lax.all_gather(mixed, TP, axis=1, tiled=True)
     return jnp.dot(mixed_all, w_out_cols, preferred_element_type=jnp.float32).astype(jnp.bfloat16)
 

time: 153 us -> 139 us (0.908)
  starting transfers between devices: 16 us -> 0.04 us
  waiting for transfers between devices: 44.6 us -> 51.1 us
  local copies, waits for them, and re-layouts: 21.9 us -> 16.9 us
  matrix products: 31.9 us -> 30.3 us
    ppermute x7 -> x0, starting transfers between devices: 16 us -> none  [local(): piece = lax.ppermute(piece, TP, pairs)]
    all_gather x1, waiting for transfers between devices: 44.6 us -> 50.3 us  [local(): mixed_all = lax.all_gather(mixed, TP, axis=1, tiled=True)]
    dynamic_update_slice x8 -> x0, local copies, waits for them, and re-layouts: 4.63 us -> none  [local(): lax.dynamic_update_index_in_dim(w_out_cols, piece, (tp_index - shift) % t...]
    dynamic_slice x9 -> x1, local copies, waits for them, and re-layouts: 4.17 us -> 1.29 us  [local(): lax.dynamic_slice_in_dim(w_out_all, tp_index * local_width, local_width, 1)]
    unnamed x18 -> x9, local copies, waits for them, and re-layouts: 3.57 us -> 1 us
  transfers between devices with their start and end apart: 8 -> 2, of which waited for: 1 -> 1; matrix products, arithmetic and copies ran while one was open for 18% -> 30% of each run, Pallas kernels for 0% -> 0%
where the time goes in v6:
time: 139 us
  waiting for transfers between devices  51.1 us (37%)
  matrix products  30.3 us (22%)
  blocking collectives  23.8 us (17%)
  local copies, waits for them, and re-layouts  16.9 us (12%)
  between operations  15.5 us (11%)
    all_gather x1, waiting for transfers between devices, local(): mixed_all = lax.all_gather(mixed, TP, axis=1, tiled=True)  50.3 us
    all_gather x1, blocking collectives, local(): row_tails = lax.all_gather(tail, 'sx', axis=0, tiled=False)  12.3 us
    all_gather x1, blocking collectives, local(): row_sums = lax.all_gather(row_sum, 'sy', axis=0, tiled=False)  11.5 us
    dot_general x1, matrix products, local(): jnp.dot(tokens, w_key, preferred_element_type=jnp.float32)  6.56 us
    dot_general x1, matrix products, local(): jnp.dot(tokens, w_query, preferred_element_type=jnp.float32)  5.87 us
    dot_general x1, matrix products, local(): jnp.dot(mixed_all, w_out_cols, preferred_element_type=jnp.float32)  5.46 us
    dot_general x1, matrix products, local(): jnp.dot(tokens, w_value, preferred_element_type=jnp.float32)  4.59 us
    dot_general x1, matrix products, local(): jnp.einsum('chts,cshe->cthe', weights, value_blocks, preferred_element_ty...  3.75 us
  transfers between devices with their start and end apart: 2, of which 1 were waited for; matrix products, arithmetic and copies ran while one was open for 30% of the time, Pallas kernels for 0%

profile of v6, /device:TPU:1, one launch (start us, length us, event | category | flops | bytes accessed | tf_op | source)
XLA Modules:
  0.0 138.7 jit_solution(13437138065207866876)
XLA Ops:
  6.5 0.0 copy-start
  6.5 0.0 copy-start.1
  6.5 0.0 all-gather.5.cloned.1.call-start
  6.5 0.7 all-gather.5.cloned.1.call-update
  7.3 0.0 all-gather.7.cloned.1.call-start
  7.3 0.6 slice.41
  9.2 0.7 convert_element_type.76
  9.9 0.8 dynamic_slice.12
  10.7 0.8 dynamic-slice_bitcast_fusion
  11.4 0.9 dynamic-slice_reduce_fusion
  12.4 1.6 %gather_fusion.1 = s32[4]{0:T(128)S(1)} fusion(s32[192,192]{1,0:T(8,128)} %param.18, s32[4]{0:T(128)S(1)} %or_bitcast_fusion.1), kind=kCustom, calls=%fused_computation.1 | custom fusion | bytes 64 | tf_op jit(solution)/shard_map/gather | solution.py:62
  14.6 1.6 %gather_fusion.2 = s32[4]{0:T(128)S(1)} fusion(s32[192,192]{1,0:T(8,128)} %param.18, s32[4]{0:T(128)S(1)} %get-tuple-element.49), kind=kCustom, calls=%fused_computation.2 | custom fusion | bytes 64 | tf_op jit(solution)/shard_map/gather | solution.py:58
  16.2 0.0 copy-done.1
  16.2 0.6 gather_fusion
  16.9 0.1 iota_compare_fusion.1
  16.9 0.0 copy-done
  16.9 4.6 %fusion.1 = bf16[1536,256]{1,0:T(8,128)(2,1)S(1)} fusion(bf16[1536,2048]{1,0:T(8,128)(2,1)} %param.13, bf16[2048,256]{1,0:T(8,128)(2,1)S(1)} %copy-done, pred[1536]{0:T(1024)(128)(4,1)S(1)} %get-tuple-element.48), kind=kOutput, calls=%fused_computation.6 | convolution fusion | flops 1611399168 | bytes 8128000 | tf_op jit(solution)/shard_map/dot_general | solution.py:40
  21.5 0.2 reshape.180
  21.7 0.6 copy.24
  22.4 6.6 %fusion = bf16[1536,256]{1,0:T(8,128)(2,1)} fusion(bf16[1536,2048]{1,0:T(8,128)(2,1)} %param.13, bf16[2048,256]{1,0:T(8,128)(2,1)} %param.15, pred[1536]{0:T(1024)(128)(4,1)S(1)} %get-tuple-element.48), kind=kOutput, calls=%fused_computation.5 | convolution fusion | flops 1611399168 | bytes 8128000 | tf_op jit(solution)/shard_map/dot_general | solution.py:37
  28.9 2.0 %reshape.179 = bf16[12,128,2,128]{3,2,1,0:T(2,128)(2,1)S(1)} reshape(bf16[1536,256]{1,0:T(8,128)(2,1)} %fusion) | data formatting | bytes 1572864 | tf_op jit(solution)/shard_map/reshape | solution.py:44
  31.0 5.9 %convolution_convert_fusion.1 = bf16[1536,256]{1,0:T(8,128)(2,1)} fusion(bf16[1536,2048]{1,0:T(8,128)(2,1)} %param.13, bf16[2048,256]{1,0:T(8,128)(2,1)} %param.14), kind=kOutput, calls=%fused_computation.8 | convolution fusion | flops 1611005952 | bytes 8126464 | tf_op jit(solution)/shard_map/dot_general | solution.py:42
  36.8 2.7 %reshape.181 = bf16[12,128,2,128]{3,2,1,0:T(2,128)(2,1)} reshape(bf16[1536,256]{1,0:T(8,128)(2,1)} %convolution_convert_fusion.1) | data formatting | bytes 1572864 | tf_op jit(solution)/shard_map/reshape | solution.py:43
  39.6 0.7 convolution_convert_fusion.2
  40.3 0.0 copy-start.3
  40.3 0.5 fusion.6
  40.8 12.3 %all-gather = f32[8,128,128]{2,1,0:T(8,128)S(1)} all-gather(f32[2,128,128]{2,1,0:T(8,128)S(1)} %bitcast.56), channel_id=2, replica_groups=mesh['sy'=4,'sx'=4,'tz'=4,'tc'=2] {'sx'}, dimensions={0}, use_global_device_ids=true | all-gather | bytes 655360 | tf_op jit(solution)/shard_map/all_gather | solution.py:56
  53.1 0.2 multiply_reduce_fusion.1
  53.2 0.0 copy-start.2
  53.3 11.5 %all-gather.1 = f32[8,128,128]{2,1,0:T(8,128)S(1)} all-gather(f32[2,128,128]{2,1,0:T(8,128)S(1)} %get-tuple-element.45), channel_id=3, replica_groups=mesh['sy'=4,'sx'=4,'tz'=4,'tc'=2] {'sy'}, dimensions={0}, use_global_device_ids=true | all-gather | bytes 655360 | tf_op jit(solution)/shard_map/all_gather | solution.py:60
  64.7 0.1 multiply_reduce_fusion
  64.9 0.0 copy-done.3
  64.9 0.1 fusion.5
  65.0 0.7 add_convert_fusion
  65.8 0.0 copy-done.2
  65.8 1.9 %fusion.9 = f32[12,2,128,128]{3,2,1,0:T(8,128)} fusion(bf16[12,2,128,128]{3,0,2,1:T(8,128)(2,1)S(1)} %add_convert_fusion, bf16[12,128,2,128]{3,2,1,0:T(2,128)(2,1)S(1)} %copy-done.2), kind=kOutput, calls=%fused_computation.22 | convolution fusion | flops 100663296 | bytes 3145728 | tf_op jit(solution)/shard_map/cthd,chde->cthe/dot_general | solution.py:77
  67.7 3.7 %fusion.2 = bf16[12,128,2,128]{1,3,2,0:T(8,128)(2,1)} fusion(f32[12,2,128,128]{3,2,1,0:T(8,128)} %fusion.9, bf16[12,128,2,128]{1,3,2,0:T(8,128)(2,1)S(1)} %copy.24, f32[12]{0:T(128)S(1)} %fusion.5, pred[128,128]{1,0:T(8,128)(4,1)S(1)} %iota_compare_fusion, pred[12,128]{1,0:T(8,128)(4,1)S(1)} %get-tuple-element.47, ...), kind=kOutput, calls=%fused_computation.13 | convolution fusion | flops 203685888 | bytes 4736560 | tf_op jit(solution)/shard_map/chts,cshe->cthe/dot_general | solution.py:85
  71.5 2.3 %copy.25 = bf16[12,128,2,128]{3,2,1,0:T(2,128)(2,1)S(1)} copy(bf16[12,128,2,128]{1,3,2,0:T(8,128)(2,1)} %fusion.2) | data formatting | bytes 1572864 | tf_op jit(solution)/shard_map/convert_element_type | solution.py:94
  73.7 1.0 copy.47
  74.7 0.0 all-gather.5.cloned.1.call-done
  74.7 1.3 constant_dynamic-slice_fusion
  76.0 0.0 all-gather.7.cloned.1.call-update
  76.0 50.3 %all-gather.7.cloned.1.call-done = bf16[1536,2048]{1,0:T(8,128)(2,1)} async-done(((bf16[1536,256]{1,0:T(8,128)(2,1)}), bf16[1536,2048]{1,0:T(8,128)(2,1)}) %all-gather.7.cloned.1.call-update) | async-done | bytes 6291472 | tf_op jit(solution)/shard_map/all_gather | solution.py:98
  126.4 5.5 %convolution_convert_fusion = bf16[1536,256]{1,0:T(8,128)(2,1)} fusion(bf16[1536,2048]{1,0:T(8,128)(2,1)} %all-gather.7.cloned.1.call-done, bf16[2048,256]{1,0:T(8,128)(2,1)S(1)} %constant_dynamic-slice_fusion), kind=kOutput, calls=%fused_computation.7 | convolution fusion | flops 1611005952 | bytes 8126464 | tf_op jit(solution)/shard_map/dot_general | solution.py:99
  (12 shorter events, 0.1 us)
Async XLA Ops:
  6.5 10.4 %copy-start = (bf16[2048,256]{1,0:T(8,128)(2,1)S(1)}, bf16[2048,256]{1,0:T(8,128)(2,1)}, u32[]{:S(2)}) copy-start(bf16[2048,256]{1,0:T(8,128)(2,1)} %param.16) | copy-start | bytes 3145732
  6.5 9.7 %copy-start.1 = (s32[192,192]{1,0:T(8,128)S(1)}, s32[192,192]{1,0:T(8,128)}, u32[]{:S(2)}) copy-start(s32[192,192]{1,0:T(8,128)} %param.18) | copy-start | bytes 442372
  6.5 68.2 %all-gather.5.cloned.1.call-start = ((), (), s32[]{:S(2)}) async-start(), calls=%async_computation | async-start | bytes 9437184 | tf_op jit(solution)/shard_map/all_gather | solution.py:29
  7.3 119.1 %all-gather.7.cloned.1.call-start = ((), (), s32[]{:S(2)}) async-start(), calls=%async_computation.1 | async-start | bytes 7077888 | tf_op jit(solution)/shard_map/all_gather | solution.py:98
  40.3 24.6 %copy-start.3 = (s32[192]{0:T(256)S(1)}, s32[192]{0:T(256)}, u32[]{:S(2)}) copy-start(s32[192]{0:T(256)} %param.19) | copy-start | bytes 2308
  53.2 12.5 %copy-start.2 = (bf16[12,128,2,128]{3,2,1,0:T(2,128)(2,1)S(1)}, bf16[12,128,2,128]{3,2,1,0:T(2,128)(2,1)}, u32[]{:S(2)}) copy-start(bf16[12,128,2,128]{3,2,1,0:T(2,128)(2,1)} %reshape.181) | copy-start | bytes 2359300
Sparse Core Ops, SparseCore 0:
  9.0 53.4 all-gather.4
  76.1 50.1 all-gather.6

commit v7 on v6

--- a/solution.py
+++ b/solution.py
@@ -27,7 +27,6 @@
     first_group = seq_index * group_local
 
     w_out_all = lax.all_gather(w_out, TP, axis=0, tiled=True)
-    w_out_cols = lax.dynamic_slice_in_dim(w_out_all, tp_index * local_width, local_width, 1)
 
     local_lengths = lax.dynamic_slice_in_dim(lengths, first_group, group_local, 0)
     reader_rows = lax.dynamic_slice_in_dim(readers, first_group, group_local, 0)
@@ -94,9 +93,39 @@
     mixed = jnp.where(live_mask.reshape(group_local, CH, 1, 1), mixed, 0.0).astype(jnp.bfloat16)
     mixed = mixed.reshape(group_local * CH, local_width)
 
-    mixed, w_out_cols = lax.optimization_barrier((mixed, w_out_cols))
-    mixed_all = lax.all_gather(mixed, TP, axis=1, tiled=True)
-    return jnp.dot(mixed_all, w_out_cols, preferred_element_type=jnp.float32).astype(jnp.bfloat16)
+    mixed, w_out_all = lax.optimization_barrier((mixed, w_out_all))
+    chip_at = lax.axis_index("tz")
+    chip_count = tp_count // PAIR
+    sources = [chip_at]
+    blocks = [mixed]
+    for step in (1, chip_count - 1, 2):
+        pairs = [
+            (z * PAIR + c, ((z + step) % chip_count) * PAIR + c)
+            for z in range(chip_count)
+            for c in range(PAIR)
+        ]
+        blocks.append(lax.ppermute(mixed, TP, pairs))
+        sources.append((chip_at - step) % chip_count)
+    same_core = jnp.concatenate(blocks, axis=1)
+    other_core = lax.ppermute(same_core, "tc", [(0, 1), (1, 0)])
+    column = tp_index * local_width
+
+    def rows_of(chips, core):
+        return jnp.concatenate(
+            [
+                lax.dynamic_slice(
+                    w_out_all, ((z * PAIR + core) * local_width, column), (local_width, local_width)
+                )
+                for z in chips
+            ],
+            axis=0,
+        )
+
+    total = jnp.dot(same_core, rows_of(sources, core_at), preferred_element_type=jnp.float32)
+    total = total + jnp.dot(
+        other_core, rows_of(sources, 1 - core_at), preferred_element_type=jnp.float32
+    )
+    return total.astype(jnp.bfloat16)
 
 
 def solution(mesh):

time: 139 us -> 133 us (0.957)
  waiting for transfers between devices: 51.1 us -> 31.8 us
  starting transfers between devices: 0.04 us -> 10.7 us
  local copies, waits for them, and re-layouts: 16.9 us -> 18.5 us
  matrix products: 30.3 us -> 31.7 us
    all_gather x1 -> x0, waiting for transfers between devices: 50.3 us -> none  [local(): mixed_all = lax.all_gather(mixed, TP, axis=1, tiled=True)]
    ppermute x0 -> x4, waiting for transfers between devices: none -> 31.1 us  [the longest x3 26.8 us: local(): blocks.append(lax.ppermute(mixed, TP, pairs))]
    ppermute x0 -> x4, starting transfers between devices: none -> 10.7 us  [the longest x1 5.5 us: local(): other_core = lax.ppermute(same_core, 'tc', [(0, 1), (1, 0)])]
    unnamed x9 -> x8, local copies, waits for them, and re-layouts: 1 us -> 3.11 us
    reshape x1, local copies, waits for them, and re-layouts: 2.01 us -> 0.18 us  [local(): key_blocks = key_rows.reshape(group_local, CH, head_dev, HS)]
    dot_general x1 -> x2, matrix products: 5.46 us -> 6.71 us  [the longest x1 3.82 us: local(): jnp.dot(same_core, rows_of(sources, core_at), preferred_element_type=jnp....]
  transfers between devices with their start and end apart: 2 -> 5, of which waited for: 1 -> 4; matrix products, arithmetic and copies ran while one was open for 30% -> 33% of each run, Pallas kernels for 0% -> 0%
where the time goes in v7:
time: 133 us
  waiting for transfers between devices  31.8 us (24%)
  matrix products  31.7 us (24%)
  blocking collectives  23.4 us (18%)
  local copies, waits for them, and re-layouts  18.5 us (14%)
  between operations  15.5 us (12%)
  starting transfers between devices  10.7 us (8%)
    ppermute x3, waiting for transfers between devices, local(): blocks.append(lax.ppermute(mixed, TP, pairs))  26.8 us
    all_gather x1, blocking collectives, local(): row_tails = lax.all_gather(tail, 'sx', axis=0, tiled=False)  12.1 us
    all_gather x1, blocking collectives, local(): row_sums = lax.all_gather(row_sum, 'sy', axis=0, tiled=False)  11.3 us
    dot_general x1, matrix products, local(): jnp.dot(tokens, w_query, preferred_element_type=jnp.float32)  5.9 us
    ppermute x1, starting transfers between devices, local(): other_core = lax.ppermute(same_core, 'tc', [(0, 1), (1, 0)])  5.5 us
    dot_general x1, matrix products, local(): jnp.dot(tokens, w_key, preferred_element_type=jnp.float32)  5.48 us
    ppermute x3, starting transfers between devices, local(): blocks.append(lax.ppermute(mixed, TP, pairs))  5.18 us
    dot_general x1, matrix products, local(): jnp.dot(tokens, w_value, preferred_element_type=jnp.float32)  4.59 us
  transfers between devices with their start and end apart: 5, of which 4 were waited for; matrix products, arithmetic and copies ran while one was open for 33% of the time, Pallas kernels for 0%

profile of v7, /device:TPU:1, one launch (start us, length us, event | category | flops | bytes accessed | tf_op | source)
XLA Modules:
  0.0 132.8 jit_solution(6836057802218698793)
XLA Ops:
  6.5 0.0 copy-start
  6.5 0.0 all-gather.4.cloned.1.call-start
  6.5 0.7 all-gather.4.cloned.1.call-update
  7.3 0.6 slice.41
  9.2 0.7 convert_element_type.76
  9.8 0.8 dynamic_slice.33
  10.6 0.8 dynamic-slice_bitcast_fusion
  11.4 0.9 dynamic-slice_reduce_fusion
  12.3 1.6 %gather_fusion.1 = s32[4]{0:T(128)S(1)} fusion(s32[192,192]{1,0:T(8,128)} %param.18, s32[4]{0:T(128)S(1)} %or_bitcast_fusion.1), kind=kCustom, calls=%fused_computation.1 | custom fusion | bytes 64 | tf_op jit(solution)/shard_map/gather | solution.py:61
  14.6 1.6 %gather_fusion.2 = s32[4]{0:T(128)S(1)} fusion(s32[192,192]{1,0:T(8,128)} %param.18, s32[4]{0:T(128)S(1)} %get-tuple-element.57), kind=kCustom, calls=%fused_computation.2 | custom fusion | bytes 64 | tf_op jit(solution)/shard_map/gather | solution.py:57
  16.2 1.6 %gather_fusion = s32[4]{0:T(128)S(1)} fusion(s32[192,192]{1,0:T(8,128)} %param.18, s32[4]{0:T(128)S(1)} %get-tuple-element.58), kind=kCustom, calls=%fused_computation | custom fusion | bytes 64 | tf_op jit(solution)/shard_map/gather | solution.py:62
  17.7 0.1 iota_compare_fusion.1
  17.8 4.6 %fusion.2 = bf16[1536,256]{1,0:T(8,128)(2,1)S(1)} fusion(bf16[1536,2048]{1,0:T(8,128)(2,1)} %param.13, bf16[2048,256]{1,0:T(8,128)(2,1)S(1)} %copy-done, pred[1536]{0:T(1024)(128)(4,1)S(1)} %get-tuple-element.56), kind=kOutput, calls=%fused_computation.8 | convolution fusion | flops 1611399168 | bytes 8128000 | tf_op jit(solution)/shard_map/dot_general | solution.py:39
  22.4 0.2 reshape.180
  22.6 0.6 copy.24
  23.2 5.5 %fusion.1 = bf16[1536,256]{1,0:T(8,128)(2,1)S(1)} fusion(bf16[1536,2048]{1,0:T(8,128)(2,1)} %param.13, bf16[2048,256]{1,0:T(8,128)(2,1)} %param.15, pred[1536]{0:T(1024)(128)(4,1)S(1)} %get-tuple-element.56), kind=kOutput, calls=%fused_computation.7 | convolution fusion | flops 1611399168 | bytes 8128000 | tf_op jit(solution)/shard_map/dot_general | solution.py:36
  28.7 0.2 reshape.179
  28.9 5.9 %convolution_convert_fusion = bf16[1536,256]{1,0:T(8,128)(2,1)} fusion(bf16[1536,2048]{1,0:T(8,128)(2,1)} %param.13, bf16[2048,256]{1,0:T(8,128)(2,1)} %param.14), kind=kOutput, calls=%fused_computation.9 | convolution fusion | flops 1611005952 | bytes 8126464 | tf_op jit(solution)/shard_map/dot_general | solution.py:41
  34.8 2.0 %reshape.181 = bf16[12,128,2,128]{3,2,1,0:T(2,128)(2,1)S(1)} reshape(bf16[1536,256]{1,0:T(8,128)(2,1)} %convolution_convert_fusion) | data formatting | bytes 1572864 | tf_op jit(solution)/shard_map/reshape | solution.py:42
  36.8 0.0 copy-start.1
  36.9 0.7 convolution_convert_fusion.1
  37.5 0.5 fusion.7
  38.1 12.1 %all-gather = f32[8,128,128]{2,1,0:T(8,128)S(1)} all-gather(f32[2,128,128]{2,1,0:T(8,128)S(1)} %bitcast.59), channel_id=2, replica_groups=mesh['sy'=4,'sx'=4,'tz'=4,'tc'=2] {'sx'}, dimensions={0}, use_global_device_ids=true | all-gather | bytes 655360 | tf_op jit(solution)/shard_map/all_gather | solution.py:55
  50.2 0.2 multiply_reduce_fusion.1
  50.4 11.3 %all-gather.1 = f32[8,128,128]{2,1,0:T(8,128)S(1)} all-gather(f32[2,128,128]{2,1,0:T(8,128)S(1)} %get-tuple-element.45), channel_id=3, replica_groups=mesh['sy'=4,'sx'=4,'tz'=4,'tc'=2] {'sy'}, dimensions={0}, use_global_device_ids=true | all-gather | bytes 655360 | tf_op jit(solution)/shard_map/all_gather | solution.py:59
  61.7 0.1 multiply_reduce_fusion
  61.9 0.9 fusion.6
  62.7 1.4 %add_convert_fusion = bf16[12,2,128,128]{3,0,2,1:T(8,128)(2,1)S(1)} fusion(bf16[12,2,128,128]{3,2,1,0:T(8,128)(2,1)S(1)} %convolution_convert_fusion.1, f32[2,128,128]{2,1,0:T(8,128)S(1)} %add.209, f32[12]{0:T(128)S(1)} %convert_element_type.62, s32[192,192]{1,0:T(8,128)} %param.18, s32[]{:T(128)S(6)} %select_n.97), kind=kOutput, calls=%fused_computation.10 | convolution fusion | flops 10616976 | bytes 1712180 | tf_op jit(solution)/shard_map/ce,ehij->chij/dot_general | solution.py:68
  64.2 1.9 %fusion.10 = f32[12,2,128,128]{3,2,1,0:T(8,128)} fusion(bf16[12,2,128,128]{3,0,2,1:T(8,128)(2,1)S(1)} %add_convert_fusion, bf16[12,128,2,128]{3,2,1,0:T(2,128)(2,1)S(1)} %reshape.181), kind=kOutput, calls=%fused_computation.23 | convolution fusion | flops 100663296 | bytes 3145728 | tf_op jit(solution)/shard_map/cthd,chde->cthe/dot_general | solution.py:76
  66.1 3.5 %fusion.3 = bf16[12,128,2,128]{1,3,2,0:T(8,128)(2,1)} fusion(f32[12,2,128,128]{3,2,1,0:T(8,128)} %fusion.10, bf16[12,128,2,128]{1,3,2,0:T(8,128)(2,1)S(1)} %copy.24, f32[12]{0:T(128)S(1)} %fusion.6, pred[128,128]{1,0:T(8,128)(4,1)S(1)} %iota_compare_fusion, pred[12,128]{1,0:T(8,128)(4,1)S(1)} %get-tuple-element.55, ...), kind=kOutput, calls=%fused_computation.14 | convolution fusion | flops 203685888 | bytes 4736560 | tf_op jit(solution)/shard_map/chts,cshe->cthe/dot_general | solution.py:84
  69.6 2.3 %copy.25 = bf16[12,128,2,128]{3,2,1,0:T(2,128)(2,1)S(1)} copy(bf16[12,128,2,128]{1,3,2,0:T(8,128)(2,1)} %fusion.3) | data formatting | bytes 1572864 | tf_op jit(solution)/shard_map/convert_element_type | solution.py:93
  71.9 0.1 copy.47
  72.0 0.0 all-gather.4.cloned.1.call-done
  72.0 0.6 collective-permute-start
  72.7 3.4 %collective-permute-start.1 = (bf16[1536,256]{1,0:T(8,128)(2,1)S(1)}, bf16[1536,256]{1,0:T(8,128)(2,1)S(1)}, u32[]{:S(2)}, u32[]{:S(2)}) collective-permute-start(bf16[1536,256]{1,0:T(8,128)(2,1)S(1)} %bitcast.53), channel_id=1, source_target_pairs={{0,6},{1,7},{2,0},{3,1},{4,2},{5,3},{6,4},{7,5},{8,14},{9,15},{10,... | collective-permute-start | bytes 2359304 | tf_op jit(solution)/shard_map/ppermute | solution.py:107
  76.1 1.1 collective-permute-start.2
  77.2 1.0 constant_dynamic-update-slice_fusion.3
  78.2 11.1 %collective-permute-done = bf16[1536,256]{1,0:T(8,128)(2,1)S(1)} collective-permute-done((bf16[1536,256]{1,0:T(8,128)(2,1)S(1)}, bf16[1536,256]{1,0:T(8,128)(2,1)S(1)}, u32[]{:S(2)}, u32[]{:S(2)}) %collective-permute-start) | collective-permute-done | bytes 786464 | tf_op jit(solution)/shard_map/ppermute | solution.py:107
  89.3 1.0 constant_dynamic-update-slice_fusion.2
  90.3 0.3 collective-permute-done.1
  90.6 1.0 constant_dynamic-update-slice_fusion.1
  91.6 15.4 %collective-permute-done.2 = bf16[1536,256]{1,0:T(8,128)(2,1)S(1)} collective-permute-done((bf16[1536,256]{1,0:T(8,128)(2,1)S(1)}, bf16[1536,256]{1,0:T(8,128)(2,1)S(1)}, u32[]{:S(2)}, u32[]{:S(2)}) %collective-permute-start.2) | collective-permute-done | bytes 786464 | tf_op jit(solution)/shard_map/ppermute | solution.py:107
  107.1 1.0 constant_dynamic-update-slice_fusion
  108.1 5.5 %collective-permute-start.3 = (bf16[1536,1024]{1,0:T(8,128)(2,1)}, bf16[1536,1024]{1,0:T(8,128)(2,1)}, u32[]{:S(2)}, u32[]{:S(2)}) collective-permute-start(bf16[1536,1024]{1,0:T(8,128)(2,1)} %constant_dynamic-update-slice_fusion), channel_id=1, source_target_pairs={{0,1},{1,0},{2,3},{3,2},{4,5},{5,4},{6,7},{7,6},{8,9},{9,8},{10,11... | collective-permute-start | bytes 9437192 | tf_op jit(solution)/shard_map/ppermute | solution.py:110
  113.6 1.4 %fusion.49 = (bf16[256,256]{1,0:T(8,128)(2,1)S(1)}, bf16[256,256]{1,0:T(8,128)(2,1)S(1)}, bf16[256,256]{1,0:T(8,128)(2,1)S(1)}, bf16[256,256]{1,0:T(8,128)(2,1)S...) fusion(bf16[2048,2048]{1,0:T(8,128)(2,1)} %all-gather.4.cloned., ...), kind=kLoop, calls=%fused_computation.80 | loop fusion | bytes 2097184 | tf_op jit(solution)/shard_map/dynamic_slice | solution.py:116
  114.9 4.3 %collective-permute-done.3 = bf16[1536,1024]{1,0:T(8,128)(2,1)} collective-permute-done((bf16[1536,1024]{1,0:T(8,128)(2,1)}, bf16[1536,1024]{1,0:T(8,128)(2,1)}, u32[]{:S(2)}, u32[]{:S(2)}) %collective-permute-start.3) | collective-permute-done | bytes 3145760 | tf_op jit(solution)/shard_map/ppermute | solution.py:110
  119.2 2.9 %fusion.27 = f32[1536,256]{1,0:T(8,128)S(1)} fusion(bf16[1536,1024]{1,0:T(8,128)(2,1)} %collective-permute-done.3, bf16[256,256]{1,0:T(8,128)(2,1)S(1)} %get-tuple-element.48, bf16[256,256]{1,0:T(8,128)(2,1)S(1)} %get-tuple-element.49, bf16[256,256]{1,0:T(8,128)(2,1)S(1)} %get-tuple-element.50, bf16[256,256]{1,0:T(8,128)(2,1)S(1)} %get-tuple-element.51), kind=kOutput, calls=%fused_computation.38 | convolution fusion | flops 807403520 | bytes 5242880 | tf_op jit(solution)/shard_map/dot_general | solution.py:125
  122.1 3.8 %fusion = bf16[1536,256]{1,0:T(8,128)(2,1)} fusion(f32[1536,256]{1,0:T(8,128)S(1)} %fusion.27, bf16[1536,1024]{1,0:T(8,128)(2,1)} %constant_dynamic-update-slice_fusion, bf16[256,256]{1,0:T(8,128)(2,1)S(1)} %get-tuple-element.52, bf16[256,256]{1,0:T(8,128)(2,1)S(1)} %get-tuple-element.53, bf16[256,256]{1,0:T(8,128)(2,1)S(1)} %get-tuple-element.54, ...), kind=kOutput, calls=%fused_computation.6 | convolution fusion | flops 808189952 | bytes 6029312 | tf_op jit(solution)/shard_map/dot_general | solution.py:124
  (14 shorter events, 0.1 us)
Async XLA Ops:
  6.5 11.3 %copy-start = (bf16[2048,256]{1,0:T(8,128)(2,1)S(1)}, bf16[2048,256]{1,0:T(8,128)(2,1)}, u32[]{:S(2)}) copy-start(bf16[2048,256]{1,0:T(8,128)(2,1)} %param.16) | copy-start | bytes 3145732
  6.5 65.5 %all-gather.4.cloned.1.call-start = ((), (), s32[]{:S(2)}) async-start(), calls=%async_computation | async-start | bytes 9437184 | tf_op jit(solution)/shard_map/all_gather | solution.py:29
  36.8 25.0 %copy-start.1 = (s32[192]{0:T(256)S(1)}, s32[192]{0:T(256)}, u32[]{:S(2)}) copy-start(s32[192]{0:T(256)} %param.19) | copy-start | bytes 2308
  72.0 17.3 %collective-permute-start = (bf16[1536,256]{1,0:T(8,128)(2,1)S(1)}, bf16[1536,256]{1,0:T(8,128)(2,1)S(1)}, u32[]{:S(2)}, u32[]{:S(2)}) collective-permute-start(bf16[1536,256]{1,0:T(8,128)(2,1)S(1)} %bitcast.52), channel_id=1, source_target_pairs={{0,2},{1,3},{2,4},{3,5},{4,6},{5,7},{6,0},{7,1},{8,10},{9,11},{10,... | collective-permute-start | bytes 2359304 | tf_op jit(solution)/shard_map/ppermute | solution.py:107
  72.7 17.9 %collective-permute-start.1 = (bf16[1536,256]{1,0:T(8,128)(2,1)S(1)}, bf16[1536,256]{1,0:T(8,128)(2,1)S(1)}, u32[]{:S(2)}, u32[]{:S(2)}) collective-permute-start(bf16[1536,256]{1,0:T(8,128)(2,1)S(1)} %bitcast.53), channel_id=1, source_target_pairs={{0,6},{1,7},{2,0},{3,1},{4,2},{5,3},{6,4},{7,5},{8,14},{9,15},{10,... | collective-permute-start | bytes 2359304 | tf_op jit(solution)/shard_map/ppermute | solution.py:107
  76.1 30.9 %collective-permute-start.2 = (bf16[1536,256]{1,0:T(8,128)(2,1)S(1)}, bf16[1536,256]{1,0:T(8,128)(2,1)S(1)}, u32[]{:S(2)}, u32[]{:S(2)}) collective-permute-start(bf16[1536,256]{1,0:T(8,128)(2,1)S(1)} %bitcast.54), channel_id=1, source_target_pairs={{0,4},{1,5},{2,6},{3,7},{4,0},{5,1},{6,2},{7,3},{8,12},{9,13},{10,... | collective-permute-start | bytes 2359304 | tf_op jit(solution)/shard_map/ppermute | solution.py:107
  108.1 11.1 %collective-permute-start.3 = (bf16[1536,1024]{1,0:T(8,128)(2,1)}, bf16[1536,1024]{1,0:T(8,128)(2,1)}, u32[]{:S(2)}, u32[]{:S(2)}) collective-permute-start(bf16[1536,1024]{1,0:T(8,128)(2,1)} %constant_dynamic-update-slice_fusion), channel_id=1, source_target_pairs={{0,1},{1,0},{2,3},{3,2},{4,5},{5,4},{6,7},{7,6},{8,9},{9,8},{10,11... | collective-permute-start | bytes 9437192 | tf_op jit(solution)/shard_map/ppermute | solution.py:110
Sparse Core Ops, SparseCore 0:
  9.0 53.4 all-gather.3

commit v8 on v6

--- a/solution.py
+++ b/solution.py
@@ -27,7 +27,6 @@
     first_group = seq_index * group_local
 
     w_out_all = lax.all_gather(w_out, TP, axis=0, tiled=True)
-    w_out_cols = lax.dynamic_slice_in_dim(w_out_all, tp_index * local_width, local_width, 1)
 
     local_lengths = lax.dynamic_slice_in_dim(lengths, first_group, group_local, 0)
     reader_rows = lax.dynamic_slice_in_dim(readers, first_group, group_local, 0)
@@ -54,13 +53,16 @@
         "c,chde->hde", last_row.astype(jnp.bfloat16), states, preferred_element_type=jnp.float32
     )
     row_tails = lax.all_gather(tail, "sx", axis=0, tiled=False)
-    row_lasts = (row_at * ROW + jnp.arange(ROW)) * group_local + group_local - 1
-    in_row = readers[row_lasts[ROW - 1], row_lasts].at[ROW - 1].set(1).astype(jnp.float32)
+    row_end = (row_at * ROW + ROW - 1) * group_local + group_local - 1
+    end_lasts = lax.dynamic_index_in_dim(readers, row_end, 0, False)
+    end_lasts = end_lasts.reshape(seq_count, group_local)[:, group_local - 1]
+    first_lasts = lax.dynamic_index_in_dim(readers, first_group, 0, False)
+    first_lasts = first_lasts.reshape(seq_count, group_local)[:, group_local - 1].astype(jnp.float32)
+    in_row = lax.dynamic_slice_in_dim(end_lasts, row_at * ROW, ROW).at[ROW - 1].set(1).astype(jnp.float32)
     row_sum = (in_row[:, None, None, None] * row_tails).sum(0)
     row_sums = lax.all_gather(row_sum, "sy", axis=0, tiled=False)
-    row_ends = (jnp.arange(row_count) * ROW + ROW - 1) * group_local + group_local - 1
-    from_rows = readers[first_group, row_ends].astype(jnp.float32)
-    from_row = readers[first_group, row_lasts].astype(jnp.float32)
+    from_rows = first_lasts.reshape(row_count, ROW)[:, ROW - 1]
+    from_row = lax.dynamic_slice_in_dim(first_lasts, row_at * ROW, ROW)
     entering = (from_row[:, None, None, None] * row_tails).sum(0) + (
         from_rows[:, None, None, None] * row_sums
     ).sum(0)
@@ -94,9 +96,50 @@
     mixed = jnp.where(live_mask.reshape(group_local, CH, 1, 1), mixed, 0.0).astype(jnp.bfloat16)
     mixed = mixed.reshape(group_local * CH, local_width)
 
-    mixed, w_out_cols = lax.optimization_barrier((mixed, w_out_cols))
-    mixed_all = lax.all_gather(mixed, TP, axis=1, tiled=True)
-    return jnp.dot(mixed_all, w_out_cols, preferred_element_type=jnp.float32).astype(jnp.bfloat16)
+    mixed, w_out_all = lax.optimization_barrier((mixed, w_out_all))
+    chip_at = lax.axis_index("tz")
+    chip_count = tp_count // PAIR
+    column = tp_index * local_width
+
+    def shifted(step):
+        return [
+            (z * PAIR + c, ((z + step) % chip_count) * PAIR + c)
+            for z in range(chip_count)
+            for c in range(PAIR)
+        ]
+
+    def rows_of(z, core):
+        return lax.dynamic_slice(
+            w_out_all, ((z * PAIR + core) * local_width, column), (local_width, local_width)
+        )
+
+    def term(block, z, core):
+        return jnp.dot(block, rows_of(z, core), preferred_element_type=jnp.float32)
+
+    from_below = lax.ppermute(mixed, TP, shifted(1))
+    from_above = lax.ppermute(mixed, TP, shifted(chip_count - 1))
+    below = (chip_at - 1) % chip_count
+    above = (chip_at + 1) % chip_count
+    across = (chip_at + 2) % chip_count
+    first = jnp.concatenate([mixed, from_below, from_above], axis=1)
+    sibling_first = lax.ppermute(first, "tc", [(0, 1), (1, 0)])
+    forward = [
+        (z * PAIR, ((z + 1) % chip_count) * PAIR) for z in range(chip_count)
+    ] + [(z * PAIR + 1, ((z - 1) % chip_count) * PAIR + 1) for z in range(chip_count)]
+    relayed = lax.ppermute(jnp.where(core_at == 0, from_below, from_above), TP, forward)
+    sibling_relayed = lax.ppermute(relayed, "tc", [(0, 1), (1, 0)])
+    other = 1 - core_at
+    total = term(mixed, chip_at, core_at)
+    total = total + term(from_below, below, core_at) + term(from_above, above, core_at)
+    total = total + jnp.dot(
+        sibling_first,
+        jnp.concatenate(
+            [rows_of(chip_at, other), rows_of(below, other), rows_of(above, other)], axis=0
+        ),
+        preferred_element_type=jnp.float32,
+    )
+    total = total + term(relayed, across, core_at) + term(sibling_relayed, across, other)
+    return total.astype(jnp.bfloat16)
 
 
 def solution(mesh):

time: 139 us -> 120 us (0.86)
  waiting for transfers between devices: 51.1 us -> 20.4 us
  starting transfers between devices: 0.04 us -> 12 us
  local copies, waits for them, and re-layouts: 16.9 us -> 10.4 us
  matrix products: 30.3 us -> 34.9 us
  other arithmetic: 1.1 us -> 3.9 us
  between operations: 15.5 us -> 13.6 us
    all_gather x1 -> x0, waiting for transfers between devices: 50.3 us -> none  [local(): mixed_all = lax.all_gather(mixed, TP, axis=1, tiled=True)]
    ppermute x0 -> x5, waiting for transfers between devices: none -> 19.7 us  [the longest x1 14 us: local(): from_below = lax.ppermute(mixed, TP, shifted(1))]
    ppermute x0 -> x5, starting transfers between devices: none -> 12 us  [the longest x1 4.38 us: local(): sibling_first = lax.ppermute(first, 'tc', [(0, 1), (1, 0)])]
    dot_general x1 -> x6, matrix products: 5.46 us -> 10 us  [the longest x5 7.55 us: term(): return jnp.dot(block, rows_of(z, core), preferred_element_type=jnp.float32)]
    gather x3 -> x0, local copies, waits for them, and re-layouts: 3.78 us -> none  [the longest x1 1.57 us: local(): readers[row_lasts[ROW - 1], row_lasts].at[ROW - 1].set(1)]
    reshape x1, local copies, waits for them, and re-layouts: 2.01 us -> 0.18 us  [local(): key_blocks = key_rows.reshape(group_local, CH, head_dev, HS)]
    dot_general x1, matrix products: 6.56 us -> 4.84 us  [local(): jnp.dot(tokens, w_key, preferred_element_type=jnp.float32)]
    concatenate x2 -> x1, other arithmetic: 0.03 us -> 1.62 us  [local(): first = jnp.concatenate([mixed, from_below, from_above], axis=1)]
  transfers between devices with their start and end apart: 2 -> 6, of which waited for: 1 -> 2; matrix products, arithmetic and copies ran while one was open for 30% -> 38% of each run, Pallas kernels for 0% -> 0%
where the time goes in v8:
time: 120 us; the launch traced here: 119 us
  matrix products  34.9 us (29%)
  blocking collectives  24 us (20%)
  waiting for transfers between devices  20.4 us (17%)
  between operations  13.6 us (11%)
  starting transfers between devices  12 us (10%)
  local copies, waits for them, and re-layouts  10.4 us (9%)
  other arithmetic  3.9 us (3%)
    ppermute x1, waiting for transfers between devices, local(): from_below = lax.ppermute(mixed, TP, shifted(1))  14 us
    all_gather x1, blocking collectives, local(): row_tails = lax.all_gather(tail, 'sx', axis=0, tiled=False)  12.2 us
    all_gather x1, blocking collectives, local(): row_sums = lax.all_gather(row_sum, 'sy', axis=0, tiled=False)  11.8 us
    dot_general x5, matrix products, term(): return jnp.dot(block, rows_of(z, core), preferred_element_type=jnp.float32)  7.55 us
    dot_general x1, matrix products, local(): jnp.dot(tokens, w_query, preferred_element_type=jnp.float32)  6.5 us
    ppermute x1, waiting for transfers between devices, local(): lax.ppermute(jnp.where(core_at == 0, from_below, from_above), TP, forward)  5.62 us
    dot_general x1, matrix products, local(): jnp.dot(tokens, w_key, preferred_element_type=jnp.float32)  4.84 us
    dot_general x1, matrix products, local(): jnp.dot(tokens, w_value, preferred_element_type=jnp.float32)  4.58 us
  transfers between devices with their start and end apart: 6, of which 2 were waited for; matrix products, arithmetic and copies ran while one was open for 38% of the time, Pallas kernels for 0%

profile of v8, /device:TPU:1, one launch (start us, length us, event | category | flops | bytes accessed | tf_op | source)
XLA Modules:
  0.0 119.2 jit_solution(16096231954904864123)
XLA Ops:
  6.5 0.7 all-gather.4.cloned.1.call-update
  7.3 0.7 convert_element_type.70
  8.0 0.8 dynamic_slice.50
  8.7 0.1 iota_compare_fusion.1
  8.8 4.6 %fusion.4 = bf16[1536,256]{1,0:T(8,128)(2,1)S(1)} fusion(bf16[1536,2048]{1,0:T(8,128)(2,1)} %param.13, bf16[2048,256]{1,0:T(8,128)(2,1)S(1)} %copy-done, pred[1536]{0:T(1024)(128)(4,1)S(1)} %get-tuple-element.53), kind=kOutput, calls=%fused_computation.9 | convolution fusion | flops 1611399168 | bytes 8128000 | tf_op jit(solution)/shard_map/dot_general | solution.py:39
  13.4 0.2 reshape.145
  13.6 0.6 copy.33
  14.2 4.8 %fusion.3 = bf16[1536,256]{1,0:T(8,128)(2,1)S(1)} fusion(bf16[1536,2048]{1,0:T(8,128)(2,1)} %param.13, bf16[2048,256]{1,0:T(8,128)(2,1)} %param.15, pred[1536]{0:T(1024)(128)(4,1)S(1)} %get-tuple-element.53), kind=kOutput, calls=%fused_computation.8 | convolution fusion | flops 1611399168 | bytes 8128000 | tf_op jit(solution)/shard_map/dot_general | solution.py:36
  19.1 0.2 reshape.144
  19.3 0.7 fusion.41
  20.0 0.1 reshape.143
  20.1 0.1 reshape.146
  20.3 0.1 dynamic-slice_reduce_fusion.2
  20.5 0.1 dynamic-slice_reduce_fusion.1
  20.6 0.8 dynamic-slice_bitcast_fusion
  21.4 0.2 fusion.46
  21.6 0.1 convert_element_type.62
  21.7 0.9 dynamic-slice_reduce_fusion
  22.6 6.5 %convolution_convert_fusion = bf16[1536,256]{1,0:T(8,128)(2,1)} fusion(bf16[1536,2048]{1,0:T(8,128)(2,1)} %param.13, bf16[2048,256]{1,0:T(8,128)(2,1)} %param.14), kind=kOutput, calls=%fused_computation.10 | convolution fusion | flops 1611005952 | bytes 8126464 | tf_op jit(solution)/shard_map/dot_general | solution.py:41
  29.1 2.0 %reshape.147 = bf16[12,128,2,128]{3,2,1,0:T(2,128)(2,1)S(1)} reshape(bf16[1536,256]{1,0:T(8,128)(2,1)} %convolution_convert_fusion) | data formatting | bytes 1572864 | tf_op jit(solution)/shard_map/reshape | solution.py:42
  31.1 0.2 slice_reduce_fusion
  31.3 0.7 convolution_convert_fusion.1
  32.0 0.5 fusion.9
  32.5 12.2 %all-gather = f32[8,128,128]{2,1,0:T(8,128)S(1)} all-gather(f32[2,128,128]{2,1,0:T(8,128)S(1)} %bitcast.56), channel_id=2, replica_groups=mesh['sy'=4,'sx'=4,'tz'=4,'tc'=2] {'sx'}, dimensions={0}, use_global_device_ids=true | all-gather | bytes 655360 | tf_op jit(solution)/shard_map/all_gather | solution.py:55
  44.7 0.2 multiply_reduce_fusion.1
  44.9 11.8 %all-gather.1 = f32[8,128,128]{2,1,0:T(8,128)S(1)} all-gather(f32[2,128,128]{2,1,0:T(8,128)S(1)} %get-tuple-element.45), channel_id=3, replica_groups=mesh['sy'=4,'sx'=4,'tz'=4,'tc'=2] {'sy'}, dimensions={0}, use_global_device_ids=true | all-gather | bytes 655360 | tf_op jit(solution)/shard_map/all_gather | solution.py:63
  56.7 0.1 multiply_reduce_fusion
  56.9 0.9 fusion.8
  57.7 1.4 %add_convert_fusion = bf16[12,2,128,128]{3,0,2,1:T(8,128)(2,1)S(1)} fusion(bf16[12,2,128,128]{3,2,1,0:T(8,128)(2,1)S(1)} %convolution_convert_fusion.1, f32[2,128,128]{2,1,0:T(8,128)S(1)} %add.148, f32[12]{0:T(128)S(1)} %convert_element_type.56, s32[192,192]{1,0:T(8,128)} %param.18, s32[]{:T(128)S(6)} %select_n.88), kind=kOutput, calls=%fused_computation.12 | convolution fusion | flops 10616976 | bytes 1712180 | tf_op jit(solution)/shard_map/ce,ehij->chij/dot_general | solution.py:71
  59.2 1.9 %fusion.12 = f32[12,2,128,128]{3,2,1,0:T(8,128)} fusion(bf16[12,2,128,128]{3,0,2,1:T(8,128)(2,1)S(1)} %add_convert_fusion, bf16[12,128,2,128]{3,2,1,0:T(2,128)(2,1)S(1)} %reshape.147), kind=kOutput, calls=%fused_computation.25 | convolution fusion | flops 100663296 | bytes 3145728 | tf_op jit(solution)/shard_map/cthd,chde->cthe/dot_general | solution.py:79
  61.1 3.5 %fusion.5 = bf16[12,128,2,128]{1,3,2,0:T(8,128)(2,1)} fusion(f32[12,2,128,128]{3,2,1,0:T(8,128)} %fusion.12, bf16[12,128,2,128]{1,3,2,0:T(8,128)(2,1)S(1)} %copy.33, f32[12]{0:T(128)S(1)} %fusion.8, pred[128,128]{1,0:T(8,128)(4,1)S(1)} %iota_compare_fusion, pred[12,128]{1,0:T(8,128)(4,1)S(1)} %get-tuple-element.52, ...), kind=kOutput, calls=%fused_computation.16 | convolution fusion | flops 203685888 | bytes 4736560 | tf_op jit(solution)/shard_map/chts,cshe->cthe/dot_general | solution.py:87
  64.6 2.3 %copy.34 = bf16[12,128,2,128]{3,2,1,0:T(2,128)(2,1)S(1)} copy(bf16[12,128,2,128]{1,3,2,0:T(8,128)(2,1)} %fusion.5) | data formatting | bytes 1572864 | tf_op jit(solution)/shard_map/convert_element_type | solution.py:96
  66.9 0.1 copy.56
  67.1 3.3 %collective-permute-start.1 = (bf16[1536,256]{1,0:T(8,128)(2,1)S(1)}, bf16[1536,256]{1,0:T(8,128)(2,1)S(1)}, u32[]{:S(2)}, u32[]{:S(2)}) collective-permute-start(bf16[1536,256]{1,0:T(8,128)(2,1)S(1)} %bitcast.50), channel_id=1, source_target_pairs={{0,6},{1,7},{2,0},{3,1},{4,2},{5,3},{6,4},{7,5},{8,14},{9,15},{10,... | collective-permute-start | bytes 2359304 | tf_op jit(solution)/shard_map/ppermute | solution.py:120
  70.4 14.0 %collective-permute-done = bf16[1536,256]{1,0:T(8,128)(2,1)S(1)} collective-permute-done((bf16[1536,256]{1,0:T(8,128)(2,1)S(1)}, bf16[1536,256]{1,0:T(8,128)(2,1)S(1)}, u32[]{:S(2)}, u32[]{:S(2)}) %collective-permute-start) | collective-permute-done | bytes 786464 | tf_op jit(solution)/shard_map/ppermute | solution.py:119
  84.4 1.6 %pad_maximum_fusion = bf16[1536,768]{1,0:T(8,128)(2,1)} fusion(bf16[1536,256]{1,0:T(8,128)(2,1)S(1)} %collective-permute-done.1, bf16[1536,256]{1,0:T(8,128)(2,1)S(1)} %collective-permute-done, bf16[1536,256]{1,0:T(8,128)(2,1)S(1)} %bitcast.51), kind=kLoop, calls=%fused_computation.11 | loop fusion | flops 7077888 | bytes 4718592 | tf_op jit(solution)/shard_map/concatenate | solution.py:124
  86.0 4.4 %collective-permute-start.2 = (bf16[1536,768]{1,0:T(8,128)(2,1)}, bf16[1536,768]{1,0:T(8,128)(2,1)}, u32[]{:S(2)}, u32[]{:S(2)}) collective-permute-start(bf16[1536,768]{1,0:T(8,128)(2,1)} %pad_maximum_fusion), channel_id=1, source_target_pairs={{0,1},{1,0},{2,3},{3,2},{4,5},{5,4},{6,7},{7,6},{8,9},{9,8},{10,11... | collective-permute-start | bytes 7077896 | tf_op jit(solution)/shard_map/ppermute | solution.py:125
  90.4 1.0 broadcast_select_fusion
  91.4 2.7 %collective-permute-start.3 = (bf16[1536,256]{1,0:T(8,128)(2,1)}, bf16[1536,256]{1,0:T(8,128)(2,1)}, u32[]{:S(2)}, u32[]{:S(2)}) collective-permute-start(bf16[1536,256]{1,0:T(8,128)(2,1)} %broadcast_select_fusion), channel_id=1, source_target_pairs={{0,2},{2,4},{4,6},{6,0},{1,7},{3,1},{5,3},{7,5},{8,10},{10,12},{12... | collective-permute-start | bytes 2359304 | tf_op jit(solution)/shard_map/ppermute | solution.py:129
  94.1 1.1 fusion.48
  95.2 1.3 %fusion.33 = f32[1536,256]{1,0:T(8,128)S(1)} fusion(bf16[1536,256]{1,0:T(8,128)(2,1)S(1)} %bitcast.52, bf16[2048,2048]{1,0:T(8,128)(2,1)} %all-gather.4.cloned.1.call-done, s32[]{:T(128)S(6)} %select_n.95), kind=kOutput, calls=%fused_computation.48 | convolution fusion | flops 201326592 | bytes 2490372 | tf_op jit(solution)/shard_map/dot_general | solution.py:117
  96.5 1.3 %convolution_add_fusion.2 = f32[1536,256]{1,0:T(8,128)S(1)} fusion(f32[1536,256]{1,0:T(8,128)S(1)} %fusion.33, bf16[1536,256]{1,0:T(8,128)(2,1)S(1)} %collective-permute-done, bf16[2048,2048]{1,0:T(8,128)(2,1)} %all-gather.4.cloned.1.call-done, s32[]{:T(128)S(6)} %select_n.97, s32[]{:T(128)S(6)} %select_n.95), kind=kOutput, calls=%fused_computation.4 | convolution fusion | flops 201719808 | bytes 4063240 | tf_op jit(solution)/shard_map/dot_general | solution.py:117
  97.8 5.6 %collective-permute-done.3 = bf16[1536,256]{1,0:T(8,128)(2,1)} collective-permute-done((bf16[1536,256]{1,0:T(8,128)(2,1)}, bf16[1536,256]{1,0:T(8,128)(2,1)}, u32[]{:S(2)}, u32[]{:S(2)}) %collective-permute-start.3) | collective-permute-done | bytes 786464 | tf_op jit(solution)/shard_map/ppermute | solution.py:129
  103.4 1.5 %collective-permute-start.4 = (bf16[1536,256]{1,0:T(8,128)(2,1)}, bf16[1536,256]{1,0:T(8,128)(2,1)S(1)}, u32[]{:S(2)}, u32[]{:S(2)}) collective-permute-start(bf16[1536,256]{1,0:T(8,128)(2,1)} %collective-permute-done.3), channel_id=1, source_target_pairs={{0,1},{1,0},{2,3},{3,2},{4,5},{5,4},{6,7},{7,6},{8,9},{9,8},{10,11... | collective-permute-start | bytes 2359304 | tf_op jit(solution)/shard_map/ppermute | solution.py:130
  104.9 1.5 %fusion.29 = f32[1536,256]{1,0:T(8,128)S(1)} fusion(bf16[1536,256]{1,0:T(8,128)(2,1)} %collective-permute-done.3, bf16[2048,2048]{1,0:T(8,128)(2,1)} %all-gather.4.cloned.1.call-done, s32[]{:T(128)S(6)} %select_n.106, s32[]{:T(128)S(6)} %select_n.95), kind=kOutput, calls=%fused_computation.44 | convolution fusion | flops 201326592 | bytes 2490376 | tf_op jit(solution)/shard_map/dot_general | solution.py:117
  106.4 2.5 %fusion.22 = f32[1536,256]{1,0:T(8,128)S(1)} fusion(bf16[1536,768]{1,0:T(8,128)(2,1)} %collective-permute-done.2, bf16[256,256]{1,0:T(8,128)(2,1)S(1)} %get-tuple-element.50, bf16[256,256]{1,0:T(8,128)(2,1)S(1)} %get-tuple-element.51, bf16[256,256]{1,0:T(8,128)(2,1)S(1)} %get-tuple-element.49), kind=kOutput, calls=%fused_computation.37 | convolution fusion | flops 605159424 | bytes 4325376 | tf_op jit(solution)/shard_map/dot_general | solution.py:134
  108.9 1.3 %fusion.1 = f32[1536,256]{1,0:T(8,128)S(1)} fusion(f32[1536,256]{1,0:T(8,128)S(1)} %fusion.29, f32[1536,256]{1,0:T(8,128)S(1)} %fusion.22, f32[1536,256]{1,0:T(8,128)S(1)} %convolution_add_fusion.2, bf16[1536,256]{1,0:T(8,128)(2,1)S(1)} %collective-permute-done.1, bf16[2048,2048]{1,0:T(8,128)(2,1)} %all-gather.4.cloned.1.call-done, s32[]{:T(128)S(6)} %select_n.99, ...), kind=kOutput, calls=%fused_computation.3 | convolution fusion | flops 202506240 | bytes 7208968 | tf_op jit(solution)/shard_map/dot_general | solution.py:117
  110.2 2.2 %fusion.2 = bf16[1536,256]{1,0:T(8,128)(2,1)} fusion(f32[1536,256]{1,0:T(8,128)S(1)} %fusion.1, bf16[1536,256]{1,0:T(8,128)(2,1)S(1)} %collective-permute-done.4, bf16[2048,2048]{1,0:T(8,128)(2,1)} %all-gather.4.cloned.1.call-done, s32[]{:T(128)S(6)} %select_n.107, s32[]{:T(128)S(6)} %select_n.95), kind=kOutput, calls=%fused_computation.7 | convolution fusion | flops 202113024 | bytes 3276808 | tf_op jit(solution)/shard_map/dot_general | solution.py:117
  (19 shorter events, 0.4 us)
Async XLA Ops:
  6.5 2.2 %copy-start = (bf16[2048,256]{1,0:T(8,128)(2,1)S(1)}, bf16[2048,256]{1,0:T(8,128)(2,1)}, u32[]{:S(2)}) copy-start(bf16[2048,256]{1,0:T(8,128)(2,1)} %param.16) | copy-start | bytes 3145732
  6.5 60.5 %all-gather.4.cloned.1.call-start = ((), (), s32[]{:S(2)}) async-start(), calls=%async_computation | async-start | bytes 9437184 | tf_op jit(solution)/shard_map/all_gather | solution.py:29
  32.0 24.9 %copy-start.1 = (s32[192]{0:T(256)S(1)}, s32[192]{0:T(256)}, u32[]{:S(2)}) copy-start(s32[192]{0:T(256)} %param.19) | copy-start | bytes 2308
  67.0 17.4 %collective-permute-start = (bf16[1536,256]{1,0:T(8,128)(2,1)S(1)}, bf16[1536,256]{1,0:T(8,128)(2,1)S(1)}, u32[]{:S(2)}, u32[]{:S(2)}) collective-permute-start(bf16[1536,256]{1,0:T(8,128)(2,1)S(1)} %bitcast.49), channel_id=1, source_target_pairs={{0,2},{1,3},{2,4},{3,5},{4,6},{5,7},{6,0},{7,1},{8,10},{9,11},{10,... | collective-permute-start | bytes 2359304 | tf_op jit(solution)/shard_map/ppermute | solution.py:119
  67.1 17.3 %collective-permute-start.1 = (bf16[1536,256]{1,0:T(8,128)(2,1)S(1)}, bf16[1536,256]{1,0:T(8,128)(2,1)S(1)}, u32[]{:S(2)}, u32[]{:S(2)}) collective-permute-start(bf16[1536,256]{1,0:T(8,128)(2,1)S(1)} %bitcast.50), channel_id=1, source_target_pairs={{0,6},{1,7},{2,0},{3,1},{4,2},{5,3},{6,4},{7,5},{8,14},{9,15},{10,... | collective-permute-start | bytes 2359304 | tf_op jit(solution)/shard_map/ppermute | solution.py:120
  86.0 20.4 %collective-permute-start.2 = (bf16[1536,768]{1,0:T(8,128)(2,1)}, bf16[1536,768]{1,0:T(8,128)(2,1)}, u32[]{:S(2)}, u32[]{:S(2)}) collective-permute-start(bf16[1536,768]{1,0:T(8,128)(2,1)} %pad_maximum_fusion), channel_id=1, source_target_pairs={{0,1},{1,0},{2,3},{3,2},{4,5},{5,4},{6,7},{7,6},{8,9},{9,8},{10,11... | collective-permute-start | bytes 7077896 | tf_op jit(solution)/shard_map/ppermute | solution.py:125
  91.4 12.0 %collective-permute-start.3 = (bf16[1536,256]{1,0:T(8,128)(2,1)}, bf16[1536,256]{1,0:T(8,128)(2,1)}, u32[]{:S(2)}, u32[]{:S(2)}) collective-permute-start(bf16[1536,256]{1,0:T(8,128)(2,1)} %broadcast_select_fusion), channel_id=1, source_target_pairs={{0,2},{2,4},{4,6},{6,0},{1,7},{3,1},{5,3},{7,5},{8,10},{10,12},{12... | collective-permute-start | bytes 2359304 | tf_op jit(solution)/shard_map/ppermute | solution.py:129
  103.4 6.8 %collective-permute-start.4 = (bf16[1536,256]{1,0:T(8,128)(2,1)}, bf16[1536,256]{1,0:T(8,128)(2,1)S(1)}, u32[]{:S(2)}, u32[]{:S(2)}) collective-permute-start(bf16[1536,256]{1,0:T(8,128)(2,1)} %collective-permute-done.3), channel_id=1, source_target_pairs={{0,1},{1,0},{2,3},{3,2},{4,5},{5,4},{6,7},{7,6},{8,9},{9,8},{10,11... | collective-permute-start | bytes 2359304 | tf_op jit(solution)/shard_map/ppermute | solution.py:130
Sparse Core Ops, SparseCore 0:
  9.0 53.5 all-gather.3

commit v9 on v8

--- a/solution.py
+++ b/solution.py
@@ -52,20 +52,25 @@
     tail = jnp.einsum(
         "c,chde->hde", last_row.astype(jnp.bfloat16), states, preferred_element_type=jnp.float32
     )
-    row_tails = lax.all_gather(tail, "sx", axis=0, tiled=False)
+    col_at = lax.axis_index("sx")
     row_end = (row_at * ROW + ROW - 1) * group_local + group_local - 1
     end_lasts = lax.dynamic_index_in_dim(readers, row_end, 0, False)
     end_lasts = end_lasts.reshape(seq_count, group_local)[:, group_local - 1]
     first_lasts = lax.dynamic_index_in_dim(readers, first_group, 0, False)
     first_lasts = first_lasts.reshape(seq_count, group_local)[:, group_local - 1].astype(jnp.float32)
     in_row = lax.dynamic_slice_in_dim(end_lasts, row_at * ROW, ROW).at[ROW - 1].set(1).astype(jnp.float32)
-    row_sum = (in_row[:, None, None, None] * row_tails).sum(0)
-    row_sums = lax.all_gather(row_sum, "sy", axis=0, tiled=False)
+    from_row = lax.dynamic_slice_in_dim(first_lasts, row_at * ROW, ROW)
     from_rows = first_lasts.reshape(row_count, ROW)[:, ROW - 1]
-    from_row = lax.dynamic_slice_in_dim(first_lasts, row_at * ROW, ROW)
-    entering = (from_row[:, None, None, None] * row_tails).sum(0) + (
-        from_rows[:, None, None, None] * row_sums
-    ).sum(0)
+    row_sum = in_row[col_at] * tail
+    entering = jnp.zeros_like(tail)
+    for step in range(1, ROW):
+        moved = lax.ppermute(tail, "sx", [(i, (i + step) % ROW) for i in range(ROW)])
+        source = (col_at - step) % ROW
+        row_sum = row_sum + in_row[source] * moved
+        entering = entering + from_row[source] * moved
+    for step in range(1, row_count):
+        moved = lax.ppermute(row_sum, "sy", [(i, i + step) for i in range(row_count - step)])
+        entering = entering + from_rows[jnp.maximum(row_at - step, 0)] * moved
     enters = local_readers[:, 0].at[0].set(1).astype(jnp.float32)
     carried_in = enters[:, None, None, None] * entering[None]
     own = jnp.einsum(

time: 120 us -> 127 us (1.058)
  blocking collectives: 24 us -> 0 us
  starting transfers between devices: 12 us -> 27 us
  other arithmetic: 3.9 us -> 15.1 us
  local copies, waits for them, and re-layouts: 10.4 us -> 13.4 us
  waiting for transfers between devices: 20.4 us -> 22.1 us
    all_gather x2 -> x0, blocking collectives: 24 us -> none  [the longest x1 12.2 us: local(): row_tails = lax.all_gather(tail, 'sx', axis=0, tiled=False)]
    ppermute x0 -> x6, starting transfers between devices: none -> 16 us  [the longest x3 10.3 us: local(): lax.ppermute(row_sum, 'sy', [(i, i + step) for i in range(row_count - ste...]
    add x1 -> x2, other arithmetic: 0.02 us -> 9.24 us  [the longest x1 5.09 us: local(): entering = entering + from_rows[jnp.maximum(row_at - step, 0)] * moved]
    dynamic_slice x2 -> x4, local copies, waits for them, and re-layouts: 0.86 us -> 2.6 us  [the longest x1 0.74 us: local(): first_lasts = lax.dynamic_index_in_dim(readers, first_group, 0, False)]
    ppermute x1, starting transfers between devices: 0.08 us -> 1.79 us  [local(): from_below = lax.ppermute(mixed, TP, shifted(1))]
    ppermute x1, starting transfers between devices: 4.38 us -> 2.69 us  [local(): sibling_first = lax.ppermute(first, 'tc', [(0, 1), (1, 0)])]
    ppermute x1, waiting for transfers between devices: 14 us -> 15.7 us  [local(): from_below = lax.ppermute(mixed, TP, shifted(1))]
  transfers between devices with their start and end apart: 6 -> 12, of which waited for: 2 -> 2; matrix products, arithmetic and copies ran while one was open for 38% -> 47% of each run, Pallas kernels for 0% -> 0%
where the time goes in v9:
time: 127 us; the launch traced here: 126 us
  matrix products  34.7 us (27%)
  starting transfers between devices  27 us (21%)
  waiting for transfers between devices  22.1 us (17%)
  other arithmetic  15.1 us (12%)
  between operations  13.6 us (11%)
  local copies, waits for them, and re-layouts  13.4 us (11%)
    ppermute x1, waiting for transfers between devices, local(): from_below = lax.ppermute(mixed, TP, shifted(1))  15.7 us
    ppermute x3, starting transfers between devices, local(): lax.ppermute(row_sum, 'sy', [(i, i + step) for i in range(row_count - ste...  10.3 us
    dot_general x5, matrix products, term(): return jnp.dot(block, rows_of(z, core), preferred_element_type=jnp.float32)  7.55 us
    dot_general x1, matrix products, local(): jnp.dot(tokens, w_query, preferred_element_type=jnp.float32)  5.8 us
    ppermute x3, starting transfers between devices, local(): lax.ppermute(tail, 'sx', [(i, (i + step) % ROW) for i in range(ROW)])  5.7 us
    ppermute x1, waiting for transfers between devices, local(): lax.ppermute(jnp.where(core_at == 0, from_below, from_above), TP, forward)  5.62 us
    add x1, other arithmetic, local(): entering = entering + from_rows[jnp.maximum(row_at - step, 0)] * moved  5.09 us
    dot_general x1, matrix products, local(): jnp.dot(tokens, w_key, preferred_element_type=jnp.float32)  4.84 us
  transfers between devices with their start and end apart: 12, of which 2 were waited for; matrix products, arithmetic and copies ran while one was open for 47% of the time, Pallas kernels for 0%

profile of v9, /device:TPU:1, one launch (start us, length us, event | category | flops | bytes accessed | tf_op | source)
XLA Modules:
  0.0 126.0 jit_solution(17787589433131246925)
XLA Ops:
  6.5 0.7 all-gather.2.cloned.1.call-update
  7.3 0.7 fusion.46
  8.2 0.8 dynamic_slice.82
  8.9 0.7 iota_compare_fusion.1
  9.6 4.6 %fusion.4 = bf16[1536,256]{1,0:T(8,128)(2,1)S(1)} fusion(bf16[1536,2048]{1,0:T(8,128)(2,1)} %param.13, bf16[2048,256]{1,0:T(8,128)(2,1)S(1)} %copy-done, pred[1536]{0:T(1024)(128)(4,1)S(1)} %get-tuple-element.57), kind=kOutput, calls=%fused_computation.9 | convolution fusion | flops 1611399168 | bytes 8128000 | tf_op jit(solution)/shard_map/dot_general | solution.py:39
  14.4 0.6 copy.24
  15.0 4.8 %fusion.3 = bf16[1536,256]{1,0:T(8,128)(2,1)S(1)} fusion(bf16[1536,2048]{1,0:T(8,128)(2,1)} %param.13, bf16[2048,256]{1,0:T(8,128)(2,1)} %param.15, pred[1536]{0:T(1024)(128)(4,1)S(1)} %get-tuple-element.57), kind=kOutput, calls=%fused_computation.8 | convolution fusion | flops 1611399168 | bytes 8128000 | tf_op jit(solution)/shard_map/dot_general | solution.py:36
  20.2 0.8 dynamic-slice_bitcast_fusion
  21.0 0.7 convolution_convert_fusion.1
  22.2 2.1 %collective-permute-start = (f32[2,128,128]{2,1,0:T(8,128)S(1)}, f32[2,128,128]{2,1,0:T(8,128)}, u32[]{:S(2)}, u32[]{:S(2)}) collective-permute-start(f32[2,128,128]{2,1,0:T(8,128)S(1)} %bitcast.64), channel_id=1, source_target_pairs={{0,8},{8,16},{16,24},{24,0},{1,9},{9,17},{17,25},{25,1},{2,10},{10... | collective-permute-start | bytes 393224 | tf_op jit(solution)/shard_map/ppermute | solution.py:67
  24.3 2.4 %collective-permute-start.1 = (f32[2,128,128]{2,1,0:T(8,128)S(1)}, f32[2,128,128]{2,1,0:T(8,128)}, u32[]{:S(2)}, u32[]{:S(2)}) collective-permute-start(f32[2,128,128]{2,1,0:T(8,128)S(1)} %bitcast.65), channel_id=1, source_target_pairs={{0,16},{8,24},{16,0},{24,8},{1,17},{9,25},{17,1},{25,9},{2,18},{10... | collective-permute-start | bytes 393224 | tf_op jit(solution)/shard_map/ppermute | solution.py:67
  26.8 1.2 collective-permute-start.2
  27.9 0.6 convert_element_type.70
  28.5 0.7 convert_element_type.63
  29.3 0.7 fusion.55
  30.0 5.8 %convolution_convert_fusion = bf16[1536,256]{1,0:T(8,128)(2,1)} fusion(bf16[1536,2048]{1,0:T(8,128)(2,1)} %param.13, bf16[2048,256]{1,0:T(8,128)(2,1)} %param.14), kind=kOutput, calls=%fused_computation.10 | convolution fusion | flops 1611005952 | bytes 8126464 | tf_op jit(solution)/shard_map/dot_general | solution.py:41
  35.8 1.4 %fusion.8 = f32[12]{0:T(128)} fusion(f32[192,1]{0,1:T(1,128)S(1)} %bitcast.68, s32[192,192]{1,0:T(8,128)} %param.18, s32[]{:T(128)S(6)} %select_n.125, s32[192]{0:T(256)S(1)} %copy-done.5), kind=kOutput, calls=%fused_computation.20 | convolution fusion | flops 29988 | bytes 18272 | tf_op jit(solution)/shard_map/dot_general | solution.py:96
  37.3 4.2 %multiply_add_fusion.1 = f32[2,128,128]{2,1,0:T(8,128)} fusion(f32[2,128,128]{2,1,0:T(8,128)} %collective-permute-done.2, f32[2,128,128]{2,1,0:T(8,128)} %collective-permute-done.1, f32[2,128,128]{2,1,0:T(8,128)} %collective-permute-done, f32[2,128,128]{2,1,0:T(8,128)S(1)} %bitcast.67, f32[]{:T(128)} %bitcast.13, f32[]{:T(128)} %bitcast.12, f32[]{:T(128)} %bitcast.11, ...), kind=kLoop, calls=%fused_computation.49 | loop fusion | flops 229376 | bytes 655376 | tf_op jit(solution)/shard_map/add | solution.py:69
  41.4 3.2 %collective-permute-start.3 = (f32[2,128,128]{2,1,0:T(8,128)}, f32[2,128,128]{2,1,0:T(8,128)S(1)}, u32[]{:S(2)}, u32[]{:S(2)}) collective-permute-start(f32[2,128,128]{2,1,0:T(8,128)} %multiply_add_fusion.1), channel_id=1, source_target_pairs={{0,32},{32,64},{64,96},{1,33},{33,65},{65,97},{2,34},{34,66},{66,9... | collective-permute-start | bytes 393224 | tf_op jit(solution)/shard_map/ppermute | solution.py:72
  44.6 5.2 %collective-permute-start.4 = (f32[2,128,128]{2,1,0:T(8,128)}, f32[2,128,128]{2,1,0:T(8,128)}, u32[]{:S(2)}, u32[]{:S(2)}) collective-permute-start(f32[2,128,128]{2,1,0:T(8,128)} %multiply_add_fusion.1), channel_id=1, source_target_pairs={{0,64},{32,96},{1,65},{33,97},{2,66},{34,98},{3,67},{35,99},{4,68}... | collective-permute-start | bytes 393224 | tf_op jit(solution)/shard_map/ppermute | solution.py:72
  49.8 1.9 %collective-permute-start.5 = (f32[2,128,128]{2,1,0:T(8,128)}, f32[2,128,128]{2,1,0:T(8,128)}, u32[]{:S(2)}, u32[]{:S(2)}) collective-permute-start(f32[2,128,128]{2,1,0:T(8,128)} %multiply_add_fusion.1), channel_id=1, source_target_pairs={{0,96},{1,97},{2,98},{3,99},{4,100},{5,101},{6,102},{7,103},{8,104... | collective-permute-start | bytes 393224 | tf_op jit(solution)/shard_map/ppermute | solution.py:72
  51.7 0.7 fusion.52
  52.5 0.7 convert_element_type.62
  53.3 0.9 dynamic-slice_reduce_fusion
  54.8 2.7 %reshape.151 = bf16[12,128,2,128]{3,2,1,0:T(2,128)(2,1)} reshape(bf16[1536,256]{1,0:T(8,128)(2,1)} %convolution_convert_fusion) | data formatting | bytes 1572864 | tf_op jit(solution)/shard_map/reshape | solution.py:42
  57.5 0.6 constant_dynamic-slice_fusion.7
  58.1 0.6 constant_dynamic-slice_fusion.4
  58.7 5.1 %multiply_add_fusion = f32[2,128,128]{2,1,0:T(8,128)S(1)} fusion(f32[2,128,128]{2,1,0:T(8,128)} %collective-permute-done.5, f32[2,128,128]{2,1,0:T(8,128)} %collective-permute-done.4, f32[2,128,128]{2,1,0:T(8,128)S(1)} %collective-permute-done.3, f32[2,128,128]{2,1,0:T(8,128)} %collective-permute-done.2, f32[2,128,128]{2,1,0:T(8,128)} %collective-permute-done.1, ...), kind=kLoop, calls=%fused_computation.48 | loop fusion | flops 360448 | bytes 917528 | tf_op jit(solution)/shard_map/add | solution.py:73
  63.8 1.4 %add_convert_fusion = bf16[12,2,128,128]{3,0,2,1:T(8,128)(2,1)S(1)} fusion(f32[2,128,128]{2,1,0:T(8,128)S(1)} %multiply_add_fusion, f32[12]{0:T(128)} %convert_element_type.56, bf16[12,2,128,128]{3,2,1,0:T(8,128)(2,1)S(1)} %convolution_convert_fusion.1, s32[192,192]{1,0:T(8,128)} %param.18, s32[]{:T(128)S(6)} %select_n.126), kind=kOutput, calls=%fused_computation.12 | convolution fusion | flops 10616976 | bytes 1712644 | tf_op jit(solution)/shard_map/ce,ehij->chij/dot_general | solution.py:76
  65.3 1.9 %fusion.13 = f32[12,2,128,128]{3,2,1,0:T(8,128)} fusion(bf16[12,2,128,128]{3,0,2,1:T(8,128)(2,1)S(1)} %add_convert_fusion, bf16[12,128,2,128]{3,2,1,0:T(2,128)(2,1)S(1)} %copy-done.1), kind=kOutput, calls=%fused_computation.26 | convolution fusion | flops 100663296 | bytes 3145728 | tf_op jit(solution)/shard_map/cthd,chde->cthe/dot_general | solution.py:84
  67.2 3.5 %fusion.5 = bf16[12,128,2,128]{1,3,2,0:T(8,128)(2,1)} fusion(f32[12,2,128,128]{3,2,1,0:T(8,128)} %fusion.13, bf16[12,128,2,128]{1,3,2,0:T(8,128)(2,1)S(1)} %copy.24, f32[12]{0:T(128)S(1)} %copy-done.7, pred[128,128]{1,0:T(8,128)(4,1)S(1)} %iota_compare_fusion, pred[12,128]{1,0:T(8,128)(4,1)S(1)} %copy-done.6, bf16[12,128,2,128]{3,2,1,0:T(2,128)(2,1)S(1)} %reshape.148, ...), kind=kOutput, calls=%fused_computation.16 | convolution fusion | flops 203685888 | bytes 4736560 | tf_op jit(solution)/shard_map/chts,cshe->cthe/dot_general | solution.py:92
  70.7 2.3 %copy.25 = bf16[12,128,2,128]{3,2,1,0:T(2,128)(2,1)S(1)} copy(bf16[12,128,2,128]{1,3,2,0:T(8,128)(2,1)} %fusion.5) | data formatting | bytes 1572864 | tf_op jit(solution)/shard_map/convert_element_type | solution.py:101
  73.1 1.8 %collective-permute-start.6 = (bf16[1536,256]{1,0:T(8,128)(2,1)S(1)}, bf16[1536,256]{1,0:T(8,128)(2,1)S(1)}, u32[]{:S(2)}, u32[]{:S(2)}) collective-permute-start(bf16[1536,256]{1,0:T(8,128)(2,1)S(1)} %bitcast.59), channel_id=1, source_target_pairs={{0,2},{1,3},{2,4},{3,5},{4,6},{5,7},{6,0},{7,1},{8,10},{9,11},{10,... | collective-permute-start | bytes 2359304 | tf_op jit(solution)/shard_map/ppermute | solution.py:124
  74.9 2.2 %collective-permute-start.7 = (bf16[1536,256]{1,0:T(8,128)(2,1)S(1)}, bf16[1536,256]{1,0:T(8,128)(2,1)S(1)}, u32[]{:S(2)}, u32[]{:S(2)}) collective-permute-start(bf16[1536,256]{1,0:T(8,128)(2,1)S(1)} %bitcast.60), channel_id=1, source_target_pairs={{0,6},{1,7},{2,0},{3,1},{4,2},{5,3},{6,4},{7,5},{8,14},{9,15},{10,... | collective-permute-start | bytes 2359304 | tf_op jit(solution)/shard_map/ppermute | solution.py:125
  77.1 15.7 %collective-permute-done.6 = bf16[1536,256]{1,0:T(8,128)(2,1)S(1)} collective-permute-done((bf16[1536,256]{1,0:T(8,128)(2,1)S(1)}, bf16[1536,256]{1,0:T(8,128)(2,1)S(1)}, u32[]{:S(2)}, u32[]{:S(2)}) %collective-permute-start.6) | collective-permute-done | bytes 786464 | tf_op jit(solution)/shard_map/ppermute | solution.py:124
  92.9 1.6 %pad_maximum_fusion = bf16[1536,768]{1,0:T(8,128)(2,1)} fusion(bf16[1536,256]{1,0:T(8,128)(2,1)S(1)} %collective-permute-done.7, bf16[1536,256]{1,0:T(8,128)(2,1)S(1)} %collective-permute-done.6, bf16[1536,256]{1,0:T(8,128)(2,1)S(1)} %bitcast.61), kind=kLoop, calls=%fused_computation.11 | loop fusion | flops 7077888 | bytes 4718592 | tf_op jit(solution)/shard_map/concatenate | solution.py:129
  94.5 2.7 %collective-permute-start.8 = (bf16[1536,768]{1,0:T(8,128)(2,1)}, bf16[1536,768]{1,0:T(8,128)(2,1)}, u32[]{:S(2)}, u32[]{:S(2)}) collective-permute-start(bf16[1536,768]{1,0:T(8,128)(2,1)} %pad_maximum_fusion), channel_id=1, source_target_pairs={{0,1},{1,0},{2,3},{3,2},{4,5},{5,4},{6,7},{7,6},{8,9},{9,8},{10,11... | collective-permute-start | bytes 7077896 | tf_op jit(solution)/shard_map/ppermute | solution.py:130
  97.2 1.0 broadcast_select_fusion
  98.1 2.7 %collective-permute-start.9 = (bf16[1536,256]{1,0:T(8,128)(2,1)}, bf16[1536,256]{1,0:T(8,128)(2,1)}, u32[]{:S(2)}, u32[]{:S(2)}) collective-permute-start(bf16[1536,256]{1,0:T(8,128)(2,1)} %broadcast_select_fusion), channel_id=1, source_target_pairs={{0,2},{2,4},{4,6},{6,0},{1,7},{3,1},{5,3},{7,5},{8,10},{10,12},{12... | collective-permute-start | bytes 2359304 | tf_op jit(solution)/shard_map/ppermute | solution.py:134
  100.9 1.1 fusion.54
  102.0 1.3 %fusion.34 = f32[1536,256]{1,0:T(8,128)S(1)} fusion(bf16[1536,256]{1,0:T(8,128)(2,1)S(1)} %bitcast.62, bf16[2048,2048]{1,0:T(8,128)(2,1)} %all-gather.2.cloned.1.call-done, s32[]{:T(128)S(6)} %select_n.144), kind=kOutput, calls=%fused_computation.46 | convolution fusion | flops 201326592 | bytes 2490372 | tf_op jit(solution)/shard_map/dot_general | solution.py:122
  103.2 1.3 %convolution_add_fusion.2 = f32[1536,256]{1,0:T(8,128)S(1)} fusion(f32[1536,256]{1,0:T(8,128)S(1)} %fusion.34, bf16[1536,256]{1,0:T(8,128)(2,1)S(1)} %collective-permute-done.6, bf16[2048,2048]{1,0:T(8,128)(2,1)} %all-gather.2.cloned.1.call-done, s32[]{:T(128)S(6)} %select_n.146, s32[]{:T(128)S(6)} %select_n.144), kind=kOutput, calls=%fused_computation.4 | convolution fusion | flops 201719808 | bytes 4063240 | tf_op jit(solution)/shard_map/dot_general | solution.py:122
  104.5 5.6 %collective-permute-done.9 = bf16[1536,256]{1,0:T(8,128)(2,1)} collective-permute-done((bf16[1536,256]{1,0:T(8,128)(2,1)}, bf16[1536,256]{1,0:T(8,128)(2,1)}, u32[]{:S(2)}, u32[]{:S(2)}) %collective-permute-start.9) | collective-permute-done | bytes 786464 | tf_op jit(solution)/shard_map/ppermute | solution.py:134
  110.1 1.5 %collective-permute-start.10 = (bf16[1536,256]{1,0:T(8,128)(2,1)}, bf16[1536,256]{1,0:T(8,128)(2,1)S(1)}, u32[]{:S(2)}, u32[]{:S(2)}) collective-permute-start(bf16[1536,256]{1,0:T(8,128)(2,1)} %collective-permute-done.9), channel_id=1, source_target_pairs={{0,1},{1,0},{2,3},{3,2},{4,5},{5,4},{6,7},{7,6},{8,9},{9,8},{10,11... | collective-permute-start | bytes 2359304 | tf_op jit(solution)/shard_map/ppermute | solution.py:135
  111.7 1.5 %fusion.30 = f32[1536,256]{1,0:T(8,128)S(1)} fusion(bf16[1536,256]{1,0:T(8,128)(2,1)} %collective-permute-done.9, bf16[2048,2048]{1,0:T(8,128)(2,1)} %all-gather.2.cloned.1.call-done, s32[]{:T(128)S(6)} %select_n.155, s32[]{:T(128)S(6)} %select_n.144), kind=kOutput, calls=%fused_computation.42 | convolution fusion | flops 201326592 | bytes 2490376 | tf_op jit(solution)/shard_map/dot_general | solution.py:122
  113.2 2.5 %fusion.23 = f32[1536,256]{1,0:T(8,128)S(1)} fusion(bf16[1536,768]{1,0:T(8,128)(2,1)} %collective-permute-done.8, bf16[256,256]{1,0:T(8,128)(2,1)S(1)} %get-tuple-element.48, bf16[256,256]{1,0:T(8,128)(2,1)S(1)} %get-tuple-element.49, bf16[256,256]{1,0:T(8,128)(2,1)S(1)} %get-tuple-element.47), kind=kOutput, calls=%fused_computation.35 | convolution fusion | flops 605159424 | bytes 4325376 | tf_op jit(solution)/shard_map/dot_general | solution.py:139
  115.6 1.3 %fusion.1 = f32[1536,256]{1,0:T(8,128)S(1)} fusion(f32[1536,256]{1,0:T(8,128)S(1)} %fusion.30, f32[1536,256]{1,0:T(8,128)S(1)} %fusion.23, f32[1536,256]{1,0:T(8,128)S(1)} %convolution_add_fusion.2, bf16[1536,256]{1,0:T(8,128)(2,1)S(1)} %collective-permute-done.7, bf16[2048,2048]{1,0:T(8,128)(2,1)} %all-gather.2.cloned.1.call-done, s32[]{:T(128)S(6)} %select_n.148, ...), kind=kOutput, calls=%fused_computation.3 | convolution fusion | flops 202506240 | bytes 7208968 | tf_op jit(solution)/shard_map/dot_general | solution.py:122
  117.0 2.2 %fusion.2 = bf16[1536,256]{1,0:T(8,128)(2,1)} fusion(f32[1536,256]{1,0:T(8,128)S(1)} %fusion.1, bf16[1536,256]{1,0:T(8,128)(2,1)S(1)} %collective-permute-done.10, bf16[2048,2048]{1,0:T(8,128)(2,1)} %all-gather.2.cloned.1.call-done, s32[]{:T(128)S(6)} %select_n.156, s32[]{:T(128)S(6)} %select_n.144), kind=kOutput, calls=%fused_computation.7 | convolution fusion | flops 202113024 | bytes 3276808 | tf_op jit(solution)/shard_map/dot_general | solution.py:122
  (43 shorter events, 2.2 us)
Async XLA Ops:
  6.5 3.1 %copy-start = (bf16[2048,256]{1,0:T(8,128)(2,1)S(1)}, bf16[2048,256]{1,0:T(8,128)(2,1)}, u32[]{:S(2)}) copy-start(bf16[2048,256]{1,0:T(8,128)(2,1)} %param.16) | copy-start | bytes 3145732
  6.5 66.6 %all-gather.2.cloned.1.call-start = ((), (), s32[]{:S(2)}) async-start(), calls=%async_computation | async-start | bytes 9437184 | tf_op jit(solution)/shard_map/all_gather | solution.py:29
  20.1 7.9 %copy-start.4 = (s32[192]{0:T(256)S(1)}, s32[192]{0:T(256)}, u32[]{:S(2)}) copy-start(s32[192]{0:T(256)} %param.19) | copy-start | bytes 2308
  21.0 7.5 %copy-start.8 = (s32[4]{0:T(128)}, s32[4]{0:T(128)S(1)}, u32[]{:S(2)}) copy-start(s32[4]{0:T(128)S(1)} %get-tuple-element.63) | copy-start | bytes 52
  22.2 15.0 %collective-permute-start = (f32[2,128,128]{2,1,0:T(8,128)S(1)}, f32[2,128,128]{2,1,0:T(8,128)}, u32[]{:S(2)}, u32[]{:S(2)}) collective-permute-start(f32[2,128,128]{2,1,0:T(8,128)S(1)} %bitcast.64), channel_id=1, source_target_pairs={{0,8},{8,16},{16,24},{24,0},{1,9},{9,17},{17,25},{25,1},{2,10},{10... | collective-permute-start | bytes 393224 | tf_op jit(solution)/shard_map/ppermute | solution.py:67
  24.3 12.9 %collective-permute-start.1 = (f32[2,128,128]{2,1,0:T(8,128)S(1)}, f32[2,128,128]{2,1,0:T(8,128)}, u32[]{:S(2)}, u32[]{:S(2)}) collective-permute-start(f32[2,128,128]{2,1,0:T(8,128)S(1)} %bitcast.65), channel_id=1, source_target_pairs={{0,16},{8,24},{16,0},{24,8},{1,17},{9,25},{17,1},{25,9},{2,18},{10... | collective-permute-start | bytes 393224 | tf_op jit(solution)/shard_map/ppermute | solution.py:67
  26.8 10.5 %collective-permute-start.2 = (f32[2,128,128]{2,1,0:T(8,128)S(1)}, f32[2,128,128]{2,1,0:T(8,128)}, u32[]{:S(2)}, u32[]{:S(2)}) collective-permute-start(f32[2,128,128]{2,1,0:T(8,128)S(1)} %bitcast.66), channel_id=1, source_target_pairs={{0,24},{8,0},{16,8},{24,16},{1,25},{9,1},{17,9},{25,17},{2,26},{10... | collective-permute-start | bytes 393224 | tf_op jit(solution)/shard_map/ppermute | solution.py:67
  30.0 5.8 %copy-start.3 = (f32[192]{0:T(256)S(1)}, f32[192]{0:T(256)}, u32[]{:S(2)}) copy-start(f32[192]{0:T(256)} %convert_element_type.70) | copy-start | bytes 2308
  30.0 5.8 %copy-start.5 = (s32[192]{0:T(256)S(1)}, s32[192]{0:T(256)}, u32[]{:S(2)}) copy-start(s32[192]{0:T(256)} %param.19) | copy-start | bytes 2308
  41.4 17.3 %collective-permute-start.3 = (f32[2,128,128]{2,1,0:T(8,128)}, f32[2,128,128]{2,1,0:T(8,128)S(1)}, u32[]{:S(2)}, u32[]{:S(2)}) collective-permute-start(f32[2,128,128]{2,1,0:T(8,128)} %multiply_add_fusion.1), channel_id=1, source_target_pairs={{0,32},{32,64},{64,96},{1,33},{33,65},{65,97},{2,34},{34,66},{66,9... | collective-permute-start | bytes 393224 | tf_op jit(solution)/shard_map/ppermute | solution.py:72
  44.6 14.1 %collective-permute-start.4 = (f32[2,128,128]{2,1,0:T(8,128)}, f32[2,128,128]{2,1,0:T(8,128)}, u32[]{:S(2)}, u32[]{:S(2)}) collective-permute-start(f32[2,128,128]{2,1,0:T(8,128)} %multiply_add_fusion.1), channel_id=1, source_target_pairs={{0,64},{32,96},{1,65},{33,97},{2,66},{34,98},{3,67},{35,99},{4,68}... | collective-permute-start | bytes 393224 | tf_op jit(solution)/shard_map/ppermute | solution.py:72
  49.8 8.9 %collective-permute-start.5 = (f32[2,128,128]{2,1,0:T(8,128)}, f32[2,128,128]{2,1,0:T(8,128)}, u32[]{:S(2)}, u32[]{:S(2)}) collective-permute-start(f32[2,128,128]{2,1,0:T(8,128)} %multiply_add_fusion.1), channel_id=1, source_target_pairs={{0,96},{1,97},{2,98},{3,99},{4,100},{5,101},{6,102},{7,103},{8,104... | collective-permute-start | bytes 393224 | tf_op jit(solution)/shard_map/ppermute | solution.py:72
  57.5 7.8 %copy-start.1 = (bf16[12,128,2,128]{3,2,1,0:T(2,128)(2,1)S(1)}, bf16[12,128,2,128]{3,2,1,0:T(2,128)(2,1)}, u32[]{:S(2)}) copy-start(bf16[12,128,2,128]{3,2,1,0:T(2,128)(2,1)} %reshape.151) | copy-start | bytes 2359300
  65.3 1.9 %copy-start.2 = (bf16[12,128,2,128]{3,2,1,0:T(2,128)(2,1)S(1)}, bf16[12,128,2,128]{3,2,1,0:T(2,128)(2,1)}, u32[]{:S(2)}) copy-start(bf16[12,128,2,128]{3,2,1,0:T(2,128)(2,1)} %reshape.151) | copy-start | bytes 2359300
  65.3 1.9 %copy-start.6 = (pred[12,128]{1,0:T(8,128)(4,1)S(1)}, pred[12,128]{1,0:T(8,128)(4,1)}, u32[]{:S(2)}) copy-start(pred[12,128]{1,0:T(8,128)(4,1)} %get-tuple-element.56) | copy-start | bytes 4612
  65.3 1.9 %copy-start.7 = (f32[12]{0:T(128)S(1)}, f32[12]{0:T(128)}, u32[]{:S(2)}) copy-start(f32[12]{0:T(128)} %fusion.8) | copy-start | bytes 148
  73.1 19.7 %collective-permute-start.6 = (bf16[1536,256]{1,0:T(8,128)(2,1)S(1)}, bf16[1536,256]{1,0:T(8,128)(2,1)S(1)}, u32[]{:S(2)}, u32[]{:S(2)}) collective-permute-start(bf16[1536,256]{1,0:T(8,128)(2,1)S(1)} %bitcast.59), channel_id=1, source_target_pairs={{0,2},{1,3},{2,4},{3,5},{4,6},{5,7},{6,0},{7,1},{8,10},{9,11},{10,... | collective-permute-start | bytes 2359304 | tf_op jit(solution)/shard_map/ppermute | solution.py:124
  74.9 17.9 %collective-permute-start.7 = (bf16[1536,256]{1,0:T(8,128)(2,1)S(1)}, bf16[1536,256]{1,0:T(8,128)(2,1)S(1)}, u32[]{:S(2)}, u32[]{:S(2)}) collective-permute-start(bf16[1536,256]{1,0:T(8,128)(2,1)S(1)} %bitcast.60), channel_id=1, source_target_pairs={{0,6},{1,7},{2,0},{3,1},{4,2},{5,3},{6,4},{7,5},{8,14},{9,15},{10,... | collective-permute-start | bytes 2359304 | tf_op jit(solution)/shard_map/ppermute | solution.py:125
  94.5 18.7 %collective-permute-start.8 = (bf16[1536,768]{1,0:T(8,128)(2,1)}, bf16[1536,768]{1,0:T(8,128)(2,1)}, u32[]{:S(2)}, u32[]{:S(2)}) collective-permute-start(bf16[1536,768]{1,0:T(8,128)(2,1)} %pad_maximum_fusion), channel_id=1, source_target_pairs={{0,1},{1,0},{2,3},{3,2},{4,5},{5,4},{6,7},{7,6},{8,9},{9,8},{10,11... | collective-permute-start | bytes 7077896 | tf_op jit(solution)/shard_map/ppermute | solution.py:130
  98.1 12.0 %collective-permute-start.9 = (bf16[1536,256]{1,0:T(8,128)(2,1)}, bf16[1536,256]{1,0:T(8,128)(2,1)}, u32[]{:S(2)}, u32[]{:S(2)}) collective-permute-start(bf16[1536,256]{1,0:T(8,128)(2,1)} %broadcast_select_fusion), channel_id=1, source_target_pairs={{0,2},{2,4},{4,6},{6,0},{1,7},{3,1},{5,3},{7,5},{8,10},{10,12},{12... | collective-permute-start | bytes 2359304 | tf_op jit(solution)/shard_map/ppermute | solution.py:134
  110.1 6.8 %collective-permute-start.10 = (bf16[1536,256]{1,0:T(8,128)(2,1)}, bf16[1536,256]{1,0:T(8,128)(2,1)S(1)}, u32[]{:S(2)}, u32[]{:S(2)}) collective-permute-start(bf16[1536,256]{1,0:T(8,128)(2,1)} %collective-permute-done.9), channel_id=1, source_target_pairs={{0,1},{1,0},{2,3},{3,2},{4,5},{5,4},{6,7},{7,6},{8,9},{9,8},{10,11... | collective-permute-start | bytes 2359304 | tf_op jit(solution)/shard_map/ppermute | solution.py:135
Sparse Core Ops, SparseCore 0:
  9.0 53.4 all-gather.1

commit v10 on v8

--- a/solution.py
+++ b/solution.py
@@ -52,7 +52,7 @@
     tail = jnp.einsum(
         "c,chde->hde", last_row.astype(jnp.bfloat16), states, preferred_element_type=jnp.float32
     )
-    row_tails = lax.all_gather(tail, "sx", axis=0, tiled=False)
+    row_tails = lax.all_gather(tail.astype(jnp.bfloat16), "sx", axis=0, tiled=False).astype(jnp.float32)
     row_end = (row_at * ROW + ROW - 1) * group_local + group_local - 1
     end_lasts = lax.dynamic_index_in_dim(readers, row_end, 0, False)
     end_lasts = end_lasts.reshape(seq_count, group_local)[:, group_local - 1]
@@ -60,7 +60,7 @@
     first_lasts = first_lasts.reshape(seq_count, group_local)[:, group_local - 1].astype(jnp.float32)
     in_row = lax.dynamic_slice_in_dim(end_lasts, row_at * ROW, ROW).at[ROW - 1].set(1).astype(jnp.float32)
     row_sum = (in_row[:, None, None, None] * row_tails).sum(0)
-    row_sums = lax.all_gather(row_sum, "sy", axis=0, tiled=False)
+    row_sums = lax.all_gather(row_sum.astype(jnp.bfloat16), "sy", axis=0, tiled=False).astype(jnp.float32)
     from_rows = first_lasts.reshape(row_count, ROW)[:, ROW - 1]
     from_row = lax.dynamic_slice_in_dim(first_lasts, row_at * ROW, ROW)
     entering = (from_row[:, None, None, None] * row_tails).sum(0) + (

time: 120 us -> 120 us (level)
  blocking collectives: 24 us -> 22.7 us
    all_gather x2, blocking collectives: 24 us -> 22.7 us  [the longest x1 11.7 us: local(): lax.all_gather(tail.astype(jnp.bfloat16), 'sx', axis=0, tiled=False)]
  transfers between devices with their start and end apart: 6 -> 6, of which waited for: 2 -> 2; matrix products, arithmetic and copies ran while one was open for 38% -> 39% of each run, Pallas kernels for 0% -> 0%
where the time goes in v10:
time: 120 us; the launch traced here: 119 us
  matrix products  34.4 us (29%)
  blocking collectives  22.7 us (19%)
  waiting for transfers between devices  20.2 us (17%)
  between operations  13.6 us (11%)
  starting transfers between devices  12.7 us (11%)
  local copies, waits for them, and re-layouts  11.2 us (9%)
  other arithmetic  3.96 us (3%)
    ppermute x1, waiting for transfers between devices, local(): from_below = lax.ppermute(mixed, TP, shifted(1))  13.8 us
    all_gather x1, blocking collectives, local(): lax.all_gather(tail.astype(jnp.bfloat16), 'sx', axis=0, tiled=False)  11.7 us
    all_gather x1, blocking collectives, local(): lax.all_gather(row_sum.astype(jnp.bfloat16), 'sy', axis=0, tiled=False)  11.1 us
    dot_general x5, matrix products, term(): return jnp.dot(block, rows_of(z, core), preferred_element_type=jnp.float32)  7.53 us
    dot_general x1, matrix products, local(): jnp.dot(tokens, w_query, preferred_element_type=jnp.float32)  5.96 us
    ppermute x1, waiting for transfers between devices, local(): lax.ppermute(jnp.where(core_at == 0, from_below, from_above), TP, forward)  5.63 us
    dot_general x1, matrix products, local(): jnp.dot(tokens, w_key, preferred_element_type=jnp.float32)  4.84 us
    ppermute x1, starting transfers between devices, local(): sibling_first = lax.ppermute(first, 'tc', [(0, 1), (1, 0)])  4.59 us
  transfers between devices with their start and end apart: 6, of which 2 were waited for; matrix products, arithmetic and copies ran while one was open for 39% of the time, Pallas kernels for 0%

profile of v10, /device:TPU:1, one launch (start us, length us, event | category | flops | bytes accessed | tf_op | source)
XLA Modules:
  0.0 118.9 jit_solution(9254667863115951628)
XLA Ops:
  6.5 0.7 all-gather.4.cloned.1.call-update
  7.3 0.7 convert_element_type.97
  8.0 0.8 dynamic_slice.50
  8.7 0.1 iota_compare_fusion.1
  8.8 4.6 %fusion.4 = bf16[1536,256]{1,0:T(8,128)(2,1)S(1)} fusion(bf16[1536,2048]{1,0:T(8,128)(2,1)} %param.13, bf16[2048,256]{1,0:T(8,128)(2,1)S(1)} %copy-done, pred[1536]{0:T(1024)(128)(4,1)S(1)} %get-tuple-element.53), kind=kOutput, calls=%fused_computation.9 | convolution fusion | flops 1611399168 | bytes 8128000 | tf_op jit(solution)/shard_map/dot_general | solution.py:39
  13.4 0.2 reshape.153
  13.6 0.6 copy.33
  14.2 4.8 %fusion.3 = bf16[1536,256]{1,0:T(8,128)(2,1)S(1)} fusion(bf16[1536,2048]{1,0:T(8,128)(2,1)} %param.13, bf16[2048,256]{1,0:T(8,128)(2,1)} %param.15, pred[1536]{0:T(1024)(128)(4,1)S(1)} %get-tuple-element.53), kind=kOutput, calls=%fused_computation.8 | convolution fusion | flops 1611399168 | bytes 8128000 | tf_op jit(solution)/shard_map/dot_general | solution.py:36
  19.1 0.2 reshape.152
  19.3 0.8 dynamic-slice_bitcast_fusion
  20.1 0.7 convolution_convert_fusion.1
  20.7 0.5 fusion.9
  21.3 0.7 fusion.44
  22.1 0.1 reshape.151
  22.1 0.1 reshape.154
  22.4 0.1 dynamic-slice_reduce_fusion.2
  22.5 0.1 dynamic-slice_reduce_fusion.1
  22.7 0.2 fusion.49
  22.8 0.1 convert_element_type.86
  22.9 0.9 dynamic-slice_reduce_fusion
  23.9 6.0 %convolution_convert_fusion = bf16[1536,256]{1,0:T(8,128)(2,1)} fusion(bf16[1536,2048]{1,0:T(8,128)(2,1)} %param.13, bf16[2048,256]{1,0:T(8,128)(2,1)} %param.14), kind=kOutput, calls=%fused_computation.10 | convolution fusion | flops 1611005952 | bytes 8126464 | tf_op jit(solution)/shard_map/dot_general | solution.py:41
  29.8 2.8 %reshape.155 = bf16[12,128,2,128]{3,2,1,0:T(2,128)(2,1)} reshape(bf16[1536,256]{1,0:T(8,128)(2,1)} %convolution_convert_fusion) | data formatting | bytes 1572864 | tf_op jit(solution)/shard_map/reshape | solution.py:42
  32.6 11.7 %all-gather = bf16[8,128,128]{2,1,0:T(8,128)(2,1)S(1)} all-gather(bf16[2,128,128]{2,1,0:T(8,128)(2,1)S(1)} %convert_element_type.84), channel_id=2, replica_groups=mesh['sy'=4,'sx'=4,'tz'=4,'tc'=2] {'sx'}, dimensions={0}, use_global_device_ids=true | all-gather | bytes 327680 | tf_op jit(solution)/shard_map/all_gather | solution.py:55
  44.3 0.2 fusion.23
  44.5 11.1 %all-gather.1 = bf16[8,128,128]{2,1,0:T(8,128)(2,1)S(1)} all-gather(bf16[2,128,128]{2,1,0:T(8,128)(2,1)S(1)} %get-tuple-element.45), channel_id=3, replica_groups=mesh['sy'=4,'sx'=4,'tz'=4,'tc'=2] {'sy'}, dimensions={0}, use_global_device_ids=true | all-gather | bytes 327680 | tf_op jit(solution)/shard_map/all_gather | solution.py:63
  55.5 0.2 slice_reduce_fusion
  55.7 0.1 fusion.24
  55.9 0.9 fusion.8
  56.8 1.4 %add_convert_fusion = bf16[12,2,128,128]{3,0,2,1:T(8,128)(2,1)S(1)} fusion(bf16[12,2,128,128]{3,2,1,0:T(8,128)(2,1)S(1)} %convolution_convert_fusion.1, f32[2,128,128]{2,1,0:T(8,128)S(1)} %add.148, f32[12]{0:T(128)S(1)} %convert_element_type.78, s32[192,192]{1,0:T(8,128)} %param.18, s32[]{:T(128)S(6)} %select_n.88), kind=kOutput, calls=%fused_computation.12 | convolution fusion | flops 10616976 | bytes 1712180 | tf_op jit(solution)/shard_map/ce,ehij->chij/dot_general | solution.py:71
  58.2 1.9 %fusion.12 = f32[12,2,128,128]{3,2,1,0:T(8,128)} fusion(bf16[12,2,128,128]{3,0,2,1:T(8,128)(2,1)S(1)} %add_convert_fusion, bf16[12,128,2,128]{3,2,1,0:T(2,128)(2,1)S(1)} %copy-done.1), kind=kOutput, calls=%fused_computation.25 | convolution fusion | flops 100663296 | bytes 3145728 | tf_op jit(solution)/shard_map/cthd,chde->cthe/dot_general | solution.py:79
  60.2 3.6 %fusion.5 = bf16[12,128,2,128]{1,3,2,0:T(8,128)(2,1)} fusion(f32[12,2,128,128]{3,2,1,0:T(8,128)} %fusion.12, bf16[12,128,2,128]{1,3,2,0:T(8,128)(2,1)S(1)} %copy.33, f32[12]{0:T(128)S(1)} %fusion.8, pred[128,128]{1,0:T(8,128)(4,1)S(1)} %iota_compare_fusion, pred[12,128]{1,0:T(8,128)(4,1)S(1)} %get-tuple-element.52, ...), kind=kOutput, calls=%fused_computation.16 | convolution fusion | flops 203685888 | bytes 4736560 | tf_op jit(solution)/shard_map/chts,cshe->cthe/dot_general | solution.py:87
  63.8 2.3 %copy.34 = bf16[12,128,2,128]{3,2,1,0:T(2,128)(2,1)S(1)} copy(bf16[12,128,2,128]{1,3,2,0:T(8,128)(2,1)} %fusion.5) | data formatting | bytes 1572864 | tf_op jit(solution)/shard_map/convert_element_type | solution.py:96
  66.0 0.1 copy.56
  66.2 3.8 %collective-permute-start.1 = (bf16[1536,256]{1,0:T(8,128)(2,1)S(1)}, bf16[1536,256]{1,0:T(8,128)(2,1)S(1)}, u32[]{:S(2)}, u32[]{:S(2)}) collective-permute-start(bf16[1536,256]{1,0:T(8,128)(2,1)S(1)} %bitcast.52), channel_id=1, source_target_pairs={{0,6},{1,7},{2,0},{3,1},{4,2},{5,3},{6,4},{7,5},{8,14},{9,15},{10,... | collective-permute-start | bytes 2359304 | tf_op jit(solution)/shard_map/ppermute | solution.py:120
  70.0 13.8 %collective-permute-done = bf16[1536,256]{1,0:T(8,128)(2,1)S(1)} collective-permute-done((bf16[1536,256]{1,0:T(8,128)(2,1)S(1)}, bf16[1536,256]{1,0:T(8,128)(2,1)S(1)}, u32[]{:S(2)}, u32[]{:S(2)}) %collective-permute-start) | collective-permute-done | bytes 786464 | tf_op jit(solution)/shard_map/ppermute | solution.py:119
  83.9 1.6 %pad_maximum_fusion = bf16[1536,768]{1,0:T(8,128)(2,1)} fusion(bf16[1536,256]{1,0:T(8,128)(2,1)S(1)} %collective-permute-done.1, bf16[1536,256]{1,0:T(8,128)(2,1)S(1)} %collective-permute-done, bf16[1536,256]{1,0:T(8,128)(2,1)S(1)} %bitcast.53), kind=kLoop, calls=%fused_computation.11 | loop fusion | flops 7077888 | bytes 4718592 | tf_op jit(solution)/shard_map/concatenate | solution.py:124
  85.5 4.6 %collective-permute-start.2 = (bf16[1536,768]{1,0:T(8,128)(2,1)}, bf16[1536,768]{1,0:T(8,128)(2,1)}, u32[]{:S(2)}, u32[]{:S(2)}) collective-permute-start(bf16[1536,768]{1,0:T(8,128)(2,1)} %pad_maximum_fusion), channel_id=1, source_target_pairs={{0,1},{1,0},{2,3},{3,2},{4,5},{5,4},{6,7},{7,6},{8,9},{9,8},{10,11... | collective-permute-start | bytes 7077896 | tf_op jit(solution)/shard_map/ppermute | solution.py:125
  90.1 1.0 broadcast_select_fusion
  91.0 2.7 %collective-permute-start.3 = (bf16[1536,256]{1,0:T(8,128)(2,1)}, bf16[1536,256]{1,0:T(8,128)(2,1)}, u32[]{:S(2)}, u32[]{:S(2)}) collective-permute-start(bf16[1536,256]{1,0:T(8,128)(2,1)} %broadcast_select_fusion), channel_id=1, source_target_pairs={{0,2},{2,4},{4,6},{6,0},{1,7},{3,1},{5,3},{7,5},{8,10},{10,12},{12... | collective-permute-start | bytes 2359304 | tf_op jit(solution)/shard_map/ppermute | solution.py:129
  93.8 1.1 fusion.51
  94.9 1.3 %fusion.36 = f32[1536,256]{1,0:T(8,128)S(1)} fusion(bf16[1536,256]{1,0:T(8,128)(2,1)S(1)} %bitcast.54, bf16[2048,2048]{1,0:T(8,128)(2,1)} %all-gather.4.cloned.1.call-done, s32[]{:T(128)S(6)} %select_n.95), kind=kOutput, calls=%fused_computation.51 | convolution fusion | flops 201326592 | bytes 2490372 | tf_op jit(solution)/shard_map/dot_general | solution.py:117
  96.1 1.3 %convolution_add_fusion.2 = f32[1536,256]{1,0:T(8,128)S(1)} fusion(f32[1536,256]{1,0:T(8,128)S(1)} %fusion.36, bf16[1536,256]{1,0:T(8,128)(2,1)S(1)} %collective-permute-done, bf16[2048,2048]{1,0:T(8,128)(2,1)} %all-gather.4.cloned.1.call-done, s32[]{:T(128)S(6)} %select_n.97, s32[]{:T(128)S(6)} %select_n.95), kind=kOutput, calls=%fused_computation.4 | convolution fusion | flops 201719808 | bytes 4063240 | tf_op jit(solution)/shard_map/dot_general | solution.py:117
  97.4 5.6 %collective-permute-done.3 = bf16[1536,256]{1,0:T(8,128)(2,1)} collective-permute-done((bf16[1536,256]{1,0:T(8,128)(2,1)}, bf16[1536,256]{1,0:T(8,128)(2,1)}, u32[]{:S(2)}, u32[]{:S(2)}) %collective-permute-start.3) | collective-permute-done | bytes 786464 | tf_op jit(solution)/shard_map/ppermute | solution.py:129
  103.0 1.5 %collective-permute-start.4 = (bf16[1536,256]{1,0:T(8,128)(2,1)}, bf16[1536,256]{1,0:T(8,128)(2,1)S(1)}, u32[]{:S(2)}, u32[]{:S(2)}) collective-permute-start(bf16[1536,256]{1,0:T(8,128)(2,1)} %collective-permute-done.3), channel_id=1, source_target_pairs={{0,1},{1,0},{2,3},{3,2},{4,5},{5,4},{6,7},{7,6},{8,9},{9,8},{10,11... | collective-permute-start | bytes 2359304 | tf_op jit(solution)/shard_map/ppermute | solution.py:130
  104.6 1.5 %fusion.32 = f32[1536,256]{1,0:T(8,128)S(1)} fusion(bf16[1536,256]{1,0:T(8,128)(2,1)} %collective-permute-done.3, bf16[2048,2048]{1,0:T(8,128)(2,1)} %all-gather.4.cloned.1.call-done, s32[]{:T(128)S(6)} %select_n.106, s32[]{:T(128)S(6)} %select_n.95), kind=kOutput, calls=%fused_computation.47 | convolution fusion | flops 201326592 | bytes 2490376 | tf_op jit(solution)/shard_map/dot_general | solution.py:117
  106.1 2.5 %fusion.25 = f32[1536,256]{1,0:T(8,128)S(1)} fusion(bf16[1536,768]{1,0:T(8,128)(2,1)} %collective-permute-done.2, bf16[256,256]{1,0:T(8,128)(2,1)S(1)} %get-tuple-element.50, bf16[256,256]{1,0:T(8,128)(2,1)S(1)} %get-tuple-element.51, bf16[256,256]{1,0:T(8,128)(2,1)S(1)} %get-tuple-element.49), kind=kOutput, calls=%fused_computation.40 | convolution fusion | flops 605159424 | bytes 4325376 | tf_op jit(solution)/shard_map/dot_general | solution.py:134
  108.5 1.3 %fusion.1 = f32[1536,256]{1,0:T(8,128)S(1)} fusion(f32[1536,256]{1,0:T(8,128)S(1)} %fusion.32, f32[1536,256]{1,0:T(8,128)S(1)} %fusion.25, f32[1536,256]{1,0:T(8,128)S(1)} %convolution_add_fusion.2, bf16[1536,256]{1,0:T(8,128)(2,1)S(1)} %collective-permute-done.1, bf16[2048,2048]{1,0:T(8,128)(2,1)} %all-gather.4.cloned.1.call-done, s32[]{:T(128)S(6)} %select_n.99, ...), kind=kOutput, calls=%fused_computation.3 | convolution fusion | flops 202506240 | bytes 7208968 | tf_op jit(solution)/shard_map/dot_general | solution.py:117
  109.9 2.2 %fusion.2 = bf16[1536,256]{1,0:T(8,128)(2,1)} fusion(f32[1536,256]{1,0:T(8,128)S(1)} %fusion.1, bf16[1536,256]{1,0:T(8,128)(2,1)S(1)} %collective-permute-done.4, bf16[2048,2048]{1,0:T(8,128)(2,1)} %all-gather.4.cloned.1.call-done, s32[]{:T(128)S(6)} %select_n.107, s32[]{:T(128)S(6)} %select_n.95), kind=kOutput, calls=%fused_computation.7 | convolution fusion | flops 202113024 | bytes 3276808 | tf_op jit(solution)/shard_map/dot_general | solution.py:117
  (24 shorter events, 0.4 us)
Async XLA Ops:
  6.5 2.2 %copy-start = (bf16[2048,256]{1,0:T(8,128)(2,1)S(1)}, bf16[2048,256]{1,0:T(8,128)(2,1)}, u32[]{:S(2)}) copy-start(bf16[2048,256]{1,0:T(8,128)(2,1)} %param.16) | copy-start | bytes 3145732
  6.5 59.6 %all-gather.4.cloned.1.call-start = ((), (), s32[]{:S(2)}) async-start(), calls=%async_computation | async-start | bytes 9437184 | tf_op jit(solution)/shard_map/all_gather | solution.py:29
  29.8 26.1 %copy-start.3 = (s32[192]{0:T(256)S(1)}, s32[192]{0:T(256)}, u32[]{:S(2)}) copy-start(s32[192]{0:T(256)} %param.19) | copy-start | bytes 2308
  32.6 25.6 %copy-start.1 = (bf16[12,128,2,128]{3,2,1,0:T(2,128)(2,1)S(1)}, bf16[12,128,2,128]{3,2,1,0:T(2,128)(2,1)}, u32[]{:S(2)}) copy-start(bf16[12,128,2,128]{3,2,1,0:T(2,128)(2,1)} %reshape.155) | copy-start | bytes 2359300
  58.2 2.0 %copy-start.2 = (bf16[12,128,2,128]{3,2,1,0:T(2,128)(2,1)S(1)}, bf16[12,128,2,128]{3,2,1,0:T(2,128)(2,1)}, u32[]{:S(2)}) copy-start(bf16[12,128,2,128]{3,2,1,0:T(2,128)(2,1)} %reshape.155) | copy-start | bytes 2359300
  66.2 17.7 %collective-permute-start = (bf16[1536,256]{1,0:T(8,128)(2,1)S(1)}, bf16[1536,256]{1,0:T(8,128)(2,1)S(1)}, u32[]{:S(2)}, u32[]{:S(2)}) collective-permute-start(bf16[1536,256]{1,0:T(8,128)(2,1)S(1)} %bitcast.51), channel_id=1, source_target_pairs={{0,2},{1,3},{2,4},{3,5},{4,6},{5,7},{6,0},{7,1},{8,10},{9,11},{10,... | collective-permute-start | bytes 2359304 | tf_op jit(solution)/shard_map/ppermute | solution.py:119
  66.2 17.6 %collective-permute-start.1 = (bf16[1536,256]{1,0:T(8,128)(2,1)S(1)}, bf16[1536,256]{1,0:T(8,128)(2,1)S(1)}, u32[]{:S(2)}, u32[]{:S(2)}) collective-permute-start(bf16[1536,256]{1,0:T(8,128)(2,1)S(1)} %bitcast.52), channel_id=1, source_target_pairs={{0,6},{1,7},{2,0},{3,1},{4,2},{5,3},{6,4},{7,5},{8,14},{9,15},{10,... | collective-permute-start | bytes 2359304 | tf_op jit(solution)/shard_map/ppermute | solution.py:120
  85.5 20.6 %collective-permute-start.2 = (bf16[1536,768]{1,0:T(8,128)(2,1)}, bf16[1536,768]{1,0:T(8,128)(2,1)}, u32[]{:S(2)}, u32[]{:S(2)}) collective-permute-start(bf16[1536,768]{1,0:T(8,128)(2,1)} %pad_maximum_fusion), channel_id=1, source_target_pairs={{0,1},{1,0},{2,3},{3,2},{4,5},{5,4},{6,7},{7,6},{8,9},{9,8},{10,11... | collective-permute-start | bytes 7077896 | tf_op jit(solution)/shard_map/ppermute | solution.py:125
  91.0 12.0 %collective-permute-start.3 = (bf16[1536,256]{1,0:T(8,128)(2,1)}, bf16[1536,256]{1,0:T(8,128)(2,1)}, u32[]{:S(2)}, u32[]{:S(2)}) collective-permute-start(bf16[1536,256]{1,0:T(8,128)(2,1)} %broadcast_select_fusion), channel_id=1, source_target_pairs={{0,2},{2,4},{4,6},{6,0},{1,7},{3,1},{5,3},{7,5},{8,10},{10,12},{12... | collective-permute-start | bytes 2359304 | tf_op jit(solution)/shard_map/ppermute | solution.py:129
  103.0 6.8 %collective-permute-start.4 = (bf16[1536,256]{1,0:T(8,128)(2,1)}, bf16[1536,256]{1,0:T(8,128)(2,1)S(1)}, u32[]{:S(2)}, u32[]{:S(2)}) collective-permute-start(bf16[1536,256]{1,0:T(8,128)(2,1)} %collective-permute-done.3), channel_id=1, source_target_pairs={{0,1},{1,0},{2,3},{3,2},{4,5},{5,4},{6,7},{7,6},{8,9},{9,8},{10,11... | collective-permute-start | bytes 2359304 | tf_op jit(solution)/shard_map/ppermute | solution.py:130
Sparse Core Ops, SparseCore 0:
  9.0 53.4 all-gather.3

commit v11 on v8

--- a/solution.py
+++ b/solution.py
@@ -38,8 +38,6 @@
     value_rows = jnp.where(
         live_mask, jnp.dot(tokens, w_value, preferred_element_type=jnp.float32), 0.0
     ).astype(jnp.bfloat16)
-    query_rows = jnp.dot(tokens, w_query, preferred_element_type=jnp.float32).astype(jnp.bfloat16)
-    query_blocks = query_rows.reshape(group_local, CH, head_dev, HS)
     key_blocks = key_rows.reshape(group_local, CH, head_dev, HS)
     value_blocks = value_rows.reshape(group_local, CH, head_dev, HS)
 
@@ -76,30 +74,40 @@
     )
     prefix = (carried_in + own).astype(jnp.bfloat16)
 
-    carried = jnp.einsum(
-        "cthd,chde->cthe", query_blocks, prefix, preferred_element_type=jnp.float32
-    )
-    scores = jnp.einsum(
-        "cthd,cshd->chts", query_blocks, key_blocks, preferred_element_type=jnp.float32
-    )
-    causal = offsets[:, None] >= offsets[None, :]
-    weights = jnp.where(causal[None, None], scores, 0.0).astype(jnp.bfloat16)
-    within = jnp.einsum(
-        "chts,cshe->cthe", weights, value_blocks, preferred_element_type=jnp.float32
-    )
     length_float = lengths.astype(jnp.float32)
     keys_read = local_lengths.astype(jnp.float32) + jnp.dot(
         reader_rows.astype(jnp.float32), length_float, precision=lax.Precision.HIGHEST
     )
     row_scale = lax.rsqrt(HS * keys_read)
-    mixed = (carried + within) * row_scale[:, None, None, None]
-    mixed = jnp.where(live_mask.reshape(group_local, CH, 1, 1), mixed, 0.0).astype(jnp.bfloat16)
-    mixed = mixed.reshape(group_local * CH, local_width)
+    causal = offsets[:, None] >= offsets[None, :]
+    groups_live = live_mask.reshape(group_local, CH, 1, 1)
 
-    mixed, w_out_all = lax.optimization_barrier((mixed, w_out_all))
+    def mix(lo, hi):
+        query_rows = jnp.dot(
+            tokens[lo * CH : hi * CH], w_query, preferred_element_type=jnp.float32
+        ).astype(jnp.bfloat16)
+        query_blocks = query_rows.reshape(hi - lo, CH, head_dev, HS)
+        carried = jnp.einsum(
+            "cthd,chde->cthe", query_blocks, prefix[lo:hi], preferred_element_type=jnp.float32
+        )
+        scores = jnp.einsum(
+            "cthd,cshd->chts", query_blocks, key_blocks[lo:hi], preferred_element_type=jnp.float32
+        )
+        weights = jnp.where(causal[None, None], scores, 0.0).astype(jnp.bfloat16)
+        within = jnp.einsum(
+            "chts,cshe->cthe", weights, value_blocks[lo:hi], preferred_element_type=jnp.float32
+        )
+        mixed = (carried + within) * row_scale[lo:hi, None, None, None]
+        mixed = jnp.where(groups_live[lo:hi], mixed, 0.0).astype(jnp.bfloat16)
+        return mixed.reshape((hi - lo) * CH, local_width)
+
     chip_at = lax.axis_index("tz")
     chip_count = tp_count // PAIR
     column = tp_index * local_width
+    below = (chip_at - 1) % chip_count
+    above = (chip_at + 1) % chip_count
+    across = (chip_at + 2) % chip_count
+    other = 1 - core_at
 
     def shifted(step):
         return [
@@ -108,38 +116,43 @@
             for c in range(PAIR)
         ]
 
-    def rows_of(z, core):
-        return lax.dynamic_slice(
-            w_out_all, ((z * PAIR + core) * local_width, column), (local_width, local_width)
-        )
-
-    def term(block, z, core):
-        return jnp.dot(block, rows_of(z, core), preferred_element_type=jnp.float32)
-
-    from_below = lax.ppermute(mixed, TP, shifted(1))
-    from_above = lax.ppermute(mixed, TP, shifted(chip_count - 1))
-    below = (chip_at - 1) % chip_count
-    above = (chip_at + 1) % chip_count
-    across = (chip_at + 2) % chip_count
-    first = jnp.concatenate([mixed, from_below, from_above], axis=1)
-    sibling_first = lax.ppermute(first, "tc", [(0, 1), (1, 0)])
     forward = [
         (z * PAIR, ((z + 1) % chip_count) * PAIR) for z in range(chip_count)
     ] + [(z * PAIR + 1, ((z - 1) % chip_count) * PAIR + 1) for z in range(chip_count)]
-    relayed = lax.ppermute(jnp.where(core_at == 0, from_below, from_above), TP, forward)
-    sibling_relayed = lax.ppermute(relayed, "tc", [(0, 1), (1, 0)])
-    other = 1 - core_at
-    total = term(mixed, chip_at, core_at)
-    total = total + term(from_below, below, core_at) + term(from_above, above, core_at)
-    total = total + jnp.dot(
-        sibling_first,
-        jnp.concatenate(
-            [rows_of(chip_at, other), rows_of(below, other), rows_of(above, other)], axis=0
-        ),
-        preferred_element_type=jnp.float32,
-    )
-    total = total + term(relayed, across, core_at) + term(sibling_relayed, across, other)
-    return total.astype(jnp.bfloat16)
+
+    def project(mixed, w_all):
+        def rows_of(z, core):
+            return lax.dynamic_slice(
+                w_all, ((z * PAIR + core) * local_width, column), (local_width, local_width)
+            )
+
+        def term(block, z, core):
+            return jnp.dot(block, rows_of(z, core), preferred_element_type=jnp.float32)
+
+        from_below = lax.ppermute(mixed, TP, shifted(1))
+        from_above = lax.ppermute(mixed, TP, shifted(chip_count - 1))
+        first = jnp.concatenate([mixed, from_below, from_above], axis=1)
+        sibling_first = lax.ppermute(first, "tc", [(0, 1), (1, 0)])
+        relayed = lax.ppermute(jnp.where(core_at == 0, from_below, from_above), TP, forward)
+        sibling_relayed = lax.ppermute(relayed, "tc", [(0, 1), (1, 0)])
+        total = term(mixed, chip_at, core_at)
+        total = total + term(from_below, below, core_at) + term(from_above, above, core_at)
+        total = total + jnp.dot(
+            sibling_first,
+            jnp.concatenate(
+                [rows_of(chip_at, other), rows_of(below, other), rows_of(above, other)], axis=0
+            ),
+            preferred_element_type=jnp.float32,
+        )
+        total = total + term(relayed, across, core_at) + term(sibling_relayed, across, other)
+        return total.astype(jnp.bfloat16)
+
+    middle = group_local // 2
+    early = mix(0, middle)
+    early, w_out_all = lax.optimization_barrier((early, w_out_all))
+    first_half = project(early, w_out_all)
+    second_half = project(mix(middle, group_local), w_out_all)
+    return jnp.concatenate([first_half, second_half], axis=0)
 
 
 def solution(mesh):

time: 120 us -> 130 us (1.083)
  waiting for transfers between devices: 20.4 us -> 5.71 us
  local copies, waits for them, and re-layouts: 10.4 us -> 19.1 us
  starting transfers between devices: 12 us -> 20.6 us
  matrix products: 34.9 us -> 41.5 us
    ppermute x5 -> x10, waiting for transfers between devices: 19.7 us -> 5 us  [the longest x2 2.6 us: project(): from_below = lax.ppermute(mixed, TP, shifted(1))]
    ppermute x5 -> x10, starting transfers between devices: 12 us -> 20.6 us  [the longest x2 6.58 us: project(): sibling_first = lax.ppermute(first, 'tc', [(0, 1), (1, 0)])]
    slice x0 -> x9, local copies, waits for them, and re-layouts: none -> 7.38 us  [the longest x3 3.02 us: mix(): value_blocks[lo:hi]]
    dot_general x5 -> x10, matrix products: 7.55 us -> 11.8 us  [term(): return jnp.dot(block, rows_of(z, core), preferred_element_type=jnp.float32)]
    dot_general x4 -> x8, matrix products: 14.4 us -> 17 us  [the longest x2 7.82 us: mix(): jnp.dot(tokens[lo * CH:hi * CH], w_query, preferred_element_type=jnp.floa...]
    reshape x1 -> x2, local copies, waits for them, and re-layouts: 2.01 us -> 2.73 us  [mix(): query_blocks = query_rows.reshape(hi - lo, CH, head_dev, HS)]
  transfers between devices with their start and end apart: 6 -> 11, of which waited for: 2 -> 3; matrix products, arithmetic and copies ran while one was open for 38% -> 49% of each run, Pallas kernels for 0% -> 0%
where the time goes in v11:
time: 130 us; the launch traced here: 129 us
  matrix products  41.5 us (32%)
  blocking collectives  23.7 us (18%)
  starting transfers between devices  20.6 us (16%)
  local copies, waits for them, and re-layouts  19.1 us (15%)
  between operations  13.8 us (11%)
  waiting for transfers between devices  5.71 us (4%)
  other arithmetic  4.34 us (3%)
    all_gather x1, blocking collectives, local(): row_tails = lax.all_gather(tail, 'sx', axis=0, tiled=False)  12.1 us
    dot_general x10, matrix products, term(): return jnp.dot(block, rows_of(z, core), preferred_element_type=jnp.float32)  11.8 us
    all_gather x1, blocking collectives, local(): row_sums = lax.all_gather(row_sum, 'sy', axis=0, tiled=False)  11.6 us
    dot_general x2, matrix products, mix(): jnp.dot(tokens[lo * CH:hi * CH], w_query, preferred_element_type=jnp.floa...  7.82 us
    ppermute x2, starting transfers between devices, project(): sibling_first = lax.ppermute(first, 'tc', [(0, 1), (1, 0)])  6.58 us
    ppermute x2, starting transfers between devices, project(): from_above = lax.ppermute(mixed, TP, shifted(chip_count - 1))  5.3 us
    dot_general x2, matrix products, mix(): jnp.einsum('chts,cshe->cthe', weights, value_blocks[lo:hi], preferred_ele...  5.22 us
    ppermute x2, starting transfers between devices, project(): lax.ppermute(jnp.where(core_at == 0, from_below, from_above), TP, forward)  5.19 us
  transfers between devices with their start and end apart: 11, of which 3 were waited for; matrix products, arithmetic and copies ran while one was open for 49% of the time, Pallas kernels for 0%

profile of v11, /device:TPU:1, one launch (start us, length us, event | category | flops | bytes accessed | tf_op | source)
XLA Modules:
  0.0 128.7 jit_solution(17975856667575264889)
XLA Ops:
  8.8 4.6 %fusion.4 = bf16[1536,256]{1,0:T(8,128)(2,1)S(1)} fusion(bf16[1536,2048]{1,0:T(8,128)(2,1)} %param.13, bf16[2048,256]{1,0:T(8,128)(2,1)S(1)} %copy-done, pred[1536]{0:T(1024)(128)(4,1)S(1)} %get-tuple-element.63), kind=kOutput, calls=%fused_computation.6 | convolution fusion | flops 1611399168 | bytes 8128000 | tf_op jit(solution)/shard_map/dot_general | solution.py:36
  13.6 4.8 %fusion.5 = bf16[1536,256]{1,0:T(8,128)(2,1)S(1)} fusion(bf16[1536,2048]{1,0:T(8,128)(2,1)} %param.13, bf16[2048,256]{1,0:T(8,128)(2,1)} %param.16, pred[1536]{0:T(1024)(128)(4,1)S(1)} %get-tuple-element.63), kind=kOutput, calls=%fused_computation.7 | convolution fusion | flops 1611399168 | bytes 8128000 | tf_op jit(solution)/shard_map/dot_general | solution.py:39
  18.4 1.1 reshape.140
  20.8 0.8 dynamic-slice_bitcast_fusion
  21.9 0.9 dynamic-slice_reduce_fusion
  22.8 4.7 %fusion.23 = bf16[768,256]{1,0:T(8,128)(2,1)} fusion(bf16[2048,256]{1,0:T(8,128)(2,1)} %param.14, bf16[1536,2048]{1,0:T(8,128)(2,1)} %param.13), kind=kOutput, calls=%fused_computation.35 | convolution fusion | flops 805502976 | bytes 4587520 | tf_op jit(solution)/shard_map/dot_general | solution.py:86
  27.5 1.9 %reshape.144 = bf16[6,128,2,128]{3,2,1,0:T(2,128)(2,1)} reshape(bf16[768,256]{1,0:T(8,128)(2,1)} %fusion.23) | data formatting | bytes 786432 | tf_op jit(solution)/shard_map/reshape | solution.py:89
  29.3 1.0 fusion.90
  30.3 2.0 %slice.111 = bf16[6,128,2,128]{3,2,1,0:T(2,128)(2,1)} reshape(bf16[768,256]{1,0:T(8,128)(2,1)} %get-tuple-element.57) | data formatting | bytes 786432 | tf_op jit(solution)/shard_map/slice | solution.py:98
  32.3 0.9 fusion.89
  33.2 1.9 %slice.113 = bf16[6,128,2,128]{3,2,1,0:T(2,128)(2,1)} reshape(bf16[768,256]{1,0:T(8,128)(2,1)} %get-tuple-element.55) | data formatting | bytes 786432 | tf_op jit(solution)/shard_map/slice | solution.py:94
  36.3 12.1 %all-gather = f32[8,128,128]{2,1,0:T(8,128)S(1)} all-gather(f32[2,128,128]{2,1,0:T(8,128)S(1)} %bitcast.72), channel_id=2, replica_groups=mesh['sy'=4,'sx'=4,'tz'=4,'tc'=2] {'sx'}, dimensions={0}, use_global_device_ids=true | all-gather | bytes 655360 | tf_op jit(solution)/shard_map/all_gather | solution.py:53
  48.5 11.6 %all-gather.1 = f32[8,128,128]{2,1,0:T(8,128)S(1)} all-gather(f32[2,128,128]{2,1,0:T(8,128)S(1)} %get-tuple-element.45), channel_id=3, replica_groups=mesh['sy'=4,'sx'=4,'tz'=4,'tc'=2] {'sy'}, dimensions={0}, use_global_device_ids=true | all-gather | bytes 655360 | tf_op jit(solution)/shard_map/all_gather | solution.py:61
  60.3 0.9 fusion.30
  62.4 1.4 %add_convert_fusion = bf16[12,2,128,128]{3,0,2,1:T(8,128)(2,1)S(1)} fusion(bf16[12,2,128,128]{3,2,1,0:T(8,128)(2,1)S(1)} %convolution_convert_fusion, f32[2,128,128]{2,1,0:T(8,128)S(1)} %add.191, f32[12]{0:T(128)S(1)} %convert_element_type.71, s32[192,192]{1,0:T(8,128)} %param.18, s32[]{:T(128)S(6)} %select_n.115), kind=kOutput, calls=%fused_computation.8 | convolution fusion | flops 10616976 | bytes 1712180 | tf_op jit(solution)/shard_map/ce,ehij->chij/dot_general | solution.py:69
  64.5 2.5 %fusion.27 = bf16[6,128,2,128]{1,3,2,0:T(8,128)(2,1)} fusion(f32[6,2,128,128]{3,2,1,0:T(8,128)S(1)} %fusion.39, bf16[6,128,2,128]{3,2,1,0:T(2,128)(2,1)} %slice.111, bf16[6,128,2,128]{3,2,1,0:T(2,128)(2,1)} %slice.113, f32[6]{0:T(128)} %get-tuple-element.61, pred[6,128]{1,0:T(8,128)(4,1)} %get-tuple-element.59, pred[128,128]{1,0:T(8,128)(4,1)S(1)} %iota_compare_fusion, ...), kind=kOutput, calls=%fused_computation.37 | convolution fusion | flops 101842944 | bytes 2376472 | tf_op jit(solution)/shard_map/chts,cshe->cthe/dot_general | solution.py:97
  67.1 1.3 copy.57
  68.7 3.0 %collective-permute-start.6 = (bf16[768,256]{1,0:T(8,128)(2,1)S(1)}, bf16[768,256]{1,0:T(8,128)(2,1)S(1)}, u32[]{:S(2)}, u32[]{:S(2)}) collective-permute-start(bf16[768,256]{1,0:T(8,128)(2,1)S(1)} %bitcast.69), channel_id=1, source_target_pairs={{0,6},{1,7},{2,0},{3,1},{4,2},{5,3},{6,4},{7,5},{8,14},{9,15},{10,... | collective-permute-start | bytes 1179656 | tf_op jit(solution)/shard_map/ppermute | solution.py:133
  71.7 3.2 %fusion.20 = bf16[768,256]{1,0:T(8,128)(2,1)S(1)} fusion(bf16[2048,256]{1,0:T(8,128)(2,1)} %param.14, bf16[1536,2048]{1,0:T(8,128)(2,1)} %param.13), kind=kOutput, calls=%fused_computation.34 | convolution fusion | flops 805502976 | bytes 4587520 | tf_op jit(solution)/shard_map/dot_general | solution.py:86
  74.9 0.9 reshape.142
  75.7 1.1 collective-permute-done.5
  76.8 1.2 pad_maximum_fusion.1
  78.0 5.6 %collective-permute-start.7 = (bf16[768,768]{1,0:T(8,128)(2,1)}, bf16[768,768]{1,0:T(8,128)(2,1)}, u32[]{:S(2)}, u32[]{:S(2)}) collective-permute-start(bf16[768,768]{1,0:T(8,128)(2,1)} %pad_maximum_fusion.1), channel_id=1, source_target_pairs={{0,1},{1,0},{2,3},{3,2},{4,5},{5,4},{6,7},{7,6},{8,9},{9,8},{10,11... | collective-permute-start | bytes 3538952 | tf_op jit(solution)/shard_map/ppermute | solution.py:135
  83.6 0.8 broadcast_select_fusion
  84.4 2.5 %collective-permute-start.8 = (bf16[768,256]{1,0:T(8,128)(2,1)}, bf16[768,256]{1,0:T(8,128)(2,1)}, u32[]{:S(2)}, u32[]{:S(2)}) collective-permute-start(bf16[768,256]{1,0:T(8,128)(2,1)} %broadcast_select_fusion), channel_id=1, source_target_pairs={{0,2},{2,4},{4,6},{6,0},{1,7},{3,1},{5,3},{7,5},{8,10},{10,12},{12... | collective-permute-start | bytes 1179656 | tf_op jit(solution)/shard_map/ppermute | solution.py:136
  86.9 1.3 %fusion.44 = f32[6,2,128,128]{3,2,1,0:T(8,128)} fusion(bf16[6,2,128,128]{3,0,2,1:T(8,128)(2,1)S(1)} %get-tuple-element.52, bf16[6,128,2,128]{3,2,1,0:T(2,128)(2,1)S(1)} %copy-done.4), kind=kOutput, calls=%fused_computation.62 | convolution fusion | flops 50331648 | bytes 1572864 | tf_op jit(solution)/shard_map/cthd,chde->cthe/dot_general | solution.py:90
  88.4 2.7 %fusion.26 = bf16[6,128,2,128]{1,3,2,0:T(8,128)(2,1)} fusion(f32[6,2,128,128]{3,2,1,0:T(8,128)} %fusion.44, bf16[6,128,2,128]{3,2,1,0:T(2,128)(2,1)S(1)} %slice.103, bf16[6,128,2,128]{3,2,1,0:T(2,128)(2,1)S(1)} %slice.105, f32[6]{0:T(128)} %get-tuple-element.60, pred[128,128]{1,0:T(8,128)(4,1)S(1)} %iota_compare_fusion, ...), kind=kOutput, calls=%fused_computation.36 | convolution fusion | flops 101842944 | bytes 2376472 | tf_op jit(solution)/shard_map/chts,cshe->cthe/dot_general | solution.py:97
  91.1 1.3 copy.51
  92.5 1.2 collective-permute-start.9
  94.1 2.3 %collective-permute-start.1 = (bf16[768,256]{1,0:T(8,128)(2,1)S(1)}, bf16[768,256]{1,0:T(8,128)(2,1)S(1)}, u32[]{:S(2)}, u32[]{:S(2)}) collective-permute-start(bf16[768,256]{1,0:T(8,128)(2,1)S(1)} %bitcast.63), channel_id=1, source_target_pairs={{0,6},{1,7},{2,0},{3,1},{4,2},{5,3},{6,4},{7,5},{8,14},{9,15},{10,... | collective-permute-start | bytes 1179656 | tf_op jit(solution)/shard_map/ppermute | solution.py:133
  96.4 1.1 fusion.87
  97.5 1.2 fusion.58
  98.7 1.2 convolution_add_fusion.4
  99.9 1.7 %fusion.56 = f32[768,256]{1,0:T(8,128)S(1)} fusion(bf16[768,768]{1,0:T(8,128)(2,1)} %collective-permute-done.7, bf16[256,256]{1,0:T(8,128)(2,1)S(1)} %get-tuple-element.50, bf16[256,256]{1,0:T(8,128)(2,1)S(1)} %get-tuple-element.51, bf16[256,256]{1,0:T(8,128)(2,1)S(1)} %get-tuple-element.49), kind=kOutput, calls=%fused_computation.74 | convolution fusion | flops 303169536 | bytes 2359296 | tf_op jit(solution)/shard_map/dot_general | solution.py:140
  101.6 1.3 %fusion.64 = f32[768,256]{1,0:T(8,128)S(1)} fusion(bf16[768,256]{1,0:T(8,128)(2,1)} %collective-permute-done.8, bf16[2048,2048]{1,0:T(8,128)(2,1)} %all-gather.4.cloned.1.call-done, s32[]{:T(128)S(6)} %select_n.133, s32[]{:T(128)S(6)} %select_n.122), kind=kOutput, calls=%fused_computation.82 | convolution fusion | flops 100663296 | bytes 1310728 | tf_op jit(solution)/shard_map/dot_general | solution.py:130
  102.9 1.2 fusion.11
  104.1 1.5 %collective-permute-done = bf16[768,256]{1,0:T(8,128)(2,1)S(1)} collective-permute-done((bf16[768,256]{1,0:T(8,128)(2,1)S(1)}, bf16[768,256]{1,0:T(8,128)(2,1)S(1)}, u32[]{:S(2)}, u32[]{:S(2)}) %collective-permute-start) | collective-permute-done | bytes 393248 | tf_op jit(solution)/shard_map/ppermute | solution.py:132
  105.7 0.9 collective-permute-start.2
  106.7 1.2 fusion.17
  107.9 2.7 %collective-permute-start.3 = (bf16[768,256]{1,0:T(8,128)(2,1)S(1)}, bf16[768,256]{1,0:T(8,128)(2,1)S(1)}, u32[]{:S(2)}, u32[]{:S(2)}) collective-permute-start(bf16[768,256]{1,0:T(8,128)(2,1)S(1)} %broadcast_select_fusion.1), channel_id=1, source_target_pairs={{0,2},{2,4},{4,6},{6,0},{1,7},{3,1},{5,3},{7,5},{8,10},{10,12},{12... | collective-permute-start | bytes 1179656 | tf_op jit(solution)/shard_map/ppermute | solution.py:136
  110.6 1.2 fusion.60
  111.8 1.2 convolution_add_fusion.7
  113.0 2.4 %collective-permute-done.3 = bf16[768,256]{1,0:T(8,128)(2,1)S(1)} collective-permute-done((bf16[768,256]{1,0:T(8,128)(2,1)S(1)}, bf16[768,256]{1,0:T(8,128)(2,1)S(1)}, u32[]{:S(2)}, u32[]{:S(2)}) %collective-permute-start.3) | collective-permute-done | bytes 393248 | tf_op jit(solution)/shard_map/ppermute | solution.py:136
  115.3 1.6 %collective-permute-start.4 = (bf16[768,256]{1,0:T(8,128)(2,1)S(1)}, bf16[768,256]{1,0:T(8,128)(2,1)S(1)}, u32[]{:S(2)}, u32[]{:S(2)}) collective-permute-start(bf16[768,256]{1,0:T(8,128)(2,1)S(1)} %collective-permute-done.3), channel_id=1, source_target_pairs={{0,1},{1,0},{2,3},{3,2},{4,5},{5,4},{6,7},{7,6},{8,9},{9,8},{10,11... | collective-permute-start | bytes 1179656 | tf_op jit(solution)/shard_map/ppermute | solution.py:137
  117.0 1.2 fusion.66
  118.6 1.2 fusion.13
  119.8 1.2 fusion.16
  121.0 0.9 pad_maximum_fusion.2
  (62 shorter events, 9.0 us)
Async XLA Ops:
  6.5 2.2 %copy-start = (bf16[2048,256]{1,0:T(8,128)(2,1)S(1)}, bf16[2048,256]{1,0:T(8,128)(2,1)}, u32[]{:S(2)}) copy-start(bf16[2048,256]{1,0:T(8,128)(2,1)} %param.15) | copy-start | bytes 3145732
  6.5 87.2 %all-gather.4.cloned.1.call-start = ((), (), s32[]{:S(2)}) async-start(), calls=%async_computation | async-start | bytes 9437184 | tf_op jit(solution)/shard_map/all_gather | solution.py:29
  30.3 5.0 %copy-start.1 = (bf16[12,128,2,128]{3,2,1,0:T(2,128)(2,1)S(1)}, bf16[12,128,2,128]{3,2,1,0:T(2,128)(2,1)}, u32[]{:S(2)}) copy-start(bf16[12,128,2,128]{3,2,1,0:T(2,128)(2,1)} %reshape.140) | copy-start | bytes 2359300
  35.7 24.6 %copy-start.6 = (s32[192]{0:T(256)S(1)}, s32[192]{0:T(256)}, u32[]{:S(2)}) copy-start(s32[192]{0:T(256)} %param.19) | copy-start | bytes 2308
  60.2 3.9 %copy-start.5 = (bf16[6,128,2,128]{3,2,1,0:T(2,128)(2,1)S(1)}, bf16[6,128,2,128]{3,2,1,0:T(2,128)(2,1)}, u32[]{:S(2)}) copy-start(bf16[6,128,2,128]{3,2,1,0:T(2,128)(2,1)} %reshape.144) | copy-start | bytes 1179652
  68.4 8.4 %collective-permute-start.5 = (bf16[768,256]{1,0:T(8,128)(2,1)S(1)}, bf16[768,256]{1,0:T(8,128)(2,1)S(1)}, u32[]{:S(2)}, u32[]{:S(2)}) collective-permute-start(bf16[768,256]{1,0:T(8,128)(2,1)S(1)} %bitcast.68), channel_id=1, source_target_pairs={{0,2},{1,3},{2,4},{3,5},{4,6},{5,7},{6,0},{7,1},{8,10},{9,11},{10,... | collective-permute-start | bytes 1179656 | tf_op jit(solution)/shard_map/ppermute | solution.py:132
  68.7 8.1 %collective-permute-start.6 = (bf16[768,256]{1,0:T(8,128)(2,1)S(1)}, bf16[768,256]{1,0:T(8,128)(2,1)S(1)}, u32[]{:S(2)}, u32[]{:S(2)}) collective-permute-start(bf16[768,256]{1,0:T(8,128)(2,1)S(1)} %bitcast.69), channel_id=1, source_target_pairs={{0,6},{1,7},{2,0},{3,1},{4,2},{5,3},{6,4},{7,5},{8,14},{9,15},{10,... | collective-permute-start | bytes 1179656 | tf_op jit(solution)/shard_map/ppermute | solution.py:133
  75.7 11.2 %copy-start.4 = (bf16[6,128,2,128]{3,2,1,0:T(2,128)(2,1)S(1)}, bf16[6,128,2,128]{3,2,1,0:T(2,128)(2,1)}, u32[]{:S(2)}) copy-start(bf16[6,128,2,128]{3,2,1,0:T(2,128)(2,1)} %reshape.142) | copy-start | bytes 1179652
  75.7 12.5 %copy-start.2 = (bf16[768,256]{1,0:T(8,128)(2,1)S(1)}, bf16[768,256]{1,0:T(8,128)(2,1)}, u32[]{:S(2)}) copy-start(bf16[768,256]{1,0:T(8,128)(2,1)} %get-tuple-element.56) | copy-start | bytes 1179652
  78.0 10.3 %copy-start.3 = (bf16[768,256]{1,0:T(8,128)(2,1)S(1)}, bf16[768,256]{1,0:T(8,128)(2,1)}, u32[]{:S(2)}) copy-start(bf16[768,256]{1,0:T(8,128)(2,1)} %get-tuple-element.54) | copy-start | bytes 1179652
  78.0 21.9 %collective-permute-start.7 = (bf16[768,768]{1,0:T(8,128)(2,1)}, bf16[768,768]{1,0:T(8,128)(2,1)}, u32[]{:S(2)}, u32[]{:S(2)}) collective-permute-start(bf16[768,768]{1,0:T(8,128)(2,1)} %pad_maximum_fusion.1), channel_id=1, source_target_pairs={{0,1},{1,0},{2,3},{3,2},{4,5},{5,4},{6,7},{7,6},{8,9},{9,8},{10,11... | collective-permute-start | bytes 3538952 | tf_op jit(solution)/shard_map/ppermute | solution.py:135
  84.4 8.1 %collective-permute-start.8 = (bf16[768,256]{1,0:T(8,128)(2,1)}, bf16[768,256]{1,0:T(8,128)(2,1)}, u32[]{:S(2)}, u32[]{:S(2)}) collective-permute-start(bf16[768,256]{1,0:T(8,128)(2,1)} %broadcast_select_fusion), channel_id=1, source_target_pairs={{0,2},{2,4},{4,6},{6,0},{1,7},{3,1},{5,3},{7,5},{8,10},{10,12},{12... | collective-permute-start | bytes 1179656 | tf_op jit(solution)/shard_map/ppermute | solution.py:136
  92.5 14.2 %collective-permute-start.9 = (bf16[768,256]{1,0:T(8,128)(2,1)}, bf16[768,256]{1,0:T(8,128)(2,1)S(1)}, u32[]{:S(2)}, u32[]{:S(2)}) collective-permute-start(bf16[768,256]{1,0:T(8,128)(2,1)} %collective-permute-done.8), channel_id=1, source_target_pairs={{0,1},{1,0},{2,3},{3,2},{4,5},{5,4},{6,7},{7,6},{8,9},{9,8},{10,11... | collective-permute-start | bytes 1179656 | tf_op jit(solution)/shard_map/ppermute | solution.py:137
  93.7 11.9 %collective-permute-start = (bf16[768,256]{1,0:T(8,128)(2,1)S(1)}, bf16[768,256]{1,0:T(8,128)(2,1)S(1)}, u32[]{:S(2)}, u32[]{:S(2)}) collective-permute-start(bf16[768,256]{1,0:T(8,128)(2,1)S(1)} %bitcast.62), channel_id=1, source_target_pairs={{0,2},{1,3},{2,4},{3,5},{4,6},{5,7},{6,0},{7,1},{8,10},{9,11},{10,... | collective-permute-start | bytes 1179656 | tf_op jit(solution)/shard_map/ppermute | solution.py:132
  94.1 11.5 %collective-permute-start.1 = (bf16[768,256]{1,0:T(8,128)(2,1)S(1)}, bf16[768,256]{1,0:T(8,128)(2,1)S(1)}, u32[]{:S(2)}, u32[]{:S(2)}) collective-permute-start(bf16[768,256]{1,0:T(8,128)(2,1)S(1)} %bitcast.63), channel_id=1, source_target_pairs={{0,6},{1,7},{2,0},{3,1},{4,2},{5,3},{6,4},{7,5},{8,14},{9,15},{10,... | collective-permute-start | bytes 1179656 | tf_op jit(solution)/shard_map/ppermute | solution.py:133
  105.7 12.4 %collective-permute-start.2 = (bf16[768,768]{1,0:T(8,128)(2,1)S(1)}, bf16[768,768]{1,0:T(8,128)(2,1)S(1)}, u32[]{:S(2)}, u32[]{:S(2)}) collective-permute-start(bf16[768,768]{1,0:T(8,128)(2,1)S(1)} %pad_maximum_fusion), channel_id=1, source_target_pairs={{0,1},{1,0},{2,3},{3,2},{4,5},{5,4},{6,7},{7,6},{8,9},{9,8},{10,11... | collective-permute-start | bytes 3538952 | tf_op jit(solution)/shard_map/ppermute | solution.py:135
  107.9 7.5 %collective-permute-start.3 = (bf16[768,256]{1,0:T(8,128)(2,1)S(1)}, bf16[768,256]{1,0:T(8,128)(2,1)S(1)}, u32[]{:S(2)}, u32[]{:S(2)}) collective-permute-start(bf16[768,256]{1,0:T(8,128)(2,1)S(1)} %broadcast_select_fusion.1), channel_id=1, source_target_pairs={{0,2},{2,4},{4,6},{6,0},{1,7},{3,1},{5,3},{7,5},{8,10},{10,12},{12... | collective-permute-start | bytes 1179656 | tf_op jit(solution)/shard_map/ppermute | solution.py:136
  115.3 4.5 %collective-permute-start.4 = (bf16[768,256]{1,0:T(8,128)(2,1)S(1)}, bf16[768,256]{1,0:T(8,128)(2,1)S(1)}, u32[]{:S(2)}, u32[]{:S(2)}) collective-permute-start(bf16[768,256]{1,0:T(8,128)(2,1)S(1)} %collective-permute-done.3), channel_id=1, source_target_pairs={{0,1},{1,0},{2,3},{3,2},{4,5},{5,4},{6,7},{7,6},{8,9},{9,8},{10,11... | collective-permute-start | bytes 1179656 | tf_op jit(solution)/shard_map/ppermute | solution.py:137
Sparse Core Ops, SparseCore 0:
  9.0 53.4 all-gather.3

commit v12 on v8

--- a/solution.py
+++ b/solution.py
@@ -39,12 +39,21 @@
         live_mask, jnp.dot(tokens, w_value, preferred_element_type=jnp.float32), 0.0
     ).astype(jnp.bfloat16)
     query_rows = jnp.dot(tokens, w_query, preferred_element_type=jnp.float32).astype(jnp.bfloat16)
-    query_blocks = query_rows.reshape(group_local, CH, head_dev, HS)
-    key_blocks = key_rows.reshape(group_local, CH, head_dev, HS)
-    value_blocks = value_rows.reshape(group_local, CH, head_dev, HS)
-
-    states = jnp.einsum(
-        "cshd,cshe->chde", key_blocks, value_blocks, preferred_element_type=jnp.float32
+    query_groups = query_rows.reshape(group_local, CH, local_width)
+    key_groups = key_rows.reshape(group_local, CH, local_width)
+    value_groups = value_rows.reshape(group_local, CH, local_width)
+    heads = [slice(h * HS, (h + 1) * HS) for h in range(head_dev)]
+    states = jnp.stack(
+        [
+            jnp.einsum(
+                "csd,cse->cde",
+                key_groups[:, :, cut],
+                value_groups[:, :, cut],
+                preferred_element_type=jnp.float32,
+            )
+            for cut in heads
+        ],
+        axis=1,
     ).astype(jnp.bfloat16)
 
     local_readers = lax.dynamic_slice_in_dim(reader_rows, first_group, group_local, 1)
@@ -76,24 +85,28 @@
     )
     prefix = (carried_in + own).astype(jnp.bfloat16)
 
-    carried = jnp.einsum(
-        "cthd,chde->cthe", query_blocks, prefix, preferred_element_type=jnp.float32
-    )
-    scores = jnp.einsum(
-        "cthd,cshd->chts", query_blocks, key_blocks, preferred_element_type=jnp.float32
-    )
-    causal = offsets[:, None] >= offsets[None, :]
-    weights = jnp.where(causal[None, None], scores, 0.0).astype(jnp.bfloat16)
-    within = jnp.einsum(
-        "chts,cshe->cthe", weights, value_blocks, preferred_element_type=jnp.float32
-    )
     length_float = lengths.astype(jnp.float32)
     keys_read = local_lengths.astype(jnp.float32) + jnp.dot(
         reader_rows.astype(jnp.float32), length_float, precision=lax.Precision.HIGHEST
     )
     row_scale = lax.rsqrt(HS * keys_read)
-    mixed = (carried + within) * row_scale[:, None, None, None]
-    mixed = jnp.where(live_mask.reshape(group_local, CH, 1, 1), mixed, 0.0).astype(jnp.bfloat16)
+    causal = offsets[:, None] >= offsets[None, :]
+    pieces = []
+    for h, cut in enumerate(heads):
+        query_h = query_groups[:, :, cut]
+        carried = jnp.einsum(
+            "ctd,cde->cte", query_h, prefix[:, h], preferred_element_type=jnp.float32
+        )
+        scores = jnp.einsum(
+            "ctd,csd->cts", query_h, key_groups[:, :, cut], preferred_element_type=jnp.float32
+        )
+        weights = jnp.where(causal[None], scores, 0.0).astype(jnp.bfloat16)
+        within = jnp.einsum(
+            "cts,cse->cte", weights, value_groups[:, :, cut], preferred_element_type=jnp.float32
+        )
+        pieces.append((carried + within) * row_scale[:, None, None])
+    mixed = jnp.concatenate(pieces, axis=2)
+    mixed = jnp.where(live_mask.reshape(group_local, CH, 1), mixed, 0.0).astype(jnp.bfloat16)
     mixed = mixed.reshape(group_local * CH, local_width)
 
     mixed, w_out_all = lax.optimization_barrier((mixed, w_out_all))

time: 120 us -> 115 us (0.958)
  waiting for transfers between devices: 20.4 us -> 25.1 us
  matrix products: 34.9 us -> 30.2 us
  local copies, waits for them, and re-layouts: 10.4 us -> 5.85 us
  starting transfers between devices: 12 us -> 9.73 us
  other arithmetic: 3.9 us -> 5.35 us
    dot_general x1, matrix products: 6.5 us -> 1.86 us  [local(): jnp.dot(tokens, w_query, preferred_element_type=jnp.float32)]
    all_gather x1, waiting for transfers between devices: 0.02 us -> 3.05 us  [local(): w_out_all = lax.all_gather(w_out, TP, axis=0, tiled=True)]
    reshape x4 -> x0, local copies, waits for them, and re-layouts: 3.02 us -> none  [the longest x1 2.01 us: local(): query_blocks = query_rows.reshape(group_local, CH, head_dev, HS)]
    convert_element_type x1 -> x0, local copies, waits for them, and re-layouts: 2.25 us -> none  [local(): jnp.where(live_mask.reshape(group_local, CH, 1, 1), mixed, 0.0)]
    ppermute x1, waiting for transfers between devices: 14 us -> 15.7 us  [local(): from_below = lax.ppermute(mixed, TP, shifted(1))]
    ppermute x1, starting transfers between devices: 4.38 us -> 2.78 us  [local(): sibling_first = lax.ppermute(first, 'tc', [(0, 1), (1, 0)])]
    convert_element_type x0 -> x1, other arithmetic: none -> 1.38 us  [local(): jnp.where(live_mask.reshape(group_local, CH, 1), mixed, 0.0)]
    dot_general x3 -> x6, matrix products: 6.13 us -> 5.97 us  [the longest x2 4.81 us: local(): jnp.einsum('cts,cse->cte', weights, value_groups[:, :, cut], preferred_el...]
  transfers between devices with their start and end apart: 6 -> 6, of which waited for: 2 -> 3; matrix products, arithmetic and copies ran while one was open for 38% -> 32% of each run, Pallas kernels for 0% -> 0%
where the time goes in v12:
time: 115 us; the launch traced here: 114 us
  matrix products  30.2 us (26%)
  waiting for transfers between devices  25.1 us (22%)
  blocking collectives  24.2 us (21%)
  between operations  13.7 us (12%)
  starting transfers between devices  9.73 us (8%)
  local copies, waits for them, and re-layouts  5.85 us (5%)
  other arithmetic  5.35 us (5%)
    ppermute x1, waiting for transfers between devices, local(): from_below = lax.ppermute(mixed, TP, shifted(1))  15.7 us
    all_gather x1, blocking collectives, local(): row_tails = lax.all_gather(tail, 'sx', axis=0, tiled=False)  12.5 us
    all_gather x1, blocking collectives, local(): row_sums = lax.all_gather(row_sum, 'sy', axis=0, tiled=False)  11.7 us
    dot_general x5, matrix products, term(): return jnp.dot(block, rows_of(z, core), preferred_element_type=jnp.float32)  7.53 us
    ppermute x1, waiting for transfers between devices, local(): lax.ppermute(jnp.where(core_at == 0, from_below, from_above), TP, forward)  5.64 us
    dot_general x2, matrix products, local(): jnp.einsum('cts,cse->cte', weights, value_groups[:, :, cut], preferred_el...  4.81 us
    dot_general x1, matrix products, local(): jnp.dot(tokens, w_value, preferred_element_type=jnp.float32)  4.74 us
    dot_general x1, matrix products, local(): jnp.dot(tokens, w_key, preferred_element_type=jnp.float32)  4.73 us
  transfers between devices with their start and end apart: 6, of which 3 were waited for; matrix products, arithmetic and copies ran while one was open for 32% of the time, Pallas kernels for 0%

profile of v12, /device:TPU:1, one launch (start us, length us, event | category | flops | bytes accessed | tf_op | source)
XLA Modules:
  0.0 114.2 jit_solution(11405937330901924089)
XLA Ops:
  6.5 0.7 all-gather.4.cloned.1.call-update
  7.3 0.7 convert_element_type.68
  8.0 0.8 dynamic_slice.50
  8.7 0.7 fusion.62
  9.4 0.1 reshape.143
  9.8 0.1 dynamic-slice_reduce_fusion.2
  9.9 0.1 dynamic-slice_reduce_fusion.1
  10.0 0.8 dynamic-slice_bitcast_fusion
  10.8 0.2 fusion.68
  11.0 0.1 convert_element_type.61
  11.1 0.9 dynamic-slice_reduce_fusion
  12.0 0.2 slice_reduce_fusion
  12.3 4.7 %fusion.3 = bf16[1536,256]{1,0:T(8,128)(2,1)S(1)} fusion(bf16[1536,2048]{1,0:T(8,128)(2,1)} %param.13, bf16[2048,256]{1,0:T(8,128)(2,1)S(1)} %copy-done, pred[1536]{0:T(1024)(128)(4,1)S(1)} %fusion.57), kind=kOutput, calls=%fused_computation.8 | convolution fusion | flops 1611399168 | bytes 8128000 | tf_op jit(solution)/shard_map/dot_general | solution.py:36
  17.1 4.7 %fusion.4 = bf16[1536,256]{1,0:T(8,128)(2,1)S(1)} fusion(bf16[1536,2048]{1,0:T(8,128)(2,1)} %param.13, bf16[2048,256]{1,0:T(8,128)(2,1)S(1)} %copy-done.4, pred[1536]{0:T(1024)(128)(4,1)S(1)} %fusion.57), kind=kOutput, calls=%fused_computation.9 | convolution fusion | flops 1611399168 | bytes 8128000 | tf_op jit(solution)/shard_map/dot_general | solution.py:39
  21.8 0.3 fusion.10
  22.1 0.3 fusion.11
  22.6 0.5 fusion.15
  23.1 12.5 %all-gather = f32[8,128,128]{2,1,0:T(8,128)S(1)} all-gather(f32[2,128,128]{2,1,0:T(8,128)S(1)} %bitcast.67), channel_id=2, replica_groups=mesh['sy'=4,'sx'=4,'tz'=4,'tc'=2] {'sx'}, dimensions={0}, use_global_device_ids=true | all-gather | bytes 655360 | tf_op jit(solution)/shard_map/all_gather | solution.py:64
  35.6 0.1 multiply_reduce_fusion.1
  35.8 11.7 %all-gather.1 = f32[8,128,128]{2,1,0:T(8,128)S(1)} all-gather(f32[2,128,128]{2,1,0:T(8,128)S(1)} %get-tuple-element.45), channel_id=3, replica_groups=mesh['sy'=4,'sx'=4,'tz'=4,'tc'=2] {'sy'}, dimensions={0}, use_global_device_ids=true | all-gather | bytes 655360 | tf_op jit(solution)/shard_map/all_gather | solution.py:72
  47.5 0.1 multiply_reduce_fusion
  47.6 0.9 fusion.14
  48.5 1.5 %add_convert_fusion = bf16[12,2,128,128]{3,0,2,1:T(8,128)(2,1)S(1)} fusion(bf16[12,2,128,128]{3,2,0,1:T(8,128)(2,1)S(1)} %pad_maximum_fusion.1, f32[2,128,128]{2,1,0:T(8,128)S(1)} %add.150, f32[12]{0:T(128)S(1)} %convert_element_type.56, s32[192,192]{1,0:T(8,128)} %param.18, s32[]{:T(128)S(6)} %select_n.91), kind=kOutput, calls=%fused_computation.12 | convolution fusion | flops 10616976 | bytes 1712180 | tf_op jit(solution)/shard_map/ce,ehij->chij/dot_general | solution.py:80
  50.1 0.2 slice_bitcast_fusion.1
  50.3 1.9 %convolution_convert_fusion = bf16[1536,256]{1,0:T(8,128)(2,1)S(1)} fusion(bf16[1536,2048]{1,0:T(8,128)(2,1)S(1)} %bitcast.72, bf16[2048,256]{1,0:T(8,128)(2,1)S(1)} %copy-done.5), kind=kOutput, calls=%fused_computation.10 | convolution fusion | flops 1611005952 | bytes 8126464 | tf_op jit(solution)/shard_map/dot_general | solution.py:41
  52.2 0.3 fusion.26
  52.4 0.6 copy-done.2
  53.1 0.3 fusion.24
  53.3 2.4 %fusion.6 = bf16[12,128,128]{2,1,0:T(8,128)(2,1)} fusion(f32[12,128,128]{2,1,0:T(8,128)S(1)} %fusion.26, f32[12]{0:T(128)S(1)} %fusion.14, pred[128,128]{1,0:T(8,128)(4,1)S(1)} %iota_compare_fusion, bf16[12,128,256]{2,1,0:T(8,128)(2,1)} %bitcast.61, bf16[12,128,256]{2,1,0:T(8,128)(2,1)S(1)} %bitcast.57, bf16[12,128,256]{2,1,0:T(8,128)(2,1)} %bitcast.65), kind=kOutput, calls=%fused_computation.19 | convolution fusion | flops 101646336 | bytes 2376192 | tf_op jit(solution)/shard_map/cts,cse->cte/dot_general | solution.py:104
  55.7 2.4 %fusion.7 = bf16[12,128,128]{2,1,0:T(8,128)(2,1)} fusion(f32[12,128,128]{2,1,0:T(8,128)S(1)} %fusion.24, f32[12]{0:T(128)S(1)} %fusion.14, pred[128,128]{1,0:T(8,128)(4,1)S(1)} %iota_compare_fusion, bf16[12,128,256]{2,1,0:T(8,128)(2,1)} %bitcast.66, bf16[12,128,256]{2,1,0:T(8,128)(2,1)} %bitcast.62, bf16[12,128,256]{2,1,0:T(8,128)(2,1)S(1)} %bitcast.58), kind=kOutput, calls=%fused_computation.20 | convolution fusion | flops 101646336 | bytes 2376192 | tf_op jit(solution)/shard_map/cts,cse->cte/dot_general | solution.py:104
  58.1 1.4 %fusion.5 = bf16[1536,256]{1,0:T(8,128)(2,1)S(1)} fusion(bf16[1536,128]{1,0:T(8,128)(2,1)} %bitcast.69, bf16[1536,128]{1,0:T(8,128)(2,1)} %bitcast.68, pred[1536]{0:T(1024)(128)(4,1)S(1)} %fusion.57), kind=kLoop, calls=%fused_computation.14 | loop fusion | flops 1966080 | bytes 1574400 | tf_op jit(solution)/shard_map/convert_element_type | solution.py:109
  59.5 3.1 %all-gather.4.cloned.1.call-done = bf16[2048,2048]{1,0:T(8,128)(2,1)} async-done(((bf16[256,2048]{1,0:T(8,128)(2,1)}), bf16[2048,2048]{1,0:T(8,128)(2,1)}) %all-gather.4.cloned.1.call-update) | async-done | bytes 8388624 | tf_op jit(solution)/shard_map/all_gather | solution.py:29
  62.6 0.3 collective-permute-start
  62.9 2.4 %collective-permute-start.1 = (bf16[1536,256]{1,0:T(8,128)(2,1)S(1)}, bf16[1536,256]{1,0:T(8,128)(2,1)S(1)}, u32[]{:S(2)}, u32[]{:S(2)}) collective-permute-start(bf16[1536,256]{1,0:T(8,128)(2,1)S(1)} %fusion.5), channel_id=1, source_target_pairs={{0,6},{1,7},{2,0},{3,1},{4,2},{5,3},{6,4},{7,5},{8,14},{9,15},{10,... | collective-permute-start | bytes 2359304 | tf_op jit(solution)/shard_map/ppermute | solution.py:133
  65.2 15.7 %collective-permute-done = bf16[1536,256]{1,0:T(8,128)(2,1)S(1)} collective-permute-done((bf16[1536,256]{1,0:T(8,128)(2,1)S(1)}, bf16[1536,256]{1,0:T(8,128)(2,1)S(1)}, u32[]{:S(2)}, u32[]{:S(2)}) %collective-permute-start) | collective-permute-done | bytes 786464 | tf_op jit(solution)/shard_map/ppermute | solution.py:132
  81.0 1.6 %pad_maximum_fusion = bf16[1536,768]{1,0:T(8,128)(2,1)} fusion(bf16[1536,256]{1,0:T(8,128)(2,1)S(1)} %collective-permute-done.1, bf16[1536,256]{1,0:T(8,128)(2,1)S(1)} %collective-permute-done, bf16[1536,256]{1,0:T(8,128)(2,1)S(1)} %fusion.5), kind=kLoop, calls=%fused_computation.11 | loop fusion | flops 7077888 | bytes 4718592 | tf_op jit(solution)/shard_map/concatenate | solution.py:137
  82.6 2.8 %collective-permute-start.2 = (bf16[1536,768]{1,0:T(8,128)(2,1)}, bf16[1536,768]{1,0:T(8,128)(2,1)}, u32[]{:S(2)}, u32[]{:S(2)}) collective-permute-start(bf16[1536,768]{1,0:T(8,128)(2,1)} %pad_maximum_fusion), channel_id=1, source_target_pairs={{0,1},{1,0},{2,3},{3,2},{4,5},{5,4},{6,7},{7,6},{8,9},{9,8},{10,11... | collective-permute-start | bytes 7077896 | tf_op jit(solution)/shard_map/ppermute | solution.py:138
  85.4 1.0 broadcast_select_fusion
  86.3 2.7 %collective-permute-start.3 = (bf16[1536,256]{1,0:T(8,128)(2,1)}, bf16[1536,256]{1,0:T(8,128)(2,1)}, u32[]{:S(2)}, u32[]{:S(2)}) collective-permute-start(bf16[1536,256]{1,0:T(8,128)(2,1)} %broadcast_select_fusion), channel_id=1, source_target_pairs={{0,2},{2,4},{4,6},{6,0},{1,7},{3,1},{5,3},{7,5},{8,10},{10,12},{12... | collective-permute-start | bytes 2359304 | tf_op jit(solution)/shard_map/ppermute | solution.py:142
  89.0 1.1 fusion.69
  90.1 1.3 %fusion.53 = f32[1536,256]{1,0:T(8,128)S(1)} fusion(bf16[1536,256]{1,0:T(8,128)(2,1)S(1)} %fusion.5, bf16[2048,2048]{1,0:T(8,128)(2,1)} %all-gather.4.cloned.1.call-done, s32[]{:T(128)S(6)} %select_n.99), kind=kOutput, calls=%fused_computation.72 | convolution fusion | flops 201326592 | bytes 2490372 | tf_op jit(solution)/shard_map/dot_general | solution.py:130
  91.3 1.3 %convolution_add_fusion.2 = f32[1536,256]{1,0:T(8,128)S(1)} fusion(f32[1536,256]{1,0:T(8,128)S(1)} %fusion.53, bf16[1536,256]{1,0:T(8,128)(2,1)S(1)} %collective-permute-done, bf16[2048,2048]{1,0:T(8,128)(2,1)} %all-gather.4.cloned.1.call-done, s32[]{:T(128)S(6)} %select_n.101, s32[]{:T(128)S(6)} %select_n.99), kind=kOutput, calls=%fused_computation.4 | convolution fusion | flops 201719808 | bytes 4063240 | tf_op jit(solution)/shard_map/dot_general | solution.py:130
  92.6 5.6 %collective-permute-done.3 = bf16[1536,256]{1,0:T(8,128)(2,1)} collective-permute-done((bf16[1536,256]{1,0:T(8,128)(2,1)}, bf16[1536,256]{1,0:T(8,128)(2,1)}, u32[]{:S(2)}, u32[]{:S(2)}) %collective-permute-start.3) | collective-permute-done | bytes 786464 | tf_op jit(solution)/shard_map/ppermute | solution.py:142
  98.2 1.6 %collective-permute-start.4 = (bf16[1536,256]{1,0:T(8,128)(2,1)}, bf16[1536,256]{1,0:T(8,128)(2,1)S(1)}, u32[]{:S(2)}, u32[]{:S(2)}) collective-permute-start(bf16[1536,256]{1,0:T(8,128)(2,1)} %collective-permute-done.3), channel_id=1, source_target_pairs={{0,1},{1,0},{2,3},{3,2},{4,5},{5,4},{6,7},{7,6},{8,9},{9,8},{10,11... | collective-permute-start | bytes 2359304 | tf_op jit(solution)/shard_map/ppermute | solution.py:143
  99.8 1.5 %fusion.49 = f32[1536,256]{1,0:T(8,128)S(1)} fusion(bf16[1536,256]{1,0:T(8,128)(2,1)} %collective-permute-done.3, bf16[2048,2048]{1,0:T(8,128)(2,1)} %all-gather.4.cloned.1.call-done, s32[]{:T(128)S(6)} %select_n.110, s32[]{:T(128)S(6)} %select_n.99), kind=kOutput, calls=%fused_computation.68 | convolution fusion | flops 201326592 | bytes 2490376 | tf_op jit(solution)/shard_map/dot_general | solution.py:130
  101.4 2.5 %fusion.18 = f32[1536,256]{1,0:T(8,128)S(1)} fusion(bf16[1536,768]{1,0:T(8,128)(2,1)} %collective-permute-done.2, bf16[256,256]{1,0:T(8,128)(2,1)S(1)} %get-tuple-element.50, bf16[256,256]{1,0:T(8,128)(2,1)S(1)} %get-tuple-element.51, bf16[256,256]{1,0:T(8,128)(2,1)S(1)} %get-tuple-element.49), kind=kOutput, calls=%fused_computation.41 | convolution fusion | flops 605159424 | bytes 4325376 | tf_op jit(solution)/shard_map/dot_general | solution.py:147
  103.8 1.3 %fusion.1 = f32[1536,256]{1,0:T(8,128)S(1)} fusion(f32[1536,256]{1,0:T(8,128)S(1)} %fusion.49, f32[1536,256]{1,0:T(8,128)S(1)} %fusion.18, f32[1536,256]{1,0:T(8,128)S(1)} %convolution_add_fusion.2, bf16[1536,256]{1,0:T(8,128)(2,1)S(1)} %collective-permute-done.1, bf16[2048,2048]{1,0:T(8,128)(2,1)} %all-gather.4.cloned.1.call-done, s32[]{:T(128)S(6)} %select_n.103, ...), kind=kOutput, calls=%fused_computation.3 | convolution fusion | flops 202506240 | bytes 7208968 | tf_op jit(solution)/shard_map/dot_general | solution.py:130
  105.2 2.2 %fusion.2 = bf16[1536,256]{1,0:T(8,128)(2,1)} fusion(f32[1536,256]{1,0:T(8,128)S(1)} %fusion.1, bf16[1536,256]{1,0:T(8,128)(2,1)S(1)} %collective-permute-done.4, bf16[2048,2048]{1,0:T(8,128)(2,1)} %all-gather.4.cloned.1.call-done, s32[]{:T(128)S(6)} %select_n.111, s32[]{:T(128)S(6)} %select_n.99), kind=kOutput, calls=%fused_computation.7 | convolution fusion | flops 202113024 | bytes 3276808 | tf_op jit(solution)/shard_map/dot_general | solution.py:130
  (32 shorter events, 0.5 us)
Async XLA Ops:
  6.5 5.7 %copy-start = (bf16[2048,256]{1,0:T(8,128)(2,1)S(1)}, bf16[2048,256]{1,0:T(8,128)(2,1)}, u32[]{:S(2)}) copy-start(bf16[2048,256]{1,0:T(8,128)(2,1)} %param.15) | copy-start | bytes 3145732
  6.5 56.0 %all-gather.4.cloned.1.call-start = ((), (), s32[]{:S(2)}) async-start(), calls=%async_computation | async-start | bytes 9437184 | tf_op jit(solution)/shard_map/all_gather | solution.py:29
  12.3 4.8 %copy-start.4 = (bf16[2048,256]{1,0:T(8,128)(2,1)S(1)}, bf16[2048,256]{1,0:T(8,128)(2,1)}, u32[]{:S(2)}) copy-start(bf16[2048,256]{1,0:T(8,128)(2,1)} %param.16) | copy-start | bytes 3145732
  12.3 38.0 %slice-start = ((s8[6291456]{0:T(1024)(128)(4,1)}), s8[4194304]{0:T(1024)(128)(4,1)S(1)}, s32[]{:S(2)}) async-start(s8[6291456]{0:T(1024)(128)(4,1)} %bitcast.71), calls=%async_computation.1 | async-start | bytes 8388608
  17.0 33.2 %slice-start.1 = ((s8[6291456]{0:T(1024)(128)(4,1)}), s8[2097152]{0:T(1024)(128)(4,1)S(1)}, s32[]{:S(2)}) async-start(s8[6291456]{0:T(1024)(128)(4,1)} %bitcast.71), calls=%async_computation.2 | async-start | bytes 4194304
  21.8 1.3 %copy-start.1 = (bf16[1536,256]{1,0:T(8,128)(2,1)}, bf16[1536,256]{1,0:T(8,128)(2,1)S(1)}, u32[]{:S(2)}) copy-start(bf16[1536,256]{1,0:T(8,128)(2,1)S(1)} %fusion.4) | copy-start | bytes 2359300
  22.6 25.1 %copy-start.3 = (s32[192]{0:T(256)S(1)}, s32[192]{0:T(256)}, u32[]{:S(2)}) copy-start(s32[192]{0:T(256)} %param.19) | copy-start | bytes 2308
  48.5 1.7 %copy-start.5 = (bf16[2048,256]{1,0:T(8,128)(2,1)S(1)}, bf16[2048,256]{1,0:T(8,128)(2,1)}, u32[]{:S(2)}) copy-start(bf16[2048,256]{1,0:T(8,128)(2,1)} %param.14) | copy-start | bytes 3145732
  52.2 0.9 copy-start.2
  62.6 18.4 %collective-permute-start = (bf16[1536,256]{1,0:T(8,128)(2,1)S(1)}, bf16[1536,256]{1,0:T(8,128)(2,1)S(1)}, u32[]{:S(2)}, u32[]{:S(2)}) collective-permute-start(bf16[1536,256]{1,0:T(8,128)(2,1)S(1)} %fusion.5), channel_id=1, source_target_pairs={{0,2},{1,3},{2,4},{3,5},{4,6},{5,7},{6,0},{7,1},{8,10},{9,11},{10,... | collective-permute-start | bytes 2359304 | tf_op jit(solution)/shard_map/ppermute | solution.py:132
  62.9 18.1 %collective-permute-start.1 = (bf16[1536,256]{1,0:T(8,128)(2,1)S(1)}, bf16[1536,256]{1,0:T(8,128)(2,1)S(1)}, u32[]{:S(2)}, u32[]{:S(2)}) collective-permute-start(bf16[1536,256]{1,0:T(8,128)(2,1)S(1)} %fusion.5), channel_id=1, source_target_pairs={{0,6},{1,7},{2,0},{3,1},{4,2},{5,3},{6,4},{7,5},{8,14},{9,15},{10,... | collective-permute-start | bytes 2359304 | tf_op jit(solution)/shard_map/ppermute | solution.py:133
  82.6 18.8 %collective-permute-start.2 = (bf16[1536,768]{1,0:T(8,128)(2,1)}, bf16[1536,768]{1,0:T(8,128)(2,1)}, u32[]{:S(2)}, u32[]{:S(2)}) collective-permute-start(bf16[1536,768]{1,0:T(8,128)(2,1)} %pad_maximum_fusion), channel_id=1, source_target_pairs={{0,1},{1,0},{2,3},{3,2},{4,5},{5,4},{6,7},{7,6},{8,9},{9,8},{10,11... | collective-permute-start | bytes 7077896 | tf_op jit(solution)/shard_map/ppermute | solution.py:138
  86.3 11.9 %collective-permute-start.3 = (bf16[1536,256]{1,0:T(8,128)(2,1)}, bf16[1536,256]{1,0:T(8,128)(2,1)}, u32[]{:S(2)}, u32[]{:S(2)}) collective-permute-start(bf16[1536,256]{1,0:T(8,128)(2,1)} %broadcast_select_fusion), channel_id=1, source_target_pairs={{0,2},{2,4},{4,6},{6,0},{1,7},{3,1},{5,3},{7,5},{8,10},{10,12},{12... | collective-permute-start | bytes 2359304 | tf_op jit(solution)/shard_map/ppermute | solution.py:142
  98.2 6.9 %collective-permute-start.4 = (bf16[1536,256]{1,0:T(8,128)(2,1)}, bf16[1536,256]{1,0:T(8,128)(2,1)S(1)}, u32[]{:S(2)}, u32[]{:S(2)}) collective-permute-start(bf16[1536,256]{1,0:T(8,128)(2,1)} %collective-permute-done.3), channel_id=1, source_target_pairs={{0,1},{1,0},{2,3},{3,2},{4,5},{5,4},{6,7},{7,6},{8,9},{9,8},{10,11... | collective-permute-start | bytes 2359304 | tf_op jit(solution)/shard_map/ppermute | solution.py:143
Sparse Core Ops, SparseCore 0:
  9.0 53.4 all-gather.3

commit v13 on v12

--- a/solution.py
+++ b/solution.py
@@ -32,13 +32,16 @@
     reader_rows = lax.dynamic_slice_in_dim(readers, first_group, group_local, 0)
     offsets = jnp.arange(CH, dtype=jnp.int32)
     live_mask = (offsets[None, :] < local_lengths[:, None]).reshape(-1)[:, None]
-    key_rows = jnp.where(
-        live_mask, jnp.dot(tokens, w_key, preferred_element_type=jnp.float32), 0.0
+    projected = jnp.dot(
+        tokens,
+        jnp.concatenate([w_key, w_value, w_query], axis=1),
+        preferred_element_type=jnp.float32,
+    )
+    key_rows = jnp.where(live_mask, projected[:, :local_width], 0.0).astype(jnp.bfloat16)
+    value_rows = jnp.where(
+        live_mask, projected[:, local_width : 2 * local_width], 0.0
     ).astype(jnp.bfloat16)
-    value_rows = jnp.where(
-        live_mask, jnp.dot(tokens, w_value, preferred_element_type=jnp.float32), 0.0
-    ).astype(jnp.bfloat16)
-    query_rows = jnp.dot(tokens, w_query, preferred_element_type=jnp.float32).astype(jnp.bfloat16)
+    query_rows = projected[:, 2 * local_width :].astype(jnp.bfloat16)
     query_groups = query_rows.reshape(group_local, CH, local_width)
     key_groups = key_rows.reshape(group_local, CH, local_width)
     value_groups = value_rows.reshape(group_local, CH, local_width)
@@ -85,10 +88,7 @@
     )
     prefix = (carried_in + own).astype(jnp.bfloat16)
 
-    length_float = lengths.astype(jnp.float32)
-    keys_read = local_lengths.astype(jnp.float32) + jnp.dot(
-        reader_rows.astype(jnp.float32), length_float, precision=lax.Precision.HIGHEST
-    )
+    keys_read = (local_lengths + jnp.sum(reader_rows * lengths[None, :], axis=1)).astype(jnp.float32)
     row_scale = lax.rsqrt(HS * keys_read)
     causal = offsets[:, None] >= offsets[None, :]
     pieces = []

time: 115 us -> 114 us (level)
  waiting for transfers between devices: 25.1 us -> 28.7 us
  matrix products: 30.2 us -> 27.4 us
  starting transfers between devices: 9.73 us -> 8.24 us
    dot_general x4 -> x1, matrix products: 12.2 us -> 8.16 us  [local(): jnp.dot(tokens, jnp.concatenate([w_key, w_value, w_query], axis=1), prefe...]
    all_gather x1, waiting for transfers between devices: 3.05 us -> 5.44 us  [local(): w_out_all = lax.all_gather(w_out, TP, axis=0, tiled=True)]
    dot_general x2, matrix products: 0.52 us -> 2.29 us  [local(): jnp.einsum('ctd,cde->cte', query_h, prefix[:, h], preferred_element_type=...]
    ppermute x1, starting transfers between devices: 2.78 us -> 1.12 us  [local(): sibling_first = lax.ppermute(first, 'tc', [(0, 1), (1, 0)])]
    ppermute x1, waiting for transfers between devices: 15.7 us -> 17.4 us  [local(): from_below = lax.ppermute(mixed, TP, shifted(1))]
    concatenate x0 -> x2, local copies, waits for them, and re-layouts: none -> 1.36 us  [local(): mixed = jnp.concatenate(pieces, axis=2)]
    convert_element_type x1, other arithmetic: 1.38 us -> 0.14 us  [local(): jnp.where(live_mask.reshape(group_local, CH, 1), mixed, 0.0)]
  transfers between devices with their start and end apart: 6 -> 6, of which waited for: 3 -> 3; matrix products, arithmetic and copies ran while one was open for 32% -> 31% of each run, Pallas kernels for 0% -> 0%
where the time goes in v13:
time: 114 us; the launch traced here: 113 us
  waiting for transfers between devices  28.7 us (25%)
  matrix products  27.4 us (24%)
  blocking collectives  24.2 us (21%)
  between operations  13.6 us (12%)
  starting transfers between devices  8.24 us (7%)
  local copies, waits for them, and re-layouts  6.64 us (6%)
  other arithmetic  4.44 us (4%)
    ppermute x1, waiting for transfers between devices, local(): from_below = lax.ppermute(mixed, TP, shifted(1))  17.4 us
    all_gather x1, blocking collectives, local(): row_tails = lax.all_gather(tail, 'sx', axis=0, tiled=False)  12.5 us
    all_gather x1, blocking collectives, local(): row_sums = lax.all_gather(row_sum, 'sy', axis=0, tiled=False)  11.7 us
    dot_general x1, matrix products, local(): jnp.dot(tokens, jnp.concatenate([w_key, w_value, w_query], axis=1), prefe...  8.16 us
    dot_general x5, matrix products, term(): return jnp.dot(block, rows_of(z, core), preferred_element_type=jnp.float32)  7.77 us
    all_gather x1, waiting for transfers between devices, local(): w_out_all = lax.all_gather(w_out, TP, axis=0, tiled=True)  5.44 us
    ppermute x1, waiting for transfers between devices, local(): lax.ppermute(jnp.where(core_at == 0, from_below, from_above), TP, forward)  5.2 us
    dot_general x2, matrix products, local(): jnp.einsum('cts,cse->cte', weights, value_groups[:, :, cut], preferred_el...  4.13 us
  transfers between devices with their start and end apart: 6, of which 3 were waited for; matrix products, arithmetic and copies ran while one was open for 31% of the time, Pallas kernels for 0%

profile of v13, /device:TPU:1, one launch (start us, length us, event | category | flops | bytes accessed | tf_op | source)
XLA Modules:
  0.0 113.3 jit_solution(15961163449225929678)
XLA Ops:
  6.5 0.7 all-gather.4.cloned.1.call-update
  7.3 0.9 multiply_reduce_fusion.3
  8.1 0.8 multiply_rsqrt_fusion
  9.0 8.2 %convolution_bitcast_fusion = bf16[1536,768]{0,1:T(8,128)(2,1)S(1)} fusion(bf16[1536,2048]{1,0:T(8,128)(2,1)} %param.13, bf16[2048,256]{1,0:T(8,128)(2,1)} %param.14, bf16[2048,256]{1,0:T(8,128)(2,1)} %param.16, bf16[2048,256]{1,0:T(8,128)(2,1)} %param.15), kind=kOutput, calls=%fused_computation | convolution fusion | flops 4841275392 | bytes 11796480 | tf_op jit(solution)/shard_map/dot_general | solution.py:35
  17.1 0.3 fusion.9
  17.4 0.3 copy.42
  17.7 0.3 copy.44
  18.0 0.7 fusion.61
  19.0 0.1 dynamic-slice_reduce_fusion.2
  19.2 0.1 dynamic-slice_reduce_fusion.1
  19.3 0.8 dynamic-slice_bitcast_fusion
  20.1 0.2 fusion.68
  20.3 0.1 convert_element_type.52
  20.4 0.9 dynamic-slice_reduce_fusion
  21.3 0.3 copy.41
  21.6 0.2 slice_reduce_fusion
  21.8 0.3 fusion.15
  22.1 0.3 fusion.16
  22.5 0.5 fusion.17
  23.0 12.5 %all-gather = f32[8,128,128]{2,1,0:T(8,128)S(1)} all-gather(f32[2,128,128]{2,1,0:T(8,128)S(1)} %bitcast.54), channel_id=2, replica_groups=mesh['sy'=4,'sx'=4,'tz'=4,'tc'=2] {'sx'}, dimensions={0}, use_global_device_ids=true | all-gather | bytes 655360 | tf_op jit(solution)/shard_map/all_gather | solution.py:67
  35.5 0.1 multiply_reduce_fusion.1
  35.7 11.7 %all-gather.1 = f32[8,128,128]{2,1,0:T(8,128)S(1)} all-gather(f32[2,128,128]{2,1,0:T(8,128)S(1)} %get-tuple-element.45), channel_id=3, replica_groups=mesh['sy'=4,'sx'=4,'tz'=4,'tc'=2] {'sy'}, dimensions={0}, use_global_device_ids=true | all-gather | bytes 655360 | tf_op jit(solution)/shard_map/all_gather | solution.py:75
  47.4 0.1 multiply_reduce_fusion
  47.5 1.4 %add_convert_fusion = bf16[12,2,128,128]{3,0,2,1:T(8,128)(2,1)S(1)} fusion(bf16[12,2,128,128]{3,2,0,1:T(8,128)(2,1)S(1)} %pad_maximum_fusion.1, f32[2,128,128]{2,1,0:T(8,128)S(1)} %add.150, f32[12]{0:T(128)S(1)} %convert_element_type.47, s32[192,192]{1,0:T(8,128)} %param.18, s32[]{:T(128)S(6)} %select_n.91), kind=kOutput, calls=%fused_computation.13 | convolution fusion | flops 10616976 | bytes 1712180 | tf_op jit(solution)/shard_map/ce,ehij->chij/dot_general | solution.py:83
  49.0 0.2 slice_bitcast_fusion.1
  49.2 1.1 %fusion.28 = f32[12,128,128]{2,1,0:T(8,128)} fusion(bf16[12,128,128]{2,0,1:T(8,128)(2,1)S(1)} %get-tuple-element.57, bf16[12,128,256]{2,1,0:T(8,128)(2,1)S(1)} %bitcast.48), kind=kOutput, calls=%fused_computation.51 | convolution fusion | flops 50331648 | bytes 1703936 | tf_op jit(solution)/shard_map/ctd,cde->cte/dot_general | solution.py:97
  50.3 2.5 %fusion.11 = bf16[12,128,128]{2,1,0:T(8,128)(2,1)} fusion(f32[12,128,128]{2,1,0:T(8,128)} %fusion.28, f32[12]{0:T(128)S(1)} %get-tuple-element.49, pred[128,128]{1,0:T(8,128)(4,1)S(1)} %iota_compare_fusion, bf16[12,128,256]{2,1,0:T(8,128)(2,1)S(1)} %bitcast.46, bf16[12,128,256]{2,1,0:T(8,128)(2,1)S(1)} %bitcast.42, bf16[12,128,256]{2,1,0:T(8,128)(2,1)S(1)} %bitcast.49), kind=kOutput, calls=%fused_computation.25 | convolution fusion | flops 101646336 | bytes 2376192 | tf_op jit(solution)/shard_map/cts,cse->cte/dot_general | solution.py:104
  52.8 1.2 %copy.51 = bf16[1536,128]{0,1:T(8,128)(2,1)S(1)} copy(bf16[1536,128]{1,0:T(8,128)(2,1)} %bitcast.56) | data formatting | bytes 786432 | tf_op jit(solution)/shard_map/concatenate | solution.py:108
  54.0 1.1 %fusion.26 = f32[12,128,128]{2,1,0:T(8,128)} fusion(bf16[12,128,128]{2,0,1:T(8,128)(2,1)S(1)} %get-tuple-element.58, bf16[12,128,256]{2,1,0:T(8,128)(2,1)S(1)} %bitcast.50), kind=kOutput, calls=%fused_computation.49 | convolution fusion | flops 50331648 | bytes 1703936 | tf_op jit(solution)/shard_map/ctd,cde->cte/dot_general | solution.py:97
  55.1 1.7 %fusion.12 = bf16[12,128,128]{2,1,0:T(8,128)(2,1)S(1)} fusion(f32[12,128,128]{2,1,0:T(8,128)} %fusion.26, f32[12]{0:T(128)S(1)} %get-tuple-element.49, pred[128,128]{1,0:T(8,128)(4,1)S(1)} %copy-done.1, bf16[12,128,256]{2,1,0:T(8,128)(2,1)S(1)} %bitcast.51, bf16[12,128,256]{2,1,0:T(8,128)(2,1)S(1)} %bitcast.47, bf16[12,128,256]{2,1,0:T(8,128)(2,1)S(1)} %bitcast.43), kind=kOutput, calls=%fused_computation.26 | convolution fusion | flops 101646336 | bytes 2376192 | tf_op jit(solution)/shard_map/cts,cse->cte/dot_general | solution.py:104
  56.8 0.2 copy.52
  57.0 0.1 fusion.10
  57.1 5.4 %all-gather.4.cloned.1.call-done = bf16[2048,2048]{1,0:T(8,128)(2,1)} async-done(((bf16[256,2048]{1,0:T(8,128)(2,1)}), bf16[2048,2048]{1,0:T(8,128)(2,1)}) %all-gather.4.cloned.1.call-update) | async-done | bytes 8388624 | tf_op jit(solution)/shard_map/all_gather | solution.py:29
  62.6 0.3 collective-permute-start
  62.9 2.3 %collective-permute-start.1 = (bf16[1536,256]{0,1:T(8,128)(2,1)S(1)}, bf16[1536,256]{0,1:T(8,128)(2,1)S(1)}, u32[]{:S(2)}, u32[]{:S(2)}) collective-permute-start(bf16[1536,256]{0,1:T(8,128)(2,1)S(1)} %fusion.10), channel_id=1, source_target_pairs={{0,6},{1,7},{2,0},{3,1},{4,2},{5,3},{6,4},{7,5},{8,14},{9,15},{10,... | collective-permute-start | bytes 2359304 | tf_op jit(solution)/shard_map/ppermute | solution.py:133
  65.2 17.4 %collective-permute-done = bf16[1536,256]{0,1:T(8,128)(2,1)S(1)} collective-permute-done((bf16[1536,256]{0,1:T(8,128)(2,1)S(1)}, bf16[1536,256]{0,1:T(8,128)(2,1)S(1)}, u32[]{:S(2)}, u32[]{:S(2)}) %collective-permute-start) | collective-permute-done | bytes 786464 | tf_op jit(solution)/shard_map/ppermute | solution.py:132
  82.6 1.6 %pad_maximum_fusion = bf16[1536,768]{0,1:T(8,128)(2,1)} fusion(bf16[1536,256]{0,1:T(8,128)(2,1)S(1)} %collective-permute-done.1, bf16[1536,256]{0,1:T(8,128)(2,1)S(1)} %collective-permute-done, bf16[1536,256]{0,1:T(8,128)(2,1)S(1)} %fusion.10), kind=kLoop, calls=%fused_computation.12 | loop fusion | flops 7077888 | bytes 4718592 | tf_op jit(solution)/shard_map/concatenate | solution.py:137
  84.2 1.1 collective-permute-start.2
  85.4 2.7 %collective-permute-start.3 = (bf16[1536,256]{0,1:T(8,128)(2,1)S(1)}, bf16[1536,256]{0,1:T(8,128)(2,1)}, u32[]{:S(2)}, u32[]{:S(2)}) collective-permute-start(bf16[1536,256]{0,1:T(8,128)(2,1)S(1)} %broadcast_select_fusion), channel_id=1, source_target_pairs={{0,2},{2,4},{4,6},{6,0},{1,7},{3,1},{5,3},{7,5},{8,10},{10,12},{12... | collective-permute-start | bytes 2359304 | tf_op jit(solution)/shard_map/ppermute | solution.py:142
  88.2 1.1 fusion.69
  89.2 1.3 %fusion.55 = f32[1536,256]{1,0:T(8,128)S(1)} fusion(bf16[1536,256]{0,1:T(8,128)(2,1)S(1)} %fusion.10, bf16[2048,2048]{1,0:T(8,128)(2,1)} %all-gather.4.cloned.1.call-done, s32[]{:T(128)S(6)} %select_n.99), kind=kOutput, calls=%fused_computation.74 | convolution fusion | flops 201326592 | bytes 2490372 | tf_op jit(solution)/shard_map/dot_general | solution.py:130
  90.6 1.3 %convolution_add_fusion.2 = f32[1536,256]{1,0:T(8,128)S(1)} fusion(f32[1536,256]{1,0:T(8,128)S(1)} %fusion.55, bf16[1536,256]{0,1:T(8,128)(2,1)S(1)} %collective-permute-done, bf16[2048,2048]{1,0:T(8,128)(2,1)} %all-gather.4.cloned.1.call-done, s32[]{:T(128)S(6)} %select_n.101, s32[]{:T(128)S(6)} %select_n.99), kind=kOutput, calls=%fused_computation.10 | convolution fusion | flops 201719808 | bytes 4063240 | tf_op jit(solution)/shard_map/dot_general | solution.py:130
  91.9 5.2 %collective-permute-done.3 = bf16[1536,256]{0,1:T(8,128)(2,1)} collective-permute-done((bf16[1536,256]{0,1:T(8,128)(2,1)S(1)}, bf16[1536,256]{0,1:T(8,128)(2,1)}, u32[]{:S(2)}, u32[]{:S(2)}) %collective-permute-start.3) | collective-permute-done | bytes 786464 | tf_op jit(solution)/shard_map/ppermute | solution.py:142
  97.1 1.7 %collective-permute-start.4 = (bf16[1536,256]{0,1:T(8,128)(2,1)}, bf16[1536,256]{0,1:T(8,128)(2,1)S(1)}, u32[]{:S(2)}, u32[]{:S(2)}) collective-permute-start(bf16[1536,256]{0,1:T(8,128)(2,1)} %collective-permute-done.3), channel_id=1, source_target_pairs={{0,1},{1,0},{2,3},{3,2},{4,5},{5,4},{6,7},{7,6},{8,9},{9,8},{10,11... | collective-permute-start | bytes 2359304 | tf_op jit(solution)/shard_map/ppermute | solution.py:143
  98.8 1.6 %fusion.51 = f32[1536,256]{1,0:T(8,128)S(1)} fusion(bf16[1536,256]{0,1:T(8,128)(2,1)} %collective-permute-done.3, bf16[2048,2048]{1,0:T(8,128)(2,1)} %all-gather.4.cloned.1.call-done, s32[]{:T(128)S(6)} %select_n.110, s32[]{:T(128)S(6)} %select_n.99), kind=kOutput, calls=%fused_computation.70 | convolution fusion | flops 201326592 | bytes 2490376 | tf_op jit(solution)/shard_map/dot_general | solution.py:130
  100.4 2.5 %fusion.20 = f32[1536,256]{1,0:T(8,128)S(1)} fusion(bf16[1536,768]{0,1:T(8,128)(2,1)} %collective-permute-done.2, bf16[256,256]{1,0:T(8,128)(2,1)S(1)} %get-tuple-element.52, bf16[256,256]{1,0:T(8,128)(2,1)S(1)} %get-tuple-element.53, bf16[256,256]{1,0:T(8,128)(2,1)S(1)} %get-tuple-element.51), kind=kOutput, calls=%fused_computation.43 | convolution fusion | flops 605159424 | bytes 4325376 | tf_op jit(solution)/shard_map/dot_general | solution.py:147
  102.9 1.3 %fusion.6 = f32[1536,256]{1,0:T(8,128)S(1)} fusion(f32[1536,256]{1,0:T(8,128)S(1)} %fusion.51, f32[1536,256]{1,0:T(8,128)S(1)} %fusion.20, f32[1536,256]{1,0:T(8,128)S(1)} %convolution_add_fusion.2, bf16[1536,256]{0,1:T(8,128)(2,1)S(1)} %collective-permute-done.1, bf16[2048,2048]{1,0:T(8,128)(2,1)} %all-gather.4.cloned.1.call-done, s32[]{:T(128)S(6)} %select_n.103, ...), kind=kOutput, calls=%fused_computation.9 | convolution fusion | flops 202506240 | bytes 7208968 | tf_op jit(solution)/shard_map/dot_general | solution.py:130
  104.3 2.2 %fusion.7 = bf16[1536,256]{1,0:T(8,128)(2,1)} fusion(f32[1536,256]{1,0:T(8,128)S(1)} %fusion.6, bf16[1536,256]{0,1:T(8,128)(2,1)S(1)} %collective-permute-done.4, bf16[2048,2048]{1,0:T(8,128)(2,1)} %all-gather.4.cloned.1.call-done, s32[]{:T(128)S(6)} %select_n.111, s32[]{:T(128)S(6)} %select_n.99), kind=kOutput, calls=%fused_computation.11 | convolution fusion | flops 202113024 | bytes 3276808 | tf_op jit(solution)/shard_map/dot_general | solution.py:130
  (22 shorter events, 0.7 us)
Async XLA Ops:
  6.5 56.0 %all-gather.4.cloned.1.call-start = ((), (), s32[]{:S(2)}) async-start(), calls=%async_computation | async-start | bytes 9437184 | tf_op jit(solution)/shard_map/all_gather | solution.py:29
  47.5 2.8 %copy-start = (pred[128,128]{1,0:T(8,128)(4,1)}, pred[128,128]{1,0:T(8,128)(4,1)S(1)}, u32[]{:S(2)}) copy-start(pred[128,128]{1,0:T(8,128)(4,1)S(1)} %iota_compare_fusion) | copy-start | bytes 49156
  52.8 2.3 %copy-start.1 = (pred[128,128]{1,0:T(8,128)(4,1)S(1)}, pred[128,128]{1,0:T(8,128)(4,1)}, u32[]{:S(2)}) copy-start(pred[128,128]{1,0:T(8,128)(4,1)} %copy-done) | copy-start | bytes 49156
  62.6 20.0 %collective-permute-start = (bf16[1536,256]{0,1:T(8,128)(2,1)S(1)}, bf16[1536,256]{0,1:T(8,128)(2,1)S(1)}, u32[]{:S(2)}, u32[]{:S(2)}) collective-permute-start(bf16[1536,256]{0,1:T(8,128)(2,1)S(1)} %fusion.10), channel_id=1, source_target_pairs={{0,2},{1,3},{2,4},{3,5},{4,6},{5,7},{6,0},{7,1},{8,10},{9,11},{10,... | collective-permute-start | bytes 2359304 | tf_op jit(solution)/shard_map/ppermute | solution.py:132
  62.9 19.7 %collective-permute-start.1 = (bf16[1536,256]{0,1:T(8,128)(2,1)S(1)}, bf16[1536,256]{0,1:T(8,128)(2,1)S(1)}, u32[]{:S(2)}, u32[]{:S(2)}) collective-permute-start(bf16[1536,256]{0,1:T(8,128)(2,1)S(1)} %fusion.10), channel_id=1, source_target_pairs={{0,6},{1,7},{2,0},{3,1},{4,2},{5,3},{6,4},{7,5},{8,14},{9,15},{10,... | collective-permute-start | bytes 2359304 | tf_op jit(solution)/shard_map/ppermute | solution.py:133
  84.2 16.1 %collective-permute-start.2 = (bf16[1536,768]{0,1:T(8,128)(2,1)}, bf16[1536,768]{0,1:T(8,128)(2,1)}, u32[]{:S(2)}, u32[]{:S(2)}) collective-permute-start(bf16[1536,768]{0,1:T(8,128)(2,1)} %pad_maximum_fusion), channel_id=1, source_target_pairs={{0,1},{1,0},{2,3},{3,2},{4,5},{5,4},{6,7},{7,6},{8,9},{9,8},{10,11... | collective-permute-start | bytes 7077896 | tf_op jit(solution)/shard_map/ppermute | solution.py:138
  85.4 11.7 %collective-permute-start.3 = (bf16[1536,256]{0,1:T(8,128)(2,1)S(1)}, bf16[1536,256]{0,1:T(8,128)(2,1)}, u32[]{:S(2)}, u32[]{:S(2)}) collective-permute-start(bf16[1536,256]{0,1:T(8,128)(2,1)S(1)} %broadcast_select_fusion), channel_id=1, source_target_pairs={{0,2},{2,4},{4,6},{6,0},{1,7},{3,1},{5,3},{7,5},{8,10},{10,12},{12... | collective-permute-start | bytes 2359304 | tf_op jit(solution)/shard_map/ppermute | solution.py:142
  97.1 7.1 %collective-permute-start.4 = (bf16[1536,256]{0,1:T(8,128)(2,1)}, bf16[1536,256]{0,1:T(8,128)(2,1)S(1)}, u32[]{:S(2)}, u32[]{:S(2)}) collective-permute-start(bf16[1536,256]{0,1:T(8,128)(2,1)} %collective-permute-done.3), channel_id=1, source_target_pairs={{0,1},{1,0},{2,3},{3,2},{4,5},{5,4},{6,7},{7,6},{8,9},{9,8},{10,11... | collective-permute-start | bytes 2359304 | tf_op jit(solution)/shard_map/ppermute | solution.py:143
Sparse Core Ops, SparseCore 0:
  9.0 53.4 all-gather.3

commit v14 on v13

--- a/solution.py
+++ b/solution.py
@@ -2,6 +2,7 @@
 import jax.numpy as jnp
 from jax import lax
 from jax.sharding import PartitionSpec as P
+
 
 HS = 128
 CH = 128
@@ -9,11 +10,10 @@
 PAIR = 2
 
 
-SEQ = ("sy", "sx")
 TP = ("tz", "tc")
 
 
-def local(tokens, w_query, w_key, w_value, w_out, readers, lengths):
+def layer(tokens, w_query, w_key, w_value, w_out, readers, lengths):
     group_local = tokens.shape[0] // CH
     local_width = w_query.shape[1]
     head_dev = local_width // HS
@@ -109,7 +109,6 @@
     mixed = jnp.where(live_mask.reshape(group_local, CH, 1), mixed, 0.0).astype(jnp.bfloat16)
     mixed = mixed.reshape(group_local * CH, local_width)
 
-    mixed, w_out_all = lax.optimization_barrier((mixed, w_out_all))
     chip_at = lax.axis_index("tz")
     chip_count = tp_count // PAIR
     column = tp_index * local_width
@@ -131,6 +130,7 @@
 
     from_below = lax.ppermute(mixed, TP, shifted(1))
     from_above = lax.ppermute(mixed, TP, shifted(chip_count - 1))
+    from_below, from_above, w_out_all = lax.optimization_barrier((from_below, from_above, w_out_all))
     below = (chip_at - 1) % chip_count
     above = (chip_at + 1) % chip_count
     across = (chip_at + 2) % chip_count
@@ -163,7 +163,7 @@
     seq = ("sy", "sx")
     tp = ("tz", "tc")
     return jax.shard_map(
-        local,
+        layer,
         mesh=split,
         in_specs=(
             P(seq, None),

time: 114 us -> 110 us (0.965)
  waiting for transfers between devices: 28.7 us -> 20 us
  starting transfers between devices: 8.24 us -> 12.7 us
    all_gather x1, waiting for transfers between devices: 5.44 us -> 0.01 us  [layer(): w_out_all = lax.all_gather(w_out, TP, axis=0, tiled=True)]
    ppermute x5, starting transfers between devices: 8.24 us -> 12.7 us  [the longest x1 4.38 us: layer(): sibling_first = lax.ppermute(first, 'tc', [(0, 1), (1, 0)])]
    ppermute x5, waiting for transfers between devices: 22.6 us -> 19.2 us  [the longest x1 14 us: layer(): from_below = lax.ppermute(mixed, TP, shifted(1))]
  transfers between devices with their start and end apart: 6 -> 6, of which waited for: 3 -> 2; matrix products, arithmetic and copies ran while one was open for 31% -> 32% of each run, Pallas kernels for 0% -> 0%
where the time goes in v14:
time: 110 us; the launch traced here: 109 us
  matrix products  27.4 us (25%)
  blocking collectives  24.2 us (22%)
  waiting for transfers between devices  20 us (18%)
  between operations  13.6 us (12%)
  starting transfers between devices  12.7 us (12%)
  local copies, waits for them, and re-layouts  6.64 us (6%)
  other arithmetic  4.45 us (4%)
    ppermute x1, waiting for transfers between devices, layer(): from_below = lax.ppermute(mixed, TP, shifted(1))  14 us
    all_gather x1, blocking collectives, layer(): row_tails = lax.all_gather(tail, 'sx', axis=0, tiled=False)  12.5 us
    all_gather x1, blocking collectives, layer(): row_sums = lax.all_gather(row_sum, 'sy', axis=0, tiled=False)  11.7 us
    dot_general x1, matrix products, layer(): jnp.dot(tokens, jnp.concatenate([w_key, w_value, w_query], axis=1), prefe...  8.16 us
    dot_general x5, matrix products, term(): return jnp.dot(block, rows_of(z, core), preferred_element_type=jnp.float32)  7.77 us
    ppermute x1, waiting for transfers between devices, layer(): lax.ppermute(jnp.where(core_at == 0, from_below, from_above), TP, forward)  5.2 us
    ppermute x1, starting transfers between devices, layer(): sibling_first = lax.ppermute(first, 'tc', [(0, 1), (1, 0)])  4.38 us
    dot_general x2, matrix products, layer(): jnp.einsum('cts,cse->cte', weights, value_groups[:, :, cut], preferred_el...  4.13 us
  transfers between devices with their start and end apart: 6, of which 2 were waited for; matrix products, arithmetic and copies ran while one was open for 32% of the time, Pallas kernels for 0%

profile of v14, /device:TPU:1, one launch (start us, length us, event | category | flops | bytes accessed | tf_op | source)
XLA Modules:
  0.0 109.0 jit_solution(17178478322500657852)
XLA Ops:
  6.5 0.7 all-gather.4.cloned.1.call-update
  7.3 0.9 multiply_reduce_fusion.3
  8.1 0.8 multiply_rsqrt_fusion
  9.0 8.2 %convolution_bitcast_fusion = bf16[1536,768]{0,1:T(8,128)(2,1)S(1)} fusion(bf16[1536,2048]{1,0:T(8,128)(2,1)} %param.13, bf16[2048,256]{1,0:T(8,128)(2,1)} %param.14, bf16[2048,256]{1,0:T(8,128)(2,1)} %param.16, bf16[2048,256]{1,0:T(8,128)(2,1)} %param.15), kind=kOutput, calls=%fused_computation | convolution fusion | flops 4841275392 | bytes 11796480 | tf_op jit(solution)/shard_map/dot_general | solution.py:35
  17.1 0.3 fusion.9
  17.4 0.3 copy.42
  17.7 0.3 copy.44
  18.0 0.7 fusion.61
  19.0 0.1 dynamic-slice_reduce_fusion.2
  19.2 0.1 dynamic-slice_reduce_fusion.1
  19.3 0.8 dynamic-slice_bitcast_fusion
  20.1 0.2 fusion.68
  20.3 0.1 convert_element_type.52
  20.4 0.9 dynamic-slice_reduce_fusion
  21.3 0.3 copy.41
  21.6 0.2 slice_reduce_fusion
  21.8 0.3 fusion.15
  22.1 0.3 fusion.16
  22.5 0.5 fusion.17
  23.0 12.5 %all-gather = f32[8,128,128]{2,1,0:T(8,128)S(1)} all-gather(f32[2,128,128]{2,1,0:T(8,128)S(1)} %bitcast.54), channel_id=2, replica_groups=mesh['sy'=4,'sx'=4,'tz'=4,'tc'=2] {'sx'}, dimensions={0}, use_global_device_ids=true | all-gather | bytes 655360 | tf_op jit(solution)/shard_map/all_gather | solution.py:67
  35.5 0.1 multiply_reduce_fusion.1
  35.7 11.7 %all-gather.1 = f32[8,128,128]{2,1,0:T(8,128)S(1)} all-gather(f32[2,128,128]{2,1,0:T(8,128)S(1)} %get-tuple-element.47), channel_id=3, replica_groups=mesh['sy'=4,'sx'=4,'tz'=4,'tc'=2] {'sy'}, dimensions={0}, use_global_device_ids=true | all-gather | bytes 655360 | tf_op jit(solution)/shard_map/all_gather | solution.py:75
  47.4 0.1 multiply_reduce_fusion
  47.5 1.4 %add_convert_fusion = bf16[12,2,128,128]{3,0,2,1:T(8,128)(2,1)S(1)} fusion(bf16[12,2,128,128]{3,2,0,1:T(8,128)(2,1)S(1)} %pad_maximum_fusion.1, f32[2,128,128]{2,1,0:T(8,128)S(1)} %add.150, f32[12]{0:T(128)S(1)} %convert_element_type.47, s32[192,192]{1,0:T(8,128)} %param.18, s32[]{:T(128)S(6)} %select_n.91), kind=kOutput, calls=%fused_computation.13 | convolution fusion | flops 10616976 | bytes 1712180 | tf_op jit(solution)/shard_map/ce,ehij->chij/dot_general | solution.py:83
  49.0 0.2 slice_bitcast_fusion.1
  49.2 1.1 %fusion.28 = f32[12,128,128]{2,1,0:T(8,128)} fusion(bf16[12,128,128]{2,0,1:T(8,128)(2,1)S(1)} %get-tuple-element.59, bf16[12,128,256]{2,1,0:T(8,128)(2,1)S(1)} %bitcast.48), kind=kOutput, calls=%fused_computation.51 | convolution fusion | flops 50331648 | bytes 1703936 | tf_op jit(solution)/shard_map/ctd,cde->cte/dot_general | solution.py:97
  50.3 2.5 %fusion.11 = bf16[12,128,128]{2,1,0:T(8,128)(2,1)} fusion(f32[12,128,128]{2,1,0:T(8,128)} %fusion.28, f32[12]{0:T(128)S(1)} %get-tuple-element.51, pred[128,128]{1,0:T(8,128)(4,1)S(1)} %iota_compare_fusion, bf16[12,128,256]{2,1,0:T(8,128)(2,1)S(1)} %bitcast.46, bf16[12,128,256]{2,1,0:T(8,128)(2,1)S(1)} %bitcast.42, bf16[12,128,256]{2,1,0:T(8,128)(2,1)S(1)} %bitcast.49), kind=kOutput, calls=%fused_computation.25 | convolution fusion | flops 101646336 | bytes 2376192 | tf_op jit(solution)/shard_map/cts,cse->cte/dot_general | solution.py:104
  52.8 1.2 %copy.51 = bf16[1536,128]{0,1:T(8,128)(2,1)S(1)} copy(bf16[1536,128]{1,0:T(8,128)(2,1)} %bitcast.56) | data formatting | bytes 786432 | tf_op jit(solution)/shard_map/concatenate | solution.py:108
  54.0 1.1 %fusion.26 = f32[12,128,128]{2,1,0:T(8,128)} fusion(bf16[12,128,128]{2,0,1:T(8,128)(2,1)S(1)} %get-tuple-element.60, bf16[12,128,256]{2,1,0:T(8,128)(2,1)S(1)} %bitcast.50), kind=kOutput, calls=%fused_computation.49 | convolution fusion | flops 50331648 | bytes 1703936 | tf_op jit(solution)/shard_map/ctd,cde->cte/dot_general | solution.py:97
  55.1 1.7 %fusion.12 = bf16[12,128,128]{2,1,0:T(8,128)(2,1)S(1)} fusion(f32[12,128,128]{2,1,0:T(8,128)} %fusion.26, f32[12]{0:T(128)S(1)} %get-tuple-element.51, pred[128,128]{1,0:T(8,128)(4,1)S(1)} %copy-done.1, bf16[12,128,256]{2,1,0:T(8,128)(2,1)S(1)} %bitcast.51, bf16[12,128,256]{2,1,0:T(8,128)(2,1)S(1)} %bitcast.47, bf16[12,128,256]{2,1,0:T(8,128)(2,1)S(1)} %bitcast.43), kind=kOutput, calls=%fused_computation.26 | convolution fusion | flops 101646336 | bytes 2376192 | tf_op jit(solution)/shard_map/cts,cse->cte/dot_general | solution.py:104
  56.8 0.2 copy.52
  57.0 0.1 fusion.10
  57.1 0.5 collective-permute-start
  57.6 3.4 %collective-permute-start.1 = (bf16[1536,256]{0,1:T(8,128)(2,1)S(1)}, bf16[1536,256]{0,1:T(8,128)(2,1)S(1)}, u32[]{:S(2)}, u32[]{:S(2)}) collective-permute-start(bf16[1536,256]{0,1:T(8,128)(2,1)S(1)} %fusion.10), channel_id=1, source_target_pairs={{0,6},{1,7},{2,0},{3,1},{4,2},{5,3},{6,4},{7,5},{8,14},{9,15},{10,... | collective-permute-start | bytes 2359304 | tf_op jit(solution)/shard_map/ppermute | solution.py:132
  61.0 14.0 %collective-permute-done = bf16[1536,256]{0,1:T(8,128)(2,1)S(1)} collective-permute-done((bf16[1536,256]{0,1:T(8,128)(2,1)S(1)}, bf16[1536,256]{0,1:T(8,128)(2,1)S(1)}, u32[]{:S(2)}, u32[]{:S(2)}) %collective-permute-start) | collective-permute-done | bytes 786464 | tf_op jit(solution)/shard_map/ppermute | solution.py:131
  75.1 1.6 %pad_maximum_fusion = bf16[1536,768]{0,1:T(8,128)(2,1)} fusion(bf16[1536,256]{0,1:T(8,128)(2,1)S(1)} %collective-permute-done.1, bf16[1536,256]{0,1:T(8,128)(2,1)S(1)} %collective-permute-done, bf16[1536,256]{0,1:T(8,128)(2,1)S(1)} %fusion.10), kind=kLoop, calls=%fused_computation.12 | loop fusion | flops 7077888 | bytes 4718592 | tf_op jit(solution)/shard_map/concatenate | solution.py:137
  76.7 4.4 %collective-permute-start.2 = (bf16[1536,768]{0,1:T(8,128)(2,1)}, bf16[1536,768]{0,1:T(8,128)(2,1)}, u32[]{:S(2)}, u32[]{:S(2)}) collective-permute-start(bf16[1536,768]{0,1:T(8,128)(2,1)} %pad_maximum_fusion), channel_id=1, source_target_pairs={{0,1},{1,0},{2,3},{3,2},{4,5},{5,4},{6,7},{7,6},{8,9},{9,8},{10,11... | collective-permute-start | bytes 7077896 | tf_op jit(solution)/shard_map/ppermute | solution.py:138
  81.1 0.1 broadcast_select_fusion
  81.1 2.8 %collective-permute-start.3 = (bf16[1536,256]{0,1:T(8,128)(2,1)S(1)}, bf16[1536,256]{0,1:T(8,128)(2,1)}, u32[]{:S(2)}, u32[]{:S(2)}) collective-permute-start(bf16[1536,256]{0,1:T(8,128)(2,1)S(1)} %broadcast_select_fusion), channel_id=1, source_target_pairs={{0,2},{2,4},{4,6},{6,0},{1,7},{3,1},{5,3},{7,5},{8,10},{10,12},{12... | collective-permute-start | bytes 2359304 | tf_op jit(solution)/shard_map/ppermute | solution.py:142
  84.0 1.1 fusion.69
  85.0 1.3 %fusion.54 = f32[1536,256]{1,0:T(8,128)S(1)} fusion(bf16[1536,256]{0,1:T(8,128)(2,1)S(1)} %collective-permute-done, bf16[2048,2048]{1,0:T(8,128)(2,1)} %all-gather.4.cloned.1.call-done, s32[]{:T(128)S(6)} %select_n.101, s32[]{:T(128)S(6)} %select_n.99), kind=kOutput, calls=%fused_computation.73 | convolution fusion | flops 201326592 | bytes 2490376 | tf_op jit(solution)/shard_map/dot_general | solution.py:129
  86.3 1.3 %convolution_add_fusion.2 = f32[1536,256]{1,0:T(8,128)S(1)} fusion(f32[1536,256]{1,0:T(8,128)S(1)} %fusion.54, bf16[1536,256]{0,1:T(8,128)(2,1)S(1)} %fusion.10, bf16[2048,2048]{1,0:T(8,128)(2,1)} %all-gather.4.cloned.1.call-done, s32[]{:T(128)S(6)} %select_n.99), kind=kOutput, calls=%fused_computation.10 | convolution fusion | flops 201719808 | bytes 4063236 | tf_op jit(solution)/shard_map/dot_general | solution.py:129
  87.7 5.2 %collective-permute-done.3 = bf16[1536,256]{0,1:T(8,128)(2,1)} collective-permute-done((bf16[1536,256]{0,1:T(8,128)(2,1)S(1)}, bf16[1536,256]{0,1:T(8,128)(2,1)}, u32[]{:S(2)}, u32[]{:S(2)}) %collective-permute-start.3) | collective-permute-done | bytes 786464 | tf_op jit(solution)/shard_map/ppermute | solution.py:142
  92.9 1.6 %collective-permute-start.4 = (bf16[1536,256]{0,1:T(8,128)(2,1)}, bf16[1536,256]{0,1:T(8,128)(2,1)S(1)}, u32[]{:S(2)}, u32[]{:S(2)}) collective-permute-start(bf16[1536,256]{0,1:T(8,128)(2,1)} %collective-permute-done.3), channel_id=1, source_target_pairs={{0,1},{1,0},{2,3},{3,2},{4,5},{5,4},{6,7},{7,6},{8,9},{9,8},{10,11... | collective-permute-start | bytes 2359304 | tf_op jit(solution)/shard_map/ppermute | solution.py:143
  94.5 1.6 %fusion.51 = f32[1536,256]{1,0:T(8,128)S(1)} fusion(bf16[1536,256]{0,1:T(8,128)(2,1)} %collective-permute-done.3, bf16[2048,2048]{1,0:T(8,128)(2,1)} %all-gather.4.cloned.1.call-done, s32[]{:T(128)S(6)} %select_n.110, s32[]{:T(128)S(6)} %select_n.99), kind=kOutput, calls=%fused_computation.70 | convolution fusion | flops 201326592 | bytes 2490376 | tf_op jit(solution)/shard_map/dot_general | solution.py:129
  96.1 2.5 %fusion.20 = f32[1536,256]{1,0:T(8,128)S(1)} fusion(bf16[1536,768]{0,1:T(8,128)(2,1)} %collective-permute-done.2, bf16[256,256]{1,0:T(8,128)(2,1)S(1)} %get-tuple-element.54, bf16[256,256]{1,0:T(8,128)(2,1)S(1)} %get-tuple-element.55, bf16[256,256]{1,0:T(8,128)(2,1)S(1)} %get-tuple-element.53), kind=kOutput, calls=%fused_computation.43 | convolution fusion | flops 605159424 | bytes 4325376 | tf_op jit(solution)/shard_map/dot_general | solution.py:147
  98.6 1.3 %fusion.6 = f32[1536,256]{1,0:T(8,128)S(1)} fusion(f32[1536,256]{1,0:T(8,128)S(1)} %fusion.51, f32[1536,256]{1,0:T(8,128)S(1)} %fusion.20, f32[1536,256]{1,0:T(8,128)S(1)} %convolution_add_fusion.2, bf16[1536,256]{0,1:T(8,128)(2,1)S(1)} %collective-permute-done.1, bf16[2048,2048]{1,0:T(8,128)(2,1)} %all-gather.4.cloned.1.call-done, s32[]{:T(128)S(6)} %select_n.103, ...), kind=kOutput, calls=%fused_computation.9 | convolution fusion | flops 202506240 | bytes 7208968 | tf_op jit(solution)/shard_map/dot_general | solution.py:129
  100.0 2.2 %fusion.7 = bf16[1536,256]{1,0:T(8,128)(2,1)} fusion(f32[1536,256]{1,0:T(8,128)S(1)} %fusion.6, bf16[1536,256]{0,1:T(8,128)(2,1)S(1)} %collective-permute-done.4, bf16[2048,2048]{1,0:T(8,128)(2,1)} %all-gather.4.cloned.1.call-done, s32[]{:T(128)S(6)} %select_n.111, s32[]{:T(128)S(6)} %select_n.99), kind=kOutput, calls=%fused_computation.11 | convolution fusion | flops 202113024 | bytes 3276808 | tf_op jit(solution)/shard_map/dot_general | solution.py:129
  (22 shorter events, 0.6 us)
Async XLA Ops:
  6.5 68.5 %all-gather.4.cloned.1.call-start = ((), (), s32[]{:S(2)}) async-start(), calls=%async_computation | async-start | bytes 9437184 | tf_op jit(solution)/shard_map/all_gather | solution.py:29
  47.5 2.8 %copy-start = (pred[128,128]{1,0:T(8,128)(4,1)}, pred[128,128]{1,0:T(8,128)(4,1)S(1)}, u32[]{:S(2)}) copy-start(pred[128,128]{1,0:T(8,128)(4,1)S(1)} %iota_compare_fusion) | copy-start | bytes 49156
  52.8 2.3 %copy-start.1 = (pred[128,128]{1,0:T(8,128)(4,1)S(1)}, pred[128,128]{1,0:T(8,128)(4,1)}, u32[]{:S(2)}) copy-start(pred[128,128]{1,0:T(8,128)(4,1)} %copy-done) | copy-start | bytes 49156
  57.1 17.9 %collective-permute-start = (bf16[1536,256]{0,1:T(8,128)(2,1)S(1)}, bf16[1536,256]{0,1:T(8,128)(2,1)S(1)}, u32[]{:S(2)}, u32[]{:S(2)}) collective-permute-start(bf16[1536,256]{0,1:T(8,128)(2,1)S(1)} %fusion.10), channel_id=1, source_target_pairs={{0,2},{1,3},{2,4},{3,5},{4,6},{5,7},{6,0},{7,1},{8,10},{9,11},{10,... | collective-permute-start | bytes 2359304 | tf_op jit(solution)/shard_map/ppermute | solution.py:131
  57.6 17.5 %collective-permute-start.1 = (bf16[1536,256]{0,1:T(8,128)(2,1)S(1)}, bf16[1536,256]{0,1:T(8,128)(2,1)S(1)}, u32[]{:S(2)}, u32[]{:S(2)}) collective-permute-start(bf16[1536,256]{0,1:T(8,128)(2,1)S(1)} %fusion.10), channel_id=1, source_target_pairs={{0,6},{1,7},{2,0},{3,1},{4,2},{5,3},{6,4},{7,5},{8,14},{9,15},{10,... | collective-permute-start | bytes 2359304 | tf_op jit(solution)/shard_map/ppermute | solution.py:132
  76.7 19.4 %collective-permute-start.2 = (bf16[1536,768]{0,1:T(8,128)(2,1)}, bf16[1536,768]{0,1:T(8,128)(2,1)}, u32[]{:S(2)}, u32[]{:S(2)}) collective-permute-start(bf16[1536,768]{0,1:T(8,128)(2,1)} %pad_maximum_fusion), channel_id=1, source_target_pairs={{0,1},{1,0},{2,3},{3,2},{4,5},{5,4},{6,7},{7,6},{8,9},{9,8},{10,11... | collective-permute-start | bytes 7077896 | tf_op jit(solution)/shard_map/ppermute | solution.py:138
  81.1 11.8 %collective-permute-start.3 = (bf16[1536,256]{0,1:T(8,128)(2,1)S(1)}, bf16[1536,256]{0,1:T(8,128)(2,1)}, u32[]{:S(2)}, u32[]{:S(2)}) collective-permute-start(bf16[1536,256]{0,1:T(8,128)(2,1)S(1)} %broadcast_select_fusion), channel_id=1, source_target_pairs={{0,2},{2,4},{4,6},{6,0},{1,7},{3,1},{5,3},{7,5},{8,10},{10,12},{12... | collective-permute-start | bytes 2359304 | tf_op jit(solution)/shard_map/ppermute | solution.py:142
  92.9 7.1 %collective-permute-start.4 = (bf16[1536,256]{0,1:T(8,128)(2,1)}, bf16[1536,256]{0,1:T(8,128)(2,1)S(1)}, u32[]{:S(2)}, u32[]{:S(2)}) collective-permute-start(bf16[1536,256]{0,1:T(8,128)(2,1)} %collective-permute-done.3), channel_id=1, source_target_pairs={{0,1},{1,0},{2,3},{3,2},{4,5},{5,4},{6,7},{7,6},{8,9},{9,8},{10,11... | collective-permute-start | bytes 2359304 | tf_op jit(solution)/shard_map/ppermute | solution.py:143
Sparse Core Ops, SparseCore 0:
  9.0 53.4 all-gather.3

commit v15 on v14

--- a/solution.py
+++ b/solution.py
@@ -130,11 +130,12 @@
 
     from_below = lax.ppermute(mixed, TP, shifted(1))
     from_above = lax.ppermute(mixed, TP, shifted(chip_count - 1))
+    mate = lax.ppermute(mixed, "tc", [(0, 1), (1, 0)])
     from_below, from_above, w_out_all = lax.optimization_barrier((from_below, from_above, w_out_all))
     below = (chip_at - 1) % chip_count
     above = (chip_at + 1) % chip_count
     across = (chip_at + 2) % chip_count
-    first = jnp.concatenate([mixed, from_below, from_above], axis=1)
+    first = jnp.concatenate([from_below, from_above], axis=1)
     sibling_first = lax.ppermute(first, "tc", [(0, 1), (1, 0)])
     forward = [
         (z * PAIR, ((z + 1) % chip_count) * PAIR) for z in range(chip_count)
@@ -144,11 +145,10 @@
     other = 1 - core_at
     total = term(mixed, chip_at, core_at)
     total = total + term(from_below, below, core_at) + term(from_above, above, core_at)
+    total = total + term(mate, chip_at, other)
     total = total + jnp.dot(
         sibling_first,
-        jnp.concatenate(
-            [rows_of(chip_at, other), rows_of(below, other), rows_of(above, other)], axis=0
-        ),
+        jnp.concatenate([rows_of(below, other), rows_of(above, other)], axis=0),
         preferred_element_type=jnp.float32,
     )
     total = total + term(relayed, across, core_at) + term(sibling_relayed, across, other)

time: 110 us -> 106 us (0.964)
  waiting for transfers between devices: 20 us -> 14.6 us
  starting transfers between devices: 12.7 us -> 16.8 us
  other arithmetic: 4.45 us -> 2.92 us
    ppermute x1, waiting for transfers between devices: 14 us -> 9.94 us  [layer(): from_below = lax.ppermute(mixed, TP, shifted(1))]
    ppermute x0 -> x1, starting transfers between devices: none -> 4.09 us  [layer(): mate = lax.ppermute(mixed, 'tc', [(0, 1), (1, 0)])]
    dot_general x1, matrix products: 2.49 us -> 0.61 us  [layer(): jnp.dot(sibling_first, jnp.concatenate([rows_of(below, other), rows_of(ab...]
    concatenate x1, other arithmetic: 1.62 us -> 0.1 us  [layer(): first = jnp.concatenate([from_below, from_above], axis=1)]
    dot_general x5 -> x6, matrix products: 7.77 us -> 9.05 us  [term(): return jnp.dot(block, rows_of(z, core), preferred_element_type=jnp.float32)]
    ppermute x1, waiting for transfers between devices: 5.2 us -> 3.94 us  [layer(): lax.ppermute(jnp.where(core_at == 0, from_below, from_above), TP, forward)]
  transfers between devices with their start and end apart: 6 -> 7, of which waited for: 2 -> 2; matrix products, arithmetic and copies ran while one was open for 32% -> 32% of each run, Pallas kernels for 0% -> 0%
where the time goes in v15:
time: 106 us
  matrix products  26.9 us (25%)
  blocking collectives  24.2 us (23%)
  starting transfers between devices  16.8 us (16%)
  waiting for transfers between devices  14.6 us (14%)
  between operations  13.6 us (13%)
  local copies, waits for them, and re-layouts  6.58 us (6%)
  other arithmetic  2.92 us (3%)
    all_gather x1, blocking collectives, layer(): row_tails = lax.all_gather(tail, 'sx', axis=0, tiled=False)  12.5 us
    all_gather x1, blocking collectives, layer(): row_sums = lax.all_gather(row_sum, 'sy', axis=0, tiled=False)  11.7 us
    ppermute x1, waiting for transfers between devices, layer(): from_below = lax.ppermute(mixed, TP, shifted(1))  9.94 us
    dot_general x6, matrix products, term(): return jnp.dot(block, rows_of(z, core), preferred_element_type=jnp.float32)  9.05 us
    dot_general x1, matrix products, layer(): jnp.dot(tokens, jnp.concatenate([w_key, w_value, w_query], axis=1), prefe...  8.2 us
    ppermute x1, starting transfers between devices, layer(): sibling_first = lax.ppermute(first, 'tc', [(0, 1), (1, 0)])  4.46 us
    dot_general x2, matrix products, layer(): jnp.einsum('cts,cse->cte', weights, value_groups[:, :, cut], preferred_el...  4.12 us
    ppermute x1, starting transfers between devices, layer(): mate = lax.ppermute(mixed, 'tc', [(0, 1), (1, 0)])  4.09 us
  transfers between devices with their start and end apart: 7, of which 2 were waited for; matrix products, arithmetic and copies ran while one was open for 32% of the time, Pallas kernels for 0%

profile of v15, /device:TPU:1, one launch (start us, length us, event | category | flops | bytes accessed | tf_op | source)
XLA Modules:
  0.0 105.6 jit_solution(12424245028282038227)
XLA Ops:
  6.5 0.7 all-gather.4.cloned.1.call-update
  7.3 0.9 multiply_reduce_fusion.3
  8.1 0.8 multiply_rsqrt_fusion
  9.0 8.2 %convolution_bitcast_fusion = bf16[1536,768]{0,1:T(8,128)(2,1)S(1)} fusion(bf16[1536,2048]{1,0:T(8,128)(2,1)} %param.13, bf16[2048,256]{1,0:T(8,128)(2,1)} %param.14, bf16[2048,256]{1,0:T(8,128)(2,1)} %param.16, bf16[2048,256]{1,0:T(8,128)(2,1)} %param.15), kind=kOutput, calls=%fused_computation | convolution fusion | flops 4841275392 | bytes 11796480 | tf_op jit(solution)/shard_map/dot_general | solution.py:35
  17.2 0.3 fusion.10
  17.5 0.3 copy.42
  17.7 0.3 copy.44
  18.0 0.7 fusion.62
  19.1 0.1 dynamic-slice_reduce_fusion.2
  19.2 0.1 dynamic-slice_reduce_fusion.1
  19.3 0.8 dynamic-slice_bitcast_fusion
  20.1 0.2 fusion.69
  20.4 0.9 dynamic-slice_reduce_fusion
  21.3 0.3 copy.41
  21.6 0.2 slice_reduce_fusion
  21.8 0.3 fusion.16
  22.1 0.3 fusion.17
  22.5 0.5 fusion.18
  23.1 12.5 %all-gather = f32[8,128,128]{2,1,0:T(8,128)S(1)} all-gather(f32[2,128,128]{2,1,0:T(8,128)S(1)} %bitcast.55), channel_id=2, replica_groups=mesh['sy'=4,'sx'=4,'tz'=4,'tc'=2] {'sx'}, dimensions={0}, use_global_device_ids=true | all-gather | bytes 655360 | tf_op jit(solution)/shard_map/all_gather | solution.py:67
  35.6 0.2 multiply_reduce_fusion.1
  35.7 11.7 %all-gather.1 = f32[8,128,128]{2,1,0:T(8,128)S(1)} all-gather(f32[2,128,128]{2,1,0:T(8,128)S(1)} %get-tuple-element.47), channel_id=3, replica_groups=mesh['sy'=4,'sx'=4,'tz'=4,'tc'=2] {'sy'}, dimensions={0}, use_global_device_ids=true | all-gather | bytes 655360 | tf_op jit(solution)/shard_map/all_gather | solution.py:75
  47.4 0.1 multiply_reduce_fusion
  47.6 1.4 %add_convert_fusion = bf16[12,2,128,128]{3,0,2,1:T(8,128)(2,1)S(1)} fusion(bf16[12,2,128,128]{3,2,0,1:T(8,128)(2,1)S(1)} %pad_maximum_fusion.1, f32[2,128,128]{2,1,0:T(8,128)S(1)} %add.153, f32[12]{0:T(128)S(1)} %convert_element_type.47, s32[192,192]{1,0:T(8,128)} %param.18, s32[]{:T(128)S(6)} %select_n.91), kind=kOutput, calls=%fused_computation.13 | convolution fusion | flops 10616976 | bytes 1712180 | tf_op jit(solution)/shard_map/ce,ehij->chij/dot_general | solution.py:83
  49.0 0.2 slice_bitcast_fusion.1
  49.2 1.1 %fusion.23 = f32[12,128,128]{2,1,0:T(8,128)} fusion(bf16[12,128,128]{2,0,1:T(8,128)(2,1)S(1)} %get-tuple-element.58, bf16[12,128,256]{2,1,0:T(8,128)(2,1)S(1)} %bitcast.49), kind=kOutput, calls=%fused_computation.46 | convolution fusion | flops 50331648 | bytes 1703936 | tf_op jit(solution)/shard_map/ctd,cde->cte/dot_general | solution.py:97
  50.4 2.5 %fusion.12 = bf16[12,128,128]{2,1,0:T(8,128)(2,1)} fusion(f32[12,128,128]{2,1,0:T(8,128)} %fusion.23, f32[12]{0:T(128)S(1)} %get-tuple-element.51, pred[128,128]{1,0:T(8,128)(4,1)S(1)} %iota_compare_fusion, bf16[12,128,256]{2,1,0:T(8,128)(2,1)S(1)} %bitcast.47, bf16[12,128,256]{2,1,0:T(8,128)(2,1)S(1)} %bitcast.43, bf16[12,128,256]{2,1,0:T(8,128)(2,1)S(1)} %bitcast.50), kind=kOutput, calls=%fused_computation.26 | convolution fusion | flops 101646336 | bytes 2376192 | tf_op jit(solution)/shard_map/cts,cse->cte/dot_general | solution.py:104
  52.8 1.2 %copy.51 = bf16[1536,128]{0,1:T(8,128)(2,1)S(1)} copy(bf16[1536,128]{1,0:T(8,128)(2,1)} %bitcast.57) | data formatting | bytes 786432 | tf_op jit(solution)/shard_map/concatenate | solution.py:108
  54.0 1.1 %fusion.21 = f32[12,128,128]{2,1,0:T(8,128)} fusion(bf16[12,128,128]{2,0,1:T(8,128)(2,1)S(1)} %get-tuple-element.59, bf16[12,128,256]{2,1,0:T(8,128)(2,1)S(1)} %bitcast.51), kind=kOutput, calls=%fused_computation.44 | convolution fusion | flops 50331648 | bytes 1703936 | tf_op jit(solution)/shard_map/ctd,cde->cte/dot_general | solution.py:97
  55.2 1.7 %fusion.13 = bf16[12,128,128]{2,1,0:T(8,128)(2,1)S(1)} fusion(f32[12,128,128]{2,1,0:T(8,128)} %fusion.21, f32[12]{0:T(128)S(1)} %get-tuple-element.51, pred[128,128]{1,0:T(8,128)(4,1)S(1)} %copy-done.1, bf16[12,128,256]{2,1,0:T(8,128)(2,1)S(1)} %bitcast.52, bf16[12,128,256]{2,1,0:T(8,128)(2,1)S(1)} %bitcast.48, bf16[12,128,256]{2,1,0:T(8,128)(2,1)S(1)} %bitcast.44), kind=kOutput, calls=%fused_computation.27 | convolution fusion | flops 101646336 | bytes 2376192 | tf_op jit(solution)/shard_map/cts,cse->cte/dot_general | solution.py:104
  56.8 0.2 copy.52
  57.0 0.1 fusion.11
  57.2 0.5 collective-permute-start
  57.6 3.4 %collective-permute-start.1 = (bf16[1536,256]{0,1:T(8,128)(2,1)S(1)}, bf16[1536,256]{0,1:T(8,128)(2,1)S(1)}, u32[]{:S(2)}, u32[]{:S(2)}) collective-permute-start(bf16[1536,256]{0,1:T(8,128)(2,1)S(1)} %fusion.11), channel_id=1, source_target_pairs={{0,6},{1,7},{2,0},{3,1},{4,2},{5,3},{6,4},{7,5},{8,14},{9,15},{10,... | collective-permute-start | bytes 2359304 | tf_op jit(solution)/shard_map/ppermute | solution.py:132
  61.0 4.1 %collective-permute-start.2 = (bf16[1536,256]{0,1:T(8,128)(2,1)S(1)}, bf16[1536,256]{0,1:T(8,128)(2,1)S(1)}, u32[]{:S(2)}, u32[]{:S(2)}) collective-permute-start(bf16[1536,256]{0,1:T(8,128)(2,1)S(1)} %fusion.11), channel_id=1, source_target_pairs={{0,1},{1,0},{2,3},{3,2},{4,5},{5,4},{6,7},{7,6},{8,9},{9,8},{10,11... | collective-permute-start | bytes 2359304 | tf_op jit(solution)/shard_map/ppermute | solution.py:133
  65.1 9.9 %collective-permute-done = bf16[1536,256]{0,1:T(8,128)(2,1)S(1)} collective-permute-done((bf16[1536,256]{0,1:T(8,128)(2,1)S(1)}, bf16[1536,256]{0,1:T(8,128)(2,1)S(1)}, u32[]{:S(2)}, u32[]{:S(2)}) %collective-permute-start) | collective-permute-done | bytes 786464 | tf_op jit(solution)/shard_map/ppermute | solution.py:131
  75.1 0.1 pad_maximum_fusion
  75.2 4.5 %collective-permute-start.3 = (bf16[1536,512]{0,1:T(8,128)(2,1)S(1)}, bf16[1536,512]{0,1:T(8,128)(2,1)S(1)}, u32[]{:S(2)}, u32[]{:S(2)}) collective-permute-start(bf16[1536,512]{0,1:T(8,128)(2,1)S(1)} %pad_maximum_fusion), channel_id=1, source_target_pairs={{0,1},{1,0},{2,3},{3,2},{4,5},{5,4},{6,7},{7,6},{8,9},{9,8},{10,11... | collective-permute-start | bytes 4718600 | tf_op jit(solution)/shard_map/ppermute | solution.py:139
  79.7 2.8 %collective-permute-start.4 = (bf16[1536,256]{0,1:T(8,128)(2,1)S(1)}, bf16[1536,256]{0,1:T(8,128)(2,1)S(1)}, u32[]{:S(2)}, u32[]{:S(2)}) collective-permute-start(bf16[1536,256]{0,1:T(8,128)(2,1)S(1)} %broadcast_select_fusion), channel_id=1, source_target_pairs={{0,2},{2,4},{4,6},{6,0},{1,7},{3,1},{5,3},{7,5},{8,10},{10,12},{12... | collective-permute-start | bytes 2359304 | tf_op jit(solution)/shard_map/ppermute | solution.py:143
  82.6 1.3 %fusion.55 = f32[1536,256]{1,0:T(8,128)S(1)} fusion(bf16[1536,256]{0,1:T(8,128)(2,1)S(1)} %collective-permute-done, bf16[2048,2048]{1,0:T(8,128)(2,1)} %all-gather.4.cloned.1.call-done, s32[]{:T(128)S(6)} %select_n.101, s32[]{:T(128)S(6)} %select_n.99), kind=kOutput, calls=%fused_computation.74 | convolution fusion | flops 201326592 | bytes 2490376 | tf_op jit(solution)/shard_map/dot_general | solution.py:129
  83.9 1.0 fusion.70
  84.9 1.3 %fusion.52 = f32[1536,256]{1,0:T(8,128)S(1)} fusion(bf16[1536,256]{0,1:T(8,128)(2,1)S(1)} %collective-permute-done.2, bf16[2048,2048]{1,0:T(8,128)(2,1)} %all-gather.4.cloned.1.call-done, s32[]{:T(128)S(6)} %select_n.104, s32[]{:T(128)S(6)} %select_n.99), kind=kOutput, calls=%fused_computation.71 | convolution fusion | flops 201326592 | bytes 2490376 | tf_op jit(solution)/shard_map/dot_general | solution.py:129
  86.2 1.3 %convolution_add_fusion.2 = f32[1536,256]{1,0:T(8,128)S(1)} fusion(f32[1536,256]{1,0:T(8,128)S(1)} %fusion.55, bf16[1536,256]{0,1:T(8,128)(2,1)S(1)} %fusion.11, bf16[2048,2048]{1,0:T(8,128)(2,1)} %all-gather.4.cloned.1.call-done, s32[]{:T(128)S(6)} %select_n.99), kind=kOutput, calls=%fused_computation.11 | convolution fusion | flops 201719808 | bytes 4063236 | tf_op jit(solution)/shard_map/dot_general | solution.py:129
  87.6 3.9 %collective-permute-done.4 = bf16[1536,256]{0,1:T(8,128)(2,1)S(1)} collective-permute-done((bf16[1536,256]{0,1:T(8,128)(2,1)S(1)}, bf16[1536,256]{0,1:T(8,128)(2,1)S(1)}, u32[]{:S(2)}, u32[]{:S(2)}) %collective-permute-start.4) | collective-permute-done | bytes 786464 | tf_op jit(solution)/shard_map/ppermute | solution.py:143
  91.5 1.5 %collective-permute-start.5 = (bf16[1536,256]{0,1:T(8,128)(2,1)S(1)}, bf16[1536,256]{0,1:T(8,128)(2,1)S(1)}, u32[]{:S(2)}, u32[]{:S(2)}) collective-permute-start(bf16[1536,256]{0,1:T(8,128)(2,1)S(1)} %collective-permute-done.4), channel_id=1, source_target_pairs={{0,1},{1,0},{2,3},{3,2},{4,5},{5,4},{6,7},{7,6},{8,9},{9,8},{10,11... | collective-permute-start | bytes 2359304 | tf_op jit(solution)/shard_map/ppermute | solution.py:144
  93.0 1.3 %fusion.50 = f32[1536,256]{1,0:T(8,128)S(1)} fusion(bf16[1536,256]{0,1:T(8,128)(2,1)S(1)} %collective-permute-done.4, bf16[2048,2048]{1,0:T(8,128)(2,1)} %all-gather.4.cloned.1.call-done, s32[]{:T(128)S(6)} %select_n.110, s32[]{:T(128)S(6)} %select_n.99), kind=kOutput, calls=%fused_computation.69 | convolution fusion | flops 201326592 | bytes 2490376 | tf_op jit(solution)/shard_map/dot_general | solution.py:129
  94.4 0.6 fusion.45
  95.0 1.5 %fusion.7 = f32[1536,256]{1,0:T(8,128)S(1)} fusion(f32[1536,256]{1,0:T(8,128)S(1)} %fusion.50, f32[1536,256]{1,0:T(8,128)S(1)} %fusion.45, f32[1536,256]{1,0:T(8,128)S(1)} %fusion.52, f32[1536,256]{1,0:T(8,128)S(1)} %convolution_add_fusion.2, bf16[1536,256]{0,1:T(8,128)(2,1)S(1)} %collective-permute-done.1, ...), kind=kOutput, calls=%fused_computation.10 | convolution fusion | flops 202899456 | bytes 8781832 | tf_op jit(solution)/shard_map/dot_general | solution.py:129
  96.5 2.2 %fusion.8 = bf16[1536,256]{1,0:T(8,128)(2,1)} fusion(f32[1536,256]{1,0:T(8,128)S(1)} %fusion.7, bf16[1536,256]{0,1:T(8,128)(2,1)S(1)} %collective-permute-done.5, bf16[2048,2048]{1,0:T(8,128)(2,1)} %all-gather.4.cloned.1.call-done, s32[]{:T(128)S(6)} %select_n.111, s32[]{:T(128)S(6)} %select_n.99), kind=kOutput, calls=%fused_computation.12 | convolution fusion | flops 202113024 | bytes 3276808 | tf_op jit(solution)/shard_map/dot_general | solution.py:129
  (25 shorter events, 0.7 us)
Async XLA Ops:
  6.5 68.5 %all-gather.4.cloned.1.call-start = ((), (), s32[]{:S(2)}) async-start(), calls=%async_computation | async-start | bytes 9437184 | tf_op jit(solution)/shard_map/all_gather | solution.py:29
  47.6 2.8 %copy-start = (pred[128,128]{1,0:T(8,128)(4,1)}, pred[128,128]{1,0:T(8,128)(4,1)S(1)}, u32[]{:S(2)}) copy-start(pred[128,128]{1,0:T(8,128)(4,1)S(1)} %iota_compare_fusion) | copy-start | bytes 49156
  52.8 2.3 %copy-start.1 = (pred[128,128]{1,0:T(8,128)(4,1)S(1)}, pred[128,128]{1,0:T(8,128)(4,1)}, u32[]{:S(2)}) copy-start(pred[128,128]{1,0:T(8,128)(4,1)} %copy-done) | copy-start | bytes 49156
  57.2 17.9 %collective-permute-start = (bf16[1536,256]{0,1:T(8,128)(2,1)S(1)}, bf16[1536,256]{0,1:T(8,128)(2,1)S(1)}, u32[]{:S(2)}, u32[]{:S(2)}) collective-permute-start(bf16[1536,256]{0,1:T(8,128)(2,1)S(1)} %fusion.11), channel_id=1, source_target_pairs={{0,2},{1,3},{2,4},{3,5},{4,6},{5,7},{6,0},{7,1},{8,10},{9,11},{10,... | collective-permute-start | bytes 2359304 | tf_op jit(solution)/shard_map/ppermute | solution.py:131
  57.6 17.5 %collective-permute-start.1 = (bf16[1536,256]{0,1:T(8,128)(2,1)S(1)}, bf16[1536,256]{0,1:T(8,128)(2,1)S(1)}, u32[]{:S(2)}, u32[]{:S(2)}) collective-permute-start(bf16[1536,256]{0,1:T(8,128)(2,1)S(1)} %fusion.11), channel_id=1, source_target_pairs={{0,6},{1,7},{2,0},{3,1},{4,2},{5,3},{6,4},{7,5},{8,14},{9,15},{10,... | collective-permute-start | bytes 2359304 | tf_op jit(solution)/shard_map/ppermute | solution.py:132
  61.0 23.8 %collective-permute-start.2 = (bf16[1536,256]{0,1:T(8,128)(2,1)S(1)}, bf16[1536,256]{0,1:T(8,128)(2,1)S(1)}, u32[]{:S(2)}, u32[]{:S(2)}) collective-permute-start(bf16[1536,256]{0,1:T(8,128)(2,1)S(1)} %fusion.11), channel_id=1, source_target_pairs={{0,1},{1,0},{2,3},{3,2},{4,5},{5,4},{6,7},{7,6},{8,9},{9,8},{10,11... | collective-permute-start | bytes 2359304 | tf_op jit(solution)/shard_map/ppermute | solution.py:133
  75.2 19.2 %collective-permute-start.3 = (bf16[1536,512]{0,1:T(8,128)(2,1)S(1)}, bf16[1536,512]{0,1:T(8,128)(2,1)S(1)}, u32[]{:S(2)}, u32[]{:S(2)}) collective-permute-start(bf16[1536,512]{0,1:T(8,128)(2,1)S(1)} %pad_maximum_fusion), channel_id=1, source_target_pairs={{0,1},{1,0},{2,3},{3,2},{4,5},{5,4},{6,7},{7,6},{8,9},{9,8},{10,11... | collective-permute-start | bytes 4718600 | tf_op jit(solution)/shard_map/ppermute | solution.py:139
  79.7 11.8 %collective-permute-start.4 = (bf16[1536,256]{0,1:T(8,128)(2,1)S(1)}, bf16[1536,256]{0,1:T(8,128)(2,1)S(1)}, u32[]{:S(2)}, u32[]{:S(2)}) collective-permute-start(bf16[1536,256]{0,1:T(8,128)(2,1)S(1)} %broadcast_select_fusion), channel_id=1, source_target_pairs={{0,2},{2,4},{4,6},{6,0},{1,7},{3,1},{5,3},{7,5},{8,10},{10,12},{12... | collective-permute-start | bytes 2359304 | tf_op jit(solution)/shard_map/ppermute | solution.py:143
  91.5 5.0 %collective-permute-start.5 = (bf16[1536,256]{0,1:T(8,128)(2,1)S(1)}, bf16[1536,256]{0,1:T(8,128)(2,1)S(1)}, u32[]{:S(2)}, u32[]{:S(2)}) collective-permute-start(bf16[1536,256]{0,1:T(8,128)(2,1)S(1)} %collective-permute-done.4), channel_id=1, source_target_pairs={{0,1},{1,0},{2,3},{3,2},{4,5},{5,4},{6,7},{7,6},{8,9},{9,8},{10,11... | collective-permute-start | bytes 2359304 | tf_op jit(solution)/shard_map/ppermute | solution.py:144
Sparse Core Ops, SparseCore 0:
  9.0 53.4 all-gather.3

commit v16 on v14

--- a/solution.py
+++ b/solution.py
@@ -136,11 +136,12 @@
     across = (chip_at + 2) % chip_count
     first = jnp.concatenate([mixed, from_below, from_above], axis=1)
     sibling_first = lax.ppermute(first, "tc", [(0, 1), (1, 0)])
-    forward = [
-        (z * PAIR, ((z + 1) % chip_count) * PAIR) for z in range(chip_count)
-    ] + [(z * PAIR + 1, ((z - 1) % chip_count) * PAIR + 1) for z in range(chip_count)]
-    relayed = lax.ppermute(jnp.where(core_at == 0, from_below, from_above), TP, forward)
-    sibling_relayed = lax.ppermute(relayed, "tc", [(0, 1), (1, 0)])
+    up = [(z * PAIR, ((z + 1) % chip_count) * PAIR) for z in range(chip_count)]
+    down = [(z * PAIR + 1, ((z - 1) % chip_count) * PAIR + 1) for z in range(chip_count)]
+    relayed_up = lax.ppermute(from_below, TP, up)
+    relayed_down = lax.ppermute(from_above, TP, down)
+    sibling_up = lax.ppermute(relayed_up, "tc", [(0, 1)])
+    sibling_down = lax.ppermute(relayed_down, "tc", [(1, 0)])
     other = 1 - core_at
     total = term(mixed, chip_at, core_at)
     total = total + term(from_below, below, core_at) + term(from_above, above, core_at)
@@ -151,7 +152,8 @@
         ),
         preferred_element_type=jnp.float32,
     )
-    total = total + term(relayed, across, core_at) + term(sibling_relayed, across, other)
+    total = total + term(relayed_up, across, core_at) + term(relayed_down, across, core_at)
+    total = total + term(sibling_up, across, other) + term(sibling_down, across, other)
     return total.astype(jnp.bfloat16)
 
 

time: 110 us -> 118 us (1.073)
  starting transfers between devices: 12.7 us -> 16.4 us
  matrix products: 27.4 us -> 30.2 us
  waiting for transfers between devices: 20 us -> 21.5 us
    ppermute x2 -> x4, starting transfers between devices: 4.44 us -> 8.16 us  [the longest x1 4.65 us: layer(): relayed_down = lax.ppermute(from_above, TP, down)]
    dot_general x5 -> x7, matrix products: 7.77 us -> 10.5 us  [term(): return jnp.dot(block, rows_of(z, core), preferred_element_type=jnp.float32)]
    ppermute x2 -> x4, waiting for transfers between devices: 5.21 us -> 6.8 us  [the longest x1 6.79 us: layer(): relayed_down = lax.ppermute(from_above, TP, down)]
  transfers between devices with their start and end apart: 6 -> 8, of which waited for: 2 -> 2; matrix products, arithmetic and copies ran while one was open for 32% -> 32% of each run, Pallas kernels for 0% -> 0%
where the time goes in v16:
time: 118 us; the launch traced here: 117 us
  matrix products  30.2 us (26%)
  blocking collectives  24.2 us (21%)
  waiting for transfers between devices  21.5 us (18%)
  starting transfers between devices  16.4 us (14%)
  between operations  13.7 us (12%)
  local copies, waits for them, and re-layouts  6.66 us (6%)
  other arithmetic  4.36 us (4%)
    ppermute x1, waiting for transfers between devices, layer(): from_below = lax.ppermute(mixed, TP, shifted(1))  14 us
    all_gather x1, blocking collectives, layer(): row_tails = lax.all_gather(tail, 'sx', axis=0, tiled=False)  12.5 us
    all_gather x1, blocking collectives, layer(): row_sums = lax.all_gather(row_sum, 'sy', axis=0, tiled=False)  11.7 us
    dot_general x7, matrix products, term(): return jnp.dot(block, rows_of(z, core), preferred_element_type=jnp.float32)  10.5 us
    dot_general x1, matrix products, layer(): jnp.dot(tokens, jnp.concatenate([w_key, w_value, w_query], axis=1), prefe...  8.16 us
    ppermute x1, waiting for transfers between devices, layer(): relayed_down = lax.ppermute(from_above, TP, down)  6.79 us
    ppermute x1, starting transfers between devices, layer(): relayed_down = lax.ppermute(from_above, TP, down)  4.65 us
    ppermute x1, starting transfers between devices, layer(): sibling_first = lax.ppermute(first, 'tc', [(0, 1), (1, 0)])  4.38 us
  transfers between devices with their start and end apart: 8, of which 2 were waited for; matrix products, arithmetic and copies ran while one was open for 32% of the time, Pallas kernels for 0%

profile of v16, /device:TPU:1, one launch (start us, length us, event | category | flops | bytes accessed | tf_op | source)
XLA Modules:
  0.0 117.1 jit_solution(15144716798240730583)
XLA Ops:
  6.5 0.7 all-gather.4.cloned.1.call-update
  7.3 0.9 multiply_reduce_fusion.3
  8.1 0.8 multiply_rsqrt_fusion
  9.0 8.2 %convolution_bitcast_fusion = bf16[1536,768]{0,1:T(8,128)(2,1)S(1)} fusion(bf16[1536,2048]{1,0:T(8,128)(2,1)} %param.13, bf16[2048,256]{1,0:T(8,128)(2,1)} %param.14, bf16[2048,256]{1,0:T(8,128)(2,1)} %param.16, bf16[2048,256]{1,0:T(8,128)(2,1)} %param.15), kind=kOutput, calls=%fused_computation | convolution fusion | flops 4841275392 | bytes 11796480 | tf_op jit(solution)/shard_map/dot_general | solution.py:35
  17.1 0.3 fusion.11
  17.4 0.3 copy.42
  17.7 0.3 copy.44
  18.0 0.7 fusion.67
  19.0 0.1 dynamic-slice_reduce_fusion.2
  19.3 0.8 dynamic-slice_bitcast_fusion
  20.1 0.2 fusion.74
  20.4 0.9 dynamic-slice_reduce_fusion
  21.3 0.3 copy.41
  21.6 0.2 slice_reduce_fusion
  21.8 0.3 fusion.17
  22.1 0.3 fusion.18
  22.5 0.5 fusion.19
  23.0 12.5 %all-gather = f32[8,128,128]{2,1,0:T(8,128)S(1)} all-gather(f32[2,128,128]{2,1,0:T(8,128)S(1)} %bitcast.56), channel_id=2, replica_groups=mesh['sy'=4,'sx'=4,'tz'=4,'tc'=2] {'sx'}, dimensions={0}, use_global_device_ids=true | all-gather | bytes 655360 | tf_op jit(solution)/shard_map/all_gather | solution.py:67
  35.5 0.1 multiply_reduce_fusion.1
  35.7 11.7 %all-gather.1 = f32[8,128,128]{2,1,0:T(8,128)S(1)} all-gather(f32[2,128,128]{2,1,0:T(8,128)S(1)} %get-tuple-element.47), channel_id=3, replica_groups=mesh['sy'=4,'sx'=4,'tz'=4,'tc'=2] {'sy'}, dimensions={0}, use_global_device_ids=true | all-gather | bytes 655360 | tf_op jit(solution)/shard_map/all_gather | solution.py:75
  47.6 1.4 %add_convert_fusion = bf16[12,2,128,128]{3,0,2,1:T(8,128)(2,1)S(1)} fusion(bf16[12,2,128,128]{3,2,0,1:T(8,128)(2,1)S(1)} %pad_maximum_fusion.1, f32[2,128,128]{2,1,0:T(8,128)S(1)} %add.162, f32[12]{0:T(128)S(1)} %convert_element_type.47, s32[192,192]{1,0:T(8,128)} %param.18, s32[]{:T(128)S(6)} %select_n.87), kind=kOutput, calls=%fused_computation.15 | convolution fusion | flops 10616976 | bytes 1712180 | tf_op jit(solution)/shard_map/ce,ehij->chij/dot_general | solution.py:83
  49.0 0.2 slice_bitcast_fusion.1
  49.2 1.1 fusion.30
  50.3 2.5 %fusion.13 = bf16[12,128,128]{2,1,0:T(8,128)(2,1)} fusion(f32[12,128,128]{2,1,0:T(8,128)} %fusion.30, f32[12]{0:T(128)S(1)} %get-tuple-element.51, pred[128,128]{1,0:T(8,128)(4,1)S(1)} %iota_compare_fusion, bf16[12,128,256]{2,1,0:T(8,128)(2,1)S(1)} %bitcast.48, bf16[12,128,256]{2,1,0:T(8,128)(2,1)S(1)} %bitcast.44, bf16[12,128,256]{2,1,0:T(8,128)(2,1)S(1)} %bitcast.51), kind=kOutput, calls=%fused_computation.27 | convolution fusion | flops 101646336 | bytes 2376192 | tf_op jit(solution)/shard_map/cts,cse->cte/dot_general | solution.py:104
  52.8 1.2 %copy.51 = bf16[1536,128]{0,1:T(8,128)(2,1)S(1)} copy(bf16[1536,128]{1,0:T(8,128)(2,1)} %bitcast.58) | data formatting | bytes 786432 | tf_op jit(solution)/shard_map/concatenate | solution.py:108
  54.0 1.1 fusion.28
  55.1 1.7 %fusion.14 = bf16[12,128,128]{2,1,0:T(8,128)(2,1)S(1)} fusion(f32[12,128,128]{2,1,0:T(8,128)} %fusion.28, f32[12]{0:T(128)S(1)} %get-tuple-element.51, pred[128,128]{1,0:T(8,128)(4,1)S(1)} %copy-done.1, bf16[12,128,256]{2,1,0:T(8,128)(2,1)S(1)} %bitcast.53, bf16[12,128,256]{2,1,0:T(8,128)(2,1)S(1)} %bitcast.49, bf16[12,128,256]{2,1,0:T(8,128)(2,1)S(1)} %bitcast.45), kind=kOutput, calls=%fused_computation.28 | convolution fusion | flops 101646336 | bytes 2376192 | tf_op jit(solution)/shard_map/cts,cse->cte/dot_general | solution.py:104
  56.8 0.2 copy.52
  57.0 0.1 fusion.12
  57.1 0.5 collective-permute-start
  57.6 3.4 %collective-permute-start.1 = (bf16[1536,256]{0,1:T(8,128)(2,1)S(1)}, bf16[1536,256]{0,1:T(8,128)(2,1)S(1)}, u32[]{:S(2)}, u32[]{:S(2)}) collective-permute-start(bf16[1536,256]{0,1:T(8,128)(2,1)S(1)} %fusion.12), channel_id=1, source_target_pairs={{0,6},{1,7},{2,0},{3,1},{4,2},{5,3},{6,4},{7,5},{8,14},{9,15},{10,... | collective-permute-start | bytes 2359304 | tf_op jit(solution)/shard_map/ppermute | solution.py:132
  61.0 14.0 %collective-permute-done = bf16[1536,256]{0,1:T(8,128)(2,1)S(1)} collective-permute-done((bf16[1536,256]{0,1:T(8,128)(2,1)S(1)}, bf16[1536,256]{0,1:T(8,128)(2,1)S(1)}, u32[]{:S(2)}, u32[]{:S(2)}) %collective-permute-start) | collective-permute-done | bytes 786464 | tf_op jit(solution)/shard_map/ppermute | solution.py:131
  75.0 1.6 %pad_maximum_fusion = bf16[1536,768]{0,1:T(8,128)(2,1)} fusion(bf16[1536,256]{0,1:T(8,128)(2,1)S(1)} %collective-permute-done.1, bf16[1536,256]{0,1:T(8,128)(2,1)S(1)} %collective-permute-done, bf16[1536,256]{0,1:T(8,128)(2,1)S(1)} %fusion.12), kind=kLoop, calls=%fused_computation.14 | loop fusion | flops 7077888 | bytes 4718592 | tf_op jit(solution)/shard_map/concatenate | solution.py:137
  76.7 4.4 %collective-permute-start.2 = (bf16[1536,768]{0,1:T(8,128)(2,1)}, bf16[1536,768]{0,1:T(8,128)(2,1)}, u32[]{:S(2)}, u32[]{:S(2)}) collective-permute-start(bf16[1536,768]{0,1:T(8,128)(2,1)} %pad_maximum_fusion), channel_id=1, source_target_pairs={{0,1},{1,0},{2,3},{3,2},{4,5},{5,4},{6,7},{7,6},{8,9},{9,8},{10,11... | collective-permute-start | bytes 7077896 | tf_op jit(solution)/shard_map/ppermute | solution.py:138
  81.0 4.6 %collective-permute-start.4 = (bf16[1536,256]{0,1:T(8,128)(2,1)S(1)}, bf16[1536,256]{0,1:T(8,128)(2,1)}, u32[]{:S(2)}, u32[]{:S(2)}) collective-permute-start(bf16[1536,256]{0,1:T(8,128)(2,1)S(1)} %collective-permute-done.1), channel_id=1, source_target_pairs={{1,7},{3,1},{5,3},{7,5},{9,15},{11,9},{13,11},{15,13},{17,23},{19,... | collective-permute-start | bytes 2359304 | tf_op jit(solution)/shard_map/ppermute | solution.py:142
  85.7 0.7 collective-permute-start.3
  86.5 1.3 %fusion.53 = f32[1536,256]{1,0:T(8,128)S(1)} fusion(bf16[1536,256]{0,1:T(8,128)(2,1)S(1)} %collective-permute-done, bf16[2048,2048]{1,0:T(8,128)(2,1)} %all-gather.4.cloned.1.call-done, s32[]{:T(128)S(6)} %select_n.97, s32[]{:T(128)S(6)} %select_n.95), kind=kOutput, calls=%fused_computation.71 | convolution fusion | flops 201326592 | bytes 2490376 | tf_op jit(solution)/shard_map/dot_general | solution.py:129
  87.8 6.8 %collective-permute-done.4 = bf16[1536,256]{0,1:T(8,128)(2,1)} collective-permute-done((bf16[1536,256]{0,1:T(8,128)(2,1)S(1)}, bf16[1536,256]{0,1:T(8,128)(2,1)}, u32[]{:S(2)}, u32[]{:S(2)}) %collective-permute-start.4) | collective-permute-done | bytes 786464 | tf_op jit(solution)/shard_map/ppermute | solution.py:142
  94.6 1.3 %collective-permute-start.6 = (bf16[1536,256]{0,1:T(8,128)(2,1)}, bf16[1536,256]{0,1:T(8,128)(2,1)S(1)}, u32[]{:S(2)}, u32[]{:S(2)}) collective-permute-start(bf16[1536,256]{0,1:T(8,128)(2,1)} %collective-permute-done.4), channel_id=1, source_target_pairs={{1,0},{3,2},{5,4},{7,6},{9,8},{11,10},{13,12},{15,14},{17,16},{19,... | collective-permute-start | bytes 2359304 | tf_op jit(solution)/shard_map/ppermute | solution.py:144
  96.0 1.3 %convolution_add_fusion.2 = f32[1536,256]{1,0:T(8,128)S(1)} fusion(f32[1536,256]{1,0:T(8,128)S(1)} %fusion.53, bf16[1536,256]{0,1:T(8,128)(2,1)S(1)} %fusion.12, bf16[2048,2048]{1,0:T(8,128)(2,1)} %all-gather.4.cloned.1.call-done, s32[]{:T(128)S(6)} %select_n.95), kind=kOutput, calls=%fused_computation.12 | convolution fusion | flops 201719808 | bytes 4063236 | tf_op jit(solution)/shard_map/dot_general | solution.py:129
  97.3 1.1 fusion.75
  98.4 1.5 %collective-permute-start.5 = (bf16[1536,256]{0,1:T(8,128)(2,1)S(1)}, bf16[1536,256]{0,1:T(8,128)(2,1)S(1)}, u32[]{:S(2)}, u32[]{:S(2)}) collective-permute-start(bf16[1536,256]{0,1:T(8,128)(2,1)S(1)} %collective-permute-done.3), channel_id=1, source_target_pairs={{0,1},{2,3},{4,5},{6,7},{8,9},{10,11},{12,13},{14,15},{16,17},{18,... | collective-permute-start | bytes 2359304 | tf_op jit(solution)/shard_map/ppermute | solution.py:143
  99.9 1.3 %fusion.61 = f32[1536,256]{1,0:T(8,128)S(1)} fusion(bf16[1536,256]{0,1:T(8,128)(2,1)S(1)} %collective-permute-done.3, bf16[2048,2048]{1,0:T(8,128)(2,1)} %all-gather.4.cloned.1.call-done, s32[]{:T(128)S(6)} %select_n.104, s32[]{:T(128)S(6)} %select_n.95), kind=kOutput, calls=%fused_computation.79 | convolution fusion | flops 201326592 | bytes 2490376 | tf_op jit(solution)/shard_map/dot_general | solution.py:129
  101.2 1.6 %fusion.59 = f32[1536,256]{1,0:T(8,128)S(1)} fusion(bf16[1536,256]{0,1:T(8,128)(2,1)} %collective-permute-done.4, bf16[2048,2048]{1,0:T(8,128)(2,1)} %all-gather.4.cloned.1.call-done, s32[]{:T(128)S(6)} %select_n.104, s32[]{:T(128)S(6)} %select_n.95), kind=kOutput, calls=%fused_computation.77 | convolution fusion | flops 201326592 | bytes 2490376 | tf_op jit(solution)/shard_map/dot_general | solution.py:129
  102.8 1.3 %fusion.56 = f32[1536,256]{1,0:T(8,128)S(1)} fusion(bf16[1536,256]{0,1:T(8,128)(2,1)S(1)} %collective-permute-done.6, bf16[2048,2048]{1,0:T(8,128)(2,1)} %all-gather.4.cloned.1.call-done, s32[]{:T(128)S(6)} %select_n.105, s32[]{:T(128)S(6)} %select_n.95), kind=kOutput, calls=%fused_computation.74 | convolution fusion | flops 201326592 | bytes 2490376 | tf_op jit(solution)/shard_map/dot_general | solution.py:129
  104.1 2.5 %fusion.22 = f32[1536,256]{1,0:T(8,128)S(1)} fusion(bf16[1536,768]{0,1:T(8,128)(2,1)} %collective-permute-done.2, bf16[256,256]{1,0:T(8,128)(2,1)S(1)} %get-tuple-element.54, bf16[256,256]{1,0:T(8,128)(2,1)S(1)} %get-tuple-element.55, bf16[256,256]{1,0:T(8,128)(2,1)S(1)} %get-tuple-element.53), kind=kOutput, calls=%fused_computation.44 | convolution fusion | flops 605159424 | bytes 4325376 | tf_op jit(solution)/shard_map/dot_general | solution.py:148
  106.6 1.4 %fusion.8 = f32[1536,256]{1,0:T(8,128)S(1)} fusion(f32[1536,256]{1,0:T(8,128)S(1)} %fusion.59, f32[1536,256]{1,0:T(8,128)S(1)} %fusion.61, f32[1536,256]{1,0:T(8,128)S(1)} %fusion.22, f32[1536,256]{1,0:T(8,128)S(1)} %convolution_add_fusion.2, bf16[1536,256]{0,1:T(8,128)(2,1)S(1)} %collective-permute-done.1, ...), kind=kOutput, calls=%fused_computation.11 | convolution fusion | flops 202899456 | bytes 8781832 | tf_op jit(solution)/shard_map/dot_general | solution.py:129
  108.0 2.2 %fusion.9 = bf16[1536,256]{1,0:T(8,128)(2,1)} fusion(f32[1536,256]{1,0:T(8,128)S(1)} %fusion.56, f32[1536,256]{1,0:T(8,128)S(1)} %fusion.8, bf16[1536,256]{0,1:T(8,128)(2,1)S(1)} %collective-permute-done.5, bf16[2048,2048]{1,0:T(8,128)(2,1)} %all-gather.4.cloned.1.call-done, s32[]{:T(128)S(6)} %select_n.105, s32[]{:T(128)S(6)} %select_n.95), kind=kOutput, calls=%fused_computation.13 | convolution fusion | flops 202506240 | bytes 4849672 | tf_op jit(solution)/shard_map/dot_general | solution.py:129
  (27 shorter events, 0.9 us)
Async XLA Ops:
  6.5 68.5 %all-gather.4.cloned.1.call-start = ((), (), s32[]{:S(2)}) async-start(), calls=%async_computation | async-start | bytes 9437184 | tf_op jit(solution)/shard_map/all_gather | solution.py:29
  47.5 2.8 %copy-start = (pred[128,128]{1,0:T(8,128)(4,1)}, pred[128,128]{1,0:T(8,128)(4,1)S(1)}, u32[]{:S(2)}) copy-start(pred[128,128]{1,0:T(8,128)(4,1)S(1)} %iota_compare_fusion) | copy-start | bytes 49156
  52.8 2.3 %copy-start.1 = (pred[128,128]{1,0:T(8,128)(4,1)S(1)}, pred[128,128]{1,0:T(8,128)(4,1)}, u32[]{:S(2)}) copy-start(pred[128,128]{1,0:T(8,128)(4,1)} %copy-done) | copy-start | bytes 49156
  57.1 17.9 %collective-permute-start = (bf16[1536,256]{0,1:T(8,128)(2,1)S(1)}, bf16[1536,256]{0,1:T(8,128)(2,1)S(1)}, u32[]{:S(2)}, u32[]{:S(2)}) collective-permute-start(bf16[1536,256]{0,1:T(8,128)(2,1)S(1)} %fusion.12), channel_id=1, source_target_pairs={{0,2},{1,3},{2,4},{3,5},{4,6},{5,7},{6,0},{7,1},{8,10},{9,11},{10,... | collective-permute-start | bytes 2359304 | tf_op jit(solution)/shard_map/ppermute | solution.py:131
  57.6 17.5 %collective-permute-start.1 = (bf16[1536,256]{0,1:T(8,128)(2,1)S(1)}, bf16[1536,256]{0,1:T(8,128)(2,1)S(1)}, u32[]{:S(2)}, u32[]{:S(2)}) collective-permute-start(bf16[1536,256]{0,1:T(8,128)(2,1)S(1)} %fusion.12), channel_id=1, source_target_pairs={{0,6},{1,7},{2,0},{3,1},{4,2},{5,3},{6,4},{7,5},{8,14},{9,15},{10,... | collective-permute-start | bytes 2359304 | tf_op jit(solution)/shard_map/ppermute | solution.py:132
  76.7 27.4 %collective-permute-start.2 = (bf16[1536,768]{0,1:T(8,128)(2,1)}, bf16[1536,768]{0,1:T(8,128)(2,1)}, u32[]{:S(2)}, u32[]{:S(2)}) collective-permute-start(bf16[1536,768]{0,1:T(8,128)(2,1)} %pad_maximum_fusion), channel_id=1, source_target_pairs={{0,1},{1,0},{2,3},{3,2},{4,5},{5,4},{6,7},{7,6},{8,9},{9,8},{10,11... | collective-permute-start | bytes 7077896 | tf_op jit(solution)/shard_map/ppermute | solution.py:138
  81.0 13.6 %collective-permute-start.4 = (bf16[1536,256]{0,1:T(8,128)(2,1)S(1)}, bf16[1536,256]{0,1:T(8,128)(2,1)}, u32[]{:S(2)}, u32[]{:S(2)}) collective-permute-start(bf16[1536,256]{0,1:T(8,128)(2,1)S(1)} %collective-permute-done.1), channel_id=1, source_target_pairs={{1,7},{3,1},{5,3},{7,5},{9,15},{11,9},{13,11},{15,13},{17,23},{19,... | collective-permute-start | bytes 2359304 | tf_op jit(solution)/shard_map/ppermute | solution.py:142
  85.7 12.7 %collective-permute-start.3 = (bf16[1536,256]{0,1:T(8,128)(2,1)S(1)}, bf16[1536,256]{0,1:T(8,128)(2,1)S(1)}, u32[]{:S(2)}, u32[]{:S(2)}) collective-permute-start(bf16[1536,256]{0,1:T(8,128)(2,1)S(1)} %collective-permute-done), channel_id=1, source_target_pairs={{0,2},{2,4},{4,6},{6,0},{8,10},{10,12},{12,14},{14,8},{16,18},{18,... | collective-permute-start | bytes 2359304 | tf_op jit(solution)/shard_map/ppermute | solution.py:141
  94.6 8.1 %collective-permute-start.6 = (bf16[1536,256]{0,1:T(8,128)(2,1)}, bf16[1536,256]{0,1:T(8,128)(2,1)S(1)}, u32[]{:S(2)}, u32[]{:S(2)}) collective-permute-start(bf16[1536,256]{0,1:T(8,128)(2,1)} %collective-permute-done.4), channel_id=1, source_target_pairs={{1,0},{3,2},{5,4},{7,6},{9,8},{11,10},{13,12},{15,14},{17,16},{19,... | collective-permute-start | bytes 2359304 | tf_op jit(solution)/shard_map/ppermute | solution.py:144
  98.4 9.7 %collective-permute-start.5 = (bf16[1536,256]{0,1:T(8,128)(2,1)S(1)}, bf16[1536,256]{0,1:T(8,128)(2,1)S(1)}, u32[]{:S(2)}, u32[]{:S(2)}) collective-permute-start(bf16[1536,256]{0,1:T(8,128)(2,1)S(1)} %collective-permute-done.3), channel_id=1, source_target_pairs={{0,1},{2,3},{4,5},{6,7},{8,9},{10,11},{12,13},{14,15},{16,17},{18,... | collective-permute-start | bytes 2359304 | tf_op jit(solution)/shard_map/ppermute | solution.py:143
Sparse Core Ops, SparseCore 0:
  9.0 53.4 all-gather.3

commit v17 on v14

--- a/solution.py
+++ b/solution.py
@@ -26,7 +26,6 @@
     tp_index = lax.axis_index("tz") * PAIR + core_at
     first_group = seq_index * group_local
 
-    w_out_all = lax.all_gather(w_out, TP, axis=0, tiled=True)
 
     local_lengths = lax.dynamic_slice_in_dim(lengths, first_group, group_local, 0)
     reader_rows = lax.dynamic_slice_in_dim(readers, first_group, group_local, 0)
@@ -111,7 +110,6 @@
 
     chip_at = lax.axis_index("tz")
     chip_count = tp_count // PAIR
-    column = tp_index * local_width
 
     def shifted(step):
         return [
@@ -121,16 +119,23 @@
         ]
 
     def rows_of(z, core):
-        return lax.dynamic_slice(
-            w_out_all, ((z * PAIR + core) * local_width, column), (local_width, local_width)
-        )
+        return lax.dynamic_index_in_dim(w_out_cols, z * PAIR + core, 0, False)
 
     def term(block, z, core):
         return jnp.dot(block, rows_of(z, core), preferred_element_type=jnp.float32)
 
     from_below = lax.ppermute(mixed, TP, shifted(1))
     from_above = lax.ppermute(mixed, TP, shifted(chip_count - 1))
-    from_below, from_above, w_out_all = lax.optimization_barrier((from_below, from_above, w_out_all))
+    mixed, w_out = lax.optimization_barrier((mixed, w_out))
+    out_blocks = w_out.reshape(local_width, tp_count, local_width)
+    w_out_cols = jnp.zeros((tp_count, local_width, local_width), w_out.dtype)
+    for shift in range(tp_count):
+        piece = lax.dynamic_index_in_dim(out_blocks, (tp_index + shift) % tp_count, 1, False)
+        if shift:
+            piece = lax.ppermute(piece, TP, [(i, (i + shift) % tp_count) for i in range(tp_count)])
+        w_out_cols = lax.dynamic_update_index_in_dim(
+            w_out_cols, piece, (tp_index - shift) % tp_count, 0
+        )
     below = (chip_at - 1) % chip_count
     above = (chip_at + 1) % chip_count
     across = (chip_at + 2) % chip_count

time: 110 us -> 116 us (1.055)
  local copies, waits for them, and re-layouts: 6.64 us -> 25.6 us
  between operations: 13.6 us -> 0.54 us
  starting transfers between devices: 12.7 us -> 22.8 us
  waiting for transfers between devices: 20 us -> 11.6 us
  matrix products: 27.4 us -> 22.9 us
  other arithmetic: 4.45 us -> 7.81 us
    ppermute x0 -> x7, starting transfers between devices: none -> 14.1 us  [layer(): lax.ppermute(piece, TP, [(i, (i + shift) % tp_count) for i in range(tp_co...]
    ppermute x1, waiting for transfers between devices: 14 us -> 0.01 us  [layer(): from_below = lax.ppermute(mixed, TP, shifted(1))]
    dynamic_slice x1 -> x9, local copies, waits for them, and re-layouts: 1.06 us -> 13.3 us  [layer(): lax.dynamic_index_in_dim(out_blocks, (tp_index + shift) % tp_count, 1, Fa...]
    dot_general x5, matrix products: 7.77 us -> 3.13 us  [term(): return jnp.dot(block, rows_of(z, core), preferred_element_type=jnp.float32)]
    ppermute x1, starting transfers between devices: 4.38 us -> 0.1 us  [layer(): sibling_first = lax.ppermute(first, 'tc', [(0, 1), (1, 0)])]
    dynamic_update_slice x0 -> x8, local copies, waits for them, and re-layouts: none -> 3.71 us  [layer(): lax.dynamic_update_index_in_dim(w_out_cols, piece, (tp_index - shift) % t...]
    ppermute x0 -> x7, waiting for transfers between devices: none -> 3.46 us  [layer(): lax.ppermute(piece, TP, [(i, (i + shift) % tp_count) for i in range(tp_co...]
    ppermute x1, waiting for transfers between devices: 5.2 us -> 8.03 us  [layer(): lax.ppermute(jnp.where(core_at == 0, from_below, from_above), TP, forward)]
  transfers between devices with their start and end apart: 6 -> 12, of which waited for: 2 -> 4; matrix products, arithmetic and copies ran while one was open for 32% -> 19% of each run, Pallas kernels for 0% -> 0%
where the time goes in v17:
time: 116 us; the launch traced here: 115 us
  local copies, waits for them, and re-layouts  25.6 us (22%)
  blocking collectives  23.9 us (21%)
  matrix products  22.9 us (20%)
  starting transfers between devices  22.8 us (20%)
  waiting for transfers between devices  11.6 us (10%)
  other arithmetic  7.81 us (7%)
    ppermute x7, starting transfers between devices, layer(): lax.ppermute(piece, TP, [(i, (i + shift) % tp_count) for i in range(tp_co...  14.1 us
    dynamic_slice x9, local copies, waits for them, and re-layouts, layer(): lax.dynamic_index_in_dim(out_blocks, (tp_index + shift) % tp_count, 1, Fa...  13.3 us
    all_gather x1, blocking collectives, layer(): row_tails = lax.all_gather(tail, 'sx', axis=0, tiled=False)  12.8 us
    all_gather x1, blocking collectives, layer(): row_sums = lax.all_gather(row_sum, 'sy', axis=0, tiled=False)  11.2 us
    dot_general x1, matrix products, layer(): jnp.dot(tokens, jnp.concatenate([w_key, w_value, w_query], axis=1), prefe...  8.15 us
    ppermute x1, waiting for transfers between devices, layer(): lax.ppermute(jnp.where(core_at == 0, from_below, from_above), TP, forward)  8.03 us
    dot_general x2, matrix products, layer(): jnp.einsum('cts,cse->cte', weights, value_groups[:, :, cut], preferred_el...  4.08 us
    dynamic_update_slice x8, local copies, waits for them, and re-layouts, layer(): lax.dynamic_update_index_in_dim(w_out_cols, piece, (tp_index - shift) % t...  3.71 us
  transfers between devices with their start and end apart: 12, of which 4 were waited for; matrix products, arithmetic and copies ran while one was open for 19% of the time, Pallas kernels for 0%

profile of v17, /device:TPU:1, one launch (start us, length us, event | category | flops | bytes accessed | tf_op | source)
XLA Modules:
  0.0 115.2 jit_solution(16002497705686721582)
XLA Ops:
  0.0 0.9 multiply_reduce_fusion.3
  0.9 1.3 %multiply_rsqrt_fusion = (f32[12]{0:T(128)}, s32[12]{0:T(128)S(1)}) fusion(s32[12]{0:T(128)S(1)} %multiply_reduce_fusion.3, s32[192]{0:T(256)} %param.19, s32[]{:T(128)S(6)} %select_n.193), kind=kLoop, calls=%fused_computation.125 | loop fusion | flops 36 | bytes 196 | tf_op jit(solution)/shard_map/rsqrt | solution.py:91
  2.2 8.2 %convolution_bitcast_fusion = bf16[1536,768]{0,1:T(8,128)(2,1)S(1)} fusion(bf16[1536,2048]{1,0:T(8,128)(2,1)} %param.13, bf16[2048,256]{1,0:T(8,128)(2,1)} %param.14, bf16[2048,256]{1,0:T(8,128)(2,1)} %param.16, bf16[2048,256]{1,0:T(8,128)(2,1)} %param.15), kind=kOutput, calls=%fused_computation | convolution fusion | flops 4841275392 | bytes 11796480 | tf_op jit(solution)/shard_map/dot_general | solution.py:34
  11.5 1.1 fusion.16
  12.6 0.7 fusion.73
  13.5 0.8 fusion.80
  14.9 1.4 %dynamic-slice_reduce_fusion = s32[12]{0:T(128)} fusion(s32[192,192]{1,0:T(8,128)} %param.18, s32[]{:T(128)S(6)} %select_n.194), kind=kLoop, calls=%fused_computation.95 | loop fusion | bytes 100 | tf_op jit(solution)/shard_map/slice | solution.py:80
  16.3 0.8 dynamic-slice_bitcast_fusion.3
  17.1 1.1 pad_maximum_fusion.1
  18.7 12.8 %all-gather = f32[8,128,128]{2,1,0:T(8,128)} all-gather(f32[2,128,128]{2,1,0:T(8,128)S(1)} %bitcast.100), channel_id=2, replica_groups=mesh['sy'=4,'sx'=4,'tz'=4,'tc'=2] {'sx'}, dimensions={0}, use_global_device_ids=true | all-gather | bytes 655360 | tf_op jit(solution)/shard_map/all_gather | solution.py:66
  31.9 1.2 %multiply_reduce_fusion.1 = (f32[2,128,128]{2,1,0:T(8,128)S(1)}, f32[2,128,128]{2,1,0:T(8,128)S(1)}) fusion(f32[4,2,128,128]{3,2,1,0:T(8,128)} %bitcast.98, f32[4]{0:T(128)S(1)} %convert_element_type.53, f32[4]{0:T(128)S(1)} %fusion.70), kind=kLoop, calls=%fused_computation.41 | loop fusion | flops 458752 | bytes 786464 | tf_op jit(solution)/shard_map/reduce_sum | solution.py:73
  33.1 11.2 %all-gather.1 = f32[8,128,128]{2,1,0:T(8,128)} all-gather(f32[2,128,128]{2,1,0:T(8,128)S(1)} %get-tuple-element.45), channel_id=3, replica_groups=mesh['sy'=4,'sx'=4,'tz'=4,'tc'=2] {'sy'}, dimensions={0}, use_global_device_ids=true | all-gather | bytes 655360 | tf_op jit(solution)/shard_map/all_gather | solution.py:74
  44.6 1.2 %multiply_reduce_fusion = f32[2,128,128]{2,1,0:T(8,128)S(1)} fusion(f32[4,2,128,128]{3,2,1,0:T(8,128)} %bitcast.99, f32[4]{0:T(128)S(1)} %slice_reduce_fusion), kind=kLoop, calls=%fused_computation.40 | loop fusion | flops 229376 | bytes 655376 | tf_op jit(solution)/shard_map/reduce_sum | solution.py:79
  45.8 1.4 %add_convert_fusion = bf16[12,2,128,128]{3,0,2,1:T(8,128)(2,1)S(1)} fusion(bf16[12,2,128,128]{3,2,0,1:T(8,128)(2,1)S(1)} %pad_maximum_fusion.1, f32[2,128,128]{2,1,0:T(8,128)S(1)} %add.265, f32[12]{0:T(128)S(1)} %convert_element_type.47, s32[192,192]{1,0:T(8,128)} %param.18, s32[]{:T(128)S(6)} %select_n.194), kind=kOutput, calls=%fused_computation.13 | convolution fusion | flops 10616976 | bytes 1712180 | tf_op jit(solution)/shard_map/ce,ehij->chij/dot_general | solution.py:82
  47.2 1.2 %slice_bitcast_fusion.1 = (bf16[12,128,128]{2,0,1:T(8,128)(2,1)}, bf16[12,128,128]{2,0,1:T(8,128)(2,1)}) fusion(bf16[12,2,128,128]{3,0,2,1:T(8,128)(2,1)S(1)} %add_convert_fusion), kind=kLoop, calls=%fused_computation.39 | loop fusion | bytes 1572864 | tf_op jit(solution)/shard_map/squeeze | solution.py:97
  48.7 2.2 %fusion.28 = f32[12,128,128]{2,1,0:T(8,128)} fusion(bf16[12,128,128]{2,0,1:T(8,128)(2,1)} %get-tuple-element.65, bf16[12,128,256]{2,1,0:T(8,128)(2,1)S(1)} %bitcast.94), kind=kOutput, calls=%fused_computation.51 | convolution fusion | flops 50331648 | bytes 1572864 | tf_op jit(solution)/shard_map/ctd,cde->cte/dot_general | solution.py:96
  51.0 2.4 %fusion.11 = bf16[12,128,128]{2,1,0:T(8,128)(2,1)} fusion(f32[12,128,128]{2,1,0:T(8,128)} %fusion.28, f32[12]{0:T(128)S(1)} %copy-done.4, pred[128,128]{1,0:T(8,128)(4,1)S(1)} %copy-done.1, bf16[12,128,256]{2,1,0:T(8,128)(2,1)S(1)} %bitcast.92, bf16[12,128,256]{2,1,0:T(8,128)(2,1)S(1)} %bitcast.88, bf16[12,128,256]{2,1,0:T(8,128)(2,1)S(1)} %bitcast.95), kind=kOutput, calls=%fused_computation.25 | convolution fusion | flops 101646336 | bytes 2376192 | tf_op jit(solution)/shard_map/cts,cse->cte/dot_general | solution.py:103
  53.4 1.2 %copy.60 = bf16[1536,128]{0,1:T(8,128)(2,1)S(1)} copy(bf16[1536,128]{1,0:T(8,128)(2,1)} %bitcast.102) | data formatting | bytes 786432 | tf_op jit(solution)/shard_map/concatenate | solution.py:107
  54.6 1.1 fusion.26
  55.7 1.7 %fusion.12 = bf16[12,128,128]{2,1,0:T(8,128)(2,1)S(1)} fusion(f32[12,128,128]{2,1,0:T(8,128)} %fusion.26, f32[12]{0:T(128)S(1)} %copy-done.4, pred[128,128]{1,0:T(8,128)(4,1)S(1)} %copy-done.2, bf16[12,128,256]{2,1,0:T(8,128)(2,1)S(1)} %bitcast.97, bf16[12,128,256]{2,1,0:T(8,128)(2,1)S(1)} %bitcast.93, bf16[12,128,256]{2,1,0:T(8,128)(2,1)S(1)} %bitcast.89), kind=kOutput, calls=%fused_computation.26 | convolution fusion | flops 101646336 | bytes 2376192 | tf_op jit(solution)/shard_map/cts,cse->cte/dot_general | solution.py:103
  57.7 1.7 %collective-permute-start.7 = (bf16[1536,256]{0,1:T(8,128)(2,1)S(1)}, bf16[1536,256]{0,1:T(8,128)(2,1)S(1)}, u32[]{:S(2)}, u32[]{:S(2)}) collective-permute-start(bf16[1536,256]{0,1:T(8,128)(2,1)S(1)} %fusion.10), channel_id=1, source_target_pairs={{0,2},{1,3},{2,4},{3,5},{4,6},{5,7},{6,0},{7,1},{8,10},{9,11},{10,... | collective-permute-start | bytes 2359304 | tf_op jit(solution)/shard_map/ppermute | solution.py:127
  59.4 2.2 %collective-permute-start.8 = (bf16[1536,256]{0,1:T(8,128)(2,1)S(1)}, bf16[1536,256]{0,1:T(8,128)(2,1)S(1)}, u32[]{:S(2)}, u32[]{:S(2)}) collective-permute-start(bf16[1536,256]{0,1:T(8,128)(2,1)S(1)} %fusion.10), channel_id=1, source_target_pairs={{0,6},{1,7},{2,0},{3,1},{4,2},{5,3},{6,4},{7,5},{8,14},{9,15},{10,... | collective-permute-start | bytes 2359304 | tf_op jit(solution)/shard_map/ppermute | solution.py:128
  61.6 1.5 %copy.62 = bf16[256,2048]{0,1:T(8,128)(2,1)S(1)} copy(bf16[256,2048]{1,0:T(8,128)(2,1)} %param.17) | data formatting | bytes 2097152 | tf_op jit(solution)/shard_map/optimization_barrier | solution.py:129
  63.1 0.9 constant_dynamic-slice_fusion
  64.1 1.6 %copy.64 = bf16[256,1,256]{2,0,1:T(8,128)(2,1)} copy(bf16[256,1,256]{0,2,1:T(8,128)(2,1)} %get-tuple-element.63) | data formatting | bytes 262144 | tf_op jit(solution)/shard_map/jit(dynamic_index_in_dim)/dynamic_slice | solution.py:133
  65.7 5.8 %collective-permute-start = (bf16[256,256]{1,0:T(8,128)(2,1)}, bf16[256,256]{1,0:T(8,128)(2,1)}, u32[]{:S(2)}, u32[]{:S(2)}) collective-permute-start(bf16[256,256]{1,0:T(8,128)(2,1)} %bitcast.22), channel_id=1, source_target_pairs={{0,1},{1,2},{2,3},{3,4},{4,5},{5,6},{6,7},{7,0},{8,9},{9,10},{10,1... | collective-permute-start | bytes 393224 | tf_op jit(solution)/shard_map/ppermute | solution.py:135
  71.5 1.7 %copy.65 = bf16[256,1,256]{2,0,1:T(8,128)(2,1)} copy(bf16[256,1,256]{0,2,1:T(8,128)(2,1)} %get-tuple-element.62) | data formatting | bytes 262144 | tf_op jit(solution)/shard_map/jit(dynamic_index_in_dim)/dynamic_slice | solution.py:133
  73.2 1.6 %collective-permute-start.1 = (bf16[256,256]{1,0:T(8,128)(2,1)}, bf16[256,256]{1,0:T(8,128)(2,1)}, u32[]{:S(2)}, u32[]{:S(2)}) collective-permute-start(bf16[256,256]{1,0:T(8,128)(2,1)} %bitcast.24), channel_id=1, source_target_pairs={{0,2},{1,3},{2,4},{3,5},{4,6},{5,7},{6,0},{7,1},{8,10},{9,11},{10,... | collective-permute-start | bytes 393224 | tf_op jit(solution)/shard_map/ppermute | solution.py:135
  74.8 1.7 %copy.66 = bf16[256,1,256]{2,0,1:T(8,128)(2,1)} copy(bf16[256,1,256]{0,2,1:T(8,128)(2,1)} %get-tuple-element.61) | data formatting | bytes 262144 | tf_op jit(solution)/shard_map/jit(dynamic_index_in_dim)/dynamic_slice | solution.py:133
  76.4 2.0 %collective-permute-start.2 = (bf16[256,256]{1,0:T(8,128)(2,1)}, bf16[256,256]{1,0:T(8,128)(2,1)}, u32[]{:S(2)}, u32[]{:S(2)}) collective-permute-start(bf16[256,256]{1,0:T(8,128)(2,1)} %bitcast.26), channel_id=1, source_target_pairs={{0,3},{1,4},{2,5},{3,6},{4,7},{5,0},{6,1},{7,2},{8,11},{9,12},{10,... | collective-permute-start | bytes 393224 | tf_op jit(solution)/shard_map/ppermute | solution.py:135
  78.4 1.7 %copy.63 = bf16[256,1,256]{2,0,1:T(8,128)(2,1)} copy(bf16[256,1,256]{0,2,1:T(8,128)(2,1)} %get-tuple-element.64) | data formatting | bytes 262144 | tf_op jit(solution)/shard_map/jit(dynamic_index_in_dim)/dynamic_slice | solution.py:133
  80.1 0.9 bitcast_dynamic-update-slice_fusion.7
  81.3 1.7 %copy.67 = bf16[256,1,256]{2,0,1:T(8,128)(2,1)} copy(bf16[256,1,256]{0,2,1:T(8,128)(2,1)} %get-tuple-element.60) | data formatting | bytes 262144 | tf_op jit(solution)/shard_map/jit(dynamic_index_in_dim)/dynamic_slice | solution.py:133
  82.9 1.7 %copy.68 = bf16[256,1,256]{2,0,1:T(8,128)(2,1)} copy(bf16[256,1,256]{0,2,1:T(8,128)(2,1)} %get-tuple-element.59) | data formatting | bytes 262144 | tf_op jit(solution)/shard_map/jit(dynamic_index_in_dim)/dynamic_slice | solution.py:133
  84.6 1.7 %copy.69 = bf16[256,1,256]{2,0,1:T(8,128)(2,1)} copy(bf16[256,1,256]{0,2,1:T(8,128)(2,1)} %get-tuple-element.58) | data formatting | bytes 262144 | tf_op jit(solution)/shard_map/jit(dynamic_index_in_dim)/dynamic_slice | solution.py:133
  86.2 0.8 copy.70
  87.0 0.7 collective-permute-start.3
  87.7 0.9 bitcast_dynamic-update-slice_fusion.6
  88.7 2.7 %collective-permute-start.4 = (bf16[256,256]{1,0:T(8,128)(2,1)}, bf16[256,256]{1,0:T(8,128)(2,1)S(1)}, u32[]{:S(2)}, u32[]{:S(2)}) collective-permute-start(bf16[256,256]{1,0:T(8,128)(2,1)} %bitcast.105), channel_id=1, source_target_pairs={{0,5},{1,6},{2,7},{3,0},{4,1},{5,2},{6,3},{7,4},{8,13},{9,14},{10,... | collective-permute-start | bytes 393224 | tf_op jit(solution)/shard_map/ppermute | solution.py:135
  91.4 0.9 bitcast_dynamic-update-slice_fusion.5
  92.5 0.9 bitcast_dynamic-update-slice_fusion.4
  93.5 1.0 collective-permute-start.6
  95.4 2.9 %collective-permute-done.5 = bf16[256,256]{1,0:T(8,128)(2,1)S(1)} collective-permute-done((bf16[256,256]{1,0:T(8,128)(2,1)}, bf16[256,256]{1,0:T(8,128)(2,1)S(1)}, u32[]{:S(2)}, u32[]{:S(2)}) %collective-permute-start.5) | collective-permute-done | bytes 131104 | tf_op jit(solution)/shard_map/ppermute | solution.py:135
  98.3 3.1 %collective-permute-start.10 = (bf16[1536,256]{0,1:T(8,128)(2,1)S(1)}, bf16[1536,256]{0,1:T(8,128)(2,1)S(1)}, u32[]{:S(2)}, u32[]{:S(2)}) collective-permute-start(bf16[1536,256]{0,1:T(8,128)(2,1)S(1)} %broadcast_select_fusion), channel_id=1, source_target_pairs={{0,2},{2,4},{4,6},{6,0},{1,7},{3,1},{5,3},{7,5},{8,10},{10,12},{12... | collective-permute-start | bytes 2359304 | tf_op jit(solution)/shard_map/ppermute | solution.py:147
  102.3 8.0 %collective-permute-done.10 = bf16[1536,256]{0,1:T(8,128)(2,1)S(1)} collective-permute-done((bf16[1536,256]{0,1:T(8,128)(2,1)S(1)}, bf16[1536,256]{0,1:T(8,128)(2,1)S(1)}, u32[]{:S(2)}, u32[]{:S(2)}) %collective-permute-start.10) | collective-permute-done | bytes 786464 | tf_op jit(solution)/shard_map/ppermute | solution.py:147
  110.4 1.7 %collective-permute-start.11 = (bf16[1536,256]{0,1:T(8,128)(2,1)S(1)}, bf16[1536,256]{0,1:T(8,128)(2,1)S(1)}, u32[]{:S(2)}, u32[]{:S(2)}) collective-permute-start(bf16[1536,256]{0,1:T(8,128)(2,1)S(1)} %collective-permute-done.10), channel_id=1, source_target_pairs={{0,1},{1,0},{2,3},{3,2},{4,5},{5,4},{6,7},{7,6},{8,9},{9,8},{10,11... | collective-permute-start | bytes 2359304 | tf_op jit(solution)/shard_map/ppermute | solution.py:148
  112.5 0.8 fusion.20
  113.9 1.3 %fusion.7 = bf16[1536,256]{1,0:T(8,128)(2,1)} fusion(f32[1536,256]{1,0:T(8,128)S(1)} %fusion.6, bf16[1536,256]{0,1:T(8,128)(2,1)S(1)} %collective-permute-done.11, bf16[8,256,256]{2,1,0:T(8,128)(2,1)S(1)} %bitcast_dynamic-update-slice_fusion, s32[]{:T(128)S(6)} %select_n.244), kind=kOutput, calls=%fused_computation.11 | convolution fusion | flops 202113024 | bytes 3276804 | tf_op jit(solution)/shard_map/dot_general | solution.py:125
  (60 shorter events, 7.1 us)
Async XLA Ops:
  18.1 26.2 %copy-start.3 = (f32[16]{0:T(128)S(1)}, f32[16]{0:T(128)}, u32[]{:S(2)}) copy-start(f32[16]{0:T(128)} %fusion.80) | copy-start | bytes 196
  18.1 26.4 %copy-start.5 = (s32[12]{0:T(128)S(1)}, s32[12]{0:T(128)}, u32[]{:S(2)}) copy-start(s32[12]{0:T(128)} %dynamic-slice_reduce_fusion) | copy-start | bytes 148
  47.2 3.7 %copy-start.1 = (pred[128,128]{1,0:T(8,128)(4,1)S(1)}, pred[128,128]{1,0:T(8,128)(4,1)}, u32[]{:S(2)}) copy-start(pred[128,128]{1,0:T(8,128)(4,1)} %iota_compare_fusion) | copy-start | bytes 49156
  47.2 3.7 %copy-start.4 = (f32[12]{0:T(128)S(1)}, f32[12]{0:T(128)}, u32[]{:S(2)}) copy-start(f32[12]{0:T(128)} %get-tuple-element.49) | copy-start | bytes 148
  48.7 5.9 %copy-start = (bf16[12,128,128]{2,0,1:T(8,128)(2,1)S(1)}, bf16[12,128,128]{2,0,1:T(8,128)(2,1)}, u32[]{:S(2)}) copy-start(bf16[12,128,128]{2,0,1:T(8,128)(2,1)} %get-tuple-element.66) | copy-start | bytes 1179652
  51.0 4.8 %copy-start.2 = (pred[128,128]{1,0:T(8,128)(4,1)S(1)}, pred[128,128]{1,0:T(8,128)(4,1)}, u32[]{:S(2)}) copy-start(pred[128,128]{1,0:T(8,128)(4,1)} %iota_compare_fusion) | copy-start | bytes 49156
  57.7 35.8 %collective-permute-start.7 = (bf16[1536,256]{0,1:T(8,128)(2,1)S(1)}, bf16[1536,256]{0,1:T(8,128)(2,1)S(1)}, u32[]{:S(2)}, u32[]{:S(2)}) collective-permute-start(bf16[1536,256]{0,1:T(8,128)(2,1)S(1)} %fusion.10), channel_id=1, source_target_pairs={{0,2},{1,3},{2,4},{3,5},{4,6},{5,7},{6,0},{7,1},{8,10},{9,11},{10,... | collective-permute-start | bytes 2359304 | tf_op jit(solution)/shard_map/ppermute | solution.py:127
  59.4 35.1 %collective-permute-start.8 = (bf16[1536,256]{0,1:T(8,128)(2,1)S(1)}, bf16[1536,256]{0,1:T(8,128)(2,1)S(1)}, u32[]{:S(2)}, u32[]{:S(2)}) collective-permute-start(bf16[1536,256]{0,1:T(8,128)(2,1)S(1)} %fusion.10), channel_id=1, source_target_pairs={{0,6},{1,7},{2,0},{3,1},{4,2},{5,3},{6,4},{7,5},{8,14},{9,15},{10,... | collective-permute-start | bytes 2359304 | tf_op jit(solution)/shard_map/ppermute | solution.py:128
  65.7 21.3 %collective-permute-start = (bf16[256,256]{1,0:T(8,128)(2,1)}, bf16[256,256]{1,0:T(8,128)(2,1)}, u32[]{:S(2)}, u32[]{:S(2)}) collective-permute-start(bf16[256,256]{1,0:T(8,128)(2,1)} %bitcast.22), channel_id=1, source_target_pairs={{0,1},{1,2},{2,3},{3,4},{4,5},{5,6},{6,7},{7,0},{8,9},{9,10},{10,1... | collective-permute-start | bytes 393224 | tf_op jit(solution)/shard_map/ppermute | solution.py:135
  73.2 15.5 %collective-permute-start.1 = (bf16[256,256]{1,0:T(8,128)(2,1)}, bf16[256,256]{1,0:T(8,128)(2,1)}, u32[]{:S(2)}, u32[]{:S(2)}) collective-permute-start(bf16[256,256]{1,0:T(8,128)(2,1)} %bitcast.24), channel_id=1, source_target_pairs={{0,2},{1,3},{2,4},{3,5},{4,6},{5,7},{6,0},{7,1},{8,10},{9,11},{10,... | collective-permute-start | bytes 393224 | tf_op jit(solution)/shard_map/ppermute | solution.py:135
  76.4 15.8 %collective-permute-start.2 = (bf16[256,256]{1,0:T(8,128)(2,1)}, bf16[256,256]{1,0:T(8,128)(2,1)}, u32[]{:S(2)}, u32[]{:S(2)}) collective-permute-start(bf16[256,256]{1,0:T(8,128)(2,1)} %bitcast.26), channel_id=1, source_target_pairs={{0,3},{1,4},{2,5},{3,6},{4,7},{5,0},{6,1},{7,2},{8,11},{9,12},{10,... | collective-permute-start | bytes 393224 | tf_op jit(solution)/shard_map/ppermute | solution.py:135
  87.0 7.7 %collective-permute-start.3 = (bf16[256,256]{1,0:T(8,128)(2,1)}, bf16[256,256]{1,0:T(8,128)(2,1)S(1)}, u32[]{:S(2)}, u32[]{:S(2)}) collective-permute-start(bf16[256,256]{1,0:T(8,128)(2,1)} %bitcast.106), channel_id=1, source_target_pairs={{0,4},{1,5},{2,6},{3,7},{4,0},{5,1},{6,2},{7,3},{8,12},{9,13},{10,... | collective-permute-start | bytes 393224 | tf_op jit(solution)/shard_map/ppermute | solution.py:135
  88.7 6.7 %collective-permute-start.4 = (bf16[256,256]{1,0:T(8,128)(2,1)}, bf16[256,256]{1,0:T(8,128)(2,1)S(1)}, u32[]{:S(2)}, u32[]{:S(2)}) collective-permute-start(bf16[256,256]{1,0:T(8,128)(2,1)} %bitcast.105), channel_id=1, source_target_pairs={{0,5},{1,6},{2,7},{3,0},{4,1},{5,2},{6,3},{7,4},{8,13},{9,14},{10,... | collective-permute-start | bytes 393224 | tf_op jit(solution)/shard_map/ppermute | solution.py:135
  92.3 5.9 %collective-permute-start.5 = (bf16[256,256]{1,0:T(8,128)(2,1)}, bf16[256,256]{1,0:T(8,128)(2,1)S(1)}, u32[]{:S(2)}, u32[]{:S(2)}) collective-permute-start(bf16[256,256]{1,0:T(8,128)(2,1)} %bitcast.104), channel_id=1, source_target_pairs={{0,6},{1,7},{2,0},{3,1},{4,2},{5,3},{6,4},{7,5},{8,14},{9,15},{10,... | collective-permute-start | bytes 393224 | tf_op jit(solution)/shard_map/ppermute | solution.py:135
  93.5 7.9 %collective-permute-start.6 = (bf16[256,256]{1,0:T(8,128)(2,1)}, bf16[256,256]{1,0:T(8,128)(2,1)S(1)}, u32[]{:S(2)}, u32[]{:S(2)}) collective-permute-start(bf16[256,256]{1,0:T(8,128)(2,1)} %bitcast.103), channel_id=1, source_target_pairs={{0,7},{1,0},{2,1},{3,2},{4,3},{5,4},{6,5},{7,6},{8,15},{9,8},{10,9... | collective-permute-start | bytes 393224 | tf_op jit(solution)/shard_map/ppermute | solution.py:135
  94.6 17.8 %collective-permute-start.9 = (bf16[1536,768]{0,1:T(8,128)(2,1)S(1)}, bf16[1536,768]{0,1:T(8,128)(2,1)S(1)}, u32[]{:S(2)}, u32[]{:S(2)}) collective-permute-start(bf16[1536,768]{0,1:T(8,128)(2,1)S(1)} %pad_maximum_fusion), channel_id=1, source_target_pairs={{0,1},{1,0},{2,3},{3,2},{4,5},{5,4},{6,7},{7,6},{8,9},{9,8},{10,11... | collective-permute-start | bytes 7077896 | tf_op jit(solution)/shard_map/ppermute | solution.py:143
  98.3 12.0 %collective-permute-start.10 = (bf16[1536,256]{0,1:T(8,128)(2,1)S(1)}, bf16[1536,256]{0,1:T(8,128)(2,1)S(1)}, u32[]{:S(2)}, u32[]{:S(2)}) collective-permute-start(bf16[1536,256]{0,1:T(8,128)(2,1)S(1)} %broadcast_select_fusion), channel_id=1, source_target_pairs={{0,2},{2,4},{4,6},{6,0},{1,7},{3,1},{5,3},{7,5},{8,10},{10,12},{12... | collective-permute-start | bytes 2359304 | tf_op jit(solution)/shard_map/ppermute | solution.py:147
  110.4 3.6 %collective-permute-start.11 = (bf16[1536,256]{0,1:T(8,128)(2,1)S(1)}, bf16[1536,256]{0,1:T(8,128)(2,1)S(1)}, u32[]{:S(2)}, u32[]{:S(2)}) collective-permute-start(bf16[1536,256]{0,1:T(8,128)(2,1)S(1)} %collective-permute-done.10), channel_id=1, source_target_pairs={{0,1},{1,0},{2,3},{3,2},{4,5},{5,4},{6,7},{7,6},{8,9},{9,8},{10,11... | collective-permute-start | bytes 2359304 | tf_op jit(solution)/shard_map/ppermute | solution.py:148

commit v18 on v17

--- a/solution.py
+++ b/solution.py
@@ -126,11 +126,11 @@
 
     from_below = lax.ppermute(mixed, TP, shifted(1))
     from_above = lax.ppermute(mixed, TP, shifted(chip_count - 1))
-    mixed, w_out = lax.optimization_barrier((mixed, w_out))
-    out_blocks = w_out.reshape(local_width, tp_count, local_width)
+    out_blocks = jnp.transpose(w_out.reshape(local_width, tp_count, local_width), (1, 0, 2))
+    mixed, out_blocks = lax.optimization_barrier((mixed, out_blocks))
     w_out_cols = jnp.zeros((tp_count, local_width, local_width), w_out.dtype)
     for shift in range(tp_count):
-        piece = lax.dynamic_index_in_dim(out_blocks, (tp_index + shift) % tp_count, 1, False)
+        piece = lax.dynamic_index_in_dim(out_blocks, (tp_index + shift) % tp_count, 0, False)
         if shift:
             piece = lax.ppermute(piece, TP, [(i, (i + shift) % tp_count) for i in range(tp_count)])
         w_out_cols = lax.dynamic_update_index_in_dim(

time: 116 us -> 122 us (1.052)
  waiting for transfers between devices: 11.6 us -> 25 us
  local copies, waits for them, and re-layouts: 25.6 us -> 12.8 us
  starting transfers between devices: 22.8 us -> 27.4 us
    ppermute x7, waiting for transfers between devices: 3.46 us -> 16.5 us  [layer(): lax.ppermute(piece, TP, [(i, (i + shift) % tp_count) for i in range(tp_co...]
    dynamic_slice x9, local copies, waits for them, and re-layouts: 13.3 us -> 2.18 us  [layer(): lax.dynamic_index_in_dim(out_blocks, (tp_index + shift) % tp_count, 0, Fa...]
    dynamic_update_slice x8, local copies, waits for them, and re-layouts: 3.71 us -> 1.01 us  [layer(): lax.dynamic_update_index_in_dim(w_out_cols, piece, (tp_index - shift) % t...]
    ppermute x7, starting transfers between devices: 14.1 us -> 16.2 us  [layer(): lax.ppermute(piece, TP, [(i, (i + shift) % tp_count) for i in range(tp_co...]
    ppermute x1, starting transfers between devices: 0.1 us -> 2.22 us  [layer(): sibling_first = lax.ppermute(first, 'tc', [(0, 1), (1, 0)])]
    ppermute x1, starting transfers between devices: 1.68 us -> 3.48 us  [layer(): sibling_relayed = lax.ppermute(relayed, 'tc', [(0, 1), (1, 0)])]
    unnamed x12 -> x13, local copies, waits for them, and re-layouts: 0.02 us -> 1.5 us
    optimization_barrier x1 -> x0, local copies, waits for them, and re-layouts: 1.47 us -> none  [layer(): mixed, w_out = lax.optimization_barrier((mixed, w_out))]
  transfers between devices with their start and end apart: 12 -> 12, of which waited for: 4 -> 4; matrix products, arithmetic and copies ran while one was open for 19% -> 4% of each run, Pallas kernels for 0% -> 0%
where the time goes in v18:
time: 122 us; the launch traced here: 121 us
  starting transfers between devices  27.4 us (22%)
  waiting for transfers between devices  25 us (20%)
  blocking collectives  23.9 us (20%)
  matrix products  23.5 us (19%)
  local copies, waits for them, and re-layouts  12.8 us (10%)
  other arithmetic  7.81 us (6%)
    ppermute x7, waiting for transfers between devices, layer(): lax.ppermute(piece, TP, [(i, (i + shift) % tp_count) for i in range(tp_co...  16.5 us
    ppermute x7, starting transfers between devices, layer(): lax.ppermute(piece, TP, [(i, (i + shift) % tp_count) for i in range(tp_co...  16.2 us
    all_gather x1, blocking collectives, layer(): row_tails = lax.all_gather(tail, 'sx', axis=0, tiled=False)  12.8 us
    all_gather x1, blocking collectives, layer(): row_sums = lax.all_gather(row_sum, 'sy', axis=0, tiled=False)  11.2 us
    ppermute x1, waiting for transfers between devices, layer(): lax.ppermute(jnp.where(core_at == 0, from_below, from_above), TP, forward)  8.27 us
    dot_general x1, matrix products, layer(): jnp.dot(tokens, jnp.concatenate([w_key, w_value, w_query], axis=1), prefe...  8.15 us
    dot_general x2, matrix products, layer(): jnp.einsum('cts,cse->cte', weights, value_groups[:, :, cut], preferred_el...  4.82 us
    ppermute x1, starting transfers between devices, layer(): sibling_relayed = lax.ppermute(relayed, 'tc', [(0, 1), (1, 0)])  3.48 us
  transfers between devices with their start and end apart: 12, of which 4 were waited for; matrix products, arithmetic and copies ran while one was open for 4% of the time, Pallas kernels for 0%

profile of v18, /device:TPU:1, one launch (start us, length us, event | category | flops | bytes accessed | tf_op | source)
XLA Modules:
  0.0 121.0 jit_solution(1645120998855203157)
XLA Ops:
  0.0 0.9 multiply_reduce_fusion.3
  0.9 1.3 %multiply_rsqrt_fusion = (f32[12]{0:T(128)}, s32[12]{0:T(128)S(1)}) fusion(s32[12]{0:T(128)S(1)} %multiply_reduce_fusion.3, s32[192]{0:T(256)} %param.19, s32[]{:T(128)S(6)} %select_n.192), kind=kLoop, calls=%fused_computation.125 | loop fusion | flops 36 | bytes 196 | tf_op jit(solution)/shard_map/rsqrt | solution.py:91
  2.2 8.2 %convolution_bitcast_fusion = bf16[1536,768]{0,1:T(8,128)(2,1)S(1)} fusion(bf16[1536,2048]{1,0:T(8,128)(2,1)} %param.13, bf16[2048,256]{1,0:T(8,128)(2,1)} %param.14, bf16[2048,256]{1,0:T(8,128)(2,1)} %param.16, bf16[2048,256]{1,0:T(8,128)(2,1)} %param.15), kind=kOutput, calls=%fused_computation | convolution fusion | flops 4841275392 | bytes 11796480 | tf_op jit(solution)/shard_map/dot_general | solution.py:34
  10.4 0.3 fusion.9
  11.2 0.3 fusion.15
  11.5 1.1 fusion.16
  12.6 0.7 fusion.73
  13.5 0.8 fusion.80
  14.3 0.6 iota_compare_fusion
  14.9 1.4 %dynamic-slice_reduce_fusion = s32[12]{0:T(128)} fusion(s32[192,192]{1,0:T(8,128)} %param.18, s32[]{:T(128)S(6)} %select_n.193), kind=kLoop, calls=%fused_computation.94 | loop fusion | bytes 100 | tf_op jit(solution)/shard_map/slice | solution.py:80
  16.3 0.8 dynamic-slice_bitcast_fusion.3
  17.1 1.1 pad_maximum_fusion.1
  18.2 0.5 fusion.17
  18.7 12.8 %all-gather = f32[8,128,128]{2,1,0:T(8,128)} all-gather(f32[2,128,128]{2,1,0:T(8,128)S(1)} %bitcast.100), channel_id=2, replica_groups=mesh['sy'=4,'sx'=4,'tz'=4,'tc'=2] {'sx'}, dimensions={0}, use_global_device_ids=true | all-gather | bytes 655360 | tf_op jit(solution)/shard_map/all_gather | solution.py:66
  31.9 1.2 multiply_reduce_fusion.1
  33.1 11.2 %all-gather.1 = f32[8,128,128]{2,1,0:T(8,128)} all-gather(f32[2,128,128]{2,1,0:T(8,128)S(1)} %get-tuple-element.45), channel_id=3, replica_groups=mesh['sy'=4,'sx'=4,'tz'=4,'tc'=2] {'sy'}, dimensions={0}, use_global_device_ids=true | all-gather | bytes 655360 | tf_op jit(solution)/shard_map/all_gather | solution.py:74
  44.6 1.2 multiply_reduce_fusion
  45.8 1.4 %add_convert_fusion = bf16[12,2,128,128]{3,0,2,1:T(8,128)(2,1)S(1)} fusion(bf16[12,2,128,128]{3,2,0,1:T(8,128)(2,1)S(1)} %pad_maximum_fusion.1, f32[2,128,128]{2,1,0:T(8,128)S(1)} %add.264, f32[12]{0:T(128)S(1)} %convert_element_type.47, s32[192,192]{1,0:T(8,128)} %param.18, s32[]{:T(128)S(6)} %select_n.193), kind=kOutput, calls=%fused_computation.13 | convolution fusion | flops 10616976 | bytes 1712180 | tf_op jit(solution)/shard_map/ce,ehij->chij/dot_general | solution.py:82
  47.2 1.2 slice_bitcast_fusion.1
  48.7 2.2 %fusion.28 = f32[12,128,128]{2,1,0:T(8,128)} fusion(bf16[12,128,128]{2,0,1:T(8,128)(2,1)} %get-tuple-element.65, bf16[12,128,256]{2,1,0:T(8,128)(2,1)S(1)} %bitcast.94), kind=kOutput, calls=%fused_computation.51 | convolution fusion | flops 50331648 | bytes 1572864 | tf_op jit(solution)/shard_map/ctd,cde->cte/dot_general | solution.py:96
  51.0 2.4 %fusion.11 = bf16[12,128,128]{2,1,0:T(8,128)(2,1)} fusion(f32[12,128,128]{2,1,0:T(8,128)} %fusion.28, f32[12]{0:T(128)S(1)} %copy-done.4, pred[128,128]{1,0:T(8,128)(4,1)S(1)} %copy-done.1, bf16[12,128,256]{2,1,0:T(8,128)(2,1)S(1)} %bitcast.92, bf16[12,128,256]{2,1,0:T(8,128)(2,1)S(1)} %bitcast.88, bf16[12,128,256]{2,1,0:T(8,128)(2,1)S(1)} %bitcast.95), kind=kOutput, calls=%fused_computation.25 | convolution fusion | flops 101646336 | bytes 2376192 | tf_op jit(solution)/shard_map/cts,cse->cte/dot_general | solution.py:103
  53.4 1.2 copy.67
  54.6 1.1 fusion.26
  55.7 2.4 %fusion.12 = bf16[12,128,128]{2,1,0:T(8,128)(2,1)} fusion(f32[12,128,128]{2,1,0:T(8,128)} %fusion.26, f32[12]{0:T(128)S(1)} %copy-done.4, pred[128,128]{1,0:T(8,128)(4,1)S(1)} %copy-done.2, bf16[12,128,256]{2,1,0:T(8,128)(2,1)S(1)} %bitcast.97, bf16[12,128,256]{2,1,0:T(8,128)(2,1)S(1)} %bitcast.93, bf16[12,128,256]{2,1,0:T(8,128)(2,1)S(1)} %bitcast.89), kind=kOutput, calls=%fused_computation.26 | convolution fusion | flops 101646336 | bytes 2376192 | tf_op jit(solution)/shard_map/cts,cse->cte/dot_general | solution.py:103
  58.1 1.2 copy.68
  59.3 1.5 %copy.69 = bf16[256,2048]{0,1:T(8,128)(2,1)S(1)} copy(bf16[256,2048]{1,0:T(8,128)(2,1)} %param.17) | data formatting | bytes 2097152 | tf_op args[4]
  61.0 0.8 copy.71
  61.8 7.6 %collective-permute-start = (bf16[256,256]{1,0:T(8,128)(2,1)}, bf16[256,256]{1,0:T(8,128)(2,1)S(1)}, u32[]{:S(2)}, u32[]{:S(2)}) collective-permute-start(bf16[256,256]{1,0:T(8,128)(2,1)} %bitcast.22), channel_id=1, source_target_pairs={{0,1},{1,2},{2,3},{3,4},{4,5},{5,6},{6,7},{7,0},{8,9},{9,10},{10,1... | collective-permute-start | bytes 393224 | tf_op jit(solution)/shard_map/ppermute | solution.py:135
  69.4 1.6 %collective-permute-start.7 = (bf16[1536,256]{0,1:T(8,128)(2,1)S(1)}, bf16[1536,256]{0,1:T(8,128)(2,1)S(1)}, u32[]{:S(2)}, u32[]{:S(2)}) collective-permute-start(bf16[1536,256]{0,1:T(8,128)(2,1)S(1)} %fusion.10), channel_id=1, source_target_pairs={{0,2},{1,3},{2,4},{3,5},{4,6},{5,7},{6,0},{7,1},{8,10},{9,11},{10,... | collective-permute-start | bytes 2359304 | tf_op jit(solution)/shard_map/ppermute | solution.py:127
  71.0 1.1 collective-permute-start.8
  72.1 0.7 copy.72
  72.8 0.4 collective-permute-start.1
  73.4 2.6 %collective-permute-start.2 = (bf16[256,256]{1,0:T(8,128)(2,1)S(1)}, bf16[256,256]{1,0:T(8,128)(2,1)S(1)}, u32[]{:S(2)}, u32[]{:S(2)}) collective-permute-start(bf16[256,256]{1,0:T(8,128)(2,1)S(1)} %bitcast.103), channel_id=1, source_target_pairs={{0,3},{1,4},{2,5},{3,6},{4,7},{5,0},{6,1},{7,2},{8,11},{9,12},{10,... | collective-permute-start | bytes 393224 | tf_op jit(solution)/shard_map/ppermute | solution.py:135
  76.8 16.2 %collective-permute-done.1 = bf16[256,256]{1,0:T(8,128)(2,1)} collective-permute-done((bf16[256,256]{1,0:T(8,128)(2,1)}, bf16[256,256]{1,0:T(8,128)(2,1)}, u32[]{:S(2)}, u32[]{:S(2)}) %collective-permute-start.1) | collective-permute-done | bytes 131104 | tf_op jit(solution)/shard_map/ppermute | solution.py:135
  93.0 1.8 %collective-permute-start.4 = (bf16[256,256]{1,0:T(8,128)(2,1)S(1)}, bf16[256,256]{1,0:T(8,128)(2,1)S(1)}, u32[]{:S(2)}, u32[]{:S(2)}) collective-permute-start(bf16[256,256]{1,0:T(8,128)(2,1)S(1)} %bitcast.106), channel_id=1, source_target_pairs={{0,5},{1,6},{2,7},{3,0},{4,1},{5,2},{6,3},{7,4},{8,13},{9,14},{10,... | collective-permute-start | bytes 393224 | tf_op jit(solution)/shard_map/ppermute | solution.py:135
  94.9 0.9 bitcast_dynamic-update-slice_fusion.5
  95.8 1.9 %collective-permute-start.5 = (bf16[256,256]{1,0:T(8,128)(2,1)S(1)}, bf16[256,256]{1,0:T(8,128)(2,1)S(1)}, u32[]{:S(2)}, u32[]{:S(2)}) collective-permute-start(bf16[256,256]{1,0:T(8,128)(2,1)S(1)} %bitcast.105), channel_id=1, source_target_pairs={{0,6},{1,7},{2,0},{3,1},{4,2},{5,3},{6,4},{7,5},{8,14},{9,15},{10,... | collective-permute-start | bytes 393224 | tf_op jit(solution)/shard_map/ppermute | solution.py:135
  97.8 1.8 %collective-permute-start.6 = (bf16[256,256]{1,0:T(8,128)(2,1)S(1)}, bf16[256,256]{1,0:T(8,128)(2,1)S(1)}, u32[]{:S(2)}, u32[]{:S(2)}) collective-permute-start(bf16[256,256]{1,0:T(8,128)(2,1)S(1)} %bitcast.104), channel_id=1, source_target_pairs={{0,7},{1,0},{2,1},{3,2},{4,3},{5,4},{6,5},{7,6},{8,15},{9,8},{10,9... | collective-permute-start | bytes 393224 | tf_op jit(solution)/shard_map/ppermute | solution.py:135
  99.7 2.2 %collective-permute-start.9 = (bf16[1536,768]{0,1:T(8,128)(2,1)S(1)}, bf16[1536,768]{0,1:T(8,128)(2,1)S(1)}, u32[]{:S(2)}, u32[]{:S(2)}) collective-permute-start(bf16[1536,768]{0,1:T(8,128)(2,1)S(1)} %pad_maximum_fusion), channel_id=1, source_target_pairs={{0,1},{1,0},{2,3},{3,2},{4,5},{5,4},{6,7},{7,6},{8,9},{9,8},{10,11... | collective-permute-start | bytes 7077896 | tf_op jit(solution)/shard_map/ppermute | solution.py:143
  102.1 2.8 %collective-permute-start.10 = (bf16[1536,256]{0,1:T(8,128)(2,1)S(1)}, bf16[1536,256]{0,1:T(8,128)(2,1)S(1)}, u32[]{:S(2)}, u32[]{:S(2)}) collective-permute-start(bf16[1536,256]{0,1:T(8,128)(2,1)S(1)} %broadcast_select_fusion), channel_id=1, source_target_pairs={{0,2},{2,4},{4,6},{6,0},{1,7},{3,1},{5,3},{7,5},{8,10},{10,12},{12... | collective-permute-start | bytes 2359304 | tf_op jit(solution)/shard_map/ppermute | solution.py:147
  105.2 0.4 fusion.54
  105.6 0.4 convolution_add_fusion.2
  106.1 8.3 %collective-permute-done.10 = bf16[1536,256]{0,1:T(8,128)(2,1)S(1)} collective-permute-done((bf16[1536,256]{0,1:T(8,128)(2,1)S(1)}, bf16[1536,256]{0,1:T(8,128)(2,1)S(1)}, u32[]{:S(2)}, u32[]{:S(2)}) %collective-permute-start.10) | collective-permute-done | bytes 786464 | tf_op jit(solution)/shard_map/ppermute | solution.py:147
  114.3 3.5 %collective-permute-start.11 = (bf16[1536,256]{0,1:T(8,128)(2,1)S(1)}, bf16[1536,256]{0,1:T(8,128)(2,1)S(1)}, u32[]{:S(2)}, u32[]{:S(2)}) collective-permute-start(bf16[1536,256]{0,1:T(8,128)(2,1)S(1)} %collective-permute-done.10), channel_id=1, source_target_pairs={{0,1},{1,0},{2,3},{3,2},{4,5},{5,4},{6,7},{7,6},{8,9},{9,8},{10,11... | collective-permute-start | bytes 2359304 | tf_op jit(solution)/shard_map/ppermute | solution.py:148
  117.8 0.4 fusion.51
  118.3 0.8 fusion.20
  119.1 0.4 fusion.6
  119.7 1.3 %fusion.7 = bf16[1536,256]{1,0:T(8,128)(2,1)} fusion(f32[1536,256]{1,0:T(8,128)S(1)} %fusion.6, bf16[1536,256]{0,1:T(8,128)(2,1)S(1)} %collective-permute-done.11, bf16[8,256,256]{2,1,0:T(8,128)(2,1)S(1)} %bitcast_dynamic-update-slice_fusion, s32[]{:T(128)S(6)} %select_n.243), kind=kOutput, calls=%fused_computation.11 | convolution fusion | flops 202113024 | bytes 3276804 | tf_op jit(solution)/shard_map/dot_general | solution.py:125
  (60 shorter events, 3.7 us)
Async XLA Ops:
  18.1 26.2 %copy-start.3 = (f32[16]{0:T(128)S(1)}, f32[16]{0:T(128)}, u32[]{:S(2)}) copy-start(f32[16]{0:T(128)} %fusion.80) | copy-start | bytes 196
  18.1 26.4 %copy-start.5 = (s32[12]{0:T(128)S(1)}, s32[12]{0:T(128)}, u32[]{:S(2)}) copy-start(s32[12]{0:T(128)} %dynamic-slice_reduce_fusion) | copy-start | bytes 148
  47.2 3.7 %copy-start.1 = (pred[128,128]{1,0:T(8,128)(4,1)S(1)}, pred[128,128]{1,0:T(8,128)(4,1)}, u32[]{:S(2)}) copy-start(pred[128,128]{1,0:T(8,128)(4,1)} %iota_compare_fusion) | copy-start | bytes 49156
  47.2 3.7 %copy-start.4 = (f32[12]{0:T(128)S(1)}, f32[12]{0:T(128)}, u32[]{:S(2)}) copy-start(f32[12]{0:T(128)} %get-tuple-element.49) | copy-start | bytes 148
  48.7 5.9 %copy-start = (bf16[12,128,128]{2,0,1:T(8,128)(2,1)S(1)}, bf16[12,128,128]{2,0,1:T(8,128)(2,1)}, u32[]{:S(2)}) copy-start(bf16[12,128,128]{2,0,1:T(8,128)(2,1)} %get-tuple-element.66) | copy-start | bytes 1179652
  51.0 4.8 %copy-start.2 = (pred[128,128]{1,0:T(8,128)(4,1)S(1)}, pred[128,128]{1,0:T(8,128)(4,1)}, u32[]{:S(2)}) copy-start(pred[128,128]{1,0:T(8,128)(4,1)} %iota_compare_fusion) | copy-start | bytes 49156
  61.8 14.8 %collective-permute-start = (bf16[256,256]{1,0:T(8,128)(2,1)}, bf16[256,256]{1,0:T(8,128)(2,1)S(1)}, u32[]{:S(2)}, u32[]{:S(2)}) collective-permute-start(bf16[256,256]{1,0:T(8,128)(2,1)} %bitcast.22), channel_id=1, source_target_pairs={{0,1},{1,2},{2,3},{3,4},{4,5},{5,6},{6,7},{7,0},{8,9},{9,10},{10,1... | collective-permute-start | bytes 393224 | tf_op jit(solution)/shard_map/ppermute | solution.py:135
  69.4 28.3 %collective-permute-start.7 = (bf16[1536,256]{0,1:T(8,128)(2,1)S(1)}, bf16[1536,256]{0,1:T(8,128)(2,1)S(1)}, u32[]{:S(2)}, u32[]{:S(2)}) collective-permute-start(bf16[1536,256]{0,1:T(8,128)(2,1)S(1)} %fusion.10), channel_id=1, source_target_pairs={{0,2},{1,3},{2,4},{3,5},{4,6},{5,7},{6,0},{7,1},{8,10},{9,11},{10,... | collective-permute-start | bytes 2359304 | tf_op jit(solution)/shard_map/ppermute | solution.py:127
  71.0 28.5 %collective-permute-start.8 = (bf16[1536,256]{0,1:T(8,128)(2,1)S(1)}, bf16[1536,256]{0,1:T(8,128)(2,1)S(1)}, u32[]{:S(2)}, u32[]{:S(2)}) collective-permute-start(bf16[1536,256]{0,1:T(8,128)(2,1)S(1)} %fusion.10), channel_id=1, source_target_pairs={{0,6},{1,7},{2,0},{3,1},{4,2},{5,3},{6,4},{7,5},{8,14},{9,15},{10,... | collective-permute-start | bytes 2359304 | tf_op jit(solution)/shard_map/ppermute | solution.py:128
  72.8 20.2 %collective-permute-start.1 = (bf16[256,256]{1,0:T(8,128)(2,1)}, bf16[256,256]{1,0:T(8,128)(2,1)}, u32[]{:S(2)}, u32[]{:S(2)}) collective-permute-start(bf16[256,256]{1,0:T(8,128)(2,1)} %bitcast.24), channel_id=1, source_target_pairs={{0,2},{1,3},{2,4},{3,5},{4,6},{5,7},{6,0},{7,1},{8,10},{9,11},{10,... | collective-permute-start | bytes 393224 | tf_op jit(solution)/shard_map/ppermute | solution.py:135
  73.4 22.4 %collective-permute-start.2 = (bf16[256,256]{1,0:T(8,128)(2,1)S(1)}, bf16[256,256]{1,0:T(8,128)(2,1)S(1)}, u32[]{:S(2)}, u32[]{:S(2)}) collective-permute-start(bf16[256,256]{1,0:T(8,128)(2,1)S(1)} %bitcast.103), channel_id=1, source_target_pairs={{0,3},{1,4},{2,5},{3,6},{4,7},{5,0},{6,1},{7,2},{8,11},{9,12},{10,... | collective-permute-start | bytes 393224 | tf_op jit(solution)/shard_map/ppermute | solution.py:135
  76.7 25.2 %collective-permute-start.3 = (bf16[256,256]{1,0:T(8,128)(2,1)S(1)}, bf16[256,256]{1,0:T(8,128)(2,1)S(1)}, u32[]{:S(2)}, u32[]{:S(2)}) collective-permute-start(bf16[256,256]{1,0:T(8,128)(2,1)S(1)} %bitcast.107), channel_id=1, source_target_pairs={{0,4},{1,5},{2,6},{3,7},{4,0},{5,1},{6,2},{7,3},{8,12},{9,13},{10,... | collective-permute-start | bytes 393224 | tf_op jit(solution)/shard_map/ppermute | solution.py:135
  93.0 8.9 %collective-permute-start.4 = (bf16[256,256]{1,0:T(8,128)(2,1)S(1)}, bf16[256,256]{1,0:T(8,128)(2,1)S(1)}, u32[]{:S(2)}, u32[]{:S(2)}) collective-permute-start(bf16[256,256]{1,0:T(8,128)(2,1)S(1)} %bitcast.106), channel_id=1, source_target_pairs={{0,5},{1,6},{2,7},{3,0},{4,1},{5,2},{6,3},{7,4},{8,13},{9,14},{10,... | collective-permute-start | bytes 393224 | tf_op jit(solution)/shard_map/ppermute | solution.py:135
  95.8 6.2 %collective-permute-start.5 = (bf16[256,256]{1,0:T(8,128)(2,1)S(1)}, bf16[256,256]{1,0:T(8,128)(2,1)S(1)}, u32[]{:S(2)}, u32[]{:S(2)}) collective-permute-start(bf16[256,256]{1,0:T(8,128)(2,1)S(1)} %bitcast.105), channel_id=1, source_target_pairs={{0,6},{1,7},{2,0},{3,1},{4,2},{5,3},{6,4},{7,5},{8,14},{9,15},{10,... | collective-permute-start | bytes 393224 | tf_op jit(solution)/shard_map/ppermute | solution.py:135
  97.8 7.4 %collective-permute-start.6 = (bf16[256,256]{1,0:T(8,128)(2,1)S(1)}, bf16[256,256]{1,0:T(8,128)(2,1)S(1)}, u32[]{:S(2)}, u32[]{:S(2)}) collective-permute-start(bf16[256,256]{1,0:T(8,128)(2,1)S(1)} %bitcast.104), channel_id=1, source_target_pairs={{0,7},{1,0},{2,1},{3,2},{4,3},{5,4},{6,5},{7,6},{8,15},{9,8},{10,9... | collective-permute-start | bytes 393224 | tf_op jit(solution)/shard_map/ppermute | solution.py:135
  99.7 18.6 %collective-permute-start.9 = (bf16[1536,768]{0,1:T(8,128)(2,1)S(1)}, bf16[1536,768]{0,1:T(8,128)(2,1)S(1)}, u32[]{:S(2)}, u32[]{:S(2)}) collective-permute-start(bf16[1536,768]{0,1:T(8,128)(2,1)S(1)} %pad_maximum_fusion), channel_id=1, source_target_pairs={{0,1},{1,0},{2,3},{3,2},{4,5},{5,4},{6,7},{7,6},{8,9},{9,8},{10,11... | collective-permute-start | bytes 7077896 | tf_op jit(solution)/shard_map/ppermute | solution.py:143
  102.1 12.2 %collective-permute-start.10 = (bf16[1536,256]{0,1:T(8,128)(2,1)S(1)}, bf16[1536,256]{0,1:T(8,128)(2,1)S(1)}, u32[]{:S(2)}, u32[]{:S(2)}) collective-permute-start(bf16[1536,256]{0,1:T(8,128)(2,1)S(1)} %broadcast_select_fusion), channel_id=1, source_target_pairs={{0,2},{2,4},{4,6},{6,0},{1,7},{3,1},{5,3},{7,5},{8,10},{10,12},{12... | collective-permute-start | bytes 2359304 | tf_op jit(solution)/shard_map/ppermute | solution.py:147
  114.3 5.4 %collective-permute-start.11 = (bf16[1536,256]{0,1:T(8,128)(2,1)S(1)}, bf16[1536,256]{0,1:T(8,128)(2,1)S(1)}, u32[]{:S(2)}, u32[]{:S(2)}) collective-permute-start(bf16[1536,256]{0,1:T(8,128)(2,1)S(1)} %collective-permute-done.10), channel_id=1, source_target_pairs={{0,1},{1,0},{2,3},{3,2},{4,5},{5,4},{6,7},{7,6},{8,9},{9,8},{10,11... | collective-permute-start | bytes 2359304 | tf_op jit(solution)/shard_map/ppermute | solution.py:148
